TPU v7x, 512 devices: a whole 4x8x8 slice. The times are simulated.
512 devices in a mesh: section: 8 (over x, z_lo), dp: 64 (over y, z_hi, core).
Axes of the slice: x: 4, y: 8, z: 8 (z_hi: 4, z_lo: 2; z = z_hi * 2 + z_lo), core: 2. Of those that a mesh axis runs over, the one named last changes fastest.
Arguments:
- saved_input: bfloat16 [8, 256, 4096], P('section', 'dp'), may hold values from -6 to 6
- grad_sent: bfloat16 [8, 256, 4096], P('section', 'dp'), may hold values from -6 to 6
- kept_blocks: int32 [8, 1664], P('section', 'dp'), may hold values from 0 to 63, as said below
- gate_blocks: bfloat16 [8, 1664, 128, 128], P('section', 'dp'), may hold values from -0.15625 to 0.15625
- up_blocks: bfloat16 [8, 1664, 128, 128], P('section', 'dp'), may hold values from -0.15625 to 0.15625
- down_blocks: bfloat16 [8, 1664, 128, 128], P('section', 'dp'), may hold values from -0.078125 to 0.078125
Outputs:
- grad_input: bfloat16 [8, 256, 4096], P('section', 'dp')
- grad_gate: bfloat16 [8, 1664, 128, 128], P('section', 'dp')
- grad_up: bfloat16 [8, 1664, 128, 128], P('section', 'dp')
- grad_down: bfloat16 [8, 1664, 128, 128], P('section', 'dp')
Inputs may be any that keep to these rules, and one draw needn't show every extreme that they name: `kept_blocks`: each device's 26 ids are different and increasing; an id is the band along the model width times 2 plus the block among that device's hidden units; bands keep unequal shares of their blocks.
All inputs are finite; a program needn't handle non-finite values.
Results may differ from a plain program's by a relative error of at most 0.019.
Values may be sent and summed in bfloat16 or wider, within the bound.
No kernel may reach another device: no remote copies, remote signals or barrier semaphores. Data moves between devices by JAX's collectives and lax.ppermute only.
A program may use at most 64 MiB of HBM per device.

v0:
```python
import jax
import jax.numpy as jnp
from jax import lax
from jax.sharding import PartitionSpec as P

FF = 16384


def passed_along(block, axis, distance):
    devices = range(lax.axis_size(axis))
    route = [((i - distance) % len(devices), i) for i in devices]
    return lax.ppermute(block, axis, route)


def per_device(saved_input, grad_sent, kept_blocks, gate_blocks, up_blocks, down_blocks):
    width = saved_input.shape[2]
    block = gate_blocks.shape[2]
    bands = width // block
    columns = FF // lax.axis_size("dp") // block
    ids = kept_blocks[0]
    band_ids = ids // columns
    col_ids = ids % columns
    w_gate = gate_blocks[0]
    w_up = up_blocks[0]
    w_down = down_blocks[0]
    col_onehot = (col_ids[:, None] == jnp.arange(columns, dtype=jnp.int32)[None, :]).astype(
        jnp.float32
    )
    band_onehot = (band_ids[:, None] == jnp.arange(bands, dtype=jnp.int32)[None, :]).astype(
        jnp.float32
    )

    def to_columns(partial_value):
        spread = jnp.einsum("tkc,kn->tnc", partial_value, col_onehot)
        return spread.reshape(partial_value.shape[0], columns * block)

    def pick_cols(values):
        return jnp.take(values.reshape(values.shape[0], columns, block), col_ids, axis=1)

    def pick_bands(values):
        return jnp.take(values.reshape(values.shape[0], bands, block), band_ids, axis=1)

    incoming = passed_along(grad_sent, "section", -1)
    inputs = lax.all_gather(saved_input, "dp", axis=1, tiled=True)[0]
    chosen = pick_bands(inputs)
    gate = to_columns(
        jnp.einsum("tkb,kbc->tkc", chosen, w_gate, preferred_element_type=jnp.float32)
    )
    up = to_columns(jnp.einsum("tkb,kbc->tkc", chosen, w_up, preferred_element_type=jnp.float32))
    gate, up = (gate, up)
    upstream = lax.all_gather(incoming, "dp", axis=1, tiled=True)[0]
    sig = jax.nn.sigmoid(gate)
    act = gate * sig
    hidden = (act * up).astype(jnp.bfloat16)
    grad_sel = pick_bands(upstream)
    dhid = to_columns(
        jnp.einsum("tkb,kcb->tkc", grad_sel, w_down, preferred_element_type=jnp.float32)
    )
    grad_up_act = (dhid * act).astype(jnp.bfloat16)
    grad_gate_act = (dhid * up * sig * (1.0 + gate * (1.0 - sig))).astype(jnp.bfloat16)
    input_sel = pick_bands(inputs)
    tiles_down = jnp.einsum(
        "tkc,tkb->kcb", pick_cols(hidden), grad_sel, preferred_element_type=jnp.float32
    )
    tiles_gate = jnp.einsum(
        "tkb,tkc->kbc", input_sel, pick_cols(grad_gate_act), preferred_element_type=jnp.float32
    )
    tiles_up = jnp.einsum(
        "tkb,tkc->kbc", input_sel, pick_cols(grad_up_act), preferred_element_type=jnp.float32
    )
    slots = jnp.einsum(
        "tkc,kbc->tkb", pick_cols(grad_gate_act), w_gate, preferred_element_type=jnp.float32
    )
    slots = slots + jnp.einsum(
        "tkc,kbc->tkb", pick_cols(grad_up_act), w_up, preferred_element_type=jnp.float32
    )
    spread = jnp.einsum("tkb,kr->trb", slots, band_onehot)
    whole_term = spread.reshape(grad_gate_act.shape[0], bands * block)
    summed = lax.psum_scatter(whole_term, "dp", scatter_dimension=0, tiled=True)
    grad_input = summed.astype(jnp.bfloat16)[None]
    return (
        grad_input,
        tiles_gate.astype(jnp.bfloat16)[None],
        tiles_up.astype(jnp.bfloat16)[None],
        tiles_down.astype(jnp.bfloat16)[None],
    )


def solution(mesh):
    return jax.shard_map(
        per_device,
        mesh=mesh,
        in_specs=(
            P("section", "dp", None),
            P("section", "dp", None),
            P("section", "dp"),
            P("section", "dp", None, None),
            P("section", "dp", None, None),
            P("section", "dp", None, None),
        ),
        out_specs=(
            P("section", "dp", None),
            P("section", "dp", None, None),
            P("section", "dp", None, None),
            P("section", "dp", None, None),
        ),
        check_vma=False,
    )
```

profile of v0, /device:TPU:6, one launch (start us, length us, event | category | flops | bytes accessed | tf_op | source)
XLA Modules:
  0.0 580.1 jit_solution(12546906431079961328)
XLA Ops:
  7.2 1.5 copy.54
  8.8 4.5 collective-permute-start
  13.4 1.9 collective-permute-done
  15.3 0.7 copy.49
  16.0 1.3 dynamic-slice
  17.9 0.7 compare_and_fusion
  18.6 86.3 %all-gather.5.cloned.1.call-done = bf16[1,256,4096]{2,0,1:T(2,128)(2,1)} async-done(((bf16[1,4,4096]{2,0,1:T(2,128)(2,1)}), bf16[1,256,4096]{2,0,1:T(2,128)(2,1)}) %all-gather.5.cloned.1.call-update) | async-done | bytes 2097168 | tf_op jit(solution)/shard_map/all_gather | solution.py:44
  104.9 9.2 %copy.55 = bf16[1,256,4096]{1,2,0:T(8,128)(2,1)S(1)} copy(bf16[1,256,4096]{2,0,1:T(2,128)(2,1)} %all-gather.5.cloned.1.call-done) | data formatting | bytes 4194304 | tf_op jit(solution)/shard_map/all_gather | solution.py:44
  114.1 2.9 copy.56
  117.0 2.5 gather_fusion.1
  119.5 0.7 convolution_bitcast_fusion
  120.2 1.1 fusion.2
  121.3 0.7 convolution_bitcast_fusion.1
  122.0 1.1 fusion.4
  123.0 69.7 %all-gather.3.cloned.1.call-done = bf16[1,256,4096]{2,0,1:T(2,128)(2,1)} async-done(((bf16[1,4,4096]{2,0,1:T(2,128)(2,1)}), bf16[1,256,4096]{2,0,1:T(2,128)(2,1)}) %all-gather.3.cloned.1.call-update) | async-done | bytes 2097168 | tf_op jit(solution)/shard_map/all_gather | solution.py:51
  192.8 9.2 %copy.50 = bf16[1,256,4096]{1,2,0:T(8,128)(2,1)S(1)} copy(bf16[1,256,4096]{2,0,1:T(2,128)(2,1)} %all-gather.3.cloned.1.call-done) | data formatting | bytes 4194304 | tf_op jit(solution)/shard_map/all_gather | solution.py:51
  202.0 2.9 copy.51
  204.9 2.5 gather_fusion
  207.3 2.4 convolution_bitcast_fusion.2
  209.8 1.1 fusion.6
  211.0 0.9 gather_fusion.2
  211.9 3.2 fusion.50
  215.1 2.4 fusion.15
  217.4 2.1 gather_fusion.4
  219.5 3.2 fusion.40
  222.7 0.9 gather_fusion.3
  223.6 3.3 fusion.45
  226.9 0.6 add_bitcast_fusion
  227.5 1.1 fusion
  228.7 5.7 copy.88
  234.4 338.2 %all-reduce.2 = bf16[256,4096]{1,0:T(8,128)(2,1)S(1)} all-reduce(f32[256,4096]{1,0:T(8,128)} %bitcast.154), channel_id=2, replica_groups=mesh['section'=8,'dp'=64] {'dp'}, use_global_device_ids=true, to_apply=%region_0.3.clone | all-reduce | flops 1048576 | bytes 6291456
  572.6 0.6 fusion.70
  (23 shorter events, 0.4 us)
Async XLA Ops:
  7.2 112.3 %copy-start = (bf16[1,26,128,128]{3,2,1,0:T(8,128)(2,1)S(1)}, bf16[1,26,128,128]{3,2,1,0:T(8,128)(2,1)}, u32[]{:S(2)}) copy-start(bf16[1,26,128,128]{3,2,1,0:T(8,128)(2,1)} %param.13) | copy-start | bytes 2555908
  7.2 97.7 %all-gather.5.cloned.1.call-start = ((), (), s32[]{:S(2)}) async-start(), calls=%async_computation.1 | async-start | bytes 4259840 | tf_op jit(solution)/shard_map/all_gather | solution.py:44
  8.8 184.0 %all-gather.3.cloned.1.call-start = ((), (), s32[]{:S(2)}) async-start(), calls=%async_computation | async-start | bytes 4259840 | tf_op jit(solution)/shard_map/all_gather | solution.py:51
  8.8 6.4 %collective-permute-start = (bf16[1,4,4096]{2,1,0:T(4,128)(2,1)}, bf16[1,4,4096]{2,1,0:T(4,128)(2,1)S(1)}, u32[]{:S(2)}, u32[]{:S(2)}) collective-permute-start(bf16[1,4,4096]{2,1,0:T(4,128)(2,1)} %param.11), channel_id=1, source_target_pairs={{64,0},{128,64},{192,128},{256,192},{320,256},{384,320},{448,384},... | collective-permute-start | bytes 98312 | tf_op jit(solution)/shard_map/ppermute | solution.py:12
  119.5 1.7 copy-start.2
  120.2 1.2 copy-start.5
  207.3 2.4 copy-start.3
  217.4 2.1 copy-start.4
  223.5 3.3 copy-start.1
  223.5 3.3 copy-start.6
Sparse Core Ops, SparseCore 0:
  11.9 92.9 all-gather.4
  108.8 83.9 all-gather.2
where the time goes:
time: 581 us; the launch traced here: 580 us
  blocking collectives  338 us (58%)
  waiting for transfers between devices  158 us (27%)
  local copies, waits for them, and re-layouts  42.9 us (7%)
  matrix products  20.7 us (4%)
  between operations  14.9 us (3%)
    unnamed x1, blocking collectives  338 us
    all_gather x1, waiting for transfers between devices, per_device(): inputs = lax.all_gather(saved_input, 'dp', axis=1, tiled=True)[0]  86.3 us
    all_gather x1, waiting for transfers between devices, per_device(): upstream = lax.all_gather(incoming, 'dp', axis=1, tiled=True)[0]  69.7 us
  transfers between devices with their start and end apart: 3, of which 3 were waited for; matrix products, arithmetic and copies ran while one was open for 4% of the time, Pallas kernels for 0%

commit v1 on v0

--- a/solution.py
+++ b/solution.py
@@ -1,9 +1,10 @@
 import jax
 import jax.numpy as jnp
 from jax import lax
-from jax.sharding import PartitionSpec as P
+from jax.sharding import Mesh, PartitionSpec as P
 
 FF = 16384
+ROW_AXES = ("y", "zh", "core")
 
 
 def passed_along(block, axis, distance):
@@ -12,11 +13,26 @@
     return lax.ppermute(block, axis, route)
 
 
+def gather_rows(block):
+    for axis in ("zh", "y", "core"):
+        block = lax.all_gather(block, axis, axis=1, tiled=True)
+    return block
+
+
+def scatter_rows(block):
+    for axis in ("core", "y", "zh"):
+        block = lax.psum_scatter(block, axis, scatter_dimension=0, tiled=True)
+    return block
+
+
 def per_device(saved_input, grad_sent, kept_blocks, gate_blocks, up_blocks, down_blocks):
     width = saved_input.shape[2]
     block = gate_blocks.shape[2]
     bands = width // block
-    columns = FF // lax.axis_size("dp") // block
+    n_dp = 1
+    for axis in ROW_AXES:
+        n_dp *= lax.axis_size(axis)
+    columns = FF // n_dp // block
     ids = kept_blocks[0]
     band_ids = ids // columns
     col_ids = ids % columns
@@ -41,14 +57,14 @@
         return jnp.take(values.reshape(values.shape[0], bands, block), band_ids, axis=1)
 
     incoming = passed_along(grad_sent, "section", -1)
-    inputs = lax.all_gather(saved_input, "dp", axis=1, tiled=True)[0]
+    both = gather_rows(jnp.concatenate([saved_input, incoming], axis=0))
+    inputs = both[0]
+    upstream = both[1]
     chosen = pick_bands(inputs)
     gate = to_columns(
         jnp.einsum("tkb,kbc->tkc", chosen, w_gate, preferred_element_type=jnp.float32)
     )
     up = to_columns(jnp.einsum("tkb,kbc->tkc", chosen, w_up, preferred_element_type=jnp.float32))
-    gate, up = (gate, up)
-    upstream = lax.all_gather(incoming, "dp", axis=1, tiled=True)[0]
     sig = jax.nn.sigmoid(gate)
     act = gate * sig
     hidden = (act * up).astype(jnp.bfloat16)
@@ -58,7 +74,7 @@
     )
     grad_up_act = (dhid * act).astype(jnp.bfloat16)
     grad_gate_act = (dhid * up * sig * (1.0 + gate * (1.0 - sig))).astype(jnp.bfloat16)
-    input_sel = pick_bands(inputs)
+    input_sel = chosen
     tiles_down = jnp.einsum(
         "tkc,tkb->kcb", pick_cols(hidden), grad_sel, preferred_element_type=jnp.float32
     )
@@ -76,7 +92,7 @@
     )
     spread = jnp.einsum("tkb,kr->trb", slots, band_onehot)
     whole_term = spread.reshape(grad_gate_act.shape[0], bands * block)
-    summed = lax.psum_scatter(whole_term, "dp", scatter_dimension=0, tiled=True)
+    summed = scatter_rows(whole_term)
     grad_input = summed.astype(jnp.bfloat16)[None]
     return (
         grad_input,
@@ -87,22 +103,17 @@
 
 
 def solution(mesh):
+    n_dp = mesh.shape["dp"]
+    split = Mesh(
+        mesh.devices.reshape(mesh.shape["section"], n_dp // 8, 4, 2),
+        ("section",) + ROW_AXES,
+    )
+    rows = P("section", ROW_AXES, None)
+    blocks = P("section", ROW_AXES, None, None)
     return jax.shard_map(
         per_device,
-        mesh=mesh,
-        in_specs=(
-            P("section", "dp", None),
-            P("section", "dp", None),
-            P("section", "dp"),
-            P("section", "dp", None, None),
-            P("section", "dp", None, None),
-            P("section", "dp", None, None),
-        ),
-        out_specs=(
-            P("section", "dp", None),
-            P("section", "dp", None, None),
-            P("section", "dp", None, None),
-            P("section", "dp", None, None),
-        ),
+        mesh=split,
+        in_specs=(rows, rows, P("section", ROW_AXES), blocks, blocks, blocks),
+        out_specs=(rows, blocks, blocks, blocks),
         check_vma=False,
     )

time: 581 us -> 245 us (0.42)
  blocking collectives: 338 us -> 46.6 us
  waiting for transfers between devices: 158 us -> 125 us
  matrix products: 20.7 us -> 14.3 us
    unnamed x1, blocking collectives: 338 us -> 26.2 us
    all_gather x2, waiting for transfers between devices: 156 us -> 63.9 us  [gather_rows(): block = lax.all_gather(block, axis, axis=1, tiled=True)]
    reduce_scatter x0 -> x2, waiting for transfers between devices: none -> 59.3 us  [scatter_rows(): block = lax.psum_scatter(block, axis, scatter_dimension=0, tiled=True)]
    all_gather x0 -> x1, blocking collectives: none -> 20.4 us  [gather_rows(): block = lax.all_gather(block, axis, axis=1, tiled=True)]
    all_gather x2 -> x1, local copies, waits for them, and re-layouts: 18.5 us -> 6.19 us  [gather_rows(): block = lax.all_gather(block, axis, axis=1, tiled=True)]
  transfers between devices with their start and end apart: 3 -> 5, of which waited for: 3 -> 5; matrix products, arithmetic and copies ran while one was open for 4% -> 4% of each run, Pallas kernels for 0% -> 0%
where the time goes in v1:
time: 245 us; the launch traced here: 244 us
  waiting for transfers between devices  125 us (51%)
  blocking collectives  46.6 us (19%)
  local copies, waits for them, and re-layouts  38 us (16%)
  between operations  14.6 us (6%)
  matrix products  14.3 us (6%)
  starting transfers between devices  4.84 us (2%)
    all_gather x2, waiting for transfers between devices, gather_rows(): block = lax.all_gather(block, axis, axis=1, tiled=True)  63.9 us
    reduce_scatter x2, waiting for transfers between devices, scatter_rows(): block = lax.psum_scatter(block, axis, scatter_dimension=0, tiled=True)  59.3 us
    unnamed x1, blocking collectives  26.2 us
    all_gather x1, blocking collectives, gather_rows(): block = lax.all_gather(block, axis, axis=1, tiled=True)  20.4 us
    unnamed x26, local copies, waits for them, and re-layouts  9.89 us
    another operation x2, local copies, waits for them, and re-layouts, pick_bands(): values.reshape(values.shape[0], bands, block)  7.31 us
    all_gather x1, local copies, waits for them, and re-layouts, gather_rows(): block = lax.all_gather(block, axis, axis=1, tiled=True)  6.19 us
  transfers between devices with their start and end apart: 5, of which 5 were waited for; matrix products, arithmetic and copies ran while one was open for 4% of the time, Pallas kernels for 0%

profile of v1, /device:TPU:6, one launch (start us, length us, event | category | flops | bytes accessed | tf_op | source)
XLA Modules:
  0.0 244.5 jit_solution(11266522182964959274)
XLA Ops:
  7.2 4.7 %collective-permute-start = (bf16[1,4,4096]{2,1,0:T(4,128)(2,1)}, bf16[1,4,4096]{2,1,0:T(4,128)(2,1)S(1)}, u32[]{:S(2)}, u32[]{:S(2)}) collective-permute-start(bf16[1,4,4096]{2,1,0:T(4,128)(2,1)} %param.11), channel_id=1, source_target_pairs={{64,0},{128,64},{192,128},{256,192},{320,256},{384,320},{448,384},... | collective-permute-start | bytes 98312 | tf_op jit(solution)/shard_map/ppermute | solution.py:13
  11.9 1.9 collective-permute-done
  13.8 0.8 pad_maximum_fusion
  14.7 20.4 %all_gather.9 = bf16[2,16,4096]{2,0,1:T(2,128)(2,1)} all-gather(bf16[2,4,4096]{2,0,1:T(2,128)(2,1)S(1)} %copy.47), channel_id=1, replica_groups=mesh['section'=8,'y'=8,'zh'=4,'core'=2] {'zh'}, dimensions={1}, use_global_device_ids=true | all-gather | bytes 327680 | tf_op jit(solution)/shard_map/all_gather | solution.py:18
  35.1 44.1 %all-gather.3.cloned.1.call-done = bf16[2,128,4096]{2,0,1:T(2,128)(2,1)} async-done(((bf16[2,16,4096]{2,0,1:T(2,128)(2,1)}), bf16[2,128,4096]{2,0,1:T(2,128)(2,1)}) %all-gather.3.cloned.1.call-update) | async-done | bytes 2097168 | tf_op jit(solution)/shard_map/all_gather | solution.py:18
  79.2 6.2 %copy.48 = bf16[2,128,4096]{1,2,0:T(8,128)(2,1)} copy(bf16[2,128,4096]{2,0,1:T(2,128)(2,1)} %all-gather.3.cloned.1.call-done) | data formatting | bytes 4194304 | tf_op jit(solution)/shard_map/all_gather | solution.py:18
  86.1 19.8 %all-gather.5.cloned.1.call-done = bf16[2,256,4096]{1,2,0:T(8,128)(2,1)} async-done(((bf16[2,128,4096]{1,2,0:T(8,128)(2,1)}), bf16[2,256,4096]{1,2,0:T(8,128)(2,1)}) %all-gather.5.cloned.1.call-update) | async-done | bytes 4194320 | tf_op jit(solution)/shard_map/all_gather | solution.py:18
  106.0 4.5 %fusion.86 = (bf16[1,256,4096]{1,2,0:T(8,128)(2,1)}, bf16[1,256,4096]{1,2,0:T(8,128)(2,1)}) fusion(bf16[2,256,4096]{1,2,0:T(8,128)(2,1)} %all-gather.5.cloned.1.call-done), kind=kLoop, calls=%fused_computation.97 | loop fusion | bytes 8388608 | tf_op jit(solution)/shard_map/slice | solution.py:62
  110.4 3.2 %copy.49 = bf16[256,32,128]{2,0,1:T(8,128)(2,1)S(1)} copy(bf16[256,32,128]{0,2,1:T(8,128)(2,1)} %bitcast.156) | data formatting | bytes 4194304 | tf_op jit(solution)/shard_map/reshape;squeeze | solution.py:57
  113.7 4.1 %copy.52 = bf16[256,32,128]{2,0,1:T(8,128)(2,1)} copy(bf16[256,32,128]{0,2,1:T(8,128)(2,1)} %bitcast.155) | data formatting | bytes 4194304 | tf_op jit(solution)/shard_map/reshape;squeeze | solution.py:57
  117.8 2.0 gather_fusion
  119.8 2.5 %gather_fusion.1 = bf16[26,256,128]{2,1,0:T(8,128)(2,1)S(1)} fusion(bf16[256,32,128]{2,0,1:T(8,128)(2,1)} %copy.52, s32[1024]{0:T(1024)S(1)} %pad_clamp_fusion.1), kind=kCustom, calls=%fused_computation.2.clone | custom fusion | bytes 3407976 | tf_op jit(solution)/shard_map/jit(_take)/gather | solution.py:57
  122.3 0.7 convolution_bitcast_fusion
  122.9 1.1 fusion.2
  124.1 0.7 convolution_bitcast_fusion.1
  124.8 1.1 fusion.4
  126.3 0.7 convolution_bitcast_fusion.2
  126.9 1.1 fusion.6
  128.2 0.9 gather_fusion.2
  129.0 2.0 gather_fusion.3
  131.7 0.8 copy-done.1
  132.7 0.6 add_bitcast_fusion
  133.4 1.1 fusion
  134.5 5.9 %copy.84 = f32[32,8,32,128]{3,1,2,0:T(8,128)} copy(f32[32,8,32,128]{3,2,1,0:T(8,128)S(1)} %bitcast.154) | data formatting | bytes 8388608
  140.5 21.7 %reduce-scatter.3.cloned.1.call-done = f32[128,4096]{1,0:T(8,128)} async-done(((f32[256,4096]{1,0:T(8,128)}), f32[128,4096]{1,0:T(8,128)}) %reduce-scatter.3.cloned.1.call-update) | async-done | bytes 2097168 | tf_op jit(solution)/shard_map/reduce_scatter | solution.py:24
  162.2 1.3 dynamic-slice
  164.1 2.0 gather_fusion.4
  166.2 3.3 %fusion.50 = bf16[1,26,128,128]{3,2,1,0:T(8,128)(2,1)} fusion(bf16[26,256,128]{2,1,0:T(8,128)(2,1)S(1)} %gather_fusion.2, pred[26]{0:T(512)(128)(4,1)S(1)} %get-tuple-element.6, bf16[26,256,128]{2,1,0:T(8,128)(2,1)} %copy-done.5, pred[26]{0:T(512)(128)(4,1)S(1)} %get-tuple-element.15), kind=kOutput, calls=%fused_computation.44 | convolution fusion | flops 220233728 | bytes 4259892 | tf_op jit(solution)/shard_map/tkb,tkc->kbc/dot_general | solution.py:81
  169.5 1.7 fusion.45
  171.8 1.7 fusion.40
  173.5 37.6 %reduce-scatter.5.cloned.1.call-done = f32[16,4096]{1,0:T(8,128)} async-done(((f32[128,4096]{1,0:T(8,128)}), f32[16,4096]{1,0:T(8,128)}) %reduce-scatter.5.cloned.1.call-update) | async-done | bytes 262160 | tf_op jit(solution)/shard_map/reduce_scatter | solution.py:24
  211.1 26.2 %all-reduce.2 = bf16[16,4096]{1,0:T(8,128)(2,1)S(1)} all-reduce(f32[16,4096]{1,0:T(8,128)} %reduce-scatter.5.cloned.1.call-done), channel_id=4, replica_groups=mesh['section'=8,'y'=8,'zh'=4,'core'=2] {'zh'}, use_global_device_ids=true, to_apply=%region_2.5.clone | all-reduce | flops 65536 | bytes 393216
  (39 shorter events, 3.7 us)
Async XLA Ops:
  7.2 115.1 %copy-start = (bf16[1,26,128,128]{3,2,1,0:T(8,128)(2,1)S(1)}, bf16[1,26,128,128]{3,2,1,0:T(8,128)(2,1)}, u32[]{:S(2)}) copy-start(bf16[1,26,128,128]{3,2,1,0:T(8,128)(2,1)} %param.13) | copy-start | bytes 2555908
  7.2 72.1 %all-gather.3.cloned.1.call-start = ((), (), s32[]{:S(2)}) async-start(), calls=%async_computation.2 | async-start | bytes 2359296 | tf_op jit(solution)/shard_map/all_gather | solution.py:18
  7.2 6.6 %collective-permute-start = (bf16[1,4,4096]{2,1,0:T(4,128)(2,1)}, bf16[1,4,4096]{2,1,0:T(4,128)(2,1)S(1)}, u32[]{:S(2)}, u32[]{:S(2)}) collective-permute-start(bf16[1,4,4096]{2,1,0:T(4,128)(2,1)} %param.11), channel_id=1, source_target_pairs={{64,0},{128,64},{192,128},{256,192},{320,256},{384,320},{448,384},... | collective-permute-start | bytes 98312 | tf_op jit(solution)/shard_map/ppermute | solution.py:13
  35.1 70.9 %all-gather.5.cloned.1.call-start = ((), (), s32[]{:S(2)}) async-start(), calls=%async_computation.3 | async-start | bytes 6291456 | tf_op jit(solution)/shard_map/all_gather | solution.py:18
  85.4 0.7 copy-start.10
  85.5 76.7 %reduce-scatter.3.cloned.1.call-start = ((), (), s32[]{:S(2)}) async-start(), calls=%async_computation.4 | async-start | bytes 6291456 | tf_op jit(solution)/shard_map/reduce_scatter | solution.py:24
  122.2 1.7 copy-start.5
  122.9 1.2 copy-start.8
  124.1 1.7 copy-start.11
  124.8 1.5 copy-start.3
  131.0 1.5 copy-start.1
  131.0 1.7 copy-start.9
  140.4 70.6 %reduce-scatter.5.cloned.1.call-start = ((), (), s32[]{:S(2)}) async-start(), calls=%async_computation.5 | async-start | bytes 2359296 | tf_op jit(solution)/shard_map/reduce_scatter | solution.py:24
  166.2 3.3 %copy-start.2 = (bf16[26,256,128]{2,1,0:T(8,128)(2,1)S(1)}, bf16[26,256,128]{2,1,0:T(8,128)(2,1)}, u32[]{:S(2)}) copy-start(bf16[26,256,128]{2,1,0:T(8,128)(2,1)} %gather_fusion.3) | copy-start | bytes 5111812
  166.2 3.3 %copy-start.6 = (bf16[26,256,128]{2,1,0:T(8,128)(2,1)S(1)}, bf16[26,256,128]{2,1,0:T(8,128)(2,1)}, u32[]{:S(2)}) copy-start(bf16[26,256,128]{2,1,0:T(8,128)(2,1)} %copy-done.5) | copy-start | bytes 5111812
  169.5 1.7 copy-start.4
  169.5 2.3 copy-start.7
Sparse Core Ops, SparseCore 0:
  35.2 43.9 all-gather.2
  85.6 20.3 all-gather.4
  140.6 21.5 reduce-scatter.2
  165.1 45.8 reduce-scatter.4

commit v2 on v1

--- a/solution.py
+++ b/solution.py
@@ -13,16 +13,29 @@
     return lax.ppermute(block, axis, route)
 
 
+def shifted(block, axis, shift):
+    n = lax.axis_size(axis)
+    return lax.ppermute(block, axis, [(i, (i + shift) % n) for i in range(n)])
+
+
 def gather_rows(block):
-    for axis in ("zh", "y", "core"):
+    n = lax.axis_size("zh")
+    pieces = [block] + [shifted(block, "zh", k) for k in range(1, n)]
+    block = jnp.concatenate(pieces, axis=1)
+    for axis in ("y", "core"):
         block = lax.all_gather(block, axis, axis=1, tiled=True)
     return block
 
 
 def scatter_rows(block):
-    for axis in ("core", "y", "zh"):
+    for axis in ("core", "y"):
         block = lax.psum_scatter(block, axis, scatter_dimension=0, tiled=True)
-    return block
+    n = lax.axis_size("zh")
+    chunks = jnp.split(block, n, axis=0)
+    total = chunks[0]
+    for k in range(1, n):
+        total = total + shifted(chunks[k], "zh", -k)
+    return total
 
 
 def per_device(saved_input, grad_sent, kept_blocks, gate_blocks, up_blocks, down_blocks):

time: 245 us -> 243 us (level)
  blocking collectives: 46.6 us -> 0 us
  starting transfers between devices: 4.84 us -> 36.9 us
  waiting for transfers between devices: 125 us -> 135 us
    ppermute x0 -> x6, starting transfers between devices: none -> 32.1 us  [shifted(): return lax.ppermute(block, axis, [(i, (i + shift) % n) for i in range(n)])]
    unnamed x1 -> x0, blocking collectives: 26.2 us -> none
    all_gather x1 -> x0, blocking collectives: 20.4 us -> none  [gather_rows(): block = lax.all_gather(block, axis, axis=1, tiled=True)]
    ppermute x0 -> x6, waiting for transfers between devices: none -> 5.13 us  [shifted(): return lax.ppermute(block, axis, [(i, (i + shift) % n) for i in range(n)])]
    reduce_scatter x2, waiting for transfers between devices: 59.3 us -> 63 us  [scatter_rows(): block = lax.psum_scatter(block, axis, scatter_dimension=0, tiled=True)]
    unnamed x26 -> x24, local copies, waits for them, and re-layouts: 9.89 us -> 8.88 us
  transfers between devices with their start and end apart: 5 -> 11, of which waited for: 5 -> 7; matrix products, arithmetic and copies ran while one was open for 4% -> 5% of each run, Pallas kernels for 0% -> 0%
where the time goes in v2:
time: 243 us; the launch traced here: 242 us
  waiting for transfers between devices  135 us (56%)
  local copies, waits for them, and re-layouts  38.3 us (16%)
  starting transfers between devices  36.9 us (15%)
  matrix products  15.8 us (7%)
  between operations  14 us (6%)
    all_gather x2, waiting for transfers between devices, gather_rows(): block = lax.all_gather(block, axis, axis=1, tiled=True)  66.1 us
    reduce_scatter x2, waiting for transfers between devices, scatter_rows(): block = lax.psum_scatter(block, axis, scatter_dimension=0, tiled=True)  63 us
    ppermute x6, starting transfers between devices, shifted(): return lax.ppermute(block, axis, [(i, (i + shift) % n) for i in range(n)])  32.1 us
    unnamed x24, local copies, waits for them, and re-layouts  8.88 us
    another operation x2, local copies, waits for them, and re-layouts, pick_bands(): values.reshape(values.shape[0], bands, block)  7.29 us
    all_gather x1, local copies, waits for them, and re-layouts, gather_rows(): block = lax.all_gather(block, axis, axis=1, tiled=True)  6.16 us
    ppermute x6, waiting for transfers between devices, shifted(): return lax.ppermute(block, axis, [(i, (i + shift) % n) for i in range(n)])  5.13 us
    gather x3, local copies, waits for them, and re-layouts, pick_cols(): jnp.take(values.reshape(values.shape[0], columns, block), col_ids, axis=1)  4.89 us
  transfers between devices with their start and end apart: 11, of which 7 were waited for; matrix products, arithmetic and copies ran while one was open for 5% of the time, Pallas kernels for 0%

profile of v2, /device:TPU:6, one launch (start us, length us, event | category | flops | bytes accessed | tf_op | source)
XLA Modules:
  0.0 242.3 jit_solution(11132840423527257920)
XLA Ops:
  7.2 4.7 %collective-permute-start = (bf16[1,4,4096]{2,1,0:T(4,128)(2,1)}, bf16[1,4,4096]{2,1,0:T(4,128)(2,1)S(1)}, u32[]{:S(2)}, u32[]{:S(2)}) collective-permute-start(bf16[1,4,4096]{2,1,0:T(4,128)(2,1)} %param.11), channel_id=1, source_target_pairs={{64,0},{128,64},{192,128},{256,192},{320,256},{384,320},{448,384},... | collective-permute-start | bytes 98312 | tf_op jit(solution)/shard_map/ppermute | solution.py:13
  12.7 1.1 collective-permute-done
  13.8 10.5 %collective-permute-start.3 = (bf16[2,4,4096]{2,1,0:T(4,128)(2,1)S(1)}, bf16[2,4,4096]{2,1,0:T(4,128)(2,1)S(1)}, u32[]{:S(2)}, u32[]{:S(2)}) collective-permute-start(bf16[2,4,4096]{2,1,0:T(4,128)(2,1)S(1)} %constant_dynamic-update-slice_fusion), channel_id=1, source_target_pairs={{0,6},{2,0},{4,2},{6,4},{1,7},{3,1},{5,3},{7,5},{8,14},{10,8},{12,... | collective-permute-start | bytes 196616 | tf_op jit(solution)/shard_map/ppermute | solution.py:18
  24.3 1.9 collective-permute-start.2
  26.3 4.8 %collective-permute-start.1 = (bf16[2,4,4096]{2,1,0:T(4,128)(2,1)S(1)}, bf16[2,4,4096]{2,1,0:T(4,128)(2,1)S(1)}, u32[]{:S(2)}, u32[]{:S(2)}) collective-permute-start(bf16[2,4,4096]{2,1,0:T(4,128)(2,1)S(1)} %constant_dynamic-update-slice_fusion), channel_id=1, source_target_pairs={{0,2},{2,4},{4,6},{6,0},{1,3},{3,5},{5,7},{7,1},{8,10},{10,12},{12... | collective-permute-start | bytes 196616 | tf_op jit(solution)/shard_map/ppermute | solution.py:18
  31.1 4.1 %collective-permute-done.2 = bf16[2,4,4096]{2,1,0:T(4,128)(2,1)S(1)} collective-permute-done((bf16[2,4,4096]{2,1,0:T(4,128)(2,1)S(1)}, bf16[2,4,4096]{2,1,0:T(4,128)(2,1)S(1)}, u32[]{:S(2)}, u32[]{:S(2)}) %collective-permute-start.2) | collective-permute-done | bytes 65568 | tf_op jit(solution)/shard_map/ppermute | solution.py:18
  36.4 46.3 %all-gather.3.cloned.1.call-done = bf16[2,128,4096]{2,0,1:T(2,128)(2,1)} async-done(((bf16[2,16,4096]{2,0,1:T(2,128)(2,1)}), bf16[2,128,4096]{2,0,1:T(2,128)(2,1)}) %all-gather.3.cloned.1.call-update) | async-done | bytes 2097168 | tf_op jit(solution)/shard_map/all_gather | solution.py:26
  82.7 6.2 %copy.48 = bf16[2,128,4096]{1,2,0:T(8,128)(2,1)} copy(bf16[2,128,4096]{2,0,1:T(2,128)(2,1)} %all-gather.3.cloned.1.call-done) | data formatting | bytes 4194304 | tf_op jit(solution)/shard_map/all_gather | solution.py:26
  89.6 19.8 %all-gather.5.cloned.1.call-done = bf16[2,256,4096]{1,2,0:T(8,128)(2,1)} async-done(((bf16[2,128,4096]{1,2,0:T(8,128)(2,1)}), bf16[2,256,4096]{1,2,0:T(8,128)(2,1)}) %all-gather.5.cloned.1.call-update) | async-done | bytes 4194320 | tf_op jit(solution)/shard_map/all_gather | solution.py:26
  109.4 4.5 %fusion.89 = (bf16[1,256,4096]{1,2,0:T(8,128)(2,1)}, bf16[1,256,4096]{1,2,0:T(8,128)(2,1)}) fusion(bf16[2,256,4096]{1,2,0:T(8,128)(2,1)} %all-gather.5.cloned.1.call-done), kind=kLoop, calls=%fused_computation.102 | loop fusion | bytes 8388608 | tf_op jit(solution)/shard_map/slice | solution.py:75
  113.9 3.2 %copy.49 = bf16[256,32,128]{2,0,1:T(8,128)(2,1)S(1)} copy(bf16[256,32,128]{0,2,1:T(8,128)(2,1)} %bitcast.155) | data formatting | bytes 4194304 | tf_op jit(solution)/shard_map/reshape;squeeze | solution.py:70
  117.1 4.1 %copy.52 = bf16[256,32,128]{2,0,1:T(8,128)(2,1)} copy(bf16[256,32,128]{0,2,1:T(8,128)(2,1)} %bitcast.154) | data formatting | bytes 4194304 | tf_op jit(solution)/shard_map/reshape;squeeze | solution.py:70
  121.2 2.0 gather_fusion
  123.2 2.5 %gather_fusion.1 = bf16[26,256,128]{2,1,0:T(8,128)(2,1)S(1)} fusion(bf16[256,32,128]{2,0,1:T(8,128)(2,1)} %copy.52, s32[1024]{0:T(1024)S(1)} %pad_clamp_fusion.1), kind=kCustom, calls=%fused_computation.2.clone | custom fusion | bytes 3407976 | tf_op jit(solution)/shard_map/jit(_take)/gather | solution.py:70
  126.4 1.1 fusion.2
  128.2 1.1 fusion.4
  130.4 1.1 fusion.6
  132.5 2.0 gather_fusion.3
  136.8 1.1 fusion
  137.9 5.9 %copy.84 = f32[32,8,32,128]{3,1,2,0:T(8,128)} copy(f32[32,8,32,128]{3,2,1,0:T(8,128)S(1)} %bitcast.153) | data formatting | bytes 8388608
  143.9 21.7 %reduce-scatter.3.cloned.1.call-done = f32[128,4096]{1,0:T(8,128)} async-done(((f32[256,4096]{1,0:T(8,128)}), f32[128,4096]{1,0:T(8,128)}) %reduce-scatter.3.cloned.1.call-update) | async-done | bytes 2097168 | tf_op jit(solution)/shard_map/reduce_scatter | solution.py:32
  165.6 2.0 gather_fusion.4
  167.7 3.3 %fusion.50 = bf16[1,26,128,128]{3,2,1,0:T(8,128)(2,1)} fusion(bf16[26,256,128]{2,1,0:T(8,128)(2,1)S(1)} %gather_fusion.2, pred[26]{0:T(512)(128)(4,1)S(1)} %get-tuple-element.6, bf16[26,256,128]{2,1,0:T(8,128)(2,1)} %copy-done.5, pred[26]{0:T(512)(128)(4,1)S(1)} %get-tuple-element.18), kind=kOutput, calls=%fused_computation.44 | convolution fusion | flops 220233728 | bytes 4259892 | tf_op jit(solution)/shard_map/tkb,tkc->kbc/dot_general | solution.py:94
  171.0 1.7 fusion.45
  172.7 41.4 %reduce-scatter.5.cloned.1.call-done = f32[16,4096]{1,0:T(8,128)} async-done(((f32[128,4096]{1,0:T(8,128)}), f32[16,4096]{1,0:T(8,128)}) %reduce-scatter.5.cloned.1.call-update) | async-done | bytes 262160 | tf_op jit(solution)/shard_map/reduce_scatter | solution.py:32
  214.1 1.1 fusion.90
  215.2 6.5 %collective-permute-start.4 = (f32[4,4096]{1,0:T(4,128)S(1)}, f32[4,4096]{1,0:T(4,128)S(1)}, u32[]{:S(2)}, u32[]{:S(2)}) collective-permute-start(f32[4,4096]{1,0:T(4,128)S(1)} %get-tuple-element.15), channel_id=1, source_target_pairs={{0,6},{2,0},{4,2},{6,4},{1,7},{3,1},{5,3},{7,5},{8,14},{10,8},{12,... | collective-permute-start | bytes 196616 | tf_op jit(solution)/shard_map/ppermute | solution.py:18
  221.7 1.9 collective-permute-start.6
  223.6 6.4 %collective-permute-start.5 = (f32[4,4096]{1,0:T(4,128)S(1)}, f32[4,4096]{1,0:T(4,128)S(1)}, u32[]{:S(2)}, u32[]{:S(2)}) collective-permute-start(f32[4,4096]{1,0:T(4,128)S(1)} %get-tuple-element.17), channel_id=1, source_target_pairs={{0,4},{2,6},{4,0},{6,2},{1,5},{3,7},{5,1},{7,3},{8,12},{10,14},{12... | collective-permute-start | bytes 196616 | tf_op jit(solution)/shard_map/ppermute | solution.py:18
  230.0 3.2 %fusion.40 = bf16[1,26,128,128]{3,2,1,0:T(8,128)(2,1)} fusion(bf16[26,256,128]{2,1,0:T(8,128)(2,1)} %gather_fusion.4, pred[26]{0:T(512)(128)(4,1)S(1)} %get-tuple-element.6, bf16[26,256,128]{2,1,0:T(8,128)(2,1)S(1)} %copy-done.4, pred[26]{0:T(512)(128)(4,1)S(1)} %get-tuple-element.18), kind=kOutput, calls=%fused_computation.42 | convolution fusion | flops 220233728 | bytes 4259892 | tf_op jit(solution)/shard_map/tkc,tkb->kcb/dot_general | solution.py:91
  233.2 1.0 collective-permute-done.5
  234.2 1.6 fusion.73
  (49 shorter events, 8.7 us)
Async XLA Ops:
  7.2 118.5 %copy-start = (bf16[1,26,128,128]{3,2,1,0:T(8,128)(2,1)S(1)}, bf16[1,26,128,128]{3,2,1,0:T(8,128)(2,1)}, u32[]{:S(2)}) copy-start(bf16[1,26,128,128]{3,2,1,0:T(8,128)(2,1)} %param.13) | copy-start | bytes 2555908
  7.2 75.5 %all-gather.3.cloned.1.call-start = ((), (), s32[]{:S(2)}) async-start(), calls=%async_computation.2 | async-start | bytes 2359296 | tf_op jit(solution)/shard_map/all_gather | solution.py:26
  7.2 6.6 %collective-permute-start = (bf16[1,4,4096]{2,1,0:T(4,128)(2,1)}, bf16[1,4,4096]{2,1,0:T(4,128)(2,1)S(1)}, u32[]{:S(2)}, u32[]{:S(2)}) collective-permute-start(bf16[1,4,4096]{2,1,0:T(4,128)(2,1)} %param.11), channel_id=1, source_target_pairs={{64,0},{128,64},{192,128},{256,192},{320,256},{384,320},{448,384},... | collective-permute-start | bytes 98312 | tf_op jit(solution)/shard_map/ppermute | solution.py:13
  13.8 17.3 %collective-permute-start.3 = (bf16[2,4,4096]{2,1,0:T(4,128)(2,1)S(1)}, bf16[2,4,4096]{2,1,0:T(4,128)(2,1)S(1)}, u32[]{:S(2)}, u32[]{:S(2)}) collective-permute-start(bf16[2,4,4096]{2,1,0:T(4,128)(2,1)S(1)} %constant_dynamic-update-slice_fusion), channel_id=1, source_target_pairs={{0,6},{2,0},{4,2},{6,4},{1,7},{3,1},{5,3},{7,5},{8,14},{10,8},{12,... | collective-permute-start | bytes 196616 | tf_op jit(solution)/shard_map/ppermute | solution.py:18
  24.3 10.9 %collective-permute-start.2 = (bf16[2,4,4096]{2,1,0:T(4,128)(2,1)S(1)}, bf16[2,4,4096]{2,1,0:T(4,128)(2,1)S(1)}, u32[]{:S(2)}, u32[]{:S(2)}) collective-permute-start(bf16[2,4,4096]{2,1,0:T(4,128)(2,1)S(1)} %constant_dynamic-update-slice_fusion), channel_id=1, source_target_pairs={{0,4},{2,6},{4,0},{6,2},{1,5},{3,7},{5,1},{7,3},{8,12},{10,14},{12... | collective-permute-start | bytes 196616 | tf_op jit(solution)/shard_map/ppermute | solution.py:18
  26.3 8.9 %collective-permute-start.1 = (bf16[2,4,4096]{2,1,0:T(4,128)(2,1)S(1)}, bf16[2,4,4096]{2,1,0:T(4,128)(2,1)S(1)}, u32[]{:S(2)}, u32[]{:S(2)}) collective-permute-start(bf16[2,4,4096]{2,1,0:T(4,128)(2,1)S(1)} %constant_dynamic-update-slice_fusion), channel_id=1, source_target_pairs={{0,2},{2,4},{4,6},{6,0},{1,3},{3,5},{5,7},{7,1},{8,10},{10,12},{12... | collective-permute-start | bytes 196616 | tf_op jit(solution)/shard_map/ppermute | solution.py:18
  36.4 73.0 %all-gather.5.cloned.1.call-start = ((), (), s32[]{:S(2)}) async-start(), calls=%async_computation.3 | async-start | bytes 6291456 | tf_op jit(solution)/shard_map/all_gather | solution.py:26
  88.9 0.7 copy-start.9
  88.9 76.7 %reduce-scatter.3.cloned.1.call-start = ((), (), s32[]{:S(2)}) async-start(), calls=%async_computation.4 | async-start | bytes 6291456 | tf_op jit(solution)/shard_map/reduce_scatter | solution.py:32
  125.7 1.7 copy-start.5
  126.4 1.2 copy-start.7
  127.5 1.7 copy-start.10
  128.2 1.5 copy-start.3
  134.5 1.5 copy-start.1
  134.5 1.7 copy-start.8
  143.9 70.2 %reduce-scatter.5.cloned.1.call-start = ((), (), s32[]{:S(2)}) async-start(), calls=%async_computation.5 | async-start | bytes 2359296 | tf_op jit(solution)/shard_map/reduce_scatter | solution.py:32
  167.7 3.3 %copy-start.2 = (bf16[26,256,128]{2,1,0:T(8,128)(2,1)S(1)}, bf16[26,256,128]{2,1,0:T(8,128)(2,1)}, u32[]{:S(2)}) copy-start(bf16[26,256,128]{2,1,0:T(8,128)(2,1)} %gather_fusion.3) | copy-start | bytes 5111812
  167.7 3.3 %copy-start.6 = (bf16[26,256,128]{2,1,0:T(8,128)(2,1)S(1)}, bf16[26,256,128]{2,1,0:T(8,128)(2,1)}, u32[]{:S(2)}) copy-start(bf16[26,256,128]{2,1,0:T(8,128)(2,1)} %copy-done.5) | copy-start | bytes 5111812
  171.0 59.0 %copy-start.4 = (bf16[26,256,128]{2,1,0:T(8,128)(2,1)S(1)}, bf16[26,256,128]{2,1,0:T(8,128)(2,1)}, u32[]{:S(2)}) copy-start(bf16[26,256,128]{2,1,0:T(8,128)(2,1)} %gather_fusion) | copy-start | bytes 5111812
  215.2 18.0 %collective-permute-start.4 = (f32[4,4096]{1,0:T(4,128)S(1)}, f32[4,4096]{1,0:T(4,128)S(1)}, u32[]{:S(2)}, u32[]{:S(2)}) collective-permute-start(f32[4,4096]{1,0:T(4,128)S(1)} %get-tuple-element.15), channel_id=1, source_target_pairs={{0,6},{2,0},{4,2},{6,4},{1,7},{3,1},{5,3},{7,5},{8,14},{10,8},{12,... | collective-permute-start | bytes 196616 | tf_op jit(solution)/shard_map/ppermute | solution.py:18
  221.7 11.5 %collective-permute-start.6 = (f32[4,4096]{1,0:T(4,128)S(1)}, f32[4,4096]{1,0:T(4,128)S(1)}, u32[]{:S(2)}, u32[]{:S(2)}) collective-permute-start(f32[4,4096]{1,0:T(4,128)S(1)} %get-tuple-element.16), channel_id=1, source_target_pairs={{0,2},{2,4},{4,6},{6,0},{1,3},{3,5},{5,7},{7,1},{8,10},{10,12},{12... | collective-permute-start | bytes 196616 | tf_op jit(solution)/shard_map/ppermute | solution.py:18
  223.6 10.6 %collective-permute-start.5 = (f32[4,4096]{1,0:T(4,128)S(1)}, f32[4,4096]{1,0:T(4,128)S(1)}, u32[]{:S(2)}, u32[]{:S(2)}) collective-permute-start(f32[4,4096]{1,0:T(4,128)S(1)} %get-tuple-element.17), channel_id=1, source_target_pairs={{0,4},{2,6},{4,0},{6,2},{1,5},{3,7},{5,1},{7,3},{8,12},{10,14},{12... | collective-permute-start | bytes 196616 | tf_op jit(solution)/shard_map/ppermute | solution.py:18
Sparse Core Ops, SparseCore 0:
  36.5 46.1 all-gather.2
  89.0 20.3 all-gather.4
  144.0 21.5 reduce-scatter.2
  168.6 45.4 reduce-scatter.4

commit v3 on v2

--- a/solution.py
+++ b/solution.py
@@ -18,11 +18,13 @@
     return lax.ppermute(block, axis, [(i, (i + shift) % n) for i in range(n)])
 
 
+def shifted(block, axis, shift):
+    n = lax.axis_size(axis)
+    return lax.ppermute(block, axis, [(i, (i + shift) % n) for i in range(n)])
+
+
 def gather_rows(block):
-    n = lax.axis_size("zh")
-    pieces = [block] + [shifted(block, "zh", k) for k in range(1, n)]
-    block = jnp.concatenate(pieces, axis=1)
-    for axis in ("y", "core"):
+    for axis in (("y", "zh"), "core"):
         block = lax.all_gather(block, axis, axis=1, tiled=True)
     return block
 
@@ -31,11 +33,14 @@
     for axis in ("core", "y"):
         block = lax.psum_scatter(block, axis, scatter_dimension=0, tiled=True)
     n = lax.axis_size("zh")
+    idx = lax.axis_index("zh")
     chunks = jnp.split(block, n, axis=0)
-    total = chunks[0]
+    total = None
     for k in range(1, n):
-        total = total + shifted(chunks[k], "zh", -k)
-    return total
+        sent = jnp.stack(chunks)[(idx - k) % n]
+        got = shifted(sent, "zh", -k)
+        total = got if total is None else total + got
+    return total + jnp.stack(chunks)[idx]
 
 
 def per_device(saved_input, grad_sent, kept_blocks, gate_blocks, up_blocks, down_blocks):

time: 243 us -> 265 us (1.091)
  waiting for transfers between devices: 135 us -> 175 us
  starting transfers between devices: 36.9 us -> 20.6 us
    all_gather x2, waiting for transfers between devices: 66.1 us -> 110 us  [gather_rows(): block = lax.all_gather(block, axis, axis=1, tiled=True)]
    ppermute x6 -> x3, starting transfers between devices: 32.1 us -> 15.7 us  [shifted(): return lax.ppermute(block, axis, [(i, (i + shift) % n) for i in range(n)])]
    ppermute x6 -> x3, waiting for transfers between devices: 5.13 us -> 0.01 us  [shifted(): return lax.ppermute(block, axis, [(i, (i + shift) % n) for i in range(n)])]
    unnamed x24 -> x23, local copies, waits for them, and re-layouts: 8.88 us -> 8.1 us
  transfers between devices with their start and end apart: 11 -> 8, of which waited for: 7 -> 5; matrix products, arithmetic and copies ran while one was open for 5% -> 4% of each run, Pallas kernels for 0% -> 0%
where the time goes in v3:
time: 265 us; the launch traced here: 264 us
  waiting for transfers between devices  175 us (66%)
  local copies, waits for them, and re-layouts  37.3 us (14%)
  starting transfers between devices  20.6 us (8%)
  matrix products  15.8 us (6%)
  between operations  14 us (5%)
    all_gather x2, waiting for transfers between devices, gather_rows(): block = lax.all_gather(block, axis, axis=1, tiled=True)  110 us
    reduce_scatter x2, waiting for transfers between devices, scatter_rows(): block = lax.psum_scatter(block, axis, scatter_dimension=0, tiled=True)  63.3 us
    ppermute x3, starting transfers between devices, shifted(): return lax.ppermute(block, axis, [(i, (i + shift) % n) for i in range(n)])  15.7 us
    unnamed x23, local copies, waits for them, and re-layouts  8.1 us
    another operation x2, local copies, waits for them, and re-layouts, pick_bands(): values.reshape(values.shape[0], bands, block)  7.28 us
    all_gather x1, local copies, waits for them, and re-layouts, gather_rows(): block = lax.all_gather(block, axis, axis=1, tiled=True)  6.16 us
  transfers between devices with their start and end apart: 8, of which 5 were waited for; matrix products, arithmetic and copies ran while one was open for 4% of the time, Pallas kernels for 0%

profile of v3, /device:TPU:6, one launch (start us, length us, event | category | flops | bytes accessed | tf_op | source)
XLA Modules:
  0.0 264.3 jit_solution(5527434780666227582)
XLA Ops:
  7.2 4.7 %collective-permute-start = (bf16[1,4,4096]{2,1,0:T(4,128)(2,1)}, bf16[1,4,4096]{2,1,0:T(4,128)(2,1)S(1)}, u32[]{:S(2)}, u32[]{:S(2)}) collective-permute-start(bf16[1,4,4096]{2,1,0:T(4,128)(2,1)} %param.11), channel_id=1, source_target_pairs={{64,0},{128,64},{192,128},{256,192},{320,256},{384,320},{448,384},... | collective-permute-start | bytes 98312 | tf_op jit(solution)/shard_map/ppermute | solution.py:13
  11.9 1.9 collective-permute-done
  13.8 0.8 pad_maximum_fusion.1
  14.6 0.7 copy.47
  15.4 93.6 %all-gather.3.cloned.1.call-done = bf16[2,128,4096]{2,0,1:T(2,128)(2,1)} async-done(((bf16[2,4,4096]{2,0,1:T(2,128)(2,1)}), bf16[2,128,4096]{2,0,1:T(2,128)(2,1)}) %all-gather.3.cloned.1.call-update) | async-done | bytes 2097168 | tf_op jit(solution)/shard_map/all_gather | solution.py:28
  109.0 6.2 %copy.48 = bf16[2,128,4096]{1,2,0:T(8,128)(2,1)} copy(bf16[2,128,4096]{2,0,1:T(2,128)(2,1)} %all-gather.3.cloned.1.call-done) | data formatting | bytes 4194304 | tf_op jit(solution)/shard_map/all_gather | solution.py:28
  115.9 16.0 %all-gather.5.cloned.1.call-done = bf16[2,256,4096]{1,2,0:T(8,128)(2,1)} async-done(((bf16[2,128,4096]{1,2,0:T(8,128)(2,1)}), bf16[2,256,4096]{1,2,0:T(8,128)(2,1)}) %all-gather.5.cloned.1.call-update) | async-done | bytes 4194320 | tf_op jit(solution)/shard_map/all_gather | solution.py:28
  131.9 4.5 %fusion.87 = (bf16[1,256,4096]{1,2,0:T(8,128)(2,1)}, bf16[1,256,4096]{1,2,0:T(8,128)(2,1)}) fusion(bf16[2,256,4096]{1,2,0:T(8,128)(2,1)} %all-gather.5.cloned.1.call-done), kind=kLoop, calls=%fused_computation.106 | loop fusion | bytes 8388608 | tf_op jit(solution)/shard_map/slice | solution.py:80
  136.4 3.2 %copy.49 = bf16[256,32,128]{2,0,1:T(8,128)(2,1)S(1)} copy(bf16[256,32,128]{0,2,1:T(8,128)(2,1)} %bitcast.175) | data formatting | bytes 4194304 | tf_op jit(solution)/shard_map/reshape;squeeze | solution.py:75
  139.7 4.1 %copy.52 = bf16[256,32,128]{2,0,1:T(8,128)(2,1)} copy(bf16[256,32,128]{0,2,1:T(8,128)(2,1)} %bitcast.174) | data formatting | bytes 4194304 | tf_op jit(solution)/shard_map/reshape;squeeze | solution.py:75
  143.7 2.0 gather_fusion
  145.7 2.5 gather_fusion.1
  148.2 0.7 convolution_bitcast_fusion
  148.9 1.1 fusion.2
  150.1 0.7 convolution_bitcast_fusion.1
  150.7 1.1 fusion.4
  152.9 1.1 fusion.6
  154.1 0.9 gather_fusion.2
  155.0 2.0 gather_fusion.3
  157.7 0.8 copy-done.1
  159.3 1.1 fusion
  160.5 5.9 %copy.84 = f32[32,8,32,128]{3,1,2,0:T(8,128)} copy(f32[32,8,32,128]{3,2,1,0:T(8,128)S(1)} %bitcast.173) | data formatting | bytes 8388608
  166.5 21.7 %reduce-scatter.3.cloned.1.call-done = f32[128,4096]{1,0:T(8,128)} async-done(((f32[256,4096]{1,0:T(8,128)}), f32[128,4096]{1,0:T(8,128)}) %reduce-scatter.3.cloned.1.call-update) | async-done | bytes 2097168 | tf_op jit(solution)/shard_map/reduce_scatter | solution.py:34
  188.2 2.0 gather_fusion.4
  190.3 3.3 %fusion.50 = bf16[1,26,128,128]{3,2,1,0:T(8,128)(2,1)} fusion(bf16[26,256,128]{2,1,0:T(8,128)(2,1)S(1)} %gather_fusion.2, pred[26]{0:T(512)(128)(4,1)S(1)} %get-tuple-element.6, bf16[26,256,128]{2,1,0:T(8,128)(2,1)} %copy-done.5, pred[26]{0:T(512)(128)(4,1)S(1)} %get-tuple-element.22), kind=kOutput, calls=%fused_computation.44 | convolution fusion | flops 220233728 | bytes 4259892 | tf_op jit(solution)/shard_map/tkb,tkc->kbc/dot_general | solution.py:99
  193.6 1.7 fusion.45
  195.3 41.6 %reduce-scatter.5.cloned.1.call-done = f32[16,4096]{1,0:T(8,128)} async-done(((f32[128,4096]{1,0:T(8,128)}), f32[16,4096]{1,0:T(8,128)}) %reduce-scatter.5.cloned.1.call-update) | async-done | bytes 262160 | tf_op jit(solution)/shard_map/reduce_scatter | solution.py:34
  236.9 1.1 slice_bitcast_fusion.3
  238.2 7.8 %collective-permute-start.2 = (f32[4,4096]{1,0:T(4,128)S(1)}, f32[4,4096]{1,0:T(4,128)S(1)}, u32[]{:S(2)}, u32[]{:S(2)}) collective-permute-start(f32[4,4096]{1,0:T(4,128)S(1)} %get-tuple-element.15), channel_id=1, source_target_pairs={{0,4},{2,6},{4,0},{6,2},{1,5},{3,7},{5,1},{7,3},{8,12},{10,14},{12... | collective-permute-start | bytes 196616 | tf_op jit(solution)/shard_map/ppermute | solution.py:23
  246.0 2.8 %collective-permute-start.3 = (f32[4,4096]{1,0:T(4,128)S(1)}, f32[4,4096]{1,0:T(4,128)S(1)}, u32[]{:S(2)}, u32[]{:S(2)}) collective-permute-start(f32[4,4096]{1,0:T(4,128)S(1)} %get-tuple-element.16), channel_id=1, source_target_pairs={{0,2},{2,4},{4,6},{6,0},{1,3},{3,5},{5,7},{7,1},{8,10},{10,12},{12... | collective-permute-start | bytes 196616 | tf_op jit(solution)/shard_map/ppermute | solution.py:23
  248.7 5.2 %collective-permute-start.1 = (f32[4,4096]{1,0:T(4,128)S(1)}, f32[4,4096]{1,0:T(4,128)S(1)}, u32[]{:S(2)}, u32[]{:S(2)}) collective-permute-start(f32[4,4096]{1,0:T(4,128)S(1)} %get-tuple-element.17), channel_id=1, source_target_pairs={{0,6},{2,0},{4,2},{6,4},{1,7},{3,1},{5,3},{7,5},{8,14},{10,8},{12,... | collective-permute-start | bytes 196616 | tf_op jit(solution)/shard_map/ppermute | solution.py:23
  254.0 3.2 %fusion.40 = bf16[1,26,128,128]{3,2,1,0:T(8,128)(2,1)} fusion(bf16[26,256,128]{2,1,0:T(8,128)(2,1)} %gather_fusion.4, pred[26]{0:T(512)(128)(4,1)S(1)} %get-tuple-element.6, bf16[26,256,128]{2,1,0:T(8,128)(2,1)S(1)} %copy-done.4, pred[26]{0:T(512)(128)(4,1)S(1)} %get-tuple-element.22), kind=kOutput, calls=%fused_computation.42 | convolution fusion | flops 220233728 | bytes 4259892 | tf_op jit(solution)/shard_map/tkc,tkb->kcb/dot_general | solution.py:96
  (43 shorter events, 4.5 us)
Async XLA Ops:
  7.2 141.1 %copy-start = (bf16[1,26,128,128]{3,2,1,0:T(8,128)(2,1)S(1)}, bf16[1,26,128,128]{3,2,1,0:T(8,128)(2,1)}, u32[]{:S(2)}) copy-start(bf16[1,26,128,128]{3,2,1,0:T(8,128)(2,1)} %param.13) | copy-start | bytes 2555908
  7.2 101.8 %all-gather.3.cloned.1.call-start = ((), (), s32[]{:S(2)}) async-start(), calls=%async_computation.2 | async-start | bytes 2162688 | tf_op jit(solution)/shard_map/all_gather | solution.py:28
  7.2 6.6 %collective-permute-start = (bf16[1,4,4096]{2,1,0:T(4,128)(2,1)}, bf16[1,4,4096]{2,1,0:T(4,128)(2,1)S(1)}, u32[]{:S(2)}, u32[]{:S(2)}) collective-permute-start(bf16[1,4,4096]{2,1,0:T(4,128)(2,1)} %param.11), channel_id=1, source_target_pairs={{64,0},{128,64},{192,128},{256,192},{320,256},{384,320},{448,384},... | collective-permute-start | bytes 98312 | tf_op jit(solution)/shard_map/ppermute | solution.py:13
  15.3 116.6 %all-gather.5.cloned.1.call-start = ((), (), s32[]{:S(2)}) async-start(), calls=%async_computation.3 | async-start | bytes 6291456 | tf_op jit(solution)/shard_map/all_gather | solution.py:28
  115.2 0.7 copy-start.9
  115.2 72.9 %reduce-scatter.3.cloned.1.call-start = ((), (), s32[]{:S(2)}) async-start(), calls=%async_computation.4 | async-start | bytes 6291456 | tf_op jit(solution)/shard_map/reduce_scatter | solution.py:34
  148.2 1.7 copy-start.5
  148.9 1.2 copy-start.7
  150.0 1.7 copy-start.10
  150.7 1.5 copy-start.3
  157.0 1.5 copy-start.1
  157.0 1.7 copy-start.8
  166.4 70.5 %reduce-scatter.5.cloned.1.call-start = ((), (), s32[]{:S(2)}) async-start(), calls=%async_computation.5 | async-start | bytes 2359296 | tf_op jit(solution)/shard_map/reduce_scatter | solution.py:34
  190.3 3.3 %copy-start.2 = (bf16[26,256,128]{2,1,0:T(8,128)(2,1)S(1)}, bf16[26,256,128]{2,1,0:T(8,128)(2,1)}, u32[]{:S(2)}) copy-start(bf16[26,256,128]{2,1,0:T(8,128)(2,1)} %gather_fusion.3) | copy-start | bytes 5111812
  190.3 3.3 %copy-start.6 = (bf16[26,256,128]{2,1,0:T(8,128)(2,1)S(1)}, bf16[26,256,128]{2,1,0:T(8,128)(2,1)}, u32[]{:S(2)}) copy-start(bf16[26,256,128]{2,1,0:T(8,128)(2,1)} %copy-done.5) | copy-start | bytes 5111812
  193.6 60.4 %copy-start.4 = (bf16[26,256,128]{2,1,0:T(8,128)(2,1)S(1)}, bf16[26,256,128]{2,1,0:T(8,128)(2,1)}, u32[]{:S(2)}) copy-start(bf16[26,256,128]{2,1,0:T(8,128)(2,1)} %gather_fusion) | copy-start | bytes 5111812
  238.2 18.9 %collective-permute-start.2 = (f32[4,4096]{1,0:T(4,128)S(1)}, f32[4,4096]{1,0:T(4,128)S(1)}, u32[]{:S(2)}, u32[]{:S(2)}) collective-permute-start(f32[4,4096]{1,0:T(4,128)S(1)} %get-tuple-element.15), channel_id=1, source_target_pairs={{0,4},{2,6},{4,0},{6,2},{1,5},{3,7},{5,1},{7,3},{8,12},{10,14},{12... | collective-permute-start | bytes 196616 | tf_op jit(solution)/shard_map/ppermute | solution.py:23
  246.0 11.2 %collective-permute-start.3 = (f32[4,4096]{1,0:T(4,128)S(1)}, f32[4,4096]{1,0:T(4,128)S(1)}, u32[]{:S(2)}, u32[]{:S(2)}) collective-permute-start(f32[4,4096]{1,0:T(4,128)S(1)} %get-tuple-element.16), channel_id=1, source_target_pairs={{0,2},{2,4},{4,6},{6,0},{1,3},{3,5},{5,7},{7,1},{8,10},{10,12},{12... | collective-permute-start | bytes 196616 | tf_op jit(solution)/shard_map/ppermute | solution.py:23
  248.7 8.4 %collective-permute-start.1 = (f32[4,4096]{1,0:T(4,128)S(1)}, f32[4,4096]{1,0:T(4,128)S(1)}, u32[]{:S(2)}, u32[]{:S(2)}) collective-permute-start(f32[4,4096]{1,0:T(4,128)S(1)} %get-tuple-element.17), channel_id=1, source_target_pairs={{0,6},{2,0},{4,2},{6,4},{1,7},{3,1},{5,3},{7,5},{8,14},{10,8},{12,... | collective-permute-start | bytes 196616 | tf_op jit(solution)/shard_map/ppermute | solution.py:23
Sparse Core Ops, SparseCore 0:
  15.5 93.5 all-gather.2
  115.3 16.5 all-gather.4
  166.5 21.5 reduce-scatter.2
  191.1 45.8 reduce-scatter.4

commit v4 on v2

--- a/solution.py
+++ b/solution.py
@@ -28,13 +28,14 @@
 
 
 def scatter_rows(block):
+    block = block.astype(jnp.bfloat16)
     for axis in ("core", "y"):
         block = lax.psum_scatter(block, axis, scatter_dimension=0, tiled=True)
     n = lax.axis_size("zh")
     chunks = jnp.split(block, n, axis=0)
-    total = chunks[0]
+    total = chunks[0].astype(jnp.float32)
     for k in range(1, n):
-        total = total + shifted(chunks[k], "zh", -k)
+        total = total + shifted(chunks[k], "zh", -k).astype(jnp.float32)
     return total
 
 

time: 243 us -> 233 us (0.959)
  waiting for transfers between devices: 135 us -> 129 us
  local copies, waits for them, and re-layouts: 38.3 us -> 34.6 us
    reduce_scatter x2, waiting for transfers between devices: 63 us -> 57 us  [scatter_rows(): block = lax.psum_scatter(block, axis, scatter_dimension=0, tiled=True)]
    unnamed x24, local copies, waits for them, and re-layouts: 8.88 us -> 5.26 us
where the time goes in v4:
time: 233 us; the launch traced here: 232 us
  waiting for transfers between devices  129 us (55%)
  starting transfers between devices  37.1 us (16%)
  local copies, waits for them, and re-layouts  34.6 us (15%)
  matrix products  15.9 us (7%)
  between operations  14 us (6%)
    all_gather x2, waiting for transfers between devices, gather_rows(): block = lax.all_gather(block, axis, axis=1, tiled=True)  66.1 us
    reduce_scatter x2, waiting for transfers between devices, scatter_rows(): block = lax.psum_scatter(block, axis, scatter_dimension=0, tiled=True)  57 us
    ppermute x6, starting transfers between devices, shifted(): return lax.ppermute(block, axis, [(i, (i + shift) % n) for i in range(n)])  32.1 us
    another operation x2, local copies, waits for them, and re-layouts, pick_bands(): values.reshape(values.shape[0], bands, block)  7.29 us
    all_gather x1, local copies, waits for them, and re-layouts, gather_rows(): block = lax.all_gather(block, axis, axis=1, tiled=True)  6.16 us
    unnamed x24, local copies, waits for them, and re-layouts  5.26 us
    gather x3, local copies, waits for them, and re-layouts, pick_cols(): jnp.take(values.reshape(values.shape[0], columns, block), col_ids, axis=1)  4.94 us
    ppermute x1, starting transfers between devices, passed_along(): return lax.ppermute(block, axis, route)  4.68 us
  transfers between devices with their start and end apart: 11, of which 7 were waited for; matrix products, arithmetic and copies ran while one was open for 5% of the time, Pallas kernels for 0%

profile of v4, /device:TPU:6, one launch (start us, length us, event | category | flops | bytes accessed | tf_op | source)
XLA Modules:
  0.0 232.2 jit_solution(5412101404899752014)
XLA Ops:
  7.2 4.7 %collective-permute-start = (bf16[1,4,4096]{2,1,0:T(4,128)(2,1)}, bf16[1,4,4096]{2,1,0:T(4,128)(2,1)S(1)}, u32[]{:S(2)}, u32[]{:S(2)}) collective-permute-start(bf16[1,4,4096]{2,1,0:T(4,128)(2,1)} %param.11), channel_id=1, source_target_pairs={{64,0},{128,64},{192,128},{256,192},{320,256},{384,320},{448,384},... | collective-permute-start | bytes 98312 | tf_op jit(solution)/shard_map/ppermute | solution.py:13
  12.7 1.1 collective-permute-done
  13.8 10.5 %collective-permute-start.3 = (bf16[2,4,4096]{2,1,0:T(4,128)(2,1)S(1)}, bf16[2,4,4096]{2,1,0:T(4,128)(2,1)S(1)}, u32[]{:S(2)}, u32[]{:S(2)}) collective-permute-start(bf16[2,4,4096]{2,1,0:T(4,128)(2,1)S(1)} %constant_dynamic-update-slice_fusion), channel_id=1, source_target_pairs={{0,6},{2,0},{4,2},{6,4},{1,7},{3,1},{5,3},{7,5},{8,14},{10,8},{12,... | collective-permute-start | bytes 196616 | tf_op jit(solution)/shard_map/ppermute | solution.py:18
  24.3 1.9 collective-permute-start.2
  26.3 4.8 %collective-permute-start.1 = (bf16[2,4,4096]{2,1,0:T(4,128)(2,1)S(1)}, bf16[2,4,4096]{2,1,0:T(4,128)(2,1)S(1)}, u32[]{:S(2)}, u32[]{:S(2)}) collective-permute-start(bf16[2,4,4096]{2,1,0:T(4,128)(2,1)S(1)} %constant_dynamic-update-slice_fusion), channel_id=1, source_target_pairs={{0,2},{2,4},{4,6},{6,0},{1,3},{3,5},{5,7},{7,1},{8,10},{10,12},{12... | collective-permute-start | bytes 196616 | tf_op jit(solution)/shard_map/ppermute | solution.py:18
  31.1 4.1 %collective-permute-done.2 = bf16[2,4,4096]{2,1,0:T(4,128)(2,1)S(1)} collective-permute-done((bf16[2,4,4096]{2,1,0:T(4,128)(2,1)S(1)}, bf16[2,4,4096]{2,1,0:T(4,128)(2,1)S(1)}, u32[]{:S(2)}, u32[]{:S(2)}) %collective-permute-start.2) | collective-permute-done | bytes 65568 | tf_op jit(solution)/shard_map/ppermute | solution.py:18
  35.4 1.0 copy.47
  36.4 46.3 %all-gather.3.cloned.1.call-done = bf16[2,128,4096]{2,0,1:T(2,128)(2,1)} async-done(((bf16[2,16,4096]{2,0,1:T(2,128)(2,1)}), bf16[2,128,4096]{2,0,1:T(2,128)(2,1)}) %all-gather.3.cloned.1.call-update) | async-done | bytes 2097168 | tf_op jit(solution)/shard_map/all_gather | solution.py:26
  82.7 6.2 %copy.48 = bf16[2,128,4096]{1,2,0:T(8,128)(2,1)} copy(bf16[2,128,4096]{2,0,1:T(2,128)(2,1)} %all-gather.3.cloned.1.call-done) | data formatting | bytes 4194304 | tf_op jit(solution)/shard_map/all_gather | solution.py:26
  89.6 19.8 %all-gather.5.cloned.1.call-done = bf16[2,256,4096]{1,2,0:T(8,128)(2,1)} async-done(((bf16[2,128,4096]{1,2,0:T(8,128)(2,1)}), bf16[2,256,4096]{1,2,0:T(8,128)(2,1)}) %all-gather.5.cloned.1.call-update) | async-done | bytes 4194320 | tf_op jit(solution)/shard_map/all_gather | solution.py:26
  109.4 4.5 %fusion.89 = (bf16[1,256,4096]{1,2,0:T(8,128)(2,1)}, bf16[1,256,4096]{1,2,0:T(8,128)(2,1)}) fusion(bf16[2,256,4096]{1,2,0:T(8,128)(2,1)} %all-gather.5.cloned.1.call-done), kind=kLoop, calls=%fused_computation.100 | loop fusion | bytes 8388608 | tf_op jit(solution)/shard_map/slice | solution.py:76
  113.9 3.2 %copy.49 = bf16[256,32,128]{2,0,1:T(8,128)(2,1)S(1)} copy(bf16[256,32,128]{0,2,1:T(8,128)(2,1)} %bitcast.155) | data formatting | bytes 4194304 | tf_op jit(solution)/shard_map/reshape;squeeze | solution.py:71
  117.1 4.1 %copy.52 = bf16[256,32,128]{2,0,1:T(8,128)(2,1)} copy(bf16[256,32,128]{0,2,1:T(8,128)(2,1)} %bitcast.154) | data formatting | bytes 4194304 | tf_op jit(solution)/shard_map/reshape;squeeze | solution.py:71
  121.2 2.0 gather_fusion
  123.2 2.5 %gather_fusion.1 = bf16[26,256,128]{2,1,0:T(8,128)(2,1)S(1)} fusion(bf16[256,32,128]{2,0,1:T(8,128)(2,1)} %copy.52, s32[1024]{0:T(1024)S(1)} %pad_clamp_fusion.1), kind=kCustom, calls=%fused_computation.2.clone | custom fusion | bytes 3407976 | tf_op jit(solution)/shard_map/jit(_take)/gather | solution.py:71
  126.3 1.1 fusion.2
  128.2 1.1 fusion.4
  130.3 1.1 fusion.6
  132.4 2.0 gather_fusion.3
  136.8 1.2 fusion.8
  138.0 2.3 copy.86
  140.6 19.0 %reduce-scatter.3.cloned.1.call-done = bf16[128,4096]{1,0:T(8,128)(2,1)} async-done(((bf16[256,4096]{1,0:T(8,128)(2,1)}), bf16[128,4096]{1,0:T(8,128)(2,1)}) %reduce-scatter.3.cloned.1.call-update) | async-done | bytes 1048592 | tf_op jit(solution)/shard_map/reduce_scatter | solution.py:33
  159.6 2.0 gather_fusion.4
  161.7 3.3 %fusion.53 = bf16[1,26,128,128]{3,2,1,0:T(8,128)(2,1)} fusion(bf16[26,256,128]{2,1,0:T(8,128)(2,1)S(1)} %gather_fusion.2, pred[26]{0:T(512)(128)(4,1)S(1)} %get-tuple-element.6, bf16[26,256,128]{2,1,0:T(8,128)(2,1)} %copy-done.5, pred[26]{0:T(512)(128)(4,1)S(1)} %get-tuple-element.18), kind=kOutput, calls=%fused_computation.45 | convolution fusion | flops 220233728 | bytes 4259892 | tf_op jit(solution)/shard_map/tkb,tkc->kbc/dot_general | solution.py:95
  165.0 1.7 fusion.48
  166.7 38.1 %reduce-scatter.5.cloned.1.call-done = bf16[16,4096]{1,0:T(8,128)(2,1)} async-done(((bf16[128,4096]{1,0:T(8,128)(2,1)}), bf16[16,4096]{1,0:T(8,128)(2,1)}) %reduce-scatter.5.cloned.1.call-update) | async-done | bytes 131088 | tf_op jit(solution)/shard_map/reduce_scatter | solution.py:33
  204.8 1.0 fusion.90
  205.7 6.7 %collective-permute-start.4 = (bf16[4,4096]{1,0:T(4,128)(2,1)S(1)}, bf16[4,4096]{1,0:T(4,128)(2,1)S(1)}, u32[]{:S(2)}, u32[]{:S(2)}) collective-permute-start(bf16[4,4096]{1,0:T(4,128)(2,1)S(1)} %get-tuple-element.15), channel_id=1, source_target_pairs={{0,6},{2,0},{4,2},{6,4},{1,7},{3,1},{5,3},{7,5},{8,14},{10,8},{12,... | collective-permute-start | bytes 98312 | tf_op jit(solution)/shard_map/ppermute | solution.py:18
  212.4 1.9 collective-permute-start.6
  214.4 6.2 %collective-permute-start.5 = (bf16[4,4096]{1,0:T(4,128)(2,1)S(1)}, bf16[4,4096]{1,0:T(4,128)(2,1)S(1)}, u32[]{:S(2)}, u32[]{:S(2)}) collective-permute-start(bf16[4,4096]{1,0:T(4,128)(2,1)S(1)} %get-tuple-element.17), channel_id=1, source_target_pairs={{0,4},{2,6},{4,0},{6,2},{1,5},{3,7},{5,1},{7,3},{8,12},{10,14},{12... | collective-permute-start | bytes 98312 | tf_op jit(solution)/shard_map/ppermute | solution.py:18
  220.6 3.2 %fusion.43 = bf16[1,26,128,128]{3,2,1,0:T(8,128)(2,1)} fusion(bf16[26,256,128]{2,1,0:T(8,128)(2,1)} %gather_fusion.4, pred[26]{0:T(512)(128)(4,1)S(1)} %get-tuple-element.6, bf16[26,256,128]{2,1,0:T(8,128)(2,1)S(1)} %copy-done.4, pred[26]{0:T(512)(128)(4,1)S(1)} %get-tuple-element.18), kind=kOutput, calls=%fused_computation.43 | convolution fusion | flops 220233728 | bytes 4259892 | tf_op jit(solution)/shard_map/tkc,tkb->kcb/dot_general | solution.py:92
  224.2 1.5 fusion.73
  (49 shorter events, 8.3 us)
Async XLA Ops:
  7.2 118.5 %copy-start = (bf16[1,26,128,128]{3,2,1,0:T(8,128)(2,1)S(1)}, bf16[1,26,128,128]{3,2,1,0:T(8,128)(2,1)}, u32[]{:S(2)}) copy-start(bf16[1,26,128,128]{3,2,1,0:T(8,128)(2,1)} %param.13) | copy-start | bytes 2555908
  7.2 75.5 %all-gather.3.cloned.1.call-start = ((), (), s32[]{:S(2)}) async-start(), calls=%async_computation.2 | async-start | bytes 2359296 | tf_op jit(solution)/shard_map/all_gather | solution.py:26
  7.2 6.6 %collective-permute-start = (bf16[1,4,4096]{2,1,0:T(4,128)(2,1)}, bf16[1,4,4096]{2,1,0:T(4,128)(2,1)S(1)}, u32[]{:S(2)}, u32[]{:S(2)}) collective-permute-start(bf16[1,4,4096]{2,1,0:T(4,128)(2,1)} %param.11), channel_id=1, source_target_pairs={{64,0},{128,64},{192,128},{256,192},{320,256},{384,320},{448,384},... | collective-permute-start | bytes 98312 | tf_op jit(solution)/shard_map/ppermute | solution.py:13
  13.8 17.3 %collective-permute-start.3 = (bf16[2,4,4096]{2,1,0:T(4,128)(2,1)S(1)}, bf16[2,4,4096]{2,1,0:T(4,128)(2,1)S(1)}, u32[]{:S(2)}, u32[]{:S(2)}) collective-permute-start(bf16[2,4,4096]{2,1,0:T(4,128)(2,1)S(1)} %constant_dynamic-update-slice_fusion), channel_id=1, source_target_pairs={{0,6},{2,0},{4,2},{6,4},{1,7},{3,1},{5,3},{7,5},{8,14},{10,8},{12,... | collective-permute-start | bytes 196616 | tf_op jit(solution)/shard_map/ppermute | solution.py:18
  24.3 10.9 %collective-permute-start.2 = (bf16[2,4,4096]{2,1,0:T(4,128)(2,1)S(1)}, bf16[2,4,4096]{2,1,0:T(4,128)(2,1)S(1)}, u32[]{:S(2)}, u32[]{:S(2)}) collective-permute-start(bf16[2,4,4096]{2,1,0:T(4,128)(2,1)S(1)} %constant_dynamic-update-slice_fusion), channel_id=1, source_target_pairs={{0,4},{2,6},{4,0},{6,2},{1,5},{3,7},{5,1},{7,3},{8,12},{10,14},{12... | collective-permute-start | bytes 196616 | tf_op jit(solution)/shard_map/ppermute | solution.py:18
  26.3 8.9 %collective-permute-start.1 = (bf16[2,4,4096]{2,1,0:T(4,128)(2,1)S(1)}, bf16[2,4,4096]{2,1,0:T(4,128)(2,1)S(1)}, u32[]{:S(2)}, u32[]{:S(2)}) collective-permute-start(bf16[2,4,4096]{2,1,0:T(4,128)(2,1)S(1)} %constant_dynamic-update-slice_fusion), channel_id=1, source_target_pairs={{0,2},{2,4},{4,6},{6,0},{1,3},{3,5},{5,7},{7,1},{8,10},{10,12},{12... | collective-permute-start | bytes 196616 | tf_op jit(solution)/shard_map/ppermute | solution.py:18
  36.4 73.0 %all-gather.5.cloned.1.call-start = ((), (), s32[]{:S(2)}) async-start(), calls=%async_computation.3 | async-start | bytes 6291456 | tf_op jit(solution)/shard_map/all_gather | solution.py:26
  88.9 0.7 copy-start.9
  88.9 70.7 %reduce-scatter.3.cloned.1.call-start = ((), (), s32[]{:S(2)}) async-start(), calls=%async_computation.4 | async-start | bytes 3145728 | tf_op jit(solution)/shard_map/reduce_scatter | solution.py:33
  125.7 1.7 copy-start.5
  126.3 1.2 copy-start.7
  127.5 1.7 copy-start.10
  128.2 1.5 copy-start.3
  134.5 1.5 copy-start.1
  134.5 1.7 copy-start.8
  140.4 64.4 %reduce-scatter.5.cloned.1.call-start = ((), (), s32[]{:S(2)}) async-start(), calls=%async_computation.5 | async-start | bytes 1179648 | tf_op jit(solution)/shard_map/reduce_scatter | solution.py:33
  161.6 3.3 %copy-start.2 = (bf16[26,256,128]{2,1,0:T(8,128)(2,1)S(1)}, bf16[26,256,128]{2,1,0:T(8,128)(2,1)}, u32[]{:S(2)}) copy-start(bf16[26,256,128]{2,1,0:T(8,128)(2,1)} %gather_fusion.3) | copy-start | bytes 5111812
  161.6 3.3 %copy-start.6 = (bf16[26,256,128]{2,1,0:T(8,128)(2,1)S(1)}, bf16[26,256,128]{2,1,0:T(8,128)(2,1)}, u32[]{:S(2)}) copy-start(bf16[26,256,128]{2,1,0:T(8,128)(2,1)} %copy-done.5) | copy-start | bytes 5111812
  165.0 55.6 %copy-start.4 = (bf16[26,256,128]{2,1,0:T(8,128)(2,1)S(1)}, bf16[26,256,128]{2,1,0:T(8,128)(2,1)}, u32[]{:S(2)}) copy-start(bf16[26,256,128]{2,1,0:T(8,128)(2,1)} %gather_fusion) | copy-start | bytes 5111812
  205.7 18.0 %collective-permute-start.4 = (bf16[4,4096]{1,0:T(4,128)(2,1)S(1)}, bf16[4,4096]{1,0:T(4,128)(2,1)S(1)}, u32[]{:S(2)}, u32[]{:S(2)}) collective-permute-start(bf16[4,4096]{1,0:T(4,128)(2,1)S(1)} %get-tuple-element.15), channel_id=1, source_target_pairs={{0,6},{2,0},{4,2},{6,4},{1,7},{3,1},{5,3},{7,5},{8,14},{10,8},{12,... | collective-permute-start | bytes 98312 | tf_op jit(solution)/shard_map/ppermute | solution.py:18
  212.4 11.4 %collective-permute-start.6 = (bf16[4,4096]{1,0:T(4,128)(2,1)S(1)}, bf16[4,4096]{1,0:T(4,128)(2,1)S(1)}, u32[]{:S(2)}, u32[]{:S(2)}) collective-permute-start(bf16[4,4096]{1,0:T(4,128)(2,1)S(1)} %get-tuple-element.16), channel_id=1, source_target_pairs={{0,2},{2,4},{4,6},{6,0},{1,3},{3,5},{5,7},{7,1},{8,10},{10,12},{12... | collective-permute-start | bytes 98312 | tf_op jit(solution)/shard_map/ppermute | solution.py:18
  214.4 9.8 %collective-permute-start.5 = (bf16[4,4096]{1,0:T(4,128)(2,1)S(1)}, bf16[4,4096]{1,0:T(4,128)(2,1)S(1)}, u32[]{:S(2)}, u32[]{:S(2)}) collective-permute-start(bf16[4,4096]{1,0:T(4,128)(2,1)S(1)} %get-tuple-element.17), channel_id=1, source_target_pairs={{0,4},{2,6},{4,0},{6,2},{1,5},{3,7},{5,1},{7,3},{8,12},{10,14},{12... | collective-permute-start | bytes 98312 | tf_op jit(solution)/shard_map/ppermute | solution.py:18
Sparse Core Ops, SparseCore 0:
  36.5 46.1 all-gather.2
  89.0 20.3 all-gather.4
  140.5 19.0 reduce-scatter.2
  162.5 42.2 reduce-scatter.4

commit v5 on v4

--- a/solution.py
+++ b/solution.py
@@ -22,15 +22,14 @@
     n = lax.axis_size("zh")
     pieces = [block] + [shifted(block, "zh", k) for k in range(1, n)]
     block = jnp.concatenate(pieces, axis=1)
-    for axis in ("y", "core"):
-        block = lax.all_gather(block, axis, axis=1, tiled=True)
-    return block
+    block = lax.all_gather(block, "y", axis=1, tiled=True)
+    return jnp.concatenate([block, shifted(block, "core", 1)], axis=1)
 
 
 def scatter_rows(block):
-    block = block.astype(jnp.bfloat16)
-    for axis in ("core", "y"):
-        block = lax.psum_scatter(block, axis, scatter_dimension=0, tiled=True)
+    own, other = jnp.split(block, 2, axis=0)
+    block = (own + shifted(other, "core", 1)).astype(jnp.bfloat16)
+    block = lax.psum_scatter(block, "y", scatter_dimension=0, tiled=True)
     n = lax.axis_size("zh")
     chunks = jnp.split(block, n, axis=0)
     total = chunks[0].astype(jnp.float32)

time: 233 us -> 199 us (0.85)
  waiting for transfers between devices: 129 us -> 92.8 us
  local copies, waits for them, and re-layouts: 34.6 us -> 28 us
  other arithmetic: 1.86 us -> 6.34 us
  starting transfers between devices: 37.1 us -> 41 us
    reduce_scatter x2 -> x1, waiting for transfers between devices: 57 us -> 33.1 us  [scatter_rows(): block = lax.psum_scatter(block, 'y', scatter_dimension=0, tiled=True)]
    all_gather x2 -> x1, waiting for transfers between devices: 66.1 us -> 46.3 us  [gather_rows(): block = lax.all_gather(block, 'y', axis=1, tiled=True)]
    ppermute x6 -> x8, waiting for transfers between devices: 4.53 us -> 12.3 us  [shifted(): return lax.ppermute(block, axis, [(i, (i + shift) % n) for i in range(n)])]
    slice x1 -> x0, local copies, waits for them, and re-layouts: 4.51 us -> none  [per_device(): upstream = both[1]]
    ppermute x6 -> x8, starting transfers between devices: 32.1 us -> 36.3 us  [shifted(): return lax.ppermute(block, axis, [(i, (i + shift) % n) for i in range(n)])]
  transfers between devices with their start and end apart: 11 -> 11, of which waited for: 7 -> 7; matrix products, arithmetic and copies ran while one was open for 5% -> 6% of each run, Pallas kernels for 0% -> 0%
where the time goes in v5:
time: 199 us; the launch traced here: 198 us
  waiting for transfers between devices  92.8 us (47%)
  starting transfers between devices  41 us (21%)
  local copies, waits for them, and re-layouts  28 us (14%)
  matrix products  15.8 us (8%)
  between operations  14.3 us (7%)
  other arithmetic  6.34 us (3%)
    all_gather x1, waiting for transfers between devices, gather_rows(): block = lax.all_gather(block, 'y', axis=1, tiled=True)  46.3 us
    ppermute x8, starting transfers between devices, shifted(): return lax.ppermute(block, axis, [(i, (i + shift) % n) for i in range(n)])  36.3 us
    reduce_scatter x1, waiting for transfers between devices, scatter_rows(): block = lax.psum_scatter(block, 'y', scatter_dimension=0, tiled=True)  33.1 us
    ppermute x8, waiting for transfers between devices, shifted(): return lax.ppermute(block, axis, [(i, (i + shift) % n) for i in range(n)])  12.3 us
    another operation x2, local copies, waits for them, and re-layouts, pick_bands(): values.reshape(values.shape[0], bands, block)  7.28 us
    gather x3, local copies, waits for them, and re-layouts, pick_cols(): jnp.take(values.reshape(values.shape[0], columns, block), col_ids, axis=1)  4.91 us
    all_gather x1, local copies, waits for them, and re-layouts, gather_rows(): block = lax.all_gather(block, 'y', axis=1, tiled=True)  4.88 us
    ppermute x1, starting transfers between devices, passed_along(): return lax.ppermute(block, axis, route)  4.68 us
  transfers between devices with their start and end apart: 11, of which 7 were waited for; matrix products, arithmetic and copies ran while one was open for 6% of the time, Pallas kernels for 0%

profile of v5, /device:TPU:6, one launch (start us, length us, event | category | flops | bytes accessed | tf_op | source)
XLA Modules:
  0.0 198.3 jit_solution(9811766940556241641)
XLA Ops:
  7.2 4.7 %collective-permute-start = (bf16[1,4,4096]{2,1,0:T(4,128)(2,1)}, bf16[1,4,4096]{2,1,0:T(4,128)(2,1)S(1)}, u32[]{:S(2)}, u32[]{:S(2)}) collective-permute-start(bf16[1,4,4096]{2,1,0:T(4,128)(2,1)} %param.11), channel_id=1, source_target_pairs={{64,0},{128,64},{192,128},{256,192},{320,256},{384,320},{448,384},... | collective-permute-start | bytes 98312 | tf_op jit(solution)/shard_map/ppermute | solution.py:13
  12.7 1.1 collective-permute-done
  13.8 10.5 %collective-permute-start.3 = (bf16[2,4,4096]{2,1,0:T(4,128)(2,1)S(1)}, bf16[2,4,4096]{2,1,0:T(4,128)(2,1)S(1)}, u32[]{:S(2)}, u32[]{:S(2)}) collective-permute-start(bf16[2,4,4096]{2,1,0:T(4,128)(2,1)S(1)} %constant_dynamic-update-slice_fusion), channel_id=1, source_target_pairs={{0,6},{2,0},{4,2},{6,4},{1,7},{3,1},{5,3},{7,5},{8,14},{10,8},{12,... | collective-permute-start | bytes 196616 | tf_op jit(solution)/shard_map/ppermute | solution.py:18
  24.3 1.9 collective-permute-start.2
  26.3 4.8 %collective-permute-start.1 = (bf16[2,4,4096]{2,1,0:T(4,128)(2,1)S(1)}, bf16[2,4,4096]{2,1,0:T(4,128)(2,1)S(1)}, u32[]{:S(2)}, u32[]{:S(2)}) collective-permute-start(bf16[2,4,4096]{2,1,0:T(4,128)(2,1)S(1)} %constant_dynamic-update-slice_fusion), channel_id=1, source_target_pairs={{0,2},{2,4},{4,6},{6,0},{1,3},{3,5},{5,7},{7,1},{8,10},{10,12},{12... | collective-permute-start | bytes 196616 | tf_op jit(solution)/shard_map/ppermute | solution.py:18
  31.1 4.1 %collective-permute-done.2 = bf16[2,4,4096]{2,1,0:T(4,128)(2,1)S(1)} collective-permute-done((bf16[2,4,4096]{2,1,0:T(4,128)(2,1)S(1)}, bf16[2,4,4096]{2,1,0:T(4,128)(2,1)S(1)}, u32[]{:S(2)}, u32[]{:S(2)}) %collective-permute-start.2) | collective-permute-done | bytes 65568 | tf_op jit(solution)/shard_map/ppermute | solution.py:18
  36.4 46.3 %all-gather.2.cloned.1.call-done = bf16[2,128,4096]{2,0,1:T(2,128)(2,1)} async-done(((bf16[2,16,4096]{2,0,1:T(2,128)(2,1)}), bf16[2,128,4096]{2,0,1:T(2,128)(2,1)}) %all-gather.2.cloned.1.call-update) | async-done | bytes 2097168 | tf_op jit(solution)/shard_map/all_gather | solution.py:25
  82.7 4.9 %copy.50 = bf16[2,128,4096]{1,2,0:T(8,128)(2,1)S(1)} copy(bf16[2,128,4096]{2,0,1:T(2,128)(2,1)} %all-gather.2.cloned.1.call-done) | data formatting | bytes 4194304 | tf_op jit(solution)/shard_map/all_gather | solution.py:25
  87.6 1.9 collective-permute-start.4
  89.6 4.1 %collective-permute-done.4 = bf16[2,128,4096]{1,2,0:T(8,128)(2,1)S(1)} collective-permute-done((bf16[2,128,4096]{1,2,0:T(8,128)(2,1)S(1)}, bf16[2,128,4096]{1,2,0:T(8,128)(2,1)S(1)}, u32[]{:S(2)}, u32[]{:S(2)}) %collective-permute-start.4) | collective-permute-done | bytes 2097184 | tf_op jit(solution)/shard_map/ppermute | solution.py:18
  93.7 2.2 %fusion.11 = (bf16[1,256,4096]{1,2,0:T(8,128)(2,1)}, bf16[1,256,4096]{1,2,0:T(8,128)(2,1)}) fusion(bf16[2,128,4096]{1,2,0:T(8,128)(2,1)S(1)} %copy.50, bf16[2,128,4096]{1,2,0:T(8,128)(2,1)S(1)} %collective-permute-done.4), kind=kLoop, calls=%fused_computation.17 | loop fusion | flops 8388608 | bytes 8388608 | tf_op jit(solution)/shard_map/concatenate | solution.py:26
  95.9 3.2 %copy.51 = bf16[256,32,128]{2,0,1:T(8,128)(2,1)S(1)} copy(bf16[256,32,128]{0,2,1:T(8,128)(2,1)} %bitcast.160) | data formatting | bytes 4194304 | tf_op jit(solution)/shard_map/reshape;squeeze | solution.py:70
  99.1 4.1 %copy.54 = bf16[256,32,128]{2,0,1:T(8,128)(2,1)} copy(bf16[256,32,128]{0,2,1:T(8,128)(2,1)} %bitcast.159) | data formatting | bytes 4194304 | tf_op jit(solution)/shard_map/reshape;squeeze | solution.py:70
  103.2 2.0 %gather_fusion = bf16[26,256,128]{2,1,0:T(8,128)(2,1)} fusion(bf16[256,32,128]{2,0,1:T(8,128)(2,1)S(1)} %copy.51, s32[1024]{0:T(1024)S(1)} %pad_clamp_fusion.1), kind=kCustom, calls=%fused_computation.clone | custom fusion | bytes 3407976 | tf_op jit(solution)/shard_map/jit(_take)/gather | solution.py:70
  105.2 2.5 %gather_fusion.1 = bf16[26,256,128]{2,1,0:T(8,128)(2,1)S(1)} fusion(bf16[256,32,128]{2,0,1:T(8,128)(2,1)} %copy.54, s32[1024]{0:T(1024)S(1)} %pad_clamp_fusion.1), kind=kCustom, calls=%fused_computation.2.clone | custom fusion | bytes 3407976 | tf_op jit(solution)/shard_map/jit(_take)/gather | solution.py:70
  108.4 1.1 fusion.2
  110.2 1.1 fusion.4
  114.5 2.0 %gather_fusion.3 = bf16[26,256,128]{2,1,0:T(8,128)(2,1)} fusion(bf16[256,2,128]{2,0,1:T(8,128)(2,1)S(1)} %get-tuple-element.16, s32[1024]{0:T(1024)S(1)} %pad_clamp_fusion), kind=kCustom, calls=%fused_computation.3.clone | custom fusion | bytes 3407976 | tf_op jit(solution)/shard_map/jit(_take)/gather | solution.py:67
  118.8 1.1 fusion.8
  120.4 1.6 copy.90
  122.0 2.2 %collective-permute-start.5 = (f32[128,4096]{1,0:T(8,128)S(1)}, f32[128,4096]{1,0:T(8,128)S(1)}, u32[]{:S(2)}, u32[]{:S(2)}) collective-permute-start(f32[128,4096]{1,0:T(8,128)S(1)} %bitcast.162), channel_id=1, source_target_pairs={{0,1},{1,0},{2,3},{3,2},{4,5},{5,4},{6,7},{7,6},{8,9},{9,8},{10,11... | collective-permute-start | bytes 6291464 | tf_op jit(solution)/shard_map/ppermute | solution.py:18
  124.3 3.8 %collective-permute-done.5 = f32[128,4096]{1,0:T(8,128)S(1)} collective-permute-done((f32[128,4096]{1,0:T(8,128)S(1)}, f32[128,4096]{1,0:T(8,128)S(1)}, u32[]{:S(2)}, u32[]{:S(2)}) %collective-permute-start.5) | collective-permute-done | bytes 2097184 | tf_op jit(solution)/shard_map/ppermute | solution.py:18
  128.1 2.3 %fusion.12 = bf16[128,4096]{1,0:T(8,128)(2,1)} fusion(f32[128,4096]{1,0:T(8,128)S(1)} %collective-permute-done.5, f32[16,8,32,128]{3,2,1,0:T(8,128)S(1)} %bitcast.158), kind=kLoop, calls=%fused_computation.20 | loop fusion | flops 1048576 | bytes 5242880 | tf_op jit(solution)/shard_map/convert_element_type | solution.py:31
  130.4 2.0 %gather_fusion.4 = bf16[26,256,128]{2,1,0:T(8,128)(2,1)} fusion(bf16[256,2,128]{2,0,1:T(8,128)(2,1)S(1)} %get-tuple-element.14, s32[1024]{0:T(1024)S(1)} %pad_clamp_fusion), kind=kCustom, calls=%fused_computation.4.clone | custom fusion | bytes 3407976 | tf_op jit(solution)/shard_map/jit(_take)/gather | solution.py:67
  132.4 3.3 %fusion.55 = bf16[1,26,128,128]{3,2,1,0:T(8,128)(2,1)} fusion(bf16[26,256,128]{2,1,0:T(8,128)(2,1)S(1)} %gather_fusion.2, pred[26]{0:T(512)(128)(4,1)S(1)} %get-tuple-element.6, bf16[26,256,128]{2,1,0:T(8,128)(2,1)} %copy-done.5, pred[26]{0:T(512)(128)(4,1)S(1)} %get-tuple-element.20), kind=kOutput, calls=%fused_computation.51 | convolution fusion | flops 220233728 | bytes 4259892 | tf_op jit(solution)/shard_map/tkb,tkc->kbc/dot_general | solution.py:94
  135.7 1.7 fusion.50
  137.5 33.1 %reduce-scatter.2.cloned.1.call-done = bf16[16,4096]{1,0:T(8,128)(2,1)} async-done(((bf16[128,4096]{1,0:T(8,128)(2,1)}), bf16[16,4096]{1,0:T(8,128)(2,1)}) %reduce-scatter.2.cloned.1.call-update) | async-done | bytes 131088 | tf_op jit(solution)/shard_map/reduce_scatter | solution.py:32
  171.6 6.6 %collective-permute-start.6 = (bf16[4,4096]{1,0:T(4,128)(2,1)S(1)}, bf16[4,4096]{1,0:T(4,128)(2,1)S(1)}, u32[]{:S(2)}, u32[]{:S(2)}) collective-permute-start(bf16[4,4096]{1,0:T(4,128)(2,1)S(1)} %get-tuple-element.17), channel_id=1, source_target_pairs={{0,6},{2,0},{4,2},{6,4},{1,7},{3,1},{5,3},{7,5},{8,14},{10,8},{12,... | collective-permute-start | bytes 98312 | tf_op jit(solution)/shard_map/ppermute | solution.py:18
  178.2 1.9 collective-permute-start.8
  180.1 6.4 %collective-permute-start.7 = (bf16[4,4096]{1,0:T(4,128)(2,1)S(1)}, bf16[4,4096]{1,0:T(4,128)(2,1)S(1)}, u32[]{:S(2)}, u32[]{:S(2)}) collective-permute-start(bf16[4,4096]{1,0:T(4,128)(2,1)S(1)} %get-tuple-element.19), channel_id=1, source_target_pairs={{0,4},{2,6},{4,0},{6,2},{1,5},{3,7},{5,1},{7,3},{8,12},{10,14},{12... | collective-permute-start | bytes 98312 | tf_op jit(solution)/shard_map/ppermute | solution.py:18
  186.5 3.2 %fusion.45 = bf16[1,26,128,128]{3,2,1,0:T(8,128)(2,1)} fusion(bf16[26,256,128]{2,1,0:T(8,128)(2,1)} %gather_fusion.4, pred[26]{0:T(512)(128)(4,1)S(1)} %get-tuple-element.6, bf16[26,256,128]{2,1,0:T(8,128)(2,1)S(1)} %copy-done.4, pred[26]{0:T(512)(128)(4,1)S(1)} %get-tuple-element.20), kind=kOutput, calls=%fused_computation.49 | convolution fusion | flops 220233728 | bytes 4259892 | tf_op jit(solution)/shard_map/tkc,tkb->kcb/dot_general | solution.py:91
  189.9 1.5 fusion.75
  (49 shorter events, 10.7 us)
Async XLA Ops:
  7.2 100.5 %copy-start = (bf16[1,26,128,128]{3,2,1,0:T(8,128)(2,1)S(1)}, bf16[1,26,128,128]{3,2,1,0:T(8,128)(2,1)}, u32[]{:S(2)}) copy-start(bf16[1,26,128,128]{3,2,1,0:T(8,128)(2,1)} %param.13) | copy-start | bytes 2555908
  7.2 75.5 %all-gather.2.cloned.1.call-start = ((), (), s32[]{:S(2)}) async-start(), calls=%async_computation.1 | async-start | bytes 2359296 | tf_op jit(solution)/shard_map/all_gather | solution.py:25
  7.2 6.6 %collective-permute-start = (bf16[1,4,4096]{2,1,0:T(4,128)(2,1)}, bf16[1,4,4096]{2,1,0:T(4,128)(2,1)S(1)}, u32[]{:S(2)}, u32[]{:S(2)}) collective-permute-start(bf16[1,4,4096]{2,1,0:T(4,128)(2,1)} %param.11), channel_id=1, source_target_pairs={{64,0},{128,64},{192,128},{256,192},{320,256},{384,320},{448,384},... | collective-permute-start | bytes 98312 | tf_op jit(solution)/shard_map/ppermute | solution.py:13
  13.8 17.3 %collective-permute-start.3 = (bf16[2,4,4096]{2,1,0:T(4,128)(2,1)S(1)}, bf16[2,4,4096]{2,1,0:T(4,128)(2,1)S(1)}, u32[]{:S(2)}, u32[]{:S(2)}) collective-permute-start(bf16[2,4,4096]{2,1,0:T(4,128)(2,1)S(1)} %constant_dynamic-update-slice_fusion), channel_id=1, source_target_pairs={{0,6},{2,0},{4,2},{6,4},{1,7},{3,1},{5,3},{7,5},{8,14},{10,8},{12,... | collective-permute-start | bytes 196616 | tf_op jit(solution)/shard_map/ppermute | solution.py:18
  24.3 10.9 %collective-permute-start.2 = (bf16[2,4,4096]{2,1,0:T(4,128)(2,1)S(1)}, bf16[2,4,4096]{2,1,0:T(4,128)(2,1)S(1)}, u32[]{:S(2)}, u32[]{:S(2)}) collective-permute-start(bf16[2,4,4096]{2,1,0:T(4,128)(2,1)S(1)} %constant_dynamic-update-slice_fusion), channel_id=1, source_target_pairs={{0,4},{2,6},{4,0},{6,2},{1,5},{3,7},{5,1},{7,3},{8,12},{10,14},{12... | collective-permute-start | bytes 196616 | tf_op jit(solution)/shard_map/ppermute | solution.py:18
  26.3 8.9 %collective-permute-start.1 = (bf16[2,4,4096]{2,1,0:T(4,128)(2,1)S(1)}, bf16[2,4,4096]{2,1,0:T(4,128)(2,1)S(1)}, u32[]{:S(2)}, u32[]{:S(2)}) collective-permute-start(bf16[2,4,4096]{2,1,0:T(4,128)(2,1)S(1)} %constant_dynamic-update-slice_fusion), channel_id=1, source_target_pairs={{0,2},{2,4},{4,6},{6,0},{1,3},{3,5},{5,7},{7,1},{8,10},{10,12},{12... | collective-permute-start | bytes 196616 | tf_op jit(solution)/shard_map/ppermute | solution.py:18
  36.4 53.2 %copy-start.9 = (s32[1,26]{1,0:T(1,128)S(1)}, s32[1,26]{1,0:T(1,128)}, u32[]{:S(2)}) copy-start(s32[1,26]{1,0:T(1,128)} %param.12) | copy-start | bytes 316
  36.4 134.2 %reduce-scatter.2.cloned.1.call-start = ((), (), s32[]{:S(2)}) async-start(), calls=%async_computation.2 | async-start | bytes 1179648 | tf_op jit(solution)/shard_map/reduce_scatter | solution.py:32
  87.6 6.1 %collective-permute-start.4 = (bf16[2,128,4096]{1,2,0:T(8,128)(2,1)S(1)}, bf16[2,128,4096]{1,2,0:T(8,128)(2,1)S(1)}, u32[]{:S(2)}, u32[]{:S(2)}) collective-permute-start(bf16[2,128,4096]{1,2,0:T(8,128)(2,1)S(1)} %copy.50), channel_id=1, source_target_pairs={{0,1},{1,0},{2,3},{3,2},{4,5},{5,4},{6,7},{7,6},{8,9},{9,8},{10,11... | collective-permute-start | bytes 6291464 | tf_op jit(solution)/shard_map/ppermute | solution.py:18
  107.7 1.7 copy-start.5
  108.4 1.2 copy-start.7
  109.5 1.7 copy-start.10
  110.2 1.5 copy-start.3
  116.5 1.5 copy-start.1
  116.5 1.7 copy-start.8
  122.0 6.1 %collective-permute-start.5 = (f32[128,4096]{1,0:T(8,128)S(1)}, f32[128,4096]{1,0:T(8,128)S(1)}, u32[]{:S(2)}, u32[]{:S(2)}) collective-permute-start(f32[128,4096]{1,0:T(8,128)S(1)} %bitcast.162), channel_id=1, source_target_pairs={{0,1},{1,0},{2,3},{3,2},{4,5},{5,4},{6,7},{7,6},{8,9},{9,8},{10,11... | collective-permute-start | bytes 6291464 | tf_op jit(solution)/shard_map/ppermute | solution.py:18
  132.4 3.3 %copy-start.2 = (bf16[26,256,128]{2,1,0:T(8,128)(2,1)S(1)}, bf16[26,256,128]{2,1,0:T(8,128)(2,1)}, u32[]{:S(2)}) copy-start(bf16[26,256,128]{2,1,0:T(8,128)(2,1)} %gather_fusion.3) | copy-start | bytes 5111812
  132.4 3.3 %copy-start.6 = (bf16[26,256,128]{2,1,0:T(8,128)(2,1)S(1)}, bf16[26,256,128]{2,1,0:T(8,128)(2,1)}, u32[]{:S(2)}) copy-start(bf16[26,256,128]{2,1,0:T(8,128)(2,1)} %copy-done.5) | copy-start | bytes 5111812
  135.7 50.8 %copy-start.4 = (bf16[26,256,128]{2,1,0:T(8,128)(2,1)S(1)}, bf16[26,256,128]{2,1,0:T(8,128)(2,1)}, u32[]{:S(2)}) copy-start(bf16[26,256,128]{2,1,0:T(8,128)(2,1)} %gather_fusion) | copy-start | bytes 5111812
  171.6 18.1 %collective-permute-start.6 = (bf16[4,4096]{1,0:T(4,128)(2,1)S(1)}, bf16[4,4096]{1,0:T(4,128)(2,1)S(1)}, u32[]{:S(2)}, u32[]{:S(2)}) collective-permute-start(bf16[4,4096]{1,0:T(4,128)(2,1)S(1)} %get-tuple-element.17), channel_id=1, source_target_pairs={{0,6},{2,0},{4,2},{6,4},{1,7},{3,1},{5,3},{7,5},{8,14},{10,8},{12,... | collective-permute-start | bytes 98312 | tf_op jit(solution)/shard_map/ppermute | solution.py:18
  178.2 11.5 %collective-permute-start.8 = (bf16[4,4096]{1,0:T(4,128)(2,1)S(1)}, bf16[4,4096]{1,0:T(4,128)(2,1)S(1)}, u32[]{:S(2)}, u32[]{:S(2)}) collective-permute-start(bf16[4,4096]{1,0:T(4,128)(2,1)S(1)} %get-tuple-element.18), channel_id=1, source_target_pairs={{0,2},{2,4},{4,6},{6,0},{1,3},{3,5},{5,7},{7,1},{8,10},{10,12},{12... | collective-permute-start | bytes 98312 | tf_op jit(solution)/shard_map/ppermute | solution.py:18
  180.1 9.8 %collective-permute-start.7 = (bf16[4,4096]{1,0:T(4,128)(2,1)S(1)}, bf16[4,4096]{1,0:T(4,128)(2,1)S(1)}, u32[]{:S(2)}, u32[]{:S(2)}) collective-permute-start(bf16[4,4096]{1,0:T(4,128)(2,1)S(1)} %get-tuple-element.19), channel_id=1, source_target_pairs={{0,4},{2,6},{4,0},{6,2},{1,5},{3,7},{5,1},{7,3},{8,12},{10,14},{12... | collective-permute-start | bytes 98312 | tf_op jit(solution)/shard_map/ppermute | solution.py:18
Sparse Core Ops, SparseCore 0:
  36.5 46.1 all-gather.1
  130.5 40.0 reduce-scatter.1

commit v6 on v5

v6 whole, which is shorter than its diff:
```python
import jax
import jax.numpy as jnp
from jax import lax
from jax.sharding import Mesh, PartitionSpec as P

FF = 16384
ROW_AXES = ("y", "zh", "core")


def passed_along(block, axis, distance):
    devices = range(lax.axis_size(axis))
    route = [((i - distance) % len(devices), i) for i in devices]
    return lax.ppermute(block, axis, route)


def shifted(block, axis, shift):
    n = lax.axis_size(axis)
    return lax.ppermute(block, axis, [(i, (i + shift) % n) for i in range(n)])


def gather_rows(block):
    n = lax.axis_size("zh")
    pieces = [block] + [shifted(block, "zh", k) for k in range(1, n)]
    block = jnp.concatenate(pieces, axis=1)
    block = lax.all_gather(block, "y", axis=1, tiled=True)
    return jnp.concatenate([block, shifted(block, "core", 1)], axis=1)


def scatter_rows(block):
    own, other = jnp.split(block, 2, axis=0)
    block = (own + shifted(other, "core", 1)).astype(jnp.bfloat16)
    block = lax.psum_scatter(block, "y", scatter_dimension=0, tiled=True)
    n = lax.axis_size("zh")
    chunks = jnp.split(block, n, axis=0)
    total = chunks[0].astype(jnp.float32)
    for k in range(1, n):
        total = total + shifted(chunks[k], "zh", -k).astype(jnp.float32)
    return total


def per_device(saved_input, grad_sent, kept_blocks, gate_blocks, up_blocks, down_blocks):
    width = saved_input.shape[2]
    block = gate_blocks.shape[2]
    bands = width // block
    n_dp = 1
    for axis in ROW_AXES:
        n_dp *= lax.axis_size(axis)
    columns = FF // n_dp // block
    ids = kept_blocks[0]
    band_ids = ids // columns
    col_ids = ids % columns
    band_onehot = (band_ids[:, None] == jnp.arange(bands, dtype=jnp.int32)[None, :]).astype(
        jnp.bfloat16
    )
    col_onehot = (col_ids[:, None] == jnp.arange(columns, dtype=jnp.int32)[None, :]).astype(
        jnp.bfloat16
    )
    hidden_units = columns * block

    def dense_in(blocks):
        placed = jnp.einsum(
            "kr,kc,kbn->rbcn", band_onehot, col_onehot, blocks,
            preferred_element_type=jnp.float32,
        )
        return placed.astype(jnp.bfloat16).reshape(width, hidden_units)

    def dense_down(blocks):
        placed = jnp.einsum(
            "kc,kr,knb->cnrb", col_onehot, band_onehot, blocks,
            preferred_element_type=jnp.float32,
        )
        return placed.astype(jnp.bfloat16).reshape(hidden_units, width)

    def kept_in(dense):
        tiles = dense.astype(jnp.bfloat16).reshape(bands, block, columns, block)
        picked = jnp.einsum(
            "kr,kc,rbcn->kbn", band_onehot, col_onehot, tiles,
            preferred_element_type=jnp.float32,
        )
        return picked.astype(jnp.bfloat16)

    def kept_down(dense):
        tiles = dense.astype(jnp.bfloat16).reshape(columns, block, bands, block)
        picked = jnp.einsum(
            "kc,kr,cnrb->knb", col_onehot, band_onehot, tiles,
            preferred_element_type=jnp.float32,
        )
        return picked.astype(jnp.bfloat16)

    w_gate = dense_in(gate_blocks[0])
    w_up = dense_in(up_blocks[0])
    w_down = dense_down(down_blocks[0])

    incoming = passed_along(grad_sent, "section", -1)
    both = gather_rows(jnp.concatenate([saved_input, incoming], axis=0))
    inputs = both[0]
    upstream = both[1]
    f32 = jnp.float32
    gate = jnp.dot(inputs, w_gate, preferred_element_type=f32)
    up = jnp.dot(inputs, w_up, preferred_element_type=f32)
    sig = jax.nn.sigmoid(gate)
    act = gate * sig
    hidden = (act * up).astype(jnp.bfloat16)
    dhid = lax.dot_general(upstream, w_down, (((1,), (1,)), ((), ())), preferred_element_type=f32)
    grad_up_act = (dhid * act).astype(jnp.bfloat16)
    grad_gate_act = (dhid * up * sig * (1.0 + gate * (1.0 - sig))).astype(jnp.bfloat16)
    rows_t = (((0,), (0,)), ((), ()))
    tiles_gate = kept_in(lax.dot_general(inputs, grad_gate_act, rows_t, preferred_element_type=f32))
    tiles_up = kept_in(lax.dot_general(inputs, grad_up_act, rows_t, preferred_element_type=f32))
    tiles_down = kept_down(lax.dot_general(hidden, upstream, rows_t, preferred_element_type=f32))
    hid_t = (((1,), (1,)), ((), ()))
    whole_term = lax.dot_general(grad_gate_act, w_gate, hid_t, preferred_element_type=f32)
    whole_term = whole_term + lax.dot_general(
        grad_up_act, w_up, hid_t, preferred_element_type=f32
    )
    summed = scatter_rows(whole_term)
    grad_input = summed.astype(jnp.bfloat16)[None]
    return (grad_input, tiles_gate[None], tiles_up[None], tiles_down[None])


def solution(mesh):
    n_dp = mesh.shape["dp"]
    split = Mesh(
        mesh.devices.reshape(mesh.shape["section"], n_dp // 8, 4, 2),
        ("section",) + ROW_AXES,
    )
    rows = P("section", ROW_AXES, None)
    blocks = P("section", ROW_AXES, None, None)
    return jax.shard_map(
        per_device,
        mesh=split,
        in_specs=(rows, rows, P("section", ROW_AXES), blocks, blocks, blocks),
        out_specs=(rows, blocks, blocks, blocks),
        check_vma=False,
    )
```

time: 199 us -> 190 us (0.955)
  waiting for transfers between devices: 92.8 us -> 78.5 us
  matrix products: 15.8 us -> 23.4 us
  local copies, waits for them, and re-layouts: 28 us -> 25.7 us
    reduce_scatter x1, waiting for transfers between devices: 33.1 us -> 23.3 us  [scatter_rows(): block = lax.psum_scatter(block, 'y', scatter_dimension=0, tiled=True)]
    convert_element_type x0 -> x2, local copies, waits for them, and re-layouts: none -> 9.53 us  [dense_in(): return placed.astype(jnp.bfloat16).reshape(width, hidden_units)]
    gather x5 -> x0, local copies, waits for them, and re-layouts: 9.4 us -> none  [the longest x3 4.91 us: pick_cols(): jnp.take(values.reshape(values.shape[0], columns, block), col_ids, axis=1)]
    dot_general x12 -> x14, matrix products: 15.8 us -> 23.4 us  [the longest x2 5.69 us: dense_in(): jnp.einsum('kr,kc,kbn->rbcn', band_onehot, col_onehot, blocks, preferred_...]
    another operation x2 -> x0, local copies, waits for them, and re-layouts: 7.28 us -> none  [pick_bands(): values.reshape(values.shape[0], bands, block)]
    unnamed x24 -> x22, local copies, waits for them, and re-layouts: 4.01 us -> 9.11 us
    all_gather x1 -> x0, local copies, waits for them, and re-layouts: 4.88 us -> none  [gather_rows(): block = lax.all_gather(block, 'y', axis=1, tiled=True)]
    ppermute x8, waiting for transfers between devices: 12.3 us -> 7.72 us  [shifted(): return lax.ppermute(block, axis, [(i, (i + shift) % n) for i in range(n)])]
  transfers between devices with their start and end apart: 11 -> 11, of which waited for: 7 -> 5; matrix products, arithmetic and copies ran while one was open for 6% -> 20% of each run, Pallas kernels for 0% -> 0%
where the time goes in v6:
time: 190 us; the launch traced here: 189 us
  waiting for transfers between devices  78.5 us (41%)
  starting transfers between devices  42.4 us (22%)
  local copies, waits for them, and re-layouts  25.7 us (14%)
  matrix products  23.4 us (12%)
  between operations  14.3 us (8%)
  other arithmetic  4.37 us (2%)
    all_gather x1, waiting for transfers between devices, gather_rows(): block = lax.all_gather(block, 'y', axis=1, tiled=True)  46.3 us
    ppermute x8, starting transfers between devices, shifted(): return lax.ppermute(block, axis, [(i, (i + shift) % n) for i in range(n)])  37.8 us
    reduce_scatter x1, waiting for transfers between devices, scatter_rows(): block = lax.psum_scatter(block, 'y', scatter_dimension=0, tiled=True)  23.3 us
    convert_element_type x2, local copies, waits for them, and re-layouts, dense_in(): return placed.astype(jnp.bfloat16).reshape(width, hidden_units)  9.53 us
    unnamed x22, local copies, waits for them, and re-layouts  9.11 us
    ppermute x8, waiting for transfers between devices, shifted(): return lax.ppermute(block, axis, [(i, (i + shift) % n) for i in range(n)])  7.72 us
    dot_general x2, matrix products, dense_in(): jnp.einsum('kr,kc,kbn->rbcn', band_onehot, col_onehot, blocks, preferred_...  5.69 us
    ppermute x1, starting transfers between devices, passed_along(): return lax.ppermute(block, axis, route)  4.55 us
  transfers between devices with their start and end apart: 11, of which 5 were waited for; matrix products, arithmetic and copies ran while one was open for 20% of the time, Pallas kernels for 0%

profile of v6, /device:TPU:6, one launch (start us, length us, event | category | flops | bytes accessed | tf_op | source)
XLA Modules:
  0.0 188.7 jit_solution(15187597808844752315)
XLA Ops:
  7.2 4.5 %collective-permute-start = (bf16[1,4,4096]{2,1,0:T(4,128)(2,1)}, bf16[1,4,4096]{2,1,0:T(4,128)(2,1)S(1)}, u32[]{:S(2)}, u32[]{:S(2)}) collective-permute-start(bf16[1,4,4096]{2,1,0:T(4,128)(2,1)} %param.7), channel_id=1, source_target_pairs={{64,0},{128,64},{192,128},{256,192},{320,256},{384,320},{448,384},... | collective-permute-start | bytes 98312 | tf_op jit(solution)/shard_map/ppermute | solution.py:13
  13.7 10.5 %collective-permute-start.3 = (bf16[2,4,4096]{2,1,0:T(4,128)(2,1)S(1)}, bf16[2,4,4096]{2,1,0:T(4,128)(2,1)S(1)}, u32[]{:S(2)}, u32[]{:S(2)}) collective-permute-start(bf16[2,4,4096]{2,1,0:T(4,128)(2,1)S(1)} %constant_dynamic-update-slice_fusion), channel_id=1, source_target_pairs={{0,6},{2,0},{4,2},{6,4},{1,7},{3,1},{5,3},{7,5},{8,14},{10,8},{12,... | collective-permute-start | bytes 196616 | tf_op jit(solution)/shard_map/ppermute | solution.py:18
  24.2 1.9 %collective-permute-start.2 = (bf16[2,4,4096]{2,1,0:T(4,128)(2,1)S(1)}, bf16[2,4,4096]{2,1,0:T(4,128)(2,1)S(1)}, u32[]{:S(2)}, u32[]{:S(2)}) collective-permute-start(bf16[2,4,4096]{2,1,0:T(4,128)(2,1)S(1)} %constant_dynamic-update-slice_fusion), channel_id=1, source_target_pairs={{0,4},{2,6},{4,0},{6,2},{1,5},{3,7},{5,1},{7,3},{8,12},{10,14},{12... | collective-permute-start | bytes 196616 | tf_op jit(solution)/shard_map/ppermute | solution.py:18
  26.1 4.8 %collective-permute-start.1 = (bf16[2,4,4096]{2,1,0:T(4,128)(2,1)S(1)}, bf16[2,4,4096]{2,1,0:T(4,128)(2,1)S(1)}, u32[]{:S(2)}, u32[]{:S(2)}) collective-permute-start(bf16[2,4,4096]{2,1,0:T(4,128)(2,1)S(1)} %constant_dynamic-update-slice_fusion), channel_id=1, source_target_pairs={{0,2},{2,4},{4,6},{6,0},{1,3},{3,5},{5,7},{7,1},{8,10},{10,12},{12... | collective-permute-start | bytes 196616 | tf_op jit(solution)/shard_map/ppermute | solution.py:18
  30.9 4.1 %collective-permute-done.2 = bf16[2,4,4096]{2,1,0:T(4,128)(2,1)S(1)} collective-permute-done((bf16[2,4,4096]{2,1,0:T(4,128)(2,1)S(1)}, bf16[2,4,4096]{2,1,0:T(4,128)(2,1)S(1)}, u32[]{:S(2)}, u32[]{:S(2)}) %collective-permute-start.2) | collective-permute-done | bytes 65568 | tf_op jit(solution)/shard_map/ppermute | solution.py:18
  36.0 46.3 %all-gather.2.cloned.1.call-done = bf16[2,128,4096]{2,1,0:T(8,128)(2,1)} async-done(((bf16[2,16,4096]{2,1,0:T(8,128)(2,1)}), bf16[2,128,4096]{2,1,0:T(8,128)(2,1)}) %all-gather.2.cloned.1.call-update) | async-done | bytes 2097168 | tf_op jit(solution)/shard_map/all_gather | solution.py:25
  82.3 1.9 %collective-permute-start.4 = (bf16[2,128,4096]{2,1,0:T(8,128)(2,1)}, bf16[2,128,4096]{2,1,0:T(8,128)(2,1)}, u32[]{:S(2)}, u32[]{:S(2)}) collective-permute-start(bf16[2,128,4096]{2,1,0:T(8,128)(2,1)} %all-gather.2.cloned.1.call-done), channel_id=1, source_target_pairs={{0,1},{1,0},{2,3},{3,2},{4,5},{5,4},{6,7},{7,6},{8,9},{9,8},{10,11... | collective-permute-start | bytes 6291464 | tf_op jit(solution)/shard_map/ppermute | solution.py:18
  85.0 3.4 %convert_bitcast_fusion = bf16[32,128,2,128]{3,0,1,2:T(8,128)(2,1)} fusion(bf16[26,128,128]{2,1,0:T(8,128)(2,1)} %bitcast.139, f32[26,32]{1,0:T(8,128)S(1)} %fusion.62, f32[26,2]{0,1:T(2,128)S(1)} %compare_convert_fusion), kind=kOutput, calls=%fused_computation.27 | convolution fusion | flops 55576192 | bytes 2952656 | tf_op jit(solution)/shard_map/kr,kc,kbn->rbcn/dot_general | solution.py:61
  88.4 4.3 %copy.29 = bf16[32,128,2,128]{1,0,3,2:T(8,128)(2,1)S(1)} copy(bf16[32,128,2,128]{3,0,1,2:T(8,128)(2,1)} %convert_bitcast_fusion) | data formatting | bytes 4194304 | tf_op jit(solution)/shard_map/convert_element_type | solution.py:65
  92.8 2.3 %convert_bitcast_fusion.1 = bf16[32,128,2,128]{3,0,1,2:T(8,128)(2,1)} fusion(bf16[26,128,128]{2,1,0:T(8,128)(2,1)S(1)} %bitcast.140, f32[26,32]{1,0:T(8,128)S(1)} %fusion.62, f32[26,2]{0,1:T(2,128)S(1)} %compare_convert_fusion), kind=kOutput, calls=%fused_computation.28 | convolution fusion | flops 55576192 | bytes 2952656 | tf_op jit(solution)/shard_map/kr,kc,kbn->rbcn/dot_general | solution.py:61
  95.1 5.2 %copy.26 = bf16[32,128,2,128]{1,0,3,2:T(8,128)(2,1)} copy(bf16[32,128,2,128]{3,0,1,2:T(8,128)(2,1)} %convert_bitcast_fusion.1) | data formatting | bytes 4194304 | tf_op jit(solution)/shard_map/convert_element_type | solution.py:65
  102.1 1.7 constant_dynamic-update-slice_fusion.2
  104.8 2.1 %copy-done.2 = bf16[32,128,2,128]{1,0,3,2:T(8,128)(2,1)S(1)} copy-done((bf16[32,128,2,128]{1,0,3,2:T(8,128)(2,1)S(1)}, bf16[32,128,2,128]{1,0,3,2:T(8,128)(2,1)}, u32[]{:S(2)}) %copy-start.2) | copy-done | bytes 2097176
  109.9 1.1 convolution_add_fusion
  111.2 2.6 %collective-permute-start.5 = (f32[128,4096]{1,0:T(8,128)S(1)}, f32[128,4096]{1,0:T(8,128)S(1)}, u32[]{:S(2)}, u32[]{:S(2)}) collective-permute-start(f32[128,4096]{1,0:T(8,128)S(1)} %split.25), channel_id=1, source_target_pairs={{0,1},{1,0},{2,3},{3,2},{4,5},{5,4},{6,7},{7,6},{8,9},{9,8},{10,11... | collective-permute-start | bytes 6291464 | tf_op jit(solution)/shard_map/ppermute | solution.py:18
  113.8 3.6 %collective-permute-done.5 = f32[128,4096]{1,0:T(8,128)S(1)} collective-permute-done((f32[128,4096]{1,0:T(8,128)S(1)}, f32[128,4096]{1,0:T(8,128)S(1)}, u32[]{:S(2)}, u32[]{:S(2)}) %collective-permute-start.5) | collective-permute-done | bytes 2097184 | tf_op jit(solution)/shard_map/ppermute | solution.py:18
  117.4 1.3 fusion.12
  118.7 2.4 %convolution_convert_fusion.2 = bf16[4096,256]{1,0:T(8,128)(2,1)S(1)} fusion(bf16[256,256]{1,0:T(8,128)(2,1)S(1)} %get-tuple-element.13, bf16[2,256,4096]{2,1,0:T(8,128)(2,1)} %copy-done.3), kind=kOutput, calls=%fused_computation.3 | convolution fusion | flops 537919488 | bytes 4325376 | tf_op jit(solution)/shard_map/dot_general | solution.py:108
  121.1 2.1 %reshape.78 = bf16[32,128,2,128]{3,2,1,0:T(2,128)(2,1)} reshape(bf16[4096,256]{1,0:T(8,128)(2,1)S(1)} %convolution_convert_fusion.2) | data formatting | bytes 4194304 | tf_op jit(solution)/shard_map/reshape | solution.py:75
  123.1 2.3 %convolution_convert_fusion.1 = bf16[4096,256]{1,0:T(8,128)(2,1)S(1)} fusion(bf16[256,256]{1,0:T(8,128)(2,1)S(1)} %get-tuple-element.12, bf16[2,256,4096]{2,1,0:T(8,128)(2,1)} %copy-done.3), kind=kOutput, calls=%fused_computation.2 | convolution fusion | flops 537919488 | bytes 4325376 | tf_op jit(solution)/shard_map/dot_general | solution.py:109
  125.5 2.1 %reshape.79 = bf16[32,128,2,128]{3,2,1,0:T(2,128)(2,1)} reshape(bf16[4096,256]{1,0:T(8,128)(2,1)S(1)} %convolution_convert_fusion.1) | data formatting | bytes 4194304 | tf_op jit(solution)/shard_map/reshape | solution.py:75
  127.6 2.4 %fusion.23 = bf16[32,8,32,128]{3,1,2,0:T(8,128)(2,1)S(1)} fusion(bf16[2,256,4096]{2,1,0:T(8,128)(2,1)} %copy-done.3, f32[256,256]{1,0:T(8,128)S(1)} %fusion.7, f32[256,256]{1,0:T(8,128)S(1)} %fusion.4), kind=kOutput, calls=%fused_computation.34 | convolution fusion | flops 538312704 | bytes 4718592 | tf_op jit(solution)/shard_map/dot_general | solution.py:110
  131.6 1.5 fusion.28
  133.2 2.5 %fusion.31 = bf16[1,26,128,128]{3,1,2,0:T(8,128)(2,1)} fusion(bf16[32,128,2,128]{3,2,1,0:T(2,128)(2,1)S(1)} %copy-done.1, f32[26,32]{1,0:T(8,128)S(1)} %fusion.62, f32[26,2]{0,1:T(2,128)S(1)} %compare_convert_fusion), kind=kOutput, calls=%fused_computation.36 | convolution fusion | flops 54953600 | bytes 2952656 | tf_op jit(solution)/shard_map/kr,kc,rbcn->kbn/dot_general | solution.py:76
  135.8 23.3 %reduce-scatter.2.cloned.1.call-done = bf16[16,4096]{1,0:T(8,128)(2,1)} async-done(((bf16[128,4096]{1,0:T(8,128)(2,1)}), bf16[16,4096]{1,0:T(8,128)(2,1)}) %reduce-scatter.2.cloned.1.call-update) | async-done | bytes 131088 | tf_op jit(solution)/shard_map/reduce_scatter | solution.py:32
  160.0 4.6 %collective-permute-start.8 = (bf16[4,4096]{1,0:T(4,128)(2,1)S(1)}, bf16[4,4096]{1,0:T(4,128)(2,1)S(1)}, u32[]{:S(2)}, u32[]{:S(2)}) collective-permute-start(bf16[4,4096]{1,0:T(4,128)(2,1)S(1)} %get-tuple-element.15), channel_id=1, source_target_pairs={{0,2},{2,4},{4,6},{6,0},{1,3},{3,5},{5,7},{7,1},{8,10},{10,12},{12... | collective-permute-start | bytes 98312 | tf_op jit(solution)/shard_map/ppermute | solution.py:18
  164.6 6.2 %collective-permute-start.7 = (bf16[4,4096]{1,0:T(4,128)(2,1)S(1)}, bf16[4,4096]{1,0:T(4,128)(2,1)S(1)}, u32[]{:S(2)}, u32[]{:S(2)}) collective-permute-start(bf16[4,4096]{1,0:T(4,128)(2,1)S(1)} %get-tuple-element.16), channel_id=1, source_target_pairs={{0,4},{2,6},{4,0},{6,2},{1,5},{3,7},{5,1},{7,3},{8,12},{10,14},{12... | collective-permute-start | bytes 98312 | tf_op jit(solution)/shard_map/ppermute | solution.py:18
  170.8 5.2 %collective-permute-start.6 = (bf16[4,4096]{1,0:T(4,128)(2,1)S(1)}, bf16[4,4096]{1,0:T(4,128)(2,1)S(1)}, u32[]{:S(2)}, u32[]{:S(2)}) collective-permute-start(bf16[4,4096]{1,0:T(4,128)(2,1)S(1)} %get-tuple-element.14), channel_id=1, source_target_pairs={{0,6},{2,0},{4,2},{6,4},{1,7},{3,1},{5,3},{7,5},{8,14},{10,8},{12,... | collective-permute-start | bytes 98312 | tf_op jit(solution)/shard_map/ppermute | solution.py:18
  176.6 1.2 copy.33
  177.9 1.2 copy.34
  179.1 1.2 copy.35
  180.4 1.5 fusion.45
  (42 shorter events, 12.8 us)
Async XLA Ops:
  7.2 75.2 %all-gather.2.cloned.1.call-start = ((), (), s32[]{:S(2)}) async-start(), calls=%async_computation.1 | async-start | bytes 2359296 | tf_op jit(solution)/shard_map/all_gather | solution.py:25
  7.2 6.4 %collective-permute-start = (bf16[1,4,4096]{2,1,0:T(4,128)(2,1)}, bf16[1,4,4096]{2,1,0:T(4,128)(2,1)S(1)}, u32[]{:S(2)}, u32[]{:S(2)}) collective-permute-start(bf16[1,4,4096]{2,1,0:T(4,128)(2,1)} %param.7), channel_id=1, source_target_pairs={{64,0},{128,64},{192,128},{256,192},{320,256},{384,320},{448,384},... | collective-permute-start | bytes 98312 | tf_op jit(solution)/shard_map/ppermute | solution.py:13
  13.7 17.3 %collective-permute-start.3 = (bf16[2,4,4096]{2,1,0:T(4,128)(2,1)S(1)}, bf16[2,4,4096]{2,1,0:T(4,128)(2,1)S(1)}, u32[]{:S(2)}, u32[]{:S(2)}) collective-permute-start(bf16[2,4,4096]{2,1,0:T(4,128)(2,1)S(1)} %constant_dynamic-update-slice_fusion), channel_id=1, source_target_pairs={{0,6},{2,0},{4,2},{6,4},{1,7},{3,1},{5,3},{7,5},{8,14},{10,8},{12,... | collective-permute-start | bytes 196616 | tf_op jit(solution)/shard_map/ppermute | solution.py:18
  24.2 10.9 %collective-permute-start.2 = (bf16[2,4,4096]{2,1,0:T(4,128)(2,1)S(1)}, bf16[2,4,4096]{2,1,0:T(4,128)(2,1)S(1)}, u32[]{:S(2)}, u32[]{:S(2)}) collective-permute-start(bf16[2,4,4096]{2,1,0:T(4,128)(2,1)S(1)} %constant_dynamic-update-slice_fusion), channel_id=1, source_target_pairs={{0,4},{2,6},{4,0},{6,2},{1,5},{3,7},{5,1},{7,3},{8,12},{10,14},{12... | collective-permute-start | bytes 196616 | tf_op jit(solution)/shard_map/ppermute | solution.py:18
  26.1 8.9 %collective-permute-start.1 = (bf16[2,4,4096]{2,1,0:T(4,128)(2,1)S(1)}, bf16[2,4,4096]{2,1,0:T(4,128)(2,1)S(1)}, u32[]{:S(2)}, u32[]{:S(2)}) collective-permute-start(bf16[2,4,4096]{2,1,0:T(4,128)(2,1)S(1)} %constant_dynamic-update-slice_fusion), channel_id=1, source_target_pairs={{0,2},{2,4},{4,6},{6,0},{1,3},{3,5},{5,7},{7,1},{8,10},{10,12},{12... | collective-permute-start | bytes 196616 | tf_op jit(solution)/shard_map/ppermute | solution.py:18
  36.0 123.1 %reduce-scatter.2.cloned.1.call-start = ((), (), s32[]{:S(2)}) async-start(), calls=%async_computation.2 | async-start | bytes 1179648 | tf_op jit(solution)/shard_map/reduce_scatter | solution.py:32
  82.3 19.7 %collective-permute-start.4 = (bf16[2,128,4096]{2,1,0:T(8,128)(2,1)}, bf16[2,128,4096]{2,1,0:T(8,128)(2,1)}, u32[]{:S(2)}, u32[]{:S(2)}) collective-permute-start(bf16[2,128,4096]{2,1,0:T(8,128)(2,1)} %all-gather.2.cloned.1.call-done), channel_id=1, source_target_pairs={{0,1},{1,0},{2,3},{3,2},{4,5},{5,4},{6,7},{7,6},{8,9},{9,8},{10,11... | collective-permute-start | bytes 6291464 | tf_op jit(solution)/shard_map/ppermute | solution.py:18
  88.4 4.3 %copy-start.6 = (bf16[1,26,128,128]{3,2,1,0:T(8,128)(2,1)S(1)}, bf16[1,26,128,128]{3,2,1,0:T(8,128)(2,1)}, u32[]{:S(2)}) copy-start(bf16[1,26,128,128]{3,2,1,0:T(8,128)(2,1)} %param.10) | copy-start | bytes 2555908
  95.1 5.2 %copy-start.7 = (bf16[1,26,128,128]{3,2,1,0:T(8,128)(2,1)S(1)}, bf16[1,26,128,128]{3,2,1,0:T(8,128)(2,1)}, u32[]{:S(2)}) copy-start(bf16[1,26,128,128]{3,2,1,0:T(8,128)(2,1)} %param.11) | copy-start | bytes 2555908
  100.3 1.6 copy-start.5
  103.8 4.1 %copy-start.3 = (bf16[2,256,4096]{2,1,0:T(8,128)(2,1)}, bf16[2,256,4096]{2,1,0:T(8,128)(2,1)S(1)}, u32[]{:S(2)}) copy-start(bf16[2,256,4096]{2,1,0:T(8,128)(2,1)S(1)} %constant_dynamic-update-slice_fusion.2) | copy-start | bytes 12582916
  103.8 3.1 %copy-start.2 = (bf16[32,128,2,128]{1,0,3,2:T(8,128)(2,1)S(1)}, bf16[32,128,2,128]{1,0,3,2:T(8,128)(2,1)}, u32[]{:S(2)}) copy-start(bf16[32,128,2,128]{1,0,3,2:T(8,128)(2,1)} %copy.26) | copy-start | bytes 6291460
  111.2 6.2 %collective-permute-start.5 = (f32[128,4096]{1,0:T(8,128)S(1)}, f32[128,4096]{1,0:T(8,128)S(1)}, u32[]{:S(2)}, u32[]{:S(2)}) collective-permute-start(f32[128,4096]{1,0:T(8,128)S(1)} %split.25), channel_id=1, source_target_pairs={{0,1},{1,0},{2,3},{3,2},{4,5},{5,4},{6,7},{7,6},{8,9},{9,8},{10,11... | collective-permute-start | bytes 6291464 | tf_op jit(solution)/shard_map/ppermute | solution.py:18
  130.0 1.6 copy-start
  131.6 1.6 copy-start.1
  160.0 20.3 %collective-permute-start.8 = (bf16[4,4096]{1,0:T(4,128)(2,1)S(1)}, bf16[4,4096]{1,0:T(4,128)(2,1)S(1)}, u32[]{:S(2)}, u32[]{:S(2)}) collective-permute-start(bf16[4,4096]{1,0:T(4,128)(2,1)S(1)} %get-tuple-element.15), channel_id=1, source_target_pairs={{0,2},{2,4},{4,6},{6,0},{1,3},{3,5},{5,7},{7,1},{8,10},{10,12},{12... | collective-permute-start | bytes 98312 | tf_op jit(solution)/shard_map/ppermute | solution.py:18
  164.6 15.7 %collective-permute-start.7 = (bf16[4,4096]{1,0:T(4,128)(2,1)S(1)}, bf16[4,4096]{1,0:T(4,128)(2,1)S(1)}, u32[]{:S(2)}, u32[]{:S(2)}) collective-permute-start(bf16[4,4096]{1,0:T(4,128)(2,1)S(1)} %get-tuple-element.16), channel_id=1, source_target_pairs={{0,4},{2,6},{4,0},{6,2},{1,5},{3,7},{5,1},{7,3},{8,12},{10,14},{12... | collective-permute-start | bytes 98312 | tf_op jit(solution)/shard_map/ppermute | solution.py:18
  170.8 9.5 %collective-permute-start.6 = (bf16[4,4096]{1,0:T(4,128)(2,1)S(1)}, bf16[4,4096]{1,0:T(4,128)(2,1)S(1)}, u32[]{:S(2)}, u32[]{:S(2)}) collective-permute-start(bf16[4,4096]{1,0:T(4,128)(2,1)S(1)} %get-tuple-element.14), channel_id=1, source_target_pairs={{0,6},{2,0},{4,2},{6,4},{1,7},{3,1},{5,3},{7,5},{8,14},{10,8},{12,... | collective-permute-start | bytes 98312 | tf_op jit(solution)/shard_map/ppermute | solution.py:18
  176.1 1.8 copy-start.4
Sparse Core Ops, SparseCore 0:
  36.1 46.2 all-gather.1
  118.8 40.1 reduce-scatter.1

commit v7 on v6

--- a/solution.py
+++ b/solution.py
@@ -18,12 +18,13 @@
     return lax.ppermute(block, axis, [(i, (i + shift) % n) for i in range(n)])
 
 
-def gather_rows(block):
+def gather_rows(block, weights):
     n = lax.axis_size("zh")
     pieces = [block] + [shifted(block, "zh", k) for k in range(1, n)]
     block = jnp.concatenate(pieces, axis=1)
+    block, weights = lax.optimization_barrier((block, weights))
     block = lax.all_gather(block, "y", axis=1, tiled=True)
-    return jnp.concatenate([block, shifted(block, "core", 1)], axis=1)
+    return jnp.concatenate([block, shifted(block, "core", 1)], axis=1), weights
 
 
 def scatter_rows(block):
@@ -58,41 +59,26 @@
     hidden_units = columns * block
 
     def dense_in(blocks):
-        placed = jnp.einsum(
-            "kr,kc,kbn->rbcn", band_onehot, col_onehot, blocks,
-            preferred_element_type=jnp.float32,
+        spread = blocks[:, :, None, :] * col_onehot[:, None, :, None]
+        placed = lax.dot_general(
+            band_onehot, spread, (((0,), (0,)), ((), ())), preferred_element_type=jnp.float32
         )
         return placed.astype(jnp.bfloat16).reshape(width, hidden_units)
 
-    def dense_down(blocks):
-        placed = jnp.einsum(
-            "kc,kr,knb->cnrb", col_onehot, band_onehot, blocks,
-            preferred_element_type=jnp.float32,
-        )
-        return placed.astype(jnp.bfloat16).reshape(hidden_units, width)
-
     def kept_in(dense):
-        tiles = dense.astype(jnp.bfloat16).reshape(bands, block, columns, block)
-        picked = jnp.einsum(
-            "kr,kc,rbcn->kbn", band_onehot, col_onehot, tiles,
-            preferred_element_type=jnp.float32,
-        )
-        return picked.astype(jnp.bfloat16)
-
-    def kept_down(dense):
-        tiles = dense.astype(jnp.bfloat16).reshape(columns, block, bands, block)
-        picked = jnp.einsum(
-            "kc,kr,cnrb->knb", col_onehot, band_onehot, tiles,
-            preferred_element_type=jnp.float32,
-        )
-        return picked.astype(jnp.bfloat16)
+        tiles = dense.astype(jnp.bfloat16).reshape(bands, block * columns * block)
+        picked = jnp.dot(band_onehot, tiles, preferred_element_type=jnp.float32)
+        picked = picked.reshape(-1, block, columns, block) * col_onehot[:, None, :, None]
+        return jnp.sum(picked, axis=2).astype(jnp.bfloat16)
 
     w_gate = dense_in(gate_blocks[0])
     w_up = dense_in(up_blocks[0])
-    w_down = dense_down(down_blocks[0])
+    w_down_t = dense_in(jnp.swapaxes(down_blocks[0], 1, 2))
 
     incoming = passed_along(grad_sent, "section", -1)
-    both = gather_rows(jnp.concatenate([saved_input, incoming], axis=0))
+    both, (w_gate, w_up, w_down_t) = gather_rows(
+        jnp.concatenate([saved_input, incoming], axis=0), (w_gate, w_up, w_down_t)
+    )
     inputs = both[0]
     upstream = both[1]
     f32 = jnp.float32
@@ -101,13 +87,15 @@
     sig = jax.nn.sigmoid(gate)
     act = gate * sig
     hidden = (act * up).astype(jnp.bfloat16)
-    dhid = lax.dot_general(upstream, w_down, (((1,), (1,)), ((), ())), preferred_element_type=f32)
+    dhid = jnp.dot(upstream, w_down_t, preferred_element_type=f32)
     grad_up_act = (dhid * act).astype(jnp.bfloat16)
     grad_gate_act = (dhid * up * sig * (1.0 + gate * (1.0 - sig))).astype(jnp.bfloat16)
     rows_t = (((0,), (0,)), ((), ()))
     tiles_gate = kept_in(lax.dot_general(inputs, grad_gate_act, rows_t, preferred_element_type=f32))
     tiles_up = kept_in(lax.dot_general(inputs, grad_up_act, rows_t, preferred_element_type=f32))
-    tiles_down = kept_down(lax.dot_general(hidden, upstream, rows_t, preferred_element_type=f32))
+    tiles_down = jnp.swapaxes(
+        kept_in(lax.dot_general(upstream, hidden, rows_t, preferred_element_type=f32)), 1, 2
+    )
     hid_t = (((1,), (1,)), ((), ()))
     whole_term = lax.dot_general(grad_gate_act, w_gate, hid_t, preferred_element_type=f32)
     whole_term = whole_term + lax.dot_general(

time: 190 us -> 196 us (1.032)
  local copies, waits for them, and re-layouts: 25.7 us -> 55.6 us
  waiting for transfers between devices: 78.5 us -> 55.5 us
    reduce_scatter x1, waiting for transfers between devices: 23.3 us -> 6.46 us  [scatter_rows(): block = lax.psum_scatter(block, 'y', scatter_dimension=0, tiled=True)]
    reshape x2 -> x4, local copies, waits for them, and re-layouts: 4.2 us -> 17 us  [the longest x3 8.63 us: kept_in(): tiles = dense.astype(jnp.bfloat16).reshape(bands, block * columns * block)]
    dot_general x0 -> x3, local copies, waits for them, and re-layouts: none -> 8.34 us  [kept_in(): picked = jnp.dot(band_onehot, tiles, preferred_element_type=jnp.float32)]
    all_gather x1, waiting for transfers between devices: 46.3 us -> 42.6 us  [gather_rows(): block = lax.all_gather(block, 'y', axis=1, tiled=True)]
    unnamed x22, local copies, waits for them, and re-layouts: 9.11 us -> 12.8 us
    mul x0 -> x2, local copies, waits for them, and re-layouts: none -> 2.3 us  [dense_in(): spread = blocks[:, :, None, :] * col_onehot[:, None, :, None]]
    convert_element_type x2 -> x3, local copies, waits for them, and re-layouts: 9.53 us -> 11.8 us  [dense_in(): return placed.astype(jnp.bfloat16).reshape(width, hidden_units)]
  transfers between devices with their start and end apart: 11 -> 11, of which waited for: 5 -> 4; matrix products, arithmetic and copies ran while one was open for 20% -> 37% of each run, Pallas kernels for 0% -> 0%
where the time goes in v7:
time: 196 us; the launch traced here: 195 us
  local copies, waits for them, and re-layouts  55.6 us (28%)
  waiting for transfers between devices  55.5 us (28%)
  starting transfers between devices  40.5 us (21%)
  matrix products  25.3 us (13%)
  between operations  14.4 us (7%)
  other arithmetic  4.22 us (2%)
    all_gather x1, waiting for transfers between devices, gather_rows(): block = lax.all_gather(block, 'y', axis=1, tiled=True)  42.6 us
    ppermute x8, starting transfers between devices, shifted(): return lax.ppermute(block, axis, [(i, (i + shift) % n) for i in range(n)])  35.9 us
    unnamed x22, local copies, waits for them, and re-layouts  12.8 us
    convert_element_type x3, local copies, waits for them, and re-layouts, dense_in(): return placed.astype(jnp.bfloat16).reshape(width, hidden_units)  11.8 us
    reshape x3, local copies, waits for them, and re-layouts, kept_in(): tiles = dense.astype(jnp.bfloat16).reshape(bands, block * columns * block)  8.63 us
    reshape x1, local copies, waits for them, and re-layouts, dense_in(): return placed.astype(jnp.bfloat16).reshape(width, hidden_units)  8.39 us
    dot_general x3, local copies, waits for them, and re-layouts, kept_in(): picked = jnp.dot(band_onehot, tiles, preferred_element_type=jnp.float32)  8.34 us
    dot_general x3, matrix products, kept_in(): picked = jnp.dot(band_onehot, tiles, preferred_element_type=jnp.float32)  7.94 us
  transfers between devices with their start and end apart: 11, of which 4 were waited for; matrix products, arithmetic and copies ran while one was open for 37% of the time, Pallas kernels for 0%

profile of v7, /device:TPU:6, one launch (start us, length us, event | category | flops | bytes accessed | tf_op | source)
XLA Modules:
  0.0 195.5 jit_solution(12868037251570259282)
XLA Ops:
  7.2 4.5 %collective-permute-start = (bf16[1,4,4096]{2,1,0:T(4,128)(2,1)}, bf16[1,4,4096]{2,1,0:T(4,128)(2,1)S(1)}, u32[]{:S(2)}, u32[]{:S(2)}) collective-permute-start(bf16[1,4,4096]{2,1,0:T(4,128)(2,1)} %param.7), channel_id=1, source_target_pairs={{64,0},{128,64},{192,128},{256,192},{320,256},{384,320},{448,384},... | collective-permute-start | bytes 98312 | tf_op jit(solution)/shard_map/ppermute | solution.py:13
  15.0 3.9 %copy.33 = bf16[32,128,2,128]{1,0,3,2:T(8,128)(2,1)} copy(bf16[32,128,2,128]{3,0,2,1:T(8,128)(2,1)S(1)} %fusion.13) | data formatting | bytes 4194304 | tf_op jit(solution)/shard_map/convert_element_type | solution.py:66
  18.9 1.9 copy.34
  21.7 3.9 %copy.36 = bf16[32,128,2,128]{1,0,3,2:T(8,128)(2,1)} copy(bf16[32,128,2,128]{3,0,2,1:T(8,128)(2,1)S(1)} %fusion.16) | data formatting | bytes 4194304 | tf_op jit(solution)/shard_map/convert_element_type | solution.py:66
  25.7 8.4 %copy_bitcast_fusion = (bf16[4096,256]{0,1:T(8,128)(2,1)}, bf16[4096,256]{0,1:T(8,128)(2,1)}) fusion(bf16[32,8,32,128]{3,2,1,0:T(8,128)(2,1)} %bitcast.102, bf16[32,8,32,128]{3,2,1,0:T(8,128)(2,1)} %bitcast.101), kind=kLoop, calls=%fused_computation.7 | loop fusion | bytes 8388608 | tf_op jit(solution)/shard_map/reshape | solution.py:66
  34.7 10.0 %collective-permute-start.3 = (bf16[2,4,4096]{2,1,0:T(4,128)(2,1)S(1)}, bf16[2,4,4096]{2,1,0:T(4,128)(2,1)S(1)}, u32[]{:S(2)}, u32[]{:S(2)}) collective-permute-start(bf16[2,4,4096]{2,1,0:T(4,128)(2,1)S(1)} %constant_dynamic-update-slice_fusion), channel_id=1, source_target_pairs={{0,6},{2,0},{4,2},{6,4},{1,7},{3,1},{5,3},{7,5},{8,14},{10,8},{12,... | collective-permute-start | bytes 196616 | tf_op jit(solution)/shard_map/ppermute | solution.py:18
  44.7 1.9 collective-permute-start.2
  46.7 5.0 %collective-permute-start.1 = (bf16[2,4,4096]{2,1,0:T(4,128)(2,1)S(1)}, bf16[2,4,4096]{2,1,0:T(4,128)(2,1)S(1)}, u32[]{:S(2)}, u32[]{:S(2)}) collective-permute-start(bf16[2,4,4096]{2,1,0:T(4,128)(2,1)S(1)} %constant_dynamic-update-slice_fusion), channel_id=1, source_target_pairs={{0,2},{2,4},{4,6},{6,0},{1,3},{3,5},{5,7},{7,1},{8,10},{10,12},{12... | collective-permute-start | bytes 196616 | tf_op jit(solution)/shard_map/ppermute | solution.py:18
  52.5 3.9 %copy.30 = bf16[32,128,2,128]{1,0,3,2:T(8,128)(2,1)} copy(bf16[32,128,2,128]{3,0,2,1:T(8,128)(2,1)S(1)} %fusion.10) | data formatting | bytes 4194304 | tf_op jit(solution)/shard_map/convert_element_type | solution.py:66
  56.4 2.6 %copy.62 = bf16[32,8,32,128]{3,1,2,0:T(8,128)(2,1)S(1)} copy(bf16[32,8,32,128]{3,2,1,0:T(8,128)(2,1)} %bitcast.97) | data formatting | bytes 4194304
  60.0 42.6 %all-gather.2.cloned.1.call-done = bf16[2,128,4096]{2,1,0:T(8,128)(2,1)} async-done(((bf16[2,16,4096]{2,1,0:T(8,128)(2,1)}), bf16[2,128,4096]{2,1,0:T(8,128)(2,1)}) %all-gather.2.cloned.1.call-update) | async-done | bytes 2097168 | tf_op jit(solution)/shard_map/all_gather | solution.py:26
  106.2 2.6 %collective-permute-done.4 = bf16[2,128,4096]{2,1,0:T(8,128)(2,1)S(1)} collective-permute-done((bf16[2,128,4096]{2,1,0:T(8,128)(2,1)}, bf16[2,128,4096]{2,1,0:T(8,128)(2,1)S(1)}, u32[]{:S(2)}, u32[]{:S(2)}) %collective-permute-start.4) | collective-permute-done | bytes 2097184 | tf_op jit(solution)/shard_map/ppermute | solution.py:18
  109.8 2.3 %copy-done = bf16[4096,256]{0,1:T(8,128)(2,1)S(1)} copy-done((bf16[4096,256]{0,1:T(8,128)(2,1)S(1)}, bf16[4096,256]{0,1:T(8,128)(2,1)}, u32[]{:S(2)}) %copy-start) | copy-done | bytes 2097176
  116.2 2.3 %collective-permute-start.5 = (f32[128,4096]{1,0:T(8,128)S(1)}, f32[128,4096]{1,0:T(8,128)S(1)}, u32[]{:S(2)}, u32[]{:S(2)}) collective-permute-start(f32[128,4096]{1,0:T(8,128)S(1)} %split.25), channel_id=1, source_target_pairs={{0,1},{1,0},{2,3},{3,2},{4,5},{5,4},{6,7},{7,6},{8,9},{9,8},{10,11... | collective-permute-start | bytes 6291464 | tf_op jit(solution)/shard_map/ppermute | solution.py:18
  118.4 3.8 %collective-permute-done.5 = f32[128,4096]{1,0:T(8,128)S(1)} collective-permute-done((f32[128,4096]{1,0:T(8,128)S(1)}, f32[128,4096]{1,0:T(8,128)S(1)}, u32[]{:S(2)}, u32[]{:S(2)}) %collective-permute-start.5) | collective-permute-done | bytes 2097184 | tf_op jit(solution)/shard_map/ppermute | solution.py:18
  123.4 3.7 %convolution_convert_fusion = bf16[4096,256]{1,0:T(8,128)(2,1)} fusion(bf16[2,256,4096]{2,1,0:T(8,128)(2,1)} %copy-done.4, f32[256,256]{1,0:T(8,128)S(1)} %fusion.21, f32[256,256]{1,0:T(8,128)S(1)} %fusion.20), kind=kOutput, calls=%fused_computation.1 | convolution fusion | flops 538312704 | bytes 4718592 | tf_op jit(solution)/shard_map/dot_general | solution.py:97
  127.2 2.9 %reshape.146 = bf16[32,32768]{1,0:T(8,128)(2,1)S(1)} reshape(bf16[4096,256]{1,0:T(8,128)(2,1)} %convolution_convert_fusion) | data formatting | bytes 4194304 | tf_op jit(solution)/shard_map/reshape | solution.py:69
  130.1 2.8 %dot_general.72 = bf16[128,2,128,32]{2,1,0,3:T(2,128)(2,1)} reshape(bf16[32768,32]{0,1:T(8,128)(2,1)S(1)} %bitcast.98) | data formatting | bytes 4194304 | tf_op jit(solution)/shard_map/dot_general | solution.py:70
  132.8 3.7 %convolution_convert_fusion.2 = bf16[4096,256]{1,0:T(8,128)(2,1)} fusion(bf16[256,256]{1,0:T(8,128)(2,1)S(1)} %get-tuple-element.17, bf16[2,256,4096]{2,1,0:T(8,128)(2,1)} %copy-done.4), kind=kOutput, calls=%fused_computation.3 | convolution fusion | flops 537919488 | bytes 4325376 | tf_op jit(solution)/shard_map/dot_general | solution.py:94
  136.5 2.9 %reshape.144 = bf16[32,32768]{1,0:T(8,128)(2,1)S(1)} reshape(bf16[4096,256]{1,0:T(8,128)(2,1)} %convolution_convert_fusion.2) | data formatting | bytes 4194304 | tf_op jit(solution)/shard_map/reshape | solution.py:69
  139.4 2.8 %dot_general.64 = bf16[128,2,128,32]{2,1,0,3:T(2,128)(2,1)} reshape(bf16[32768,32]{0,1:T(8,128)(2,1)S(1)} %bitcast.99) | data formatting | bytes 4194304 | tf_op jit(solution)/shard_map/dot_general | solution.py:70
  142.2 3.7 %convolution_convert_fusion.1 = bf16[4096,256]{1,0:T(8,128)(2,1)} fusion(bf16[256,256]{1,0:T(8,128)(2,1)S(1)} %get-tuple-element.16, bf16[2,256,4096]{2,1,0:T(8,128)(2,1)} %copy-done.4), kind=kOutput, calls=%fused_computation.2 | convolution fusion | flops 537919488 | bytes 4325376 | tf_op jit(solution)/shard_map/dot_general | solution.py:95
  146.0 2.9 %reshape.145 = bf16[32,32768]{1,0:T(8,128)(2,1)S(1)} reshape(bf16[4096,256]{1,0:T(8,128)(2,1)} %convolution_convert_fusion.1) | data formatting | bytes 4194304 | tf_op jit(solution)/shard_map/reshape | solution.py:69
  148.8 2.8 %dot_general.68 = bf16[128,2,128,32]{2,1,0,3:T(2,128)(2,1)} reshape(bf16[32768,32]{0,1:T(8,128)(2,1)S(1)} %bitcast.100) | data formatting | bytes 4194304 | tf_op jit(solution)/shard_map/dot_general | solution.py:70
  151.6 3.3 %multiply_reduce_fusion = bf16[26,128,128]{2,0,1:T(8,128)(2,1)S(1)} fusion(bf16[128,2,128,32]{2,1,0,3:T(2,128)(2,1)} %dot_general.72, f32[26,2]{0,1:T(2,128)S(1)} %get-tuple-element.21, s32[26]{0:T(128)S(1)} %get-tuple-element.23), kind=kOutput, calls=%fused_computation.4 | convolution fusion | flops 55804736 | bytes 2949432 | tf_op jit(solution)/shard_map/dot_general | solution.py:70
  154.9 2.3 %multiply_reduce_fusion.2 = bf16[26,128,128]{2,0,1:T(8,128)(2,1)} fusion(bf16[128,2,128,32]{2,1,0,3:T(2,128)(2,1)S(1)} %copy-done.2, f32[26,2]{0,1:T(2,128)S(1)} %get-tuple-element.21, s32[26]{0:T(128)S(1)} %get-tuple-element.23), kind=kOutput, calls=%fused_computation.6 | convolution fusion | flops 55804736 | bytes 2949432 | tf_op jit(solution)/shard_map/dot_general | solution.py:70
  157.2 6.5 %reduce-scatter.2.cloned.1.call-done = bf16[16,4096]{1,0:T(8,128)(2,1)} async-done(((bf16[128,4096]{1,0:T(8,128)(2,1)}), bf16[16,4096]{1,0:T(8,128)(2,1)}) %reduce-scatter.2.cloned.1.call-update) | async-done | bytes 131088 | tf_op jit(solution)/shard_map/reduce_scatter | solution.py:33
  164.7 6.6 %collective-permute-start.6 = (bf16[4,4096]{1,0:T(4,128)(2,1)S(1)}, bf16[4,4096]{1,0:T(4,128)(2,1)S(1)}, u32[]{:S(2)}, u32[]{:S(2)}) collective-permute-start(bf16[4,4096]{1,0:T(4,128)(2,1)S(1)} %get-tuple-element.18), channel_id=1, source_target_pairs={{0,6},{2,0},{4,2},{6,4},{1,7},{3,1},{5,3},{7,5},{8,14},{10,8},{12,... | collective-permute-start | bytes 98312 | tf_op jit(solution)/shard_map/ppermute | solution.py:18
  171.3 1.9 collective-permute-start.8
  173.2 6.3 %collective-permute-start.7 = (bf16[4,4096]{1,0:T(4,128)(2,1)S(1)}, bf16[4,4096]{1,0:T(4,128)(2,1)S(1)}, u32[]{:S(2)}, u32[]{:S(2)}) collective-permute-start(bf16[4,4096]{1,0:T(4,128)(2,1)S(1)} %get-tuple-element.20), channel_id=1, source_target_pairs={{0,4},{2,6},{4,0},{6,2},{1,5},{3,7},{5,1},{7,3},{8,12},{10,14},{12... | collective-permute-start | bytes 98312 | tf_op jit(solution)/shard_map/ppermute | solution.py:18
  179.5 2.3 %multiply_reduce_fusion.1 = bf16[26,128,128]{2,0,1:T(8,128)(2,1)} fusion(bf16[128,2,128,32]{2,1,0,3:T(2,128)(2,1)S(1)} %copy-done.1, f32[26,2]{0,1:T(2,128)S(1)} %get-tuple-element.21, s32[26]{0:T(128)S(1)} %get-tuple-element.23), kind=kOutput, calls=%fused_computation.5 | convolution fusion | flops 55804736 | bytes 2949432 | tf_op jit(solution)/shard_map/dot_general | solution.py:70
  183.4 2.5 %copy.40 = bf16[1,26,128,128]{3,2,1,0:T(8,128)(2,1)} copy(bf16[1,26,128,128]{3,1,2,0:T(8,128)(2,1)} %bitcast.104) | data formatting | bytes 1703936
  (50 shorter events, 21.6 us)
Async XLA Ops:
  7.2 95.4 %all-gather.2.cloned.1.call-start = ((), (), s32[]{:S(2)}) async-start(), calls=%async_computation.1 | async-start | bytes 2359296 | tf_op jit(solution)/shard_map/all_gather | solution.py:26
  7.2 27.4 %collective-permute-start = (bf16[1,4,4096]{2,1,0:T(4,128)(2,1)}, bf16[1,4,4096]{2,1,0:T(4,128)(2,1)S(1)}, u32[]{:S(2)}, u32[]{:S(2)}) collective-permute-start(bf16[1,4,4096]{2,1,0:T(4,128)(2,1)} %param.7), channel_id=1, source_target_pairs={{64,0},{128,64},{192,128},{256,192},{320,256},{384,320},{448,384},... | collective-permute-start | bytes 98312 | tf_op jit(solution)/shard_map/ppermute | solution.py:13
  25.7 8.4 %copy-start.7 = (bf16[1,4,4096]{2,1,0:T(4,128)(2,1)S(1)}, bf16[1,4,4096]{2,1,0:T(4,128)(2,1)}, u32[]{:S(2)}) copy-start(bf16[1,4,4096]{2,1,0:T(4,128)(2,1)} %param.6) | copy-start | bytes 98308
  25.7 8.4 %copy-start.6 = (bf16[1,26,128,128]{3,2,1,0:T(8,128)(2,1)S(1)}, bf16[1,26,128,128]{3,2,1,0:T(8,128)(2,1)}, u32[]{:S(2)}) copy-start(bf16[1,26,128,128]{3,2,1,0:T(8,128)(2,1)} %param.9) | copy-start | bytes 2555908
  34.7 24.3 %collective-permute-start.3 = (bf16[2,4,4096]{2,1,0:T(4,128)(2,1)S(1)}, bf16[2,4,4096]{2,1,0:T(4,128)(2,1)S(1)}, u32[]{:S(2)}, u32[]{:S(2)}) collective-permute-start(bf16[2,4,4096]{2,1,0:T(4,128)(2,1)S(1)} %constant_dynamic-update-slice_fusion), channel_id=1, source_target_pairs={{0,6},{2,0},{4,2},{6,4},{1,7},{3,1},{5,3},{7,5},{8,14},{10,8},{12,... | collective-permute-start | bytes 196616 | tf_op jit(solution)/shard_map/ppermute | solution.py:18
  44.7 14.3 %collective-permute-start.2 = (bf16[2,4,4096]{2,1,0:T(4,128)(2,1)S(1)}, bf16[2,4,4096]{2,1,0:T(4,128)(2,1)S(1)}, u32[]{:S(2)}, u32[]{:S(2)}) collective-permute-start(bf16[2,4,4096]{2,1,0:T(4,128)(2,1)S(1)} %constant_dynamic-update-slice_fusion), channel_id=1, source_target_pairs={{0,4},{2,6},{4,0},{6,2},{1,5},{3,7},{5,1},{7,3},{8,12},{10,14},{12... | collective-permute-start | bytes 196616 | tf_op jit(solution)/shard_map/ppermute | solution.py:18
  46.7 12.3 %collective-permute-start.1 = (bf16[2,4,4096]{2,1,0:T(4,128)(2,1)S(1)}, bf16[2,4,4096]{2,1,0:T(4,128)(2,1)S(1)}, u32[]{:S(2)}, u32[]{:S(2)}) collective-permute-start(bf16[2,4,4096]{2,1,0:T(4,128)(2,1)S(1)} %constant_dynamic-update-slice_fusion), channel_id=1, source_target_pairs={{0,2},{2,4},{4,6},{6,0},{1,3},{3,5},{5,7},{7,1},{8,10},{10,12},{12... | collective-permute-start | bytes 196616 | tf_op jit(solution)/shard_map/ppermute | solution.py:18
  59.9 103.8 %reduce-scatter.2.cloned.1.call-start = ((), (), s32[]{:S(2)}) async-start(), calls=%async_computation.2 | async-start | bytes 1179648 | tf_op jit(solution)/shard_map/reduce_scatter | solution.py:33
  102.5 6.3 %collective-permute-start.4 = (bf16[2,128,4096]{2,1,0:T(8,128)(2,1)}, bf16[2,128,4096]{2,1,0:T(8,128)(2,1)S(1)}, u32[]{:S(2)}, u32[]{:S(2)}) collective-permute-start(bf16[2,128,4096]{2,1,0:T(8,128)(2,1)} %all-gather.2.cloned.1.call-done), channel_id=1, source_target_pairs={{0,1},{1,0},{2,3},{3,2},{4,5},{5,4},{6,7},{7,6},{8,9},{9,8},{10,11... | collective-permute-start | bytes 6291464 | tf_op jit(solution)/shard_map/ppermute | solution.py:18
  109.0 3.9 %copy-start.4 = (bf16[2,256,4096]{2,1,0:T(8,128)(2,1)}, bf16[2,256,4096]{2,1,0:T(8,128)(2,1)S(1)}, u32[]{:S(2)}) copy-start(bf16[2,256,4096]{2,1,0:T(8,128)(2,1)S(1)} %constant_dynamic-update-slice_fusion.2) | copy-start | bytes 12582916
  109.0 3.1 %copy-start = (bf16[4096,256]{0,1:T(8,128)(2,1)S(1)}, bf16[4096,256]{0,1:T(8,128)(2,1)}, u32[]{:S(2)}) copy-start(bf16[4096,256]{0,1:T(8,128)(2,1)} %get-tuple-element.10) | copy-start | bytes 6291460
  112.1 1.6 copy-start.3
  116.2 6.1 %collective-permute-start.5 = (f32[128,4096]{1,0:T(8,128)S(1)}, f32[128,4096]{1,0:T(8,128)S(1)}, u32[]{:S(2)}, u32[]{:S(2)}) collective-permute-start(f32[128,4096]{1,0:T(8,128)S(1)} %split.25), channel_id=1, source_target_pairs={{0,1},{1,0},{2,3},{3,2},{4,5},{5,4},{6,7},{7,6},{8,9},{9,8},{10,11... | collective-permute-start | bytes 6291464 | tf_op jit(solution)/shard_map/ppermute | solution.py:18
  151.6 3.3 %copy-start.2 = (bf16[128,2,128,32]{2,1,0,3:T(2,128)(2,1)S(1)}, bf16[128,2,128,32]{2,1,0,3:T(2,128)(2,1)}, u32[]{:S(2)}) copy-start(bf16[128,2,128,32]{2,1,0,3:T(2,128)(2,1)} %dot_general.64) | copy-start | bytes 6291460
  154.9 24.6 %copy-start.1 = (bf16[128,2,128,32]{2,1,0,3:T(2,128)(2,1)S(1)}, bf16[128,2,128,32]{2,1,0,3:T(2,128)(2,1)}, u32[]{:S(2)}) copy-start(bf16[128,2,128,32]{2,1,0,3:T(2,128)(2,1)} %dot_general.68) | copy-start | bytes 6291460
  164.7 22.5 %collective-permute-start.6 = (bf16[4,4096]{1,0:T(4,128)(2,1)S(1)}, bf16[4,4096]{1,0:T(4,128)(2,1)S(1)}, u32[]{:S(2)}, u32[]{:S(2)}) collective-permute-start(bf16[4,4096]{1,0:T(4,128)(2,1)S(1)} %get-tuple-element.18), channel_id=1, source_target_pairs={{0,6},{2,0},{4,2},{6,4},{1,7},{3,1},{5,3},{7,5},{8,14},{10,8},{12,... | collective-permute-start | bytes 98312 | tf_op jit(solution)/shard_map/ppermute | solution.py:18
  171.3 15.9 %collective-permute-start.8 = (bf16[4,4096]{1,0:T(4,128)(2,1)S(1)}, bf16[4,4096]{1,0:T(4,128)(2,1)S(1)}, u32[]{:S(2)}, u32[]{:S(2)}) collective-permute-start(bf16[4,4096]{1,0:T(4,128)(2,1)S(1)} %get-tuple-element.19), channel_id=1, source_target_pairs={{0,2},{2,4},{4,6},{6,0},{1,3},{3,5},{5,7},{7,1},{8,10},{10,12},{12... | collective-permute-start | bytes 98312 | tf_op jit(solution)/shard_map/ppermute | solution.py:18
  173.2 13.9 %collective-permute-start.7 = (bf16[4,4096]{1,0:T(4,128)(2,1)S(1)}, bf16[4,4096]{1,0:T(4,128)(2,1)S(1)}, u32[]{:S(2)}, u32[]{:S(2)}) collective-permute-start(bf16[4,4096]{1,0:T(4,128)(2,1)S(1)} %get-tuple-element.20), channel_id=1, source_target_pairs={{0,4},{2,6},{4,0},{6,2},{1,5},{3,7},{5,1},{7,3},{8,12},{10,14},{12... | collective-permute-start | bytes 98312 | tf_op jit(solution)/shard_map/ppermute | solution.py:18
  181.8 4.1 %copy-start.5 = (bf16[26,128,128]{2,0,1:T(8,128)(2,1)S(1)}, bf16[26,128,128]{2,0,1:T(8,128)(2,1)}, u32[]{:S(2)}) copy-start(bf16[26,128,128]{2,0,1:T(8,128)(2,1)} %multiply_reduce_fusion.1) | copy-start | bytes 2555908
Sparse Core Ops, SparseCore 0:
  60.0 42.4 all-gather.1
  123.5 40.1 reduce-scatter.1

commit v8 on v6

--- a/solution.py
+++ b/solution.py
@@ -18,12 +18,13 @@
     return lax.ppermute(block, axis, [(i, (i + shift) % n) for i in range(n)])
 
 
-def gather_rows(block):
+def gather_rows(block, weights):
     n = lax.axis_size("zh")
     pieces = [block] + [shifted(block, "zh", k) for k in range(1, n)]
     block = jnp.concatenate(pieces, axis=1)
     block = lax.all_gather(block, "y", axis=1, tiled=True)
-    return jnp.concatenate([block, shifted(block, "core", 1)], axis=1)
+    block, weights = lax.optimization_barrier((block, weights))
+    return jnp.concatenate([block, shifted(block, "core", 1)], axis=1), weights
 
 
 def scatter_rows(block):
@@ -92,7 +93,9 @@
     w_down = dense_down(down_blocks[0])
 
     incoming = passed_along(grad_sent, "section", -1)
-    both = gather_rows(jnp.concatenate([saved_input, incoming], axis=0))
+    both, (w_gate, w_up, w_down) = gather_rows(
+        jnp.concatenate([saved_input, incoming], axis=0), (w_gate, w_up, w_down)
+    )
     inputs = both[0]
     upstream = both[1]
     f32 = jnp.float32

time: 190 us -> 173 us (0.911)
  waiting for transfers between devices: 78.5 us -> 49.6 us
  local copies, waits for them, and re-layouts: 25.7 us -> 39.4 us
    all_gather x1, waiting for transfers between devices: 46.3 us -> 21.9 us  [gather_rows(): block = lax.all_gather(block, 'y', axis=1, tiled=True)]
    reduce_scatter x1, waiting for transfers between devices: 23.3 us -> 16.1 us  [scatter_rows(): block = lax.psum_scatter(block, 'y', scatter_dimension=0, tiled=True)]
    reshape x0 -> x1, local copies, waits for them, and re-layouts: none -> 6.15 us  [dense_down(): return placed.astype(jnp.bfloat16).reshape(hidden_units, width)]
    unnamed x22 -> x25, local copies, waits for them, and re-layouts: 9.11 us -> 14.9 us
    reshape x2, local copies, waits for them, and re-layouts: 4.2 us -> 7.95 us  [kept_in(): tiles = dense.astype(jnp.bfloat16).reshape(bands, block, columns, block)]
    ppermute x8, waiting for transfers between devices: 7.72 us -> 10.6 us  [shifted(): return lax.ppermute(block, axis, [(i, (i + shift) % n) for i in range(n)])]
  transfers between devices with their start and end apart: 11 -> 11, of which waited for: 5 -> 6; matrix products, arithmetic and copies ran while one was open for 20% -> 31% of each run, Pallas kernels for 0% -> 0%
where the time goes in v8:
time: 173 us; the launch traced here: 172 us
  waiting for transfers between devices  49.6 us (29%)
  starting transfers between devices  40.7 us (24%)
  local copies, waits for them, and re-layouts  39.4 us (23%)
  matrix products  23.5 us (14%)
  between operations  14.3 us (8%)
  other arithmetic  4.4 us (3%)
    ppermute x8, starting transfers between devices, shifted(): return lax.ppermute(block, axis, [(i, (i + shift) % n) for i in range(n)])  36.1 us
    all_gather x1, waiting for transfers between devices, gather_rows(): block = lax.all_gather(block, 'y', axis=1, tiled=True)  21.9 us
    reduce_scatter x1, waiting for transfers between devices, scatter_rows(): block = lax.psum_scatter(block, 'y', scatter_dimension=0, tiled=True)  16.1 us
    unnamed x25, local copies, waits for them, and re-layouts  14.9 us
    ppermute x8, waiting for transfers between devices, shifted(): return lax.ppermute(block, axis, [(i, (i + shift) % n) for i in range(n)])  10.6 us
    convert_element_type x2, local copies, waits for them, and re-layouts, dense_in(): return placed.astype(jnp.bfloat16).reshape(width, hidden_units)  9.03 us
    reshape x2, local copies, waits for them, and re-layouts, kept_in(): tiles = dense.astype(jnp.bfloat16).reshape(bands, block, columns, block)  7.95 us
    reshape x1, local copies, waits for them, and re-layouts, dense_down(): return placed.astype(jnp.bfloat16).reshape(hidden_units, width)  6.15 us
  transfers between devices with their start and end apart: 11, of which 6 were waited for; matrix products, arithmetic and copies ran while one was open for 31% of the time, Pallas kernels for 0%

profile of v8, /device:TPU:6, one launch (start us, length us, event | category | flops | bytes accessed | tf_op | source)
XLA Modules:
  0.0 172.0 jit_solution(1164565796400092476)
XLA Ops:
  7.2 4.5 %collective-permute-start = (bf16[1,4,4096]{2,1,0:T(4,128)(2,1)}, bf16[1,4,4096]{2,1,0:T(4,128)(2,1)S(1)}, u32[]{:S(2)}, u32[]{:S(2)}) collective-permute-start(bf16[1,4,4096]{2,1,0:T(4,128)(2,1)} %param.7), channel_id=1, source_target_pairs={{64,0},{128,64},{192,128},{256,192},{320,256},{384,320},{448,384},... | collective-permute-start | bytes 98312 | tf_op jit(solution)/shard_map/ppermute | solution.py:13
  13.7 10.5 %collective-permute-start.3 = (bf16[2,4,4096]{2,1,0:T(4,128)(2,1)S(1)}, bf16[2,4,4096]{2,1,0:T(4,128)(2,1)S(1)}, u32[]{:S(2)}, u32[]{:S(2)}) collective-permute-start(bf16[2,4,4096]{2,1,0:T(4,128)(2,1)S(1)} %constant_dynamic-update-slice_fusion), channel_id=1, source_target_pairs={{0,6},{2,0},{4,2},{6,4},{1,7},{3,1},{5,3},{7,5},{8,14},{10,8},{12,... | collective-permute-start | bytes 196616 | tf_op jit(solution)/shard_map/ppermute | solution.py:18
  24.2 1.9 %collective-permute-start.2 = (bf16[2,4,4096]{2,1,0:T(4,128)(2,1)S(1)}, bf16[2,4,4096]{2,1,0:T(4,128)(2,1)S(1)}, u32[]{:S(2)}, u32[]{:S(2)}) collective-permute-start(bf16[2,4,4096]{2,1,0:T(4,128)(2,1)S(1)} %constant_dynamic-update-slice_fusion), channel_id=1, source_target_pairs={{0,4},{2,6},{4,0},{6,2},{1,5},{3,7},{5,1},{7,3},{8,12},{10,14},{12... | collective-permute-start | bytes 196616 | tf_op jit(solution)/shard_map/ppermute | solution.py:18
  26.1 4.8 %collective-permute-start.1 = (bf16[2,4,4096]{2,1,0:T(4,128)(2,1)S(1)}, bf16[2,4,4096]{2,1,0:T(4,128)(2,1)S(1)}, u32[]{:S(2)}, u32[]{:S(2)}) collective-permute-start(bf16[2,4,4096]{2,1,0:T(4,128)(2,1)S(1)} %constant_dynamic-update-slice_fusion), channel_id=1, source_target_pairs={{0,2},{2,4},{4,6},{6,0},{1,3},{3,5},{5,7},{7,1},{8,10},{10,12},{12... | collective-permute-start | bytes 196616 | tf_op jit(solution)/shard_map/ppermute | solution.py:18
  30.9 4.1 %collective-permute-done.2 = bf16[2,4,4096]{2,1,0:T(4,128)(2,1)S(1)} collective-permute-done((bf16[2,4,4096]{2,1,0:T(4,128)(2,1)S(1)}, bf16[2,4,4096]{2,1,0:T(4,128)(2,1)S(1)}, u32[]{:S(2)}, u32[]{:S(2)}) %collective-permute-start.2) | collective-permute-done | bytes 65568 | tf_op jit(solution)/shard_map/ppermute | solution.py:18
  36.8 2.1 %convert_bitcast_fusion.1 = bf16[32,128,2,128]{3,0,1,2:T(8,128)(2,1)S(1)} fusion(bf16[26,128,128]{2,1,0:T(8,128)(2,1)} %bitcast.136, f32[26,32]{1,0:T(8,128)S(1)} %fusion.51, f32[26,2]{0,1:T(2,128)S(1)} %compare_convert_fusion), kind=kOutput, calls=%fused_computation.21 | convolution fusion | flops 55576192 | bytes 2952656 | tf_op jit(solution)/shard_map/kr,kc,kbn->rbcn/dot_general | solution.py:62
  38.8 3.8 %copy.24 = bf16[32,128,2,128]{1,0,3,2:T(8,128)(2,1)} copy(bf16[32,128,2,128]{3,0,1,2:T(8,128)(2,1)S(1)} %convert_bitcast_fusion.1) | data formatting | bytes 4194304 | tf_op jit(solution)/shard_map/convert_element_type | solution.py:66
  42.6 2.7 %copy.79 = bf16[32,8,32,128]{3,1,2,0:T(8,128)(2,1)S(1)} copy(bf16[32,8,32,128]{3,2,1,0:T(8,128)(2,1)} %bitcast.133) | data formatting | bytes 4194304
  45.3 2.2 %convert_bitcast_fusion = bf16[32,128,2,128]{3,0,1,2:T(8,128)(2,1)} fusion(bf16[26,128,128]{2,1,0:T(8,128)(2,1)S(1)} %bitcast.137, f32[26,32]{1,0:T(8,128)S(1)} %fusion.51, f32[26,2]{0,1:T(2,128)S(1)} %compare_convert_fusion), kind=kOutput, calls=%fused_computation.20 | convolution fusion | flops 55576192 | bytes 2952656 | tf_op jit(solution)/shard_map/kr,kc,kbn->rbcn/dot_general | solution.py:62
  47.5 5.2 %copy.27 = bf16[32,128,2,128]{1,0,3,2:T(8,128)(2,1)} copy(bf16[32,128,2,128]{3,0,1,2:T(8,128)(2,1)} %convert_bitcast_fusion) | data formatting | bytes 4194304 | tf_op jit(solution)/shard_map/convert_element_type | solution.py:66
  54.3 6.2 %copy_bitcast_fusion = (bf16[256,4096]{1,0:T(8,128)(2,1)}, bf16[4096,256]{0,1:T(8,128)(2,1)}) fusion(bf16[32,8,32,128]{3,2,1,0:T(8,128)(2,1)S(1)} %bitcast.135, bf16[32,8,32,128]{3,2,1,0:T(8,128)(2,1)S(1)} %bitcast.134), kind=kLoop, calls=%fused_computation.6 | loop fusion | bytes 8388608 | tf_op jit(solution)/shard_map/reshape | solution.py:73
  60.5 21.9 %all-gather.2.cloned.1.call-done = bf16[2,128,4096]{2,1,0:T(8,128)(2,1)} async-done(((bf16[2,16,4096]{2,1,0:T(8,128)(2,1)}), bf16[2,128,4096]{2,1,0:T(8,128)(2,1)}) %all-gather.2.cloned.1.call-update) | async-done | bytes 2097168 | tf_op jit(solution)/shard_map/all_gather | solution.py:25
  82.3 2.1 %collective-permute-start.4 = (bf16[2,128,4096]{2,1,0:T(8,128)(2,1)}, bf16[2,128,4096]{2,1,0:T(8,128)(2,1)S(1)}, u32[]{:S(2)}, u32[]{:S(2)}) collective-permute-start(bf16[2,128,4096]{2,1,0:T(8,128)(2,1)} %all-gather.2.cloned.1.call-done), channel_id=1, source_target_pairs={{0,1},{1,0},{2,3},{3,2},{4,5},{5,4},{6,7},{7,6},{8,9},{9,8},{10,11... | collective-permute-start | bytes 6291464 | tf_op jit(solution)/shard_map/ppermute | solution.py:18
  84.4 1.7 %constant_dynamic-update-slice_fusion.3 = bf16[2,256,4096]{2,1,0:T(8,128)(2,1)S(1)} fusion(bf16[2,128,4096]{2,1,0:T(8,128)(2,1)} %all-gather.2.cloned.1.call-done), kind=kLoop, calls=%fused_computation.67 | loop fusion | bytes 4194304
  86.2 2.4 %collective-permute-done.4 = bf16[2,128,4096]{2,1,0:T(8,128)(2,1)S(1)} collective-permute-done((bf16[2,128,4096]{2,1,0:T(8,128)(2,1)}, bf16[2,128,4096]{2,1,0:T(8,128)(2,1)S(1)}, u32[]{:S(2)}, u32[]{:S(2)}) %collective-permute-start.4) | collective-permute-done | bytes 2097184 | tf_op jit(solution)/shard_map/ppermute | solution.py:18
  89.6 2.3 %copy-done.2 = bf16[4096,256]{0,1:T(8,128)(2,1)S(1)} copy-done((bf16[4096,256]{0,1:T(8,128)(2,1)S(1)}, bf16[4096,256]{0,1:T(8,128)(2,1)}, u32[]{:S(2)}) %copy-start.2) | copy-done | bytes 2097176
  96.0 2.0 %collective-permute-start.5 = (f32[128,4096]{1,0:T(8,128)S(1)}, f32[128,4096]{1,0:T(8,128)S(1)}, u32[]{:S(2)}, u32[]{:S(2)}) collective-permute-start(f32[128,4096]{1,0:T(8,128)S(1)} %split.25), channel_id=1, source_target_pairs={{0,1},{1,0},{2,3},{3,2},{4,5},{5,4},{6,7},{7,6},{8,9},{9,8},{10,11... | collective-permute-start | bytes 6291464 | tf_op jit(solution)/shard_map/ppermute | solution.py:18
  98.0 4.0 %collective-permute-done.5 = f32[128,4096]{1,0:T(8,128)S(1)} collective-permute-done((f32[128,4096]{1,0:T(8,128)S(1)}, f32[128,4096]{1,0:T(8,128)S(1)}, u32[]{:S(2)}, u32[]{:S(2)}) %collective-permute-start.5) | collective-permute-done | bytes 2097184 | tf_op jit(solution)/shard_map/ppermute | solution.py:18
  102.0 1.3 fusion.2
  103.3 2.4 %fusion.10 = bf16[32,8,32,128]{3,1,2,0:T(8,128)(2,1)S(1)} fusion(bf16[2,256,4096]{2,1,0:T(8,128)(2,1)} %copy-done.3, f32[256,256]{1,0:T(8,128)S(1)} %fusion.25, f32[256,256]{1,0:T(8,128)S(1)} %fusion.24), kind=kOutput, calls=%fused_computation.24 | convolution fusion | flops 538312704 | bytes 4718592 | tf_op jit(solution)/shard_map/dot_general | solution.py:113
  106.2 1.7 copy-done.4
  107.9 2.2 %convolution_convert_fusion.2 = bf16[4096,256]{1,0:T(8,128)(2,1)} fusion(bf16[256,256]{1,0:T(8,128)(2,1)S(1)} %get-tuple-element.21, bf16[2,256,4096]{2,1,0:T(8,128)(2,1)S(1)} %copy-done.4), kind=kOutput, calls=%fused_computation.3 | convolution fusion | flops 537919488 | bytes 4325376 | tf_op jit(solution)/shard_map/dot_general | solution.py:111
  110.0 4.0 %reshape.78 = bf16[32,128,2,128]{3,2,1,0:T(2,128)(2,1)} reshape(bf16[4096,256]{1,0:T(8,128)(2,1)} %convolution_convert_fusion.2) | data formatting | bytes 4194304 | tf_op jit(solution)/shard_map/reshape | solution.py:76
  114.0 3.7 %convolution_convert_fusion.1 = bf16[4096,256]{1,0:T(8,128)(2,1)} fusion(bf16[256,256]{1,0:T(8,128)(2,1)S(1)} %get-tuple-element.20, bf16[2,256,4096]{2,1,0:T(8,128)(2,1)} %copy-done.3), kind=kOutput, calls=%fused_computation.2 | convolution fusion | flops 537919488 | bytes 4325376 | tf_op jit(solution)/shard_map/dot_general | solution.py:112
  117.8 4.0 %reshape.79 = bf16[32,128,2,128]{3,2,1,0:T(2,128)(2,1)} reshape(bf16[4096,256]{1,0:T(8,128)(2,1)} %convolution_convert_fusion.1) | data formatting | bytes 4194304 | tf_op jit(solution)/shard_map/reshape | solution.py:76
  121.7 3.3 %fusion.15 = bf16[1,26,128,128]{3,1,2,0:T(8,128)(2,1)S(1)} fusion(bf16[32,128,2,128]{3,2,1,0:T(2,128)(2,1)} %reshape.78, f32[26,32]{1,0:T(8,128)S(1)} %fusion.51, f32[26,2]{0,1:T(2,128)S(1)} %compare_convert_fusion), kind=kOutput, calls=%fused_computation.25 | convolution fusion | flops 54953600 | bytes 2952656 | tf_op jit(solution)/shard_map/kr,kc,rbcn->kbn/dot_general | solution.py:77
  125.0 2.6 %fusion.18 = bf16[1,26,128,128]{3,1,2,0:T(8,128)(2,1)} fusion(bf16[32,128,2,128]{3,2,1,0:T(2,128)(2,1)S(1)} %copy-done, f32[26,32]{1,0:T(8,128)S(1)} %fusion.51, f32[26,2]{0,1:T(2,128)S(1)} %compare_convert_fusion), kind=kOutput, calls=%fused_computation.26 | convolution fusion | flops 54953600 | bytes 2952656 | tf_op jit(solution)/shard_map/kr,kc,rbcn->kbn/dot_general | solution.py:77
  127.6 16.1 %reduce-scatter.2.cloned.1.call-done = bf16[16,4096]{1,0:T(8,128)(2,1)} async-done(((bf16[128,4096]{1,0:T(8,128)(2,1)}), bf16[16,4096]{1,0:T(8,128)(2,1)}) %reduce-scatter.2.cloned.1.call-update) | async-done | bytes 131088 | tf_op jit(solution)/shard_map/reduce_scatter | solution.py:33
  144.6 6.5 %collective-permute-start.6 = (bf16[4,4096]{1,0:T(4,128)(2,1)S(1)}, bf16[4,4096]{1,0:T(4,128)(2,1)S(1)}, u32[]{:S(2)}, u32[]{:S(2)}) collective-permute-start(bf16[4,4096]{1,0:T(4,128)(2,1)S(1)} %get-tuple-element.22), channel_id=1, source_target_pairs={{0,6},{2,0},{4,2},{6,4},{1,7},{3,1},{5,3},{7,5},{8,14},{10,8},{12,... | collective-permute-start | bytes 98312 | tf_op jit(solution)/shard_map/ppermute | solution.py:18
  151.2 1.9 %collective-permute-start.8 = (bf16[4,4096]{1,0:T(4,128)(2,1)S(1)}, bf16[4,4096]{1,0:T(4,128)(2,1)S(1)}, u32[]{:S(2)}, u32[]{:S(2)}) collective-permute-start(bf16[4,4096]{1,0:T(4,128)(2,1)S(1)} %get-tuple-element.23), channel_id=1, source_target_pairs={{0,2},{2,4},{4,6},{6,0},{1,3},{3,5},{5,7},{7,1},{8,10},{10,12},{12... | collective-permute-start | bytes 98312 | tf_op jit(solution)/shard_map/ppermute | solution.py:18
  153.1 6.3 %collective-permute-start.7 = (bf16[4,4096]{1,0:T(4,128)(2,1)S(1)}, bf16[4,4096]{1,0:T(4,128)(2,1)S(1)}, u32[]{:S(2)}, u32[]{:S(2)}) collective-permute-start(bf16[4,4096]{1,0:T(4,128)(2,1)S(1)} %get-tuple-element.24), channel_id=1, source_target_pairs={{0,4},{2,6},{4,0},{6,2},{1,5},{3,7},{5,1},{7,3},{8,12},{10,14},{12... | collective-permute-start | bytes 98312 | tf_op jit(solution)/shard_map/ppermute | solution.py:18
  163.6 1.5 fusion.34
  (46 shorter events, 15.9 us)
Async XLA Ops:
  7.2 75.2 %all-gather.2.cloned.1.call-start = ((), (), s32[]{:S(2)}) async-start(), calls=%async_computation.1 | async-start | bytes 2359296 | tf_op jit(solution)/shard_map/all_gather | solution.py:25
  7.2 6.4 %collective-permute-start = (bf16[1,4,4096]{2,1,0:T(4,128)(2,1)}, bf16[1,4,4096]{2,1,0:T(4,128)(2,1)S(1)}, u32[]{:S(2)}, u32[]{:S(2)}) collective-permute-start(bf16[1,4,4096]{2,1,0:T(4,128)(2,1)} %param.7), channel_id=1, source_target_pairs={{64,0},{128,64},{192,128},{256,192},{320,256},{384,320},{448,384},... | collective-permute-start | bytes 98312 | tf_op jit(solution)/shard_map/ppermute | solution.py:13
  13.7 17.3 %collective-permute-start.3 = (bf16[2,4,4096]{2,1,0:T(4,128)(2,1)S(1)}, bf16[2,4,4096]{2,1,0:T(4,128)(2,1)S(1)}, u32[]{:S(2)}, u32[]{:S(2)}) collective-permute-start(bf16[2,4,4096]{2,1,0:T(4,128)(2,1)S(1)} %constant_dynamic-update-slice_fusion), channel_id=1, source_target_pairs={{0,6},{2,0},{4,2},{6,4},{1,7},{3,1},{5,3},{7,5},{8,14},{10,8},{12,... | collective-permute-start | bytes 196616 | tf_op jit(solution)/shard_map/ppermute | solution.py:18
  24.2 10.9 %collective-permute-start.2 = (bf16[2,4,4096]{2,1,0:T(4,128)(2,1)S(1)}, bf16[2,4,4096]{2,1,0:T(4,128)(2,1)S(1)}, u32[]{:S(2)}, u32[]{:S(2)}) collective-permute-start(bf16[2,4,4096]{2,1,0:T(4,128)(2,1)S(1)} %constant_dynamic-update-slice_fusion), channel_id=1, source_target_pairs={{0,4},{2,6},{4,0},{6,2},{1,5},{3,7},{5,1},{7,3},{8,12},{10,14},{12... | collective-permute-start | bytes 196616 | tf_op jit(solution)/shard_map/ppermute | solution.py:18
  26.1 8.9 %collective-permute-start.1 = (bf16[2,4,4096]{2,1,0:T(4,128)(2,1)S(1)}, bf16[2,4,4096]{2,1,0:T(4,128)(2,1)S(1)}, u32[]{:S(2)}, u32[]{:S(2)}) collective-permute-start(bf16[2,4,4096]{2,1,0:T(4,128)(2,1)S(1)} %constant_dynamic-update-slice_fusion), channel_id=1, source_target_pairs={{0,2},{2,4},{4,6},{6,0},{1,3},{3,5},{5,7},{7,1},{8,10},{10,12},{12... | collective-permute-start | bytes 196616 | tf_op jit(solution)/shard_map/ppermute | solution.py:18
  36.0 107.7 %reduce-scatter.2.cloned.1.call-start = ((), (), s32[]{:S(2)}) async-start(), calls=%async_computation.2 | async-start | bytes 1179648 | tf_op jit(solution)/shard_map/reduce_scatter | solution.py:33
  42.6 2.7 %copy-start.7 = (bf16[1,26,128,128]{3,2,1,0:T(8,128)(2,1)S(1)}, bf16[1,26,128,128]{3,2,1,0:T(8,128)(2,1)}, u32[]{:S(2)}) copy-start(bf16[1,26,128,128]{3,2,1,0:T(8,128)(2,1)} %param.10) | copy-start | bytes 2555908
  47.5 5.2 %copy-start.8 = (bf16[1,26,128,128]{3,2,1,0:T(8,128)(2,1)S(1)}, bf16[1,26,128,128]{3,2,1,0:T(8,128)(2,1)}, u32[]{:S(2)}) copy-start(bf16[1,26,128,128]{3,2,1,0:T(8,128)(2,1)} %param.11) | copy-start | bytes 2555908
  52.7 1.6 copy-start.1
  82.3 6.3 %collective-permute-start.4 = (bf16[2,128,4096]{2,1,0:T(8,128)(2,1)}, bf16[2,128,4096]{2,1,0:T(8,128)(2,1)S(1)}, u32[]{:S(2)}, u32[]{:S(2)}) collective-permute-start(bf16[2,128,4096]{2,1,0:T(8,128)(2,1)} %all-gather.2.cloned.1.call-done), channel_id=1, source_target_pairs={{0,1},{1,0},{2,3},{3,2},{4,5},{5,4},{6,7},{7,6},{8,9},{9,8},{10,11... | collective-permute-start | bytes 6291464 | tf_op jit(solution)/shard_map/ppermute | solution.py:18
  88.8 3.9 %copy-start.3 = (bf16[2,256,4096]{2,1,0:T(8,128)(2,1)}, bf16[2,256,4096]{2,1,0:T(8,128)(2,1)S(1)}, u32[]{:S(2)}) copy-start(bf16[2,256,4096]{2,1,0:T(8,128)(2,1)S(1)} %constant_dynamic-update-slice_fusion.2) | copy-start | bytes 12582916
  88.8 3.1 %copy-start.2 = (bf16[4096,256]{0,1:T(8,128)(2,1)S(1)}, bf16[4096,256]{0,1:T(8,128)(2,1)}, u32[]{:S(2)}) copy-start(bf16[4096,256]{0,1:T(8,128)(2,1)} %get-tuple-element.10) | copy-start | bytes 6291460
  91.9 1.6 copy-start.6
  96.0 6.1 %collective-permute-start.5 = (f32[128,4096]{1,0:T(8,128)S(1)}, f32[128,4096]{1,0:T(8,128)S(1)}, u32[]{:S(2)}, u32[]{:S(2)}) collective-permute-start(f32[128,4096]{1,0:T(8,128)S(1)} %split.25), channel_id=1, source_target_pairs={{0,1},{1,0},{2,3},{3,2},{4,5},{5,4},{6,7},{7,6},{8,9},{9,8},{10,11... | collective-permute-start | bytes 6291464 | tf_op jit(solution)/shard_map/ppermute | solution.py:18
  105.7 2.2 %copy-start.4 = (bf16[2,256,4096]{2,1,0:T(8,128)(2,1)S(1)}, bf16[2,256,4096]{2,1,0:T(8,128)(2,1)}, u32[]{:S(2)}) copy-start(bf16[2,256,4096]{2,1,0:T(8,128)(2,1)} %copy-done.3) | copy-start | bytes 12582916
  121.7 3.3 %copy-start = (bf16[32,128,2,128]{3,2,1,0:T(2,128)(2,1)S(1)}, bf16[32,128,2,128]{3,2,1,0:T(2,128)(2,1)}, u32[]{:S(2)}) copy-start(bf16[32,128,2,128]{3,2,1,0:T(2,128)(2,1)} %reshape.79) | copy-start | bytes 6291460
  144.6 19.0 %collective-permute-start.6 = (bf16[4,4096]{1,0:T(4,128)(2,1)S(1)}, bf16[4,4096]{1,0:T(4,128)(2,1)S(1)}, u32[]{:S(2)}, u32[]{:S(2)}) collective-permute-start(bf16[4,4096]{1,0:T(4,128)(2,1)S(1)} %get-tuple-element.22), channel_id=1, source_target_pairs={{0,6},{2,0},{4,2},{6,4},{1,7},{3,1},{5,3},{7,5},{8,14},{10,8},{12,... | collective-permute-start | bytes 98312 | tf_op jit(solution)/shard_map/ppermute | solution.py:18
  151.2 12.5 %collective-permute-start.8 = (bf16[4,4096]{1,0:T(4,128)(2,1)S(1)}, bf16[4,4096]{1,0:T(4,128)(2,1)S(1)}, u32[]{:S(2)}, u32[]{:S(2)}) collective-permute-start(bf16[4,4096]{1,0:T(4,128)(2,1)S(1)} %get-tuple-element.23), channel_id=1, source_target_pairs={{0,2},{2,4},{4,6},{6,0},{1,3},{3,5},{5,7},{7,1},{8,10},{10,12},{12... | collective-permute-start | bytes 98312 | tf_op jit(solution)/shard_map/ppermute | solution.py:18
  153.1 10.5 %collective-permute-start.7 = (bf16[4,4096]{1,0:T(4,128)(2,1)S(1)}, bf16[4,4096]{1,0:T(4,128)(2,1)S(1)}, u32[]{:S(2)}, u32[]{:S(2)}) collective-permute-start(bf16[4,4096]{1,0:T(4,128)(2,1)S(1)} %get-tuple-element.24), channel_id=1, source_target_pairs={{0,4},{2,6},{4,0},{6,2},{1,5},{3,7},{5,1},{7,3},{8,12},{10,14},{12... | collective-permute-start | bytes 98312 | tf_op jit(solution)/shard_map/ppermute | solution.py:18
  159.9 2.5 %copy-start.5 = (bf16[1,26,128,128]{3,1,2,0:T(8,128)(2,1)S(1)}, bf16[1,26,128,128]{3,1,2,0:T(8,128)(2,1)}, u32[]{:S(2)}) copy-start(bf16[1,26,128,128]{3,1,2,0:T(8,128)(2,1)} %fusion.18) | copy-start | bytes 2555908
Sparse Core Ops, SparseCore 0:
  36.1 46.2 all-gather.1
  103.5 40.1 reduce-scatter.1

commit v9 on v8

--- a/solution.py
+++ b/solution.py
@@ -20,8 +20,9 @@
 
 def gather_rows(block, weights):
     n = lax.axis_size("zh")
-    pieces = [block] + [shifted(block, "zh", k) for k in range(1, n)]
-    block = jnp.concatenate(pieces, axis=1)
+    copies = jnp.broadcast_to(block[None], (n,) + block.shape)
+    block = lax.all_to_all(copies, "zh", 0, 0, tiled=True)
+    block = jnp.swapaxes(block, 0, 1).reshape(block.shape[1], -1, block.shape[3])
     block = lax.all_gather(block, "y", axis=1, tiled=True)
     block, weights = lax.optimization_barrier((block, weights))
     return jnp.concatenate([block, shifted(block, "core", 1)], axis=1), weights
@@ -32,11 +33,9 @@
     block = (own + shifted(other, "core", 1)).astype(jnp.bfloat16)
     block = lax.psum_scatter(block, "y", scatter_dimension=0, tiled=True)
     n = lax.axis_size("zh")
-    chunks = jnp.split(block, n, axis=0)
-    total = chunks[0].astype(jnp.float32)
-    for k in range(1, n):
-        total = total + shifted(chunks[k], "zh", -k).astype(jnp.float32)
-    return total
+    chunks = block.reshape(n, -1, block.shape[1])
+    got = lax.all_to_all(chunks, "zh", 0, 0, tiled=True)
+    return jnp.sum(got.astype(jnp.float32), axis=0)
 
 
 def per_device(saved_input, grad_sent, kept_blocks, gate_blocks, up_blocks, down_blocks):

time: 173 us -> 167 us (0.965)
  starting transfers between devices: 40.7 us -> 16.4 us
  blocking collectives: 0 us -> 20.8 us
  waiting for transfers between devices: 49.6 us -> 56.6 us
  matrix products: 23.5 us -> 18 us
  local copies, waits for them, and re-layouts: 39.4 us -> 36.9 us
    ppermute x8 -> x2, starting transfers between devices: 36.1 us -> 4.14 us  [shifted(): return lax.ppermute(block, axis, [(i, (i + shift) % n) for i in range(n)])]
    all_to_all x0 -> x1, blocking collectives: none -> 20.8 us  [gather_rows(): block = lax.all_to_all(copies, 'zh', 0, 0, tiled=True)]
    all_to_all x0 -> x1, starting transfers between devices: none -> 7.45 us  [scatter_rows(): got = lax.all_to_all(chunks, 'zh', 0, 0, tiled=True)]
    reduce_scatter x1, waiting for transfers between devices: 16.1 us -> 22.8 us  [scatter_rows(): block = lax.psum_scatter(block, 'y', scatter_dimension=0, tiled=True)]
    all_to_all x0 -> x1, waiting for transfers between devices: none -> 5.94 us  [scatter_rows(): got = lax.all_to_all(chunks, 'zh', 0, 0, tiled=True)]
    all_gather x1, waiting for transfers between devices: 21.9 us -> 17.9 us  [gather_rows(): block = lax.all_gather(block, 'y', axis=1, tiled=True)]
    unnamed x25 -> x23, local copies, waits for them, and re-layouts: 14.9 us -> 11.4 us
    optimization_barrier x0 -> x1, local copies, waits for them, and re-layouts: none -> 2.94 us  [gather_rows(): block, weights = lax.optimization_barrier((block, weights))]
  transfers between devices with their start and end apart: 11 -> 6, of which waited for: 6 -> 6; matrix products, arithmetic and copies ran while one was open for 31% -> 25% of each run, Pallas kernels for 0% -> 0%
where the time goes in v9:
time: 167 us; the launch traced here: 166 us
  waiting for transfers between devices  56.6 us (34%)
  local copies, waits for them, and re-layouts  36.9 us (22%)
  blocking collectives  20.8 us (12%)
  matrix products  18 us (11%)
  starting transfers between devices  16.4 us (10%)
  between operations  14.3 us (9%)
  other arithmetic  3.45 us (2%)
    reduce_scatter x1, waiting for transfers between devices, scatter_rows(): block = lax.psum_scatter(block, 'y', scatter_dimension=0, tiled=True)  22.8 us
    all_to_all x1, blocking collectives, gather_rows(): block = lax.all_to_all(copies, 'zh', 0, 0, tiled=True)  20.8 us
    all_gather x1, waiting for transfers between devices, gather_rows(): block = lax.all_gather(block, 'y', axis=1, tiled=True)  17.9 us
    unnamed x23, local copies, waits for them, and re-layouts  11.4 us
    convert_element_type x2, local copies, waits for them, and re-layouts, dense_in(): return placed.astype(jnp.bfloat16).reshape(width, hidden_units)  9.07 us
    ppermute x2, waiting for transfers between devices, shifted(): return lax.ppermute(block, axis, [(i, (i + shift) % n) for i in range(n)])  7.95 us
    all_to_all x1, starting transfers between devices, scatter_rows(): got = lax.all_to_all(chunks, 'zh', 0, 0, tiled=True)  7.45 us
    reshape x1, local copies, waits for them, and re-layouts, dense_down(): return placed.astype(jnp.bfloat16).reshape(hidden_units, width)  6.16 us
  transfers between devices with their start and end apart: 6, of which 6 were waited for; matrix products, arithmetic and copies ran while one was open for 25% of the time, Pallas kernels for 0%

profile of v9, /device:TPU:6, one launch (start us, length us, event | category | flops | bytes accessed | tf_op | source)
XLA Modules:
  0.0 166.3 jit_solution(13069135694351698275)
XLA Ops:
  7.2 4.7 %collective-permute-start = (bf16[1,4,4096]{2,1,0:T(4,128)(2,1)}, bf16[1,4,4096]{2,1,0:T(4,128)(2,1)S(1)}, u32[]{:S(2)}, u32[]{:S(2)}) collective-permute-start(bf16[1,4,4096]{2,1,0:T(4,128)(2,1)} %param.7), channel_id=1, source_target_pairs={{64,0},{128,64},{192,128},{256,192},{320,256},{384,320},{448,384},... | collective-permute-start | bytes 98312 | tf_op jit(solution)/shard_map/ppermute | solution.py:13
  11.9 1.9 %collective-permute-done = bf16[1,4,4096]{2,1,0:T(4,128)(2,1)S(1)} collective-permute-done((bf16[1,4,4096]{2,1,0:T(4,128)(2,1)}, bf16[1,4,4096]{2,1,0:T(4,128)(2,1)S(1)}, u32[]{:S(2)}, u32[]{:S(2)}) %collective-permute-start) | collective-permute-done | bytes 32800 | tf_op jit(solution)/shard_map/ppermute | solution.py:13
  14.9 20.8 %all_to_all.10 = bf16[4,2,4,4096]{3,1,2,0:T(2,128)(2,1)} all-to-all(bf16[4,2,4,4096]{3,1,2,0:T(2,128)(2,1)S(1)} %broadcast_in_dim.10), channel_id=1, replica_groups=mesh['section'=8,'y'=8,'zh'=4,'core'=2] {'zh'}, dimensions={0} | all-to-all | bytes 524288 | tf_op jit(solution)/shard_map/all_to_all | solution.py:24
  36.5 0.9 convert_bitcast_fusion.1
  37.4 3.8 %copy.55 = bf16[32,128,2,128]{1,0,3,2:T(8,128)(2,1)} copy(bf16[32,128,2,128]{3,0,1,2:T(8,128)(2,1)S(1)} %convert_bitcast_fusion.1) | data formatting | bytes 4194304 | tf_op jit(solution)/shard_map/convert_element_type | solution.py:65
  41.2 2.7 %copy.114 = bf16[32,8,32,128]{3,1,2,0:T(8,128)(2,1)S(1)} copy(bf16[32,8,32,128]{3,2,1,0:T(8,128)(2,1)} %bitcast.134) | data formatting | bytes 4194304
  43.9 2.2 %convert_bitcast_fusion = bf16[32,128,2,128]{3,0,1,2:T(8,128)(2,1)} fusion(bf16[26,128,128]{2,1,0:T(8,128)(2,1)S(1)} %bitcast.139, f32[26,32]{1,0:T(8,128)S(1)} %fusion.50, f32[26,2]{0,1:T(2,128)S(1)} %compare_convert_fusion), kind=kOutput, calls=%fused_computation.20 | convolution fusion | flops 55576192 | bytes 2952656 | tf_op jit(solution)/shard_map/kr,kc,kbn->rbcn/dot_general | solution.py:61
  46.2 5.2 %copy.58 = bf16[32,128,2,128]{1,0,3,2:T(8,128)(2,1)} copy(bf16[32,128,2,128]{3,0,1,2:T(8,128)(2,1)} %convert_bitcast_fusion) | data formatting | bytes 4194304 | tf_op jit(solution)/shard_map/convert_element_type | solution.py:65
  51.4 0.9 convolution_convert_fusion.3
  53.0 6.2 %copy_bitcast_fusion = (bf16[256,4096]{1,0:T(8,128)(2,1)}, bf16[4096,256]{0,1:T(8,128)(2,1)}) fusion(bf16[32,8,32,128]{3,2,1,0:T(8,128)(2,1)S(1)} %bitcast.137, bf16[32,8,32,128]{3,2,1,0:T(8,128)(2,1)S(1)} %bitcast.136), kind=kLoop, calls=%fused_computation.6 | loop fusion | bytes 8388608 | tf_op jit(solution)/shard_map/reshape | solution.py:72
  59.1 17.9 %all-gather.2.cloned.1.call-done = bf16[2,128,4096]{2,0,1:T(2,128)(2,1)} async-done(((bf16[2,16,4096]{2,0,1:T(2,128)(2,1)}), bf16[2,128,4096]{2,0,1:T(2,128)(2,1)}) %all-gather.2.cloned.1.call-update) | async-done | bytes 2097168 | tf_op jit(solution)/shard_map/all_gather | solution.py:26
  77.1 2.9 %fusion.52 = (bf16[2,128,4096]{2,1,0:T(8,128)(2,1)S(1)}, bf16[2,256,4096]{2,1,0:T(8,128)(2,1)S(1)}) fusion(bf16[2,128,4096]{2,0,1:T(2,128)(2,1)} %all-gather.2.cloned.1.call-done), kind=kLoop, calls=%fused_computation.72 | loop fusion | bytes 6291456 | tf_op jit(solution)/shard_map/optimization_barrier | solution.py:27
  80.0 2.1 %collective-permute-start.1 = (bf16[2,128,4096]{2,1,0:T(8,128)(2,1)S(1)}, bf16[2,128,4096]{2,1,0:T(8,128)(2,1)S(1)}, u32[]{:S(2)}, u32[]{:S(2)}) collective-permute-start(bf16[2,128,4096]{2,1,0:T(8,128)(2,1)S(1)} %get-tuple-element.28), channel_id=1, source_target_pairs={{0,1},{1,0},{2,3},{3,2},{4,5},{5,4},{6,7},{7,6},{8,9},{9,8},{10,11... | collective-permute-start | bytes 6291464 | tf_op jit(solution)/shard_map/ppermute | solution.py:18
  82.1 3.9 %collective-permute-done.1 = bf16[2,128,4096]{2,1,0:T(8,128)(2,1)S(1)} collective-permute-done((bf16[2,128,4096]{2,1,0:T(8,128)(2,1)S(1)}, bf16[2,128,4096]{2,1,0:T(8,128)(2,1)S(1)}, u32[]{:S(2)}, u32[]{:S(2)}) %collective-permute-start.1) | collective-permute-done | bytes 2097184 | tf_op jit(solution)/shard_map/ppermute | solution.py:18
  87.0 2.4 %copy-done.1 = bf16[4096,256]{0,1:T(8,128)(2,1)S(1)} copy-done((bf16[4096,256]{0,1:T(8,128)(2,1)S(1)}, bf16[4096,256]{0,1:T(8,128)(2,1)}, u32[]{:S(2)}) %copy-start.1) | copy-done | bytes 2097176
  93.4 2.0 %collective-permute-start.2 = (f32[128,4096]{1,0:T(8,128)S(1)}, f32[128,4096]{1,0:T(8,128)S(1)}, u32[]{:S(2)}, u32[]{:S(2)}) collective-permute-start(f32[128,4096]{1,0:T(8,128)S(1)} %split.9), channel_id=1, source_target_pairs={{0,1},{1,0},{2,3},{3,2},{4,5},{5,4},{6,7},{7,6},{8,9},{9,8},{10,11... | collective-permute-start | bytes 6291464 | tf_op jit(solution)/shard_map/ppermute | solution.py:18
  95.4 4.0 %collective-permute-done.2 = f32[128,4096]{1,0:T(8,128)S(1)} collective-permute-done((f32[128,4096]{1,0:T(8,128)S(1)}, f32[128,4096]{1,0:T(8,128)S(1)}, u32[]{:S(2)}, u32[]{:S(2)}) %collective-permute-start.2) | collective-permute-done | bytes 2097184 | tf_op jit(solution)/shard_map/ppermute | solution.py:18
  99.4 1.2 fusion.2
  100.7 2.4 %fusion.10 = bf16[32,8,32,128]{3,1,2,0:T(8,128)(2,1)S(1)} fusion(bf16[2,256,4096]{2,1,0:T(8,128)(2,1)} %copy-done.2, f32[256,256]{1,0:T(8,128)S(1)} %fusion.25, f32[256,256]{1,0:T(8,128)S(1)} %fusion.24), kind=kOutput, calls=%fused_computation.24 | convolution fusion | flops 538312704 | bytes 4718592 | tf_op jit(solution)/shard_map/dot_general | solution.py:112
  104.1 1.2 copy.68
  106.0 2.1 %convolution_convert_fusion.2 = bf16[4096,256]{1,0:T(8,128)(2,1)} fusion(bf16[256,256]{1,0:T(8,128)(2,1)S(1)} %get-tuple-element.31, bf16[2,256,4096]{2,1,0:T(8,128)(2,1)S(1)} %copy-done.3), kind=kOutput, calls=%fused_computation.3 | convolution fusion | flops 537919488 | bytes 4325376 | tf_op jit(solution)/shard_map/dot_general | solution.py:110
  108.1 2.5 %reshape.87 = bf16[32,128,2,128]{3,2,1,0:T(2,128)(2,1)S(1)} reshape(bf16[4096,256]{1,0:T(8,128)(2,1)} %convolution_convert_fusion.2) | data formatting | bytes 4194304 | tf_op jit(solution)/shard_map/reshape | solution.py:75
  110.7 1.5 fusion.15
  112.2 1.2 copy.66
  113.5 2.1 %convolution_convert_fusion.1 = bf16[4096,256]{1,0:T(8,128)(2,1)} fusion(bf16[256,256]{1,0:T(8,128)(2,1)S(1)} %get-tuple-element.30, bf16[2,256,4096]{2,1,0:T(8,128)(2,1)S(1)} %copy-done.4), kind=kOutput, calls=%fused_computation.2 | convolution fusion | flops 537919488 | bytes 4325376 | tf_op jit(solution)/shard_map/dot_general | solution.py:111
  115.6 2.5 %reshape.88 = bf16[32,128,2,128]{3,2,1,0:T(2,128)(2,1)S(1)} reshape(bf16[4096,256]{1,0:T(8,128)(2,1)} %convolution_convert_fusion.1) | data formatting | bytes 4194304 | tf_op jit(solution)/shard_map/reshape | solution.py:75
  118.1 22.8 %reduce-scatter.2.cloned.1.call-done = bf16[16,4096]{1,0:T(8,128)(2,1)} async-done(((bf16[128,4096]{1,0:T(8,128)(2,1)}), bf16[16,4096]{1,0:T(8,128)(2,1)}) %reduce-scatter.2.cloned.1.call-update) | async-done | bytes 131088 | tf_op jit(solution)/shard_map/reduce_scatter | solution.py:34
  140.9 1.6 reshape.86
  142.6 7.5 %all-to-all-start.1 = ((bf16[4,4,4096]{2,1,0:T(4,128)(2,1)}), bf16[4,4,4096]{2,1,0:T(4,128)(2,1)S(1)}, u32[]{:S(2)}, u32[]{:S(2)}) async-start(bf16[4,4,4096]{2,1,0:T(4,128)(2,1)} %reshape.86), calls=%async_computation.2 | async-start | bytes 262144 | tf_op jit(solution)/shard_map/all_to_all | solution.py:37
  150.0 1.5 fusion.18
  151.6 1.2 copy.67
  152.8 5.9 %all-to-all-done.1 = bf16[4,4,4096]{2,1,0:T(4,128)(2,1)S(1)} async-done(((bf16[4,4,4096]{2,1,0:T(4,128)(2,1)}), bf16[4,4,4096]{2,1,0:T(4,128)(2,1)S(1)}, u32[]{:S(2)}, u32[]{:S(2)}) %all-to-all-start.1) | async-done | bytes 131104 | tf_op jit(solution)/shard_map/all_to_all | solution.py:37
  (37 shorter events, 9.9 us)
Async XLA Ops:
  7.2 29.3 %copy-start.6 = (bf16[1,26,128,128]{3,2,1,0:T(8,128)(2,1)S(1)}, bf16[1,26,128,128]{3,2,1,0:T(8,128)(2,1)}, u32[]{:S(2)}) copy-start(bf16[1,26,128,128]{3,2,1,0:T(8,128)(2,1)} %param.9) | copy-start | bytes 2555908
  7.2 69.9 %all-gather.2.cloned.1.call-start = ((), (), s32[]{:S(2)}) async-start(), calls=%async_computation.3 | async-start | bytes 2359296 | tf_op jit(solution)/shard_map/all_gather | solution.py:26
  7.2 6.6 %collective-permute-start = (bf16[1,4,4096]{2,1,0:T(4,128)(2,1)}, bf16[1,4,4096]{2,1,0:T(4,128)(2,1)S(1)}, u32[]{:S(2)}, u32[]{:S(2)}) collective-permute-start(bf16[1,4,4096]{2,1,0:T(4,128)(2,1)} %param.7), channel_id=1, source_target_pairs={{64,0},{128,64},{192,128},{256,192},{320,256},{384,320},{448,384},... | collective-permute-start | bytes 98312 | tf_op jit(solution)/shard_map/ppermute | solution.py:13
  35.7 105.3 %reduce-scatter.2.cloned.1.call-start = ((), (), s32[]{:S(2)}) async-start(), calls=%async_computation.4 | async-start | bytes 1179648 | tf_op jit(solution)/shard_map/reduce_scatter | solution.py:34
  41.2 2.7 %copy-start.7 = (bf16[1,26,128,128]{3,2,1,0:T(8,128)(2,1)S(1)}, bf16[1,26,128,128]{3,2,1,0:T(8,128)(2,1)}, u32[]{:S(2)}) copy-start(bf16[1,26,128,128]{3,2,1,0:T(8,128)(2,1)} %param.10) | copy-start | bytes 2555908
  46.2 5.2 %copy-start.8 = (bf16[1,26,128,128]{3,2,1,0:T(8,128)(2,1)S(1)}, bf16[1,26,128,128]{3,2,1,0:T(8,128)(2,1)}, u32[]{:S(2)}) copy-start(bf16[1,26,128,128]{3,2,1,0:T(8,128)(2,1)} %param.11) | copy-start | bytes 2555908
  51.4 1.6 copy-start
  80.0 6.1 %collective-permute-start.1 = (bf16[2,128,4096]{2,1,0:T(8,128)(2,1)S(1)}, bf16[2,128,4096]{2,1,0:T(8,128)(2,1)S(1)}, u32[]{:S(2)}, u32[]{:S(2)}) collective-permute-start(bf16[2,128,4096]{2,1,0:T(8,128)(2,1)S(1)} %get-tuple-element.28), channel_id=1, source_target_pairs={{0,1},{1,0},{2,3},{3,2},{4,5},{5,4},{6,7},{7,6},{8,9},{9,8},{10,11... | collective-permute-start | bytes 6291464 | tf_op jit(solution)/shard_map/ppermute | solution.py:18
  86.2 3.9 %copy-start.2 = (bf16[2,256,4096]{2,1,0:T(8,128)(2,1)}, bf16[2,256,4096]{2,1,0:T(8,128)(2,1)S(1)}, u32[]{:S(2)}) copy-start(bf16[2,256,4096]{2,1,0:T(8,128)(2,1)S(1)} %constant_dynamic-update-slice_fusion) | copy-start | bytes 12582916
  86.2 3.1 %copy-start.1 = (bf16[4096,256]{0,1:T(8,128)(2,1)S(1)}, bf16[4096,256]{0,1:T(8,128)(2,1)}, u32[]{:S(2)}) copy-start(bf16[4096,256]{0,1:T(8,128)(2,1)} %get-tuple-element.10) | copy-start | bytes 6291460
  89.3 1.6 copy-start.5
  93.4 6.1 %collective-permute-start.2 = (f32[128,4096]{1,0:T(8,128)S(1)}, f32[128,4096]{1,0:T(8,128)S(1)}, u32[]{:S(2)}, u32[]{:S(2)}) collective-permute-start(f32[128,4096]{1,0:T(8,128)S(1)} %split.9), channel_id=1, source_target_pairs={{0,1},{1,0},{2,3},{3,2},{4,5},{5,4},{6,7},{7,6},{8,9},{9,8},{10,11... | collective-permute-start | bytes 6291464 | tf_op jit(solution)/shard_map/ppermute | solution.py:18
  103.5 2.5 %copy-start.3 = (bf16[2,256,4096]{2,1,0:T(8,128)(2,1)S(1)}, bf16[2,256,4096]{2,1,0:T(8,128)(2,1)}, u32[]{:S(2)}) copy-start(bf16[2,256,4096]{2,1,0:T(8,128)(2,1)} %copy-done.2) | copy-start | bytes 12582916
  110.7 2.8 %copy-start.4 = (bf16[2,256,4096]{2,1,0:T(8,128)(2,1)S(1)}, bf16[2,256,4096]{2,1,0:T(8,128)(2,1)}, u32[]{:S(2)}) copy-start(bf16[2,256,4096]{2,1,0:T(8,128)(2,1)} %copy-done.2) | copy-start | bytes 12582916
  142.6 16.2 %all-to-all-start.1 = ((bf16[4,4,4096]{2,1,0:T(4,128)(2,1)}), bf16[4,4,4096]{2,1,0:T(4,128)(2,1)S(1)}, u32[]{:S(2)}, u32[]{:S(2)}) async-start(bf16[4,4,4096]{2,1,0:T(4,128)(2,1)} %reshape.86), calls=%async_computation.2 | async-start | bytes 262144 | tf_op jit(solution)/shard_map/all_to_all | solution.py:37
Sparse Core Ops, SparseCore 0:
  35.8 41.2 all-gather.1
  100.8 40.1 reduce-scatter.1

commit v10 on v9

--- a/solution.py
+++ b/solution.py
@@ -28,10 +28,32 @@
     return jnp.concatenate([block, shifted(block, "core", 1)], axis=1), weights
 
 
+def ring_reduce(block, axis):
+    n = lax.axis_size(axis)
+    idx = lax.axis_index(axis)
+    chunks = block.reshape(n, -1, block.shape[1])
+
+    def chunk_for(dist):
+        return lax.dynamic_index_in_dim(chunks, (idx + dist) % n, 0, keepdims=False)
+
+    back = n // 2
+    ahead = n - 1 - back
+    acc = chunk_for(-back).astype(jnp.float32)
+    for d in range(back - 1, -1, -1):
+        acc = shifted(acc.astype(jnp.bfloat16), axis, -1).astype(jnp.float32) + chunk_for(-d)
+    total = acc
+    if ahead:
+        acc = chunk_for(ahead).astype(jnp.float32)
+        for d in range(ahead - 1, 0, -1):
+            acc = shifted(acc.astype(jnp.bfloat16), axis, 1).astype(jnp.float32) + chunk_for(d)
+        total = total + shifted(acc.astype(jnp.bfloat16), axis, 1).astype(jnp.float32)
+    return total
+
+
 def scatter_rows(block):
     own, other = jnp.split(block, 2, axis=0)
-    block = (own + shifted(other, "core", 1)).astype(jnp.bfloat16)
-    block = lax.psum_scatter(block, "y", scatter_dimension=0, tiled=True)
+    block = own + shifted(other, "core", 1)
+    block = ring_reduce(block, "y").astype(jnp.bfloat16)
     n = lax.axis_size("zh")
     chunks = block.reshape(n, -1, block.shape[1])
     got = lax.all_to_all(chunks, "zh", 0, 0, tiled=True)

time: 167 us -> 170 us (1.018)
  starting transfers between devices: 16.4 us -> 40.9 us
  waiting for transfers between devices: 56.6 us -> 35.7 us
    ppermute x2 -> x9, starting transfers between devices: 4.14 us -> 28.8 us  [shifted(): return lax.ppermute(block, axis, [(i, (i + shift) % n) for i in range(n)])]
    reduce_scatter x1 -> x0, waiting for transfers between devices: 22.8 us -> none  [scatter_rows(): block = lax.psum_scatter(block, 'y', scatter_dimension=0, tiled=True)]
    all_gather x1, waiting for transfers between devices: 17.9 us -> 20.8 us  [gather_rows(): block = lax.all_gather(block, 'y', axis=1, tiled=True)]
    dot_general x1, matrix products: 2.1 us -> 3.89 us  [per_device(): lax.dot_general(inputs, grad_up_act, rows_t, preferred_element_type=f32)]
    ppermute x2 -> x9, waiting for transfers between devices: 7.95 us -> 7.42 us  [shifted(): return lax.ppermute(block, axis, [(i, (i + shift) % n) for i in range(n)])]
    unnamed x23 -> x27, local copies, waits for them, and re-layouts: 11.4 us -> 11.6 us
  transfers between devices with their start and end apart: 6 -> 12, of which waited for: 6 -> 8; matrix products, arithmetic and copies ran while one was open for 25% -> 23% of each run, Pallas kernels for 0% -> 0%
where the time goes in v10:
time: 170 us
  starting transfers between devices  40.9 us (24%)
  local copies, waits for them, and re-layouts  36.1 us (21%)
  waiting for transfers between devices  35.7 us (21%)
  blocking collectives  20.8 us (12%)
  matrix products  16.9 us (10%)
  between operations  14.5 us (9%)
  other arithmetic  4.65 us (3%)
    ppermute x9, starting transfers between devices, shifted(): return lax.ppermute(block, axis, [(i, (i + shift) % n) for i in range(n)])  28.8 us
    all_to_all x1, blocking collectives, gather_rows(): block = lax.all_to_all(copies, 'zh', 0, 0, tiled=True)  20.8 us
    all_gather x1, waiting for transfers between devices, gather_rows(): block = lax.all_gather(block, 'y', axis=1, tiled=True)  20.8 us
    unnamed x27, local copies, waits for them, and re-layouts  11.6 us
    convert_element_type x2, local copies, waits for them, and re-layouts, dense_in(): return placed.astype(jnp.bfloat16).reshape(width, hidden_units)  7.65 us
    ppermute x9, waiting for transfers between devices, shifted(): return lax.ppermute(block, axis, [(i, (i + shift) % n) for i in range(n)])  7.42 us
    all_to_all x1, starting transfers between devices, scatter_rows(): got = lax.all_to_all(chunks, 'zh', 0, 0, tiled=True)  7.37 us
    reshape x1, local copies, waits for them, and re-layouts, dense_down(): return placed.astype(jnp.bfloat16).reshape(hidden_units, width)  6.08 us
  transfers between devices with their start and end apart: 12, of which 8 were waited for; matrix products, arithmetic and copies ran while one was open for 23% of the time, Pallas kernels for 0%

profile of v10, /device:TPU:6, one launch (start us, length us, event | category | flops | bytes accessed | tf_op | source)
XLA Modules:
  0.0 169.5 jit_solution(10278307354060403118)
XLA Ops:
  7.2 4.7 %collective-permute-start = (bf16[1,4,4096]{2,1,0:T(4,128)(2,1)}, bf16[1,4,4096]{2,1,0:T(4,128)(2,1)S(1)}, u32[]{:S(2)}, u32[]{:S(2)}) collective-permute-start(bf16[1,4,4096]{2,1,0:T(4,128)(2,1)} %param.7), channel_id=1, source_target_pairs={{64,0},{128,64},{192,128},{256,192},{320,256},{384,320},{448,384},... | collective-permute-start | bytes 98312 | tf_op jit(solution)/shard_map/ppermute | solution.py:13
  11.9 1.9 %collective-permute-done = bf16[1,4,4096]{2,1,0:T(4,128)(2,1)S(1)} collective-permute-done((bf16[1,4,4096]{2,1,0:T(4,128)(2,1)}, bf16[1,4,4096]{2,1,0:T(4,128)(2,1)S(1)}, u32[]{:S(2)}, u32[]{:S(2)}) %collective-permute-start) | collective-permute-done | bytes 32800 | tf_op jit(solution)/shard_map/ppermute | solution.py:13
  14.9 20.8 %all_to_all.10 = bf16[4,2,4,4096]{3,1,2,0:T(2,128)(2,1)} all-to-all(bf16[4,2,4,4096]{3,1,2,0:T(2,128)(2,1)S(1)} %broadcast_in_dim.10), channel_id=1, replica_groups=mesh['section'=8,'y'=8,'zh'=4,'core'=2] {'zh'}, dimensions={0} | all-to-all | bytes 524288 | tf_op jit(solution)/shard_map/all_to_all | solution.py:24
  37.4 3.8 %copy.58 = bf16[32,128,2,128]{1,0,3,2:T(8,128)(2,1)} copy(bf16[32,128,2,128]{3,0,1,2:T(8,128)(2,1)S(1)} %convert_bitcast_fusion) | data formatting | bytes 4194304 | tf_op jit(solution)/shard_map/convert_element_type | solution.py:87
  42.1 3.8 %copy.55 = bf16[32,128,2,128]{1,0,3,2:T(8,128)(2,1)} copy(bf16[32,128,2,128]{3,0,1,2:T(8,128)(2,1)S(1)} %convert_bitcast_fusion.1) | data formatting | bytes 4194304 | tf_op jit(solution)/shard_map/convert_element_type | solution.py:87
  45.9 2.7 %copy.114 = bf16[32,8,32,128]{3,1,2,0:T(8,128)(2,1)S(1)} copy(bf16[32,8,32,128]{3,2,1,0:T(8,128)(2,1)} %bitcast.166) | data formatting | bytes 4194304
  50.2 6.1 %copy_bitcast_fusion = (bf16[256,4096]{1,0:T(8,128)(2,1)}, bf16[4096,256]{0,1:T(8,128)(2,1)}) fusion(bf16[32,8,32,128]{3,2,1,0:T(8,128)(2,1)S(1)} %bitcast.168, bf16[32,8,32,128]{3,2,1,0:T(8,128)(2,1)S(1)} %bitcast.167), kind=kLoop, calls=%fused_computation.6 | loop fusion | bytes 8388608 | tf_op jit(solution)/shard_map/reshape | solution.py:94
  56.3 20.8 %all-gather.2.cloned.1.call-done = bf16[2,128,4096]{2,0,1:T(2,128)(2,1)} async-done(((bf16[2,16,4096]{2,0,1:T(2,128)(2,1)}), bf16[2,128,4096]{2,0,1:T(2,128)(2,1)}) %all-gather.2.cloned.1.call-update) | async-done | bytes 2097168 | tf_op jit(solution)/shard_map/all_gather | solution.py:26
  77.0 2.9 %fusion.60 = (bf16[2,128,4096]{2,1,0:T(8,128)(2,1)S(1)}, bf16[2,256,4096]{2,1,0:T(8,128)(2,1)S(1)}) fusion(bf16[2,128,4096]{2,0,1:T(2,128)(2,1)} %all-gather.2.cloned.1.call-done), kind=kLoop, calls=%fused_computation.88 | loop fusion | bytes 6291456 | tf_op jit(solution)/shard_map/optimization_barrier | solution.py:27
  80.0 2.1 %collective-permute-start.1 = (bf16[2,128,4096]{2,1,0:T(8,128)(2,1)S(1)}, bf16[2,128,4096]{2,1,0:T(8,128)(2,1)S(1)}, u32[]{:S(2)}, u32[]{:S(2)}) collective-permute-start(bf16[2,128,4096]{2,1,0:T(8,128)(2,1)S(1)} %get-tuple-element.34), channel_id=1, source_target_pairs={{0,1},{1,0},{2,3},{3,2},{4,5},{5,4},{6,7},{7,6},{8,9},{9,8},{10,11... | collective-permute-start | bytes 6291464 | tf_op jit(solution)/shard_map/ppermute | solution.py:18
  82.1 3.9 %collective-permute-done.1 = bf16[2,128,4096]{2,1,0:T(8,128)(2,1)S(1)} collective-permute-done((bf16[2,128,4096]{2,1,0:T(8,128)(2,1)S(1)}, bf16[2,128,4096]{2,1,0:T(8,128)(2,1)S(1)}, u32[]{:S(2)}, u32[]{:S(2)}) %collective-permute-start.1) | collective-permute-done | bytes 2097184 | tf_op jit(solution)/shard_map/ppermute | solution.py:18
  86.2 1.4 copy-done.3
  93.0 1.6 split.9
  95.6 2.0 %collective-permute-start.2 = (f32[128,4096]{1,0:T(8,128)}, f32[128,4096]{1,0:T(8,128)S(1)}, u32[]{:S(2)}, u32[]{:S(2)}) collective-permute-start(f32[128,4096]{1,0:T(8,128)} %split.9), channel_id=1, source_target_pairs={{0,1},{1,0},{2,3},{3,2},{4,5},{5,4},{6,7},{7,6},{8,9},{9,8},{10,11... | collective-permute-start | bytes 6291464 | tf_op jit(solution)/shard_map/ppermute | solution.py:18
  97.8 3.9 %convolution_convert_fusion.1 = bf16[4096,256]{1,0:T(8,128)(2,1)} fusion(bf16[256,256]{1,0:T(8,128)(2,1)S(1)} %get-tuple-element.36, bf16[2,256,4096]{2,1,0:T(8,128)(2,1)} %copy-done.5), kind=kOutput, calls=%fused_computation.2 | convolution fusion | flops 537919488 | bytes 4325376 | tf_op jit(solution)/shard_map/dot_general | solution.py:133
  102.2 4.3 %collective-permute-start.3 = (bf16[16,4096]{1,0:T(8,128)(2,1)S(1)}, bf16[16,4096]{1,0:T(8,128)(2,1)S(1)}, u32[]{:S(2)}, u32[]{:S(2)}) collective-permute-start(bf16[16,4096]{1,0:T(8,128)(2,1)S(1)} %get-tuple-element.32), channel_id=1, source_target_pairs={{0,56},{8,0},{16,8},{24,16},{32,24},{40,32},{48,40},{56,48},{1,57}... | collective-permute-start | bytes 393224 | tf_op jit(solution)/shard_map/ppermute | solution.py:18
  106.5 2.2 %convolution_convert_fusion.2 = bf16[4096,256]{1,0:T(8,128)(2,1)} fusion(bf16[256,256]{1,0:T(8,128)(2,1)S(1)} %get-tuple-element.37, bf16[2,256,4096]{2,1,0:T(8,128)(2,1)S(1)} %copy-done.6), kind=kOutput, calls=%fused_computation.3 | convolution fusion | flops 537919488 | bytes 4325376 | tf_op jit(solution)/shard_map/dot_general | solution.py:132
  108.6 1.9 %collective-permute-start.7 = (bf16[16,4096]{1,0:T(8,128)(2,1)S(1)}, bf16[16,4096]{1,0:T(8,128)(2,1)S(1)}, u32[]{:S(2)}, u32[]{:S(2)}) collective-permute-start(bf16[16,4096]{1,0:T(8,128)(2,1)S(1)} %get-tuple-element.33), channel_id=1, source_target_pairs={{0,8},{8,16},{16,24},{24,32},{32,40},{40,48},{48,56},{56,0},{1,9},... | collective-permute-start | bytes 393224 | tf_op jit(solution)/shard_map/ppermute | solution.py:18
  110.6 5.1 %collective-permute-start.4 = (bf16[16,4096]{1,0:T(8,128)(2,1)S(1)}, bf16[16,4096]{1,0:T(8,128)(2,1)S(1)}, u32[]{:S(2)}, u32[]{:S(2)}) collective-permute-start(bf16[16,4096]{1,0:T(8,128)(2,1)S(1)} %fusion.37), channel_id=1, source_target_pairs={{0,56},{8,0},{16,8},{24,16},{32,24},{40,32},{48,40},{56,48},{1,57}... | collective-permute-start | bytes 393224 | tf_op jit(solution)/shard_map/ppermute | solution.py:18
  118.3 5.6 %collective-permute-start.5 = (bf16[16,4096]{1,0:T(8,128)(2,1)S(1)}, bf16[16,4096]{1,0:T(8,128)(2,1)S(1)}, u32[]{:S(2)}, u32[]{:S(2)}) collective-permute-start(bf16[16,4096]{1,0:T(8,128)(2,1)S(1)} %get-tuple-element.30), channel_id=1, source_target_pairs={{0,56},{8,0},{16,8},{24,16},{32,24},{40,32},{48,40},{56,48},{1,57}... | collective-permute-start | bytes 393224 | tf_op jit(solution)/shard_map/ppermute | solution.py:18
  123.9 1.9 %collective-permute-start.8 = (bf16[16,4096]{1,0:T(8,128)(2,1)S(1)}, bf16[16,4096]{1,0:T(8,128)(2,1)S(1)}, u32[]{:S(2)}, u32[]{:S(2)}) collective-permute-start(bf16[16,4096]{1,0:T(8,128)(2,1)S(1)} %get-tuple-element.31), channel_id=1, source_target_pairs={{0,8},{8,16},{16,24},{24,32},{32,40},{40,48},{48,56},{56,0},{1,9},... | collective-permute-start | bytes 393224 | tf_op jit(solution)/shard_map/ppermute | solution.py:18
  126.4 1.2 copy.68
  127.7 2.5 %reshape.94 = bf16[32,128,2,128]{3,2,1,0:T(2,128)(2,1)S(1)} reshape(bf16[4096,256]{1,0:T(8,128)(2,1)} %convolution_convert_fusion.1) | data formatting | bytes 4194304 | tf_op jit(solution)/shard_map/reshape | solution.py:97
  130.2 1.8 %collective-permute-done.8 = bf16[16,4096]{1,0:T(8,128)(2,1)S(1)} collective-permute-done((bf16[16,4096]{1,0:T(8,128)(2,1)S(1)}, bf16[16,4096]{1,0:T(8,128)(2,1)S(1)}, u32[]{:S(2)}, u32[]{:S(2)}) %collective-permute-start.8) | collective-permute-done | bytes 131104 | tf_op jit(solution)/shard_map/ppermute | solution.py:18
  133.1 3.4 %collective-permute-start.6 = (bf16[16,4096]{1,0:T(8,128)(2,1)S(1)}, bf16[16,4096]{1,0:T(8,128)(2,1)S(1)}, u32[]{:S(2)}, u32[]{:S(2)}) collective-permute-start(bf16[16,4096]{1,0:T(8,128)(2,1)S(1)} %get-tuple-element.28), channel_id=1, source_target_pairs={{0,56},{8,0},{16,8},{24,16},{32,24},{40,32},{48,40},{56,48},{1,57}... | collective-permute-start | bytes 393224 | tf_op jit(solution)/shard_map/ppermute | solution.py:18
  136.5 2.5 %collective-permute-start.9 = (bf16[16,4096]{1,0:T(8,128)(2,1)S(1)}, bf16[16,4096]{1,0:T(8,128)(2,1)S(1)}, u32[]{:S(2)}, u32[]{:S(2)}) collective-permute-start(bf16[16,4096]{1,0:T(8,128)(2,1)S(1)} %get-tuple-element.29), channel_id=1, source_target_pairs={{0,8},{8,16},{16,24},{24,32},{32,40},{40,48},{48,56},{56,0},{1,9},... | collective-permute-start | bytes 393224 | tf_op jit(solution)/shard_map/ppermute | solution.py:18
  138.9 1.6 fusion.17
  140.5 1.2 copy.67
  141.7 2.5 %reshape.93 = bf16[32,128,2,128]{3,2,1,0:T(2,128)(2,1)S(1)} reshape(bf16[4096,256]{1,0:T(8,128)(2,1)} %convolution_convert_fusion.2) | data formatting | bytes 4194304 | tf_op jit(solution)/shard_map/reshape | solution.py:97
  146.2 7.4 %all-to-all-start.1 = ((bf16[4,4,4096]{2,1,0:T(4,128)(2,1)}), bf16[4,4,4096]{2,1,0:T(4,128)(2,1)S(1)}, u32[]{:S(2)}, u32[]{:S(2)}) async-start(bf16[4,4,4096]{2,1,0:T(4,128)(2,1)} %reshape.92), calls=%async_computation.1 | async-start | bytes 262144 | tf_op jit(solution)/shard_map/all_to_all | solution.py:59
  153.6 1.5 fusion.14
  156.4 5.6 %all-to-all-done.1 = bf16[4,4,4096]{2,1,0:T(4,128)(2,1)S(1)} async-done(((bf16[4,4,4096]{2,1,0:T(4,128)(2,1)}), bf16[4,4,4096]{2,1,0:T(4,128)(2,1)S(1)}, u32[]{:S(2)}, u32[]{:S(2)}) %all-to-all-start.1) | async-done | bytes 131104 | tf_op jit(solution)/shard_map/all_to_all | solution.py:59
  (57 shorter events, 20.3 us)
Async XLA Ops:
  7.2 29.3 %copy-start.8 = (bf16[1,26,128,128]{3,2,1,0:T(8,128)(2,1)S(1)}, bf16[1,26,128,128]{3,2,1,0:T(8,128)(2,1)}, u32[]{:S(2)}) copy-start(bf16[1,26,128,128]{3,2,1,0:T(8,128)(2,1)} %param.10) | copy-start | bytes 2555908
  7.2 69.9 %all-gather.2.cloned.1.call-start = ((), (), s32[]{:S(2)}) async-start(), calls=%async_computation.2 | async-start | bytes 2359296 | tf_op jit(solution)/shard_map/all_gather | solution.py:26
  7.2 6.6 %collective-permute-start = (bf16[1,4,4096]{2,1,0:T(4,128)(2,1)}, bf16[1,4,4096]{2,1,0:T(4,128)(2,1)S(1)}, u32[]{:S(2)}, u32[]{:S(2)}) collective-permute-start(bf16[1,4,4096]{2,1,0:T(4,128)(2,1)} %param.7), channel_id=1, source_target_pairs={{64,0},{128,64},{192,128},{256,192},{320,256},{384,320},{448,384},... | collective-permute-start | bytes 98312 | tf_op jit(solution)/shard_map/ppermute | solution.py:13
  37.3 3.8 %copy-start.9 = (bf16[1,26,128,128]{3,2,1,0:T(8,128)(2,1)S(1)}, bf16[1,26,128,128]{3,2,1,0:T(8,128)(2,1)}, u32[]{:S(2)}) copy-start(bf16[1,26,128,128]{3,2,1,0:T(8,128)(2,1)} %param.9) | copy-start | bytes 2555908
  45.9 2.7 %copy-start.10 = (bf16[1,26,128,128]{3,2,1,0:T(8,128)(2,1)S(1)}, bf16[1,26,128,128]{3,2,1,0:T(8,128)(2,1)}, u32[]{:S(2)}) copy-start(bf16[1,26,128,128]{3,2,1,0:T(8,128)(2,1)} %param.11) | copy-start | bytes 2555908
  48.6 1.6 copy-start.2
  80.0 6.1 %collective-permute-start.1 = (bf16[2,128,4096]{2,1,0:T(8,128)(2,1)S(1)}, bf16[2,128,4096]{2,1,0:T(8,128)(2,1)S(1)}, u32[]{:S(2)}, u32[]{:S(2)}) collective-permute-start(bf16[2,128,4096]{2,1,0:T(8,128)(2,1)S(1)} %get-tuple-element.34), channel_id=1, source_target_pairs={{0,1},{1,0},{2,3},{3,2},{4,5},{5,4},{6,7},{7,6},{8,9},{9,8},{10,11... | collective-permute-start | bytes 6291464 | tf_op jit(solution)/shard_map/ppermute | solution.py:18
  86.0 1.6 copy-start.3
  87.6 2.0 %copy-start.5 = (bf16[2,256,4096]{2,1,0:T(8,128)(2,1)}, bf16[2,256,4096]{2,1,0:T(8,128)(2,1)S(1)}, u32[]{:S(2)}) copy-start(bf16[2,256,4096]{2,1,0:T(8,128)(2,1)S(1)} %constant_dynamic-update-slice_fusion) | copy-start | bytes 12582916
  88.4 2.3 %copy-start.7 = (bf16[256,4096]{1,0:T(8,128)(2,1)S(1)}, bf16[256,4096]{1,0:T(8,128)(2,1)}, u32[]{:S(2)}) copy-start(bf16[256,4096]{1,0:T(8,128)(2,1)} %get-tuple-element.9) | copy-start | bytes 6291460
  92.9 2.6 %copy-start = (f32[256,4096]{1,0:T(8,128)}, f32[256,4096]{1,0:T(8,128)S(1)}, u32[]{:S(2)}) copy-start(f32[256,4096]{1,0:T(8,128)S(1)} %convolution_add_fusion) | copy-start | bytes 12582916
  95.6 6.3 %collective-permute-start.2 = (f32[128,4096]{1,0:T(8,128)}, f32[128,4096]{1,0:T(8,128)S(1)}, u32[]{:S(2)}, u32[]{:S(2)}) collective-permute-start(f32[128,4096]{1,0:T(8,128)} %split.9), channel_id=1, source_target_pairs={{0,1},{1,0},{2,3},{3,2},{4,5},{5,4},{6,7},{7,6},{8,9},{9,8},{10,11... | collective-permute-start | bytes 6291464 | tf_op jit(solution)/shard_map/ppermute | solution.py:18
  97.8 4.1 %copy-start.1 = (f32[256,4096]{1,0:T(8,128)S(1)}, f32[256,4096]{1,0:T(8,128)}, u32[]{:S(2)}) copy-start(f32[256,4096]{1,0:T(8,128)} %copy-done) | copy-start | bytes 12582916
  101.7 4.8 %copy-start.6 = (bf16[2,256,4096]{2,1,0:T(8,128)(2,1)S(1)}, bf16[2,256,4096]{2,1,0:T(8,128)(2,1)}, u32[]{:S(2)}) copy-start(bf16[2,256,4096]{2,1,0:T(8,128)(2,1)} %copy-done.5) | copy-start | bytes 12582916
  102.1 16.2 %copy-start.4 = (f32[128,4096]{1,0:T(8,128)}, f32[128,4096]{1,0:T(8,128)S(1)}, u32[]{:S(2)}) copy-start(f32[128,4096]{1,0:T(8,128)S(1)} %slice_add_fusion) | copy-start | bytes 6291460
  102.2 8.4 %collective-permute-start.3 = (bf16[16,4096]{1,0:T(8,128)(2,1)S(1)}, bf16[16,4096]{1,0:T(8,128)(2,1)S(1)}, u32[]{:S(2)}, u32[]{:S(2)}) collective-permute-start(bf16[16,4096]{1,0:T(8,128)(2,1)S(1)} %get-tuple-element.32), channel_id=1, source_target_pairs={{0,56},{8,0},{16,8},{24,16},{32,24},{40,32},{48,40},{56,48},{1,57}... | collective-permute-start | bytes 393224 | tf_op jit(solution)/shard_map/ppermute | solution.py:18
  108.6 8.4 %collective-permute-start.7 = (bf16[16,4096]{1,0:T(8,128)(2,1)S(1)}, bf16[16,4096]{1,0:T(8,128)(2,1)S(1)}, u32[]{:S(2)}, u32[]{:S(2)}) collective-permute-start(bf16[16,4096]{1,0:T(8,128)(2,1)S(1)} %get-tuple-element.33), channel_id=1, source_target_pairs={{0,8},{8,16},{16,24},{24,32},{32,40},{40,48},{48,56},{56,0},{1,9},... | collective-permute-start | bytes 393224 | tf_op jit(solution)/shard_map/ppermute | solution.py:18
  110.6 7.7 %collective-permute-start.4 = (bf16[16,4096]{1,0:T(8,128)(2,1)S(1)}, bf16[16,4096]{1,0:T(8,128)(2,1)S(1)}, u32[]{:S(2)}, u32[]{:S(2)}) collective-permute-start(bf16[16,4096]{1,0:T(8,128)(2,1)S(1)} %fusion.37), channel_id=1, source_target_pairs={{0,56},{8,0},{16,8},{24,16},{32,24},{40,32},{48,40},{56,48},{1,57}... | collective-permute-start | bytes 393224 | tf_op jit(solution)/shard_map/ppermute | solution.py:18
  118.3 11.9 %collective-permute-start.5 = (bf16[16,4096]{1,0:T(8,128)(2,1)S(1)}, bf16[16,4096]{1,0:T(8,128)(2,1)S(1)}, u32[]{:S(2)}, u32[]{:S(2)}) collective-permute-start(bf16[16,4096]{1,0:T(8,128)(2,1)S(1)} %get-tuple-element.30), channel_id=1, source_target_pairs={{0,56},{8,0},{16,8},{24,16},{32,24},{40,32},{48,40},{56,48},{1,57}... | collective-permute-start | bytes 393224 | tf_op jit(solution)/shard_map/ppermute | solution.py:18
  123.9 8.1 %collective-permute-start.8 = (bf16[16,4096]{1,0:T(8,128)(2,1)S(1)}, bf16[16,4096]{1,0:T(8,128)(2,1)S(1)}, u32[]{:S(2)}, u32[]{:S(2)}) collective-permute-start(bf16[16,4096]{1,0:T(8,128)(2,1)S(1)} %get-tuple-element.31), channel_id=1, source_target_pairs={{0,8},{8,16},{16,24},{24,32},{32,40},{40,48},{48,56},{56,0},{1,9},... | collective-permute-start | bytes 393224 | tf_op jit(solution)/shard_map/ppermute | solution.py:18
  133.1 11.2 %collective-permute-start.6 = (bf16[16,4096]{1,0:T(8,128)(2,1)S(1)}, bf16[16,4096]{1,0:T(8,128)(2,1)S(1)}, u32[]{:S(2)}, u32[]{:S(2)}) collective-permute-start(bf16[16,4096]{1,0:T(8,128)(2,1)S(1)} %get-tuple-element.28), channel_id=1, source_target_pairs={{0,56},{8,0},{16,8},{24,16},{32,24},{40,32},{48,40},{56,48},{1,57}... | collective-permute-start | bytes 393224 | tf_op jit(solution)/shard_map/ppermute | solution.py:18
  136.5 8.1 %collective-permute-start.9 = (bf16[16,4096]{1,0:T(8,128)(2,1)S(1)}, bf16[16,4096]{1,0:T(8,128)(2,1)S(1)}, u32[]{:S(2)}, u32[]{:S(2)}) collective-permute-start(bf16[16,4096]{1,0:T(8,128)(2,1)S(1)} %get-tuple-element.29), channel_id=1, source_target_pairs={{0,8},{8,16},{16,24},{24,32},{32,40},{40,48},{48,56},{56,0},{1,9},... | collective-permute-start | bytes 393224 | tf_op jit(solution)/shard_map/ppermute | solution.py:18
  146.2 15.8 %all-to-all-start.1 = ((bf16[4,4,4096]{2,1,0:T(4,128)(2,1)}), bf16[4,4,4096]{2,1,0:T(4,128)(2,1)S(1)}, u32[]{:S(2)}, u32[]{:S(2)}) async-start(bf16[4,4,4096]{2,1,0:T(4,128)(2,1)} %reshape.92), calls=%async_computation.1 | async-start | bytes 262144 | tf_op jit(solution)/shard_map/all_to_all | solution.py:59
Sparse Core Ops, SparseCore 0:
  35.8 41.1 all-gather.1

commit v11 on v9

--- a/solution.py
+++ b/solution.py
@@ -25,11 +25,10 @@
     block = jnp.swapaxes(block, 0, 1).reshape(block.shape[1], -1, block.shape[3])
     block = lax.all_gather(block, "y", axis=1, tiled=True)
     block, weights = lax.optimization_barrier((block, weights))
-    return jnp.concatenate([block, shifted(block, "core", 1)], axis=1), weights
+    return (block, shifted(block, "core", 1)), weights
 
 
-def scatter_rows(block):
-    own, other = jnp.split(block, 2, axis=0)
+def scatter_rows(own, other):
     block = (own + shifted(other, "core", 1)).astype(jnp.bfloat16)
     block = lax.psum_scatter(block, "y", scatter_dimension=0, tiled=True)
     n = lax.axis_size("zh")
@@ -92,30 +91,36 @@
     w_down = dense_down(down_blocks[0])
 
     incoming = passed_along(grad_sent, "section", -1)
-    both, (w_gate, w_up, w_down) = gather_rows(
+    halves, (w_gate, w_up, w_down) = gather_rows(
         jnp.concatenate([saved_input, incoming], axis=0), (w_gate, w_up, w_down)
     )
-    inputs = both[0]
-    upstream = both[1]
     f32 = jnp.float32
-    gate = jnp.dot(inputs, w_gate, preferred_element_type=f32)
-    up = jnp.dot(inputs, w_up, preferred_element_type=f32)
-    sig = jax.nn.sigmoid(gate)
-    act = gate * sig
-    hidden = (act * up).astype(jnp.bfloat16)
-    dhid = lax.dot_general(upstream, w_down, (((1,), (1,)), ((), ())), preferred_element_type=f32)
-    grad_up_act = (dhid * act).astype(jnp.bfloat16)
-    grad_gate_act = (dhid * up * sig * (1.0 + gate * (1.0 - sig))).astype(jnp.bfloat16)
+    hid_t = (((1,), (1,)), ((), ()))
+
+    def rows_part(both):
+        inputs, upstream = both[0], both[1]
+        gate = jnp.dot(inputs, w_gate, preferred_element_type=f32)
+        up = jnp.dot(inputs, w_up, preferred_element_type=f32)
+        sig = jax.nn.sigmoid(gate)
+        act = gate * sig
+        hidden = (act * up).astype(jnp.bfloat16)
+        dhid = lax.dot_general(upstream, w_down, hid_t, preferred_element_type=f32)
+        grad_up_act = (dhid * act).astype(jnp.bfloat16)
+        grad_gate_act = (dhid * up * sig * (1.0 + gate * (1.0 - sig))).astype(jnp.bfloat16)
+        term = lax.dot_general(grad_gate_act, w_gate, hid_t, preferred_element_type=f32)
+        term = term + lax.dot_general(grad_up_act, w_up, hid_t, preferred_element_type=f32)
+        return term, (inputs, upstream, hidden, grad_gate_act, grad_up_act)
+
+    term_own, saved_own = rows_part(halves[0])
+    term_other, saved_other = rows_part(halves[1])
+    inputs, upstream, hidden, grad_gate_act, grad_up_act = (
+        jnp.concatenate(pair, axis=0) for pair in zip(saved_own, saved_other)
+    )
     rows_t = (((0,), (0,)), ((), ()))
     tiles_gate = kept_in(lax.dot_general(inputs, grad_gate_act, rows_t, preferred_element_type=f32))
     tiles_up = kept_in(lax.dot_general(inputs, grad_up_act, rows_t, preferred_element_type=f32))
     tiles_down = kept_down(lax.dot_general(hidden, upstream, rows_t, preferred_element_type=f32))
-    hid_t = (((1,), (1,)), ((), ()))
-    whole_term = lax.dot_general(grad_gate_act, w_gate, hid_t, preferred_element_type=f32)
-    whole_term = whole_term + lax.dot_general(
-        grad_up_act, w_up, hid_t, preferred_element_type=f32
-    )
-    summed = scatter_rows(whole_term)
+    summed = scatter_rows(term_own, term_other)
     grad_input = summed.astype(jnp.bfloat16)[None]
     return (grad_input, tiles_gate[None], tiles_up[None], tiles_down[None])
 

time: 167 us -> 164 us (0.982)
  local copies, waits for them, and re-layouts: 36.9 us -> 34.2 us
    dot_general x5 -> x10, matrix products: 3.72 us -> 7.93 us  [the longest x2 2.01 us: rows_part(): lax.dot_general(grad_up_act, w_up, hid_t, preferred_element_type=f32)]
    ppermute x2, waiting for transfers between devices: 7.95 us -> 4.95 us  [shifted(): return lax.ppermute(block, axis, [(i, (i + shift) % n) for i in range(n)])]
    all_gather x1, waiting for transfers between devices: 17.9 us -> 20.7 us  [gather_rows(): block = lax.all_gather(block, 'y', axis=1, tiled=True)]
    unnamed x23 -> x33, local copies, waits for them, and re-layouts: 11.4 us -> 10.1 us
where the time goes in v11:
time: 164 us
  waiting for transfers between devices  56.4 us (34%)
  local copies, waits for them, and re-layouts  34.2 us (21%)
  blocking collectives  20.8 us (13%)
  matrix products  19.2 us (12%)
  starting transfers between devices  16.4 us (10%)
  between operations  14.4 us (9%)
  other arithmetic  2.23 us (1%)
    reduce_scatter x1, waiting for transfers between devices, scatter_rows(): block = lax.psum_scatter(block, 'y', scatter_dimension=0, tiled=True)  22.9 us
    all_to_all x1, blocking collectives, gather_rows(): block = lax.all_to_all(copies, 'zh', 0, 0, tiled=True)  20.8 us
    all_gather x1, waiting for transfers between devices, gather_rows(): block = lax.all_gather(block, 'y', axis=1, tiled=True)  20.7 us
    unnamed x33, local copies, waits for them, and re-layouts  10.1 us
    convert_element_type x2, local copies, waits for them, and re-layouts, dense_in(): return placed.astype(jnp.bfloat16).reshape(width, hidden_units)  7.64 us
    all_to_all x1, starting transfers between devices, scatter_rows(): got = lax.all_to_all(chunks, 'zh', 0, 0, tiled=True)  7.45 us
    reshape x1, local copies, waits for them, and re-layouts, dense_down(): return placed.astype(jnp.bfloat16).reshape(hidden_units, width)  6.1 us
    all_to_all x1, waiting for transfers between devices, scatter_rows(): got = lax.all_to_all(chunks, 'zh', 0, 0, tiled=True)  5.94 us
  transfers between devices with their start and end apart: 6, of which 6 were waited for; matrix products, arithmetic and copies ran while one was open for 25% of the time, Pallas kernels for 0%

profile of v11, /device:TPU:6, one launch (start us, length us, event | category | flops | bytes accessed | tf_op | source)
XLA Modules:
  0.0 163.6 jit_solution(15499571767778006587)
XLA Ops:
  7.2 4.7 %collective-permute-start = (bf16[1,4,4096]{2,1,0:T(4,128)(2,1)}, bf16[1,4,4096]{2,1,0:T(4,128)(2,1)S(1)}, u32[]{:S(2)}, u32[]{:S(2)}) collective-permute-start(bf16[1,4,4096]{2,1,0:T(4,128)(2,1)} %param.7), channel_id=1, source_target_pairs={{64,0},{128,64},{192,128},{256,192},{320,256},{384,320},{448,384},... | collective-permute-start | bytes 98312 | tf_op jit(solution)/shard_map/ppermute | solution.py:13
  11.9 1.9 %collective-permute-done = bf16[1,4,4096]{2,1,0:T(4,128)(2,1)S(1)} collective-permute-done((bf16[1,4,4096]{2,1,0:T(4,128)(2,1)}, bf16[1,4,4096]{2,1,0:T(4,128)(2,1)S(1)}, u32[]{:S(2)}, u32[]{:S(2)}) %collective-permute-start) | collective-permute-done | bytes 32800 | tf_op jit(solution)/shard_map/ppermute | solution.py:13
  14.9 20.8 %all_to_all.10 = bf16[4,2,4,4096]{3,1,2,0:T(2,128)(2,1)} all-to-all(bf16[4,2,4,4096]{3,1,2,0:T(2,128)(2,1)S(1)} %broadcast_in_dim.10), channel_id=1, replica_groups=mesh['section'=8,'y'=8,'zh'=4,'core'=2] {'zh'}, dimensions={0} | all-to-all | bytes 524288 | tf_op jit(solution)/shard_map/all_to_all | solution.py:24
  36.5 0.9 convert_bitcast_fusion
  37.4 3.8 %copy.75 = bf16[32,128,2,128]{1,0,3,2:T(8,128)(2,1)} copy(bf16[32,128,2,128]{3,0,1,2:T(8,128)(2,1)S(1)} %convert_bitcast_fusion) | data formatting | bytes 4194304 | tf_op jit(solution)/shard_map/convert_element_type | solution.py:64
  41.3 0.9 convert_bitcast_fusion.1
  42.2 3.8 %copy.72 = bf16[32,128,2,128]{1,0,3,2:T(8,128)(2,1)} copy(bf16[32,128,2,128]{3,0,1,2:T(8,128)(2,1)S(1)} %convert_bitcast_fusion.1) | data formatting | bytes 4194304 | tf_op jit(solution)/shard_map/convert_element_type | solution.py:64
  46.0 2.7 %copy.130 = bf16[32,8,32,128]{3,1,2,0:T(8,128)(2,1)S(1)} copy(bf16[32,8,32,128]{3,2,1,0:T(8,128)(2,1)} %bitcast.145) | data formatting | bytes 4194304
  48.7 0.9 convolution_convert_fusion.3
  50.2 6.1 %copy_bitcast_fusion = (bf16[256,4096]{1,0:T(8,128)(2,1)}, bf16[4096,256]{0,1:T(8,128)(2,1)}) fusion(bf16[32,8,32,128]{3,2,1,0:T(8,128)(2,1)S(1)} %bitcast.148, bf16[32,8,32,128]{3,2,1,0:T(8,128)(2,1)S(1)} %bitcast.147), kind=kLoop, calls=%fused_computation.9 | loop fusion | bytes 8388608 | tf_op jit(solution)/shard_map/reshape | solution.py:71
  56.3 20.7 %all-gather.2.cloned.1.call-done = bf16[2,128,4096]{2,0,1:T(2,128)(2,1)} async-done(((bf16[2,16,4096]{2,0,1:T(2,128)(2,1)}), bf16[2,128,4096]{2,0,1:T(2,128)(2,1)}) %all-gather.2.cloned.1.call-update) | async-done | bytes 2097168 | tf_op jit(solution)/shard_map/all_gather | solution.py:26
  77.0 3.1 %copy.78 = bf16[2,128,4096]{2,1,0:T(8,128)(2,1)S(1)} copy(bf16[2,128,4096]{2,0,1:T(2,128)(2,1)} %all-gather.2.cloned.1.call-done) | data formatting | bytes 4194304 | tf_op jit(solution)/shard_map/optimization_barrier | solution.py:27
  80.1 2.1 %collective-permute-start.1 = (bf16[2,128,4096]{2,1,0:T(8,128)(2,1)S(1)}, bf16[2,128,4096]{2,1,0:T(8,128)(2,1)S(1)}, u32[]{:S(2)}, u32[]{:S(2)}) collective-permute-start(bf16[2,128,4096]{2,1,0:T(8,128)(2,1)S(1)} %copy.78), channel_id=1, source_target_pairs={{0,1},{1,0},{2,3},{3,2},{4,5},{5,4},{6,7},{7,6},{8,9},{9,8},{10,11... | collective-permute-start | bytes 6291464 | tf_op jit(solution)/shard_map/ppermute | solution.py:18
  82.2 3.9 %collective-permute-done.1 = bf16[2,128,4096]{2,1,0:T(8,128)(2,1)S(1)} collective-permute-done((bf16[2,128,4096]{2,1,0:T(8,128)(2,1)S(1)}, bf16[2,128,4096]{2,1,0:T(8,128)(2,1)S(1)}, u32[]{:S(2)}, u32[]{:S(2)}) %collective-permute-start.1) | collective-permute-done | bytes 2097184 | tf_op jit(solution)/shard_map/ppermute | solution.py:18
  90.4 2.0 %collective-permute-start.2 = (f32[128,4096]{1,0:T(8,128)S(1)}, f32[128,4096]{1,0:T(8,128)S(1)}, u32[]{:S(2)}, u32[]{:S(2)}) collective-permute-start(f32[128,4096]{1,0:T(8,128)S(1)} %convolution_add_fusion), channel_id=1, source_target_pairs={{0,1},{1,0},{2,3},{3,2},{4,5},{5,4},{6,7},{7,6},{8,9},{9,8},{10,11... | collective-permute-start | bytes 6291464 | tf_op jit(solution)/shard_map/ppermute | solution.py:18
  94.1 0.8 multiply_convert_fusion.1
  95.4 1.0 collective-permute-done.2
  96.5 1.5 fusion.1
  98.4 1.4 copy-done.5
  102.0 1.2 copy.86
  103.3 2.1 %convolution_convert_fusion.1 = bf16[4096,256]{1,0:T(8,128)(2,1)} fusion(bf16[128,4096]{1,0:T(8,128)(2,1)S(1)} %get-tuple-element.35, bf16[128,4096]{1,0:T(8,128)(2,1)S(1)} %get-tuple-element.33, bf16[128,256]{1,0:T(8,128)(2,1)S(1)} %get-tuple-element.41, bf16[128,256]{1,0:T(8,128)(2,1)S(1)} %get-tuple-element.38), kind=kOutput, calls=%fused_computation.1 | convolution fusion | flops 542375936 | bytes 4325376 | tf_op jit(solution)/shard_map/dot_general | solution.py:121
  105.4 2.5 %reshape.88 = bf16[32,128,2,128]{3,2,1,0:T(2,128)(2,1)S(1)} reshape(bf16[4096,256]{1,0:T(8,128)(2,1)} %convolution_convert_fusion.1) | data formatting | bytes 4194304 | tf_op jit(solution)/shard_map/reshape | solution.py:74
  107.9 1.5 fusion.23
  109.5 1.2 copy.85
  110.7 2.1 %convolution_convert_fusion.2 = bf16[4096,256]{1,0:T(8,128)(2,1)} fusion(bf16[128,4096]{1,0:T(8,128)(2,1)S(1)} %copy-done.11, bf16[128,4096]{1,0:T(8,128)(2,1)S(1)} %get-tuple-element.33, bf16[128,256]{1,0:T(8,128)(2,1)S(1)} %get-tuple-element.40, bf16[128,256]{1,0:T(8,128)(2,1)S(1)} %get-tuple-element.37), kind=kOutput, calls=%fused_computation.2 | convolution fusion | flops 542375936 | bytes 4325376 | tf_op jit(solution)/shard_map/dot_general | solution.py:120
  112.8 2.5 %reshape.87 = bf16[32,128,2,128]{3,2,1,0:T(2,128)(2,1)S(1)} reshape(bf16[4096,256]{1,0:T(8,128)(2,1)} %convolution_convert_fusion.2) | data formatting | bytes 4194304 | tf_op jit(solution)/shard_map/reshape | solution.py:74
  115.4 22.9 %reduce-scatter.2.cloned.1.call-done = bf16[16,4096]{1,0:T(8,128)(2,1)} async-done(((bf16[128,4096]{1,0:T(8,128)(2,1)}), bf16[16,4096]{1,0:T(8,128)(2,1)}) %reduce-scatter.2.cloned.1.call-update) | async-done | bytes 131088 | tf_op jit(solution)/shard_map/reduce_scatter | solution.py:33
  138.3 1.6 reshape.86
  139.9 7.5 %all-to-all-start.1 = ((bf16[4,4,4096]{2,1,0:T(4,128)(2,1)}), bf16[4,4,4096]{2,1,0:T(4,128)(2,1)S(1)}, u32[]{:S(2)}, u32[]{:S(2)}) async-start(bf16[4,4,4096]{2,1,0:T(4,128)(2,1)} %reshape.86), calls=%async_computation.2 | async-start | bytes 262144 | tf_op jit(solution)/shard_map/all_to_all | solution.py:36
  147.3 1.5 fusion.20
  148.9 1.2 copy.84
  150.1 5.9 %all-to-all-done.1 = bf16[4,4,4096]{2,1,0:T(4,128)(2,1)S(1)} async-done(((bf16[4,4,4096]{2,1,0:T(4,128)(2,1)}), bf16[4,4,4096]{2,1,0:T(4,128)(2,1)S(1)}, u32[]{:S(2)}, u32[]{:S(2)}) %all-to-all-start.1) | async-done | bytes 131104 | tf_op jit(solution)/shard_map/all_to_all | solution.py:36
  (51 shorter events, 12.2 us)
Async XLA Ops:
  7.2 29.3 %copy-start.7 = (bf16[1,26,128,128]{3,2,1,0:T(8,128)(2,1)S(1)}, bf16[1,26,128,128]{3,2,1,0:T(8,128)(2,1)}, u32[]{:S(2)}) copy-start(bf16[1,26,128,128]{3,2,1,0:T(8,128)(2,1)} %param.10) | copy-start | bytes 2555908
  7.2 69.9 %all-gather.2.cloned.1.call-start = ((), (), s32[]{:S(2)}) async-start(), calls=%async_computation.3 | async-start | bytes 2359296 | tf_op jit(solution)/shard_map/all_gather | solution.py:26
  7.2 6.6 %collective-permute-start = (bf16[1,4,4096]{2,1,0:T(4,128)(2,1)}, bf16[1,4,4096]{2,1,0:T(4,128)(2,1)S(1)}, u32[]{:S(2)}, u32[]{:S(2)}) collective-permute-start(bf16[1,4,4096]{2,1,0:T(4,128)(2,1)} %param.7), channel_id=1, source_target_pairs={{64,0},{128,64},{192,128},{256,192},{320,256},{384,320},{448,384},... | collective-permute-start | bytes 98312 | tf_op jit(solution)/shard_map/ppermute | solution.py:13
  35.7 102.6 %reduce-scatter.2.cloned.1.call-start = ((), (), s32[]{:S(2)}) async-start(), calls=%async_computation.4 | async-start | bytes 1179648 | tf_op jit(solution)/shard_map/reduce_scatter | solution.py:33
  36.4 12.2 %copy-start.12 = (f32[26,2]{0,1:T(2,128)}, f32[26,2]{0,1:T(2,128)S(1)}, u32[]{:S(2)}) copy-start(f32[26,2]{0,1:T(2,128)S(1)} %compare_convert_fusion) | copy-start | bytes 628
  37.4 3.8 %copy-start.8 = (bf16[1,26,128,128]{3,2,1,0:T(8,128)(2,1)S(1)}, bf16[1,26,128,128]{3,2,1,0:T(8,128)(2,1)}, u32[]{:S(2)}) copy-start(bf16[1,26,128,128]{3,2,1,0:T(8,128)(2,1)} %param.9) | copy-start | bytes 2555908
  46.0 2.7 %copy-start.9 = (bf16[1,26,128,128]{3,2,1,0:T(8,128)(2,1)S(1)}, bf16[1,26,128,128]{3,2,1,0:T(8,128)(2,1)}, u32[]{:S(2)}) copy-start(bf16[1,26,128,128]{3,2,1,0:T(8,128)(2,1)} %param.11) | copy-start | bytes 2555908
  48.6 1.6 copy-start.6
  77.0 9.1 %copy-start.3 = (bf16[256,4096]{1,0:T(8,128)(2,1)S(1)}, bf16[256,4096]{1,0:T(8,128)(2,1)}, u32[]{:S(2)}) copy-start(bf16[256,4096]{1,0:T(8,128)(2,1)} %get-tuple-element.9) | copy-start | bytes 6291460
  80.1 14.0 %copy-start = (bf16[2,128,4096]{2,1,0:T(8,128)(2,1)}, bf16[2,128,4096]{2,1,0:T(8,128)(2,1)S(1)}, u32[]{:S(2)}) copy-start(bf16[2,128,4096]{2,1,0:T(8,128)(2,1)S(1)} %copy.78) | copy-start | bytes 6291460
  80.1 6.1 %collective-permute-start.1 = (bf16[2,128,4096]{2,1,0:T(8,128)(2,1)S(1)}, bf16[2,128,4096]{2,1,0:T(8,128)(2,1)S(1)}, u32[]{:S(2)}, u32[]{:S(2)}) collective-permute-start(bf16[2,128,4096]{2,1,0:T(8,128)(2,1)S(1)} %copy.78), channel_id=1, source_target_pairs={{0,1},{1,0},{2,3},{3,2},{4,5},{5,4},{6,7},{7,6},{8,9},{9,8},{10,11... | collective-permute-start | bytes 6291464 | tf_op jit(solution)/shard_map/ppermute | solution.py:18
  86.2 1.7 %copy-start.4 = (bf16[2,128,4096]{2,1,0:T(8,128)(2,1)}, bf16[2,128,4096]{2,1,0:T(8,128)(2,1)S(1)}, u32[]{:S(2)}) copy-start(bf16[2,128,4096]{2,1,0:T(8,128)(2,1)S(1)} %collective-permute-done.1) | copy-start | bytes 6291460
  87.0 1.6 copy-start.2
  90.4 6.1 %collective-permute-start.2 = (f32[128,4096]{1,0:T(8,128)S(1)}, f32[128,4096]{1,0:T(8,128)S(1)}, u32[]{:S(2)}, u32[]{:S(2)}) collective-permute-start(f32[128,4096]{1,0:T(8,128)S(1)} %convolution_add_fusion), channel_id=1, source_target_pairs={{0,1},{1,0},{2,3},{3,2},{4,5},{5,4},{6,7},{7,6},{8,9},{9,8},{10,11... | collective-permute-start | bytes 6291464 | tf_op jit(solution)/shard_map/ppermute | solution.py:18
  96.5 1.8 %copy-start.1 = (bf16[2,128,4096]{2,1,0:T(8,128)(2,1)S(1)}, bf16[2,128,4096]{2,1,0:T(8,128)(2,1)}, u32[]{:S(2)}) copy-start(bf16[2,128,4096]{2,1,0:T(8,128)(2,1)} %copy-done) | copy-start | bytes 6291460
  98.2 1.6 copy-start.5
  100.0 3.2 %copy-start.10 = (bf16[128,4096]{1,0:T(8,128)(2,1)}, bf16[128,4096]{1,0:T(8,128)(2,1)S(1)}, u32[]{:S(2)}) copy-start(bf16[128,4096]{1,0:T(8,128)(2,1)S(1)} %get-tuple-element.35) | copy-start | bytes 3145732
  100.8 0.7 copy-start.13
  107.9 2.8 %copy-start.11 = (bf16[128,4096]{1,0:T(8,128)(2,1)S(1)}, bf16[128,4096]{1,0:T(8,128)(2,1)}, u32[]{:S(2)}) copy-start(bf16[128,4096]{1,0:T(8,128)(2,1)} %copy-done.10) | copy-start | bytes 3145732
  139.9 16.2 %all-to-all-start.1 = ((bf16[4,4,4096]{2,1,0:T(4,128)(2,1)}), bf16[4,4,4096]{2,1,0:T(4,128)(2,1)S(1)}, u32[]{:S(2)}, u32[]{:S(2)}) async-start(bf16[4,4,4096]{2,1,0:T(4,128)(2,1)} %reshape.86), calls=%async_computation.2 | async-start | bytes 262144 | tf_op jit(solution)/shard_map/all_to_all | solution.py:36
Sparse Core Ops, SparseCore 0:
  35.8 41.1 all-gather.1
  98.1 40.1 reduce-scatter.1

commit v12 on v11

--- a/solution.py
+++ b/solution.py
@@ -20,10 +20,9 @@
 
 def gather_rows(block, weights):
     n = lax.axis_size("zh")
-    copies = jnp.broadcast_to(block[None], (n,) + block.shape)
+    copies = jnp.tile(block, (n, 1))
     block = lax.all_to_all(copies, "zh", 0, 0, tiled=True)
-    block = jnp.swapaxes(block, 0, 1).reshape(block.shape[1], -1, block.shape[3])
-    block = lax.all_gather(block, "y", axis=1, tiled=True)
+    block = lax.all_gather(block, "y", axis=0, tiled=True)
     block, weights = lax.optimization_barrier((block, weights))
     return (block, shifted(block, "core", 1)), weights
 
@@ -32,9 +31,12 @@
     block = (own + shifted(other, "core", 1)).astype(jnp.bfloat16)
     block = lax.psum_scatter(block, "y", scatter_dimension=0, tiled=True)
     n = lax.axis_size("zh")
-    chunks = block.reshape(n, -1, block.shape[1])
-    got = lax.all_to_all(chunks, "zh", 0, 0, tiled=True)
-    return jnp.sum(got.astype(jnp.float32), axis=0)
+    got = lax.all_to_all(block, "zh", 0, 0, tiled=True).astype(jnp.float32)
+    own_rows = got.shape[0] // n
+    total = got[:own_rows]
+    for k in range(1, n):
+        total = total + got[k * own_rows:(k + 1) * own_rows]
+    return total
 
 
 def per_device(saved_input, grad_sent, kept_blocks, gate_blocks, up_blocks, down_blocks):
@@ -92,13 +94,13 @@
 
     incoming = passed_along(grad_sent, "section", -1)
     halves, (w_gate, w_up, w_down) = gather_rows(
-        jnp.concatenate([saved_input, incoming], axis=0), (w_gate, w_up, w_down)
+        jnp.concatenate([saved_input[0], incoming[0]], axis=1), (w_gate, w_up, w_down)
     )
     f32 = jnp.float32
     hid_t = (((1,), (1,)), ((), ()))
 
     def rows_part(both):
-        inputs, upstream = both[0], both[1]
+        inputs, upstream = both[:, :width], both[:, width:]
         gate = jnp.dot(inputs, w_gate, preferred_element_type=f32)
         up = jnp.dot(inputs, w_up, preferred_element_type=f32)
         sig = jax.nn.sigmoid(gate)

time: 164 us -> 164 us (level)
  local copies, waits for them, and re-layouts: 34.2 us -> 31.7 us
  matrix products: 19.2 us -> 21.6 us
    optimization_barrier x1 -> x0, local copies, waits for them, and re-layouts: 3.07 us -> none  [gather_rows(): block, weights = lax.optimization_barrier((block, weights))]
    all_to_all x0 -> x2, local copies, waits for them, and re-layouts: none -> 2.39 us  [the longest x1 1.63 us: scatter_rows(): got = lax.all_to_all(block, 'zh', 0, 0, tiled=True).astype(jnp.float32)]
    dot_general x2, matrix products: 1.67 us -> 4.02 us  [rows_part(): dhid = lax.dot_general(upstream, w_down, hid_t, preferred_element_type=f32)]
where the time goes in v12:
time: 164 us
  waiting for transfers between devices  56.6 us (35%)
  local copies, waits for them, and re-layouts  31.7 us (19%)
  matrix products  21.6 us (13%)
  blocking collectives  20.7 us (13%)
  starting transfers between devices  16.5 us (10%)
  between operations  14.4 us (9%)
  other arithmetic  2.2 us (1%)
    reduce_scatter x1, waiting for transfers between devices, scatter_rows(): block = lax.psum_scatter(block, 'y', scatter_dimension=0, tiled=True)  22.9 us
    all_gather x1, waiting for transfers between devices, gather_rows(): block = lax.all_gather(block, 'y', axis=0, tiled=True)  20.7 us
    all_to_all x1, blocking collectives, gather_rows(): block = lax.all_to_all(copies, 'zh', 0, 0, tiled=True)  20.7 us
    unnamed x33, local copies, waits for them, and re-layouts  10.1 us
    convert_element_type x2, local copies, waits for them, and re-layouts, dense_in(): return placed.astype(jnp.bfloat16).reshape(width, hidden_units)  7.63 us
    all_to_all x1, starting transfers between devices, scatter_rows(): got = lax.all_to_all(block, 'zh', 0, 0, tiled=True).astype(jnp.float32)  7.44 us
    reshape x1, local copies, waits for them, and re-layouts, dense_down(): return placed.astype(jnp.bfloat16).reshape(hidden_units, width)  6.13 us
    all_to_all x1, waiting for transfers between devices, scatter_rows(): got = lax.all_to_all(block, 'zh', 0, 0, tiled=True).astype(jnp.float32)  5.94 us
  transfers between devices with their start and end apart: 6, of which 6 were waited for; matrix products, arithmetic and copies ran while one was open for 25% of the time, Pallas kernels for 0%

profile of v12, /device:TPU:6, one launch (start us, length us, event | category | flops | bytes accessed | tf_op | source)
XLA Modules:
  0.0 163.6 jit_solution(5974617943436028766)
XLA Ops:
  7.2 4.7 %collective-permute-start = (bf16[1,4,4096]{2,1,0:T(4,128)(2,1)}, bf16[1,4,4096]{2,1,0:T(4,128)(2,1)S(1)}, u32[]{:S(2)}, u32[]{:S(2)}) collective-permute-start(bf16[1,4,4096]{2,1,0:T(4,128)(2,1)} %param.7), channel_id=1, source_target_pairs={{64,0},{128,64},{192,128},{256,192},{320,256},{384,320},{448,384},... | collective-permute-start | bytes 98312 | tf_op jit(solution)/shard_map/ppermute | solution.py:13
  11.9 1.9 %collective-permute-done = bf16[1,4,4096]{2,1,0:T(4,128)(2,1)S(1)} collective-permute-done((bf16[1,4,4096]{2,1,0:T(4,128)(2,1)}, bf16[1,4,4096]{2,1,0:T(4,128)(2,1)S(1)}, u32[]{:S(2)}, u32[]{:S(2)}) %collective-permute-start) | collective-permute-done | bytes 32800 | tf_op jit(solution)/shard_map/ppermute | solution.py:13
  14.7 20.7 %all_to_all.18 = bf16[4,4,8192]{2,1,0:T(4,128)(2,1)S(1)} all-to-all(bf16[4,4,8192]{2,1,0:T(4,128)(2,1)S(1)} %tile.2), channel_id=1, replica_groups=mesh['section'=8,'y'=8,'zh'=4,'core'=2] {'zh'}, dimensions={0} | all-to-all | bytes 524288 | tf_op jit(solution)/shard_map/all_to_all | solution.py:24
  36.9 0.9 convert_bitcast_fusion
  37.9 3.8 %copy.27 = bf16[32,128,2,128]{1,0,3,2:T(8,128)(2,1)} copy(bf16[32,128,2,128]{3,0,1,2:T(8,128)(2,1)S(1)} %convert_bitcast_fusion) | data formatting | bytes 4194304 | tf_op jit(solution)/shard_map/convert_element_type | solution.py:66
  41.7 0.9 convert_bitcast_fusion.1
  42.6 3.8 %copy.24 = bf16[32,128,2,128]{1,0,3,2:T(8,128)(2,1)} copy(bf16[32,128,2,128]{3,0,1,2:T(8,128)(2,1)S(1)} %convert_bitcast_fusion.1) | data formatting | bytes 4194304 | tf_op jit(solution)/shard_map/convert_element_type | solution.py:66
  46.4 2.7 %copy.79 = bf16[32,8,32,128]{3,1,2,0:T(8,128)(2,1)S(1)} copy(bf16[32,8,32,128]{3,2,1,0:T(8,128)(2,1)} %bitcast.125) | data formatting | bytes 4194304
  49.1 0.9 convolution_convert_fusion.3
  50.7 6.1 %copy_bitcast_fusion = (bf16[256,4096]{1,0:T(8,128)(2,1)}, bf16[4096,256]{0,1:T(8,128)(2,1)}) fusion(bf16[32,8,32,128]{3,2,1,0:T(8,128)(2,1)S(1)} %bitcast.128, bf16[32,8,32,128]{3,2,1,0:T(8,128)(2,1)S(1)} %bitcast.127), kind=kLoop, calls=%fused_computation.9 | loop fusion | bytes 8388608 | tf_op jit(solution)/shard_map/reshape | solution.py:73
  56.8 20.7 %all-gather.2.cloned.1.call-done = bf16[128,8192]{1,0:T(8,128)(2,1)} async-done(((bf16[16,8192]{1,0:T(8,128)(2,1)}), bf16[128,8192]{1,0:T(8,128)(2,1)}) %all-gather.2.cloned.1.call-update) | async-done | bytes 2097168 | tf_op jit(solution)/shard_map/all_gather | solution.py:25
  77.5 2.1 %collective-permute-start.1 = (bf16[128,8192]{1,0:T(8,128)(2,1)}, bf16[128,8192]{1,0:T(8,128)(2,1)S(1)}, u32[]{:S(2)}, u32[]{:S(2)}) collective-permute-start(bf16[128,8192]{1,0:T(8,128)(2,1)} %all-gather.2.cloned.1.call-done), channel_id=1, source_target_pairs={{0,1},{1,0},{2,3},{3,2},{4,5},{5,4},{6,7},{7,6},{8,9},{9,8},{10,11... | collective-permute-start | bytes 6291464 | tf_op jit(solution)/shard_map/ppermute | solution.py:18
  79.6 4.2 %collective-permute-done.1 = bf16[128,8192]{1,0:T(8,128)(2,1)S(1)} collective-permute-done((bf16[128,8192]{1,0:T(8,128)(2,1)}, bf16[128,8192]{1,0:T(8,128)(2,1)S(1)}, u32[]{:S(2)}, u32[]{:S(2)}) %collective-permute-start.1) | collective-permute-done | bytes 2097184 | tf_op jit(solution)/shard_map/ppermute | solution.py:18
  83.7 3.2 %fusion.67 = f32[128,256]{1,0:T(8,128)S(1)} fusion(bf16[256,4096]{1,0:T(8,128)(2,1)} %get-tuple-element.9, bf16[128,8192]{1,0:T(8,128)(2,1)S(1)} %collective-permute-done.1), kind=kOutput, calls=%fused_computation.90 | convolution fusion | flops 268435456 | bytes 3276800 | tf_op jit(solution)/shard_map/dot_general | solution.py:109
  90.3 2.2 %collective-permute-start.2 = (f32[128,4096]{1,0:T(8,128)S(1)}, f32[128,4096]{1,0:T(8,128)S(1)}, u32[]{:S(2)}, u32[]{:S(2)}) collective-permute-start(f32[128,4096]{1,0:T(8,128)S(1)} %convolution_add_fusion), channel_id=1, source_target_pairs={{0,1},{1,0},{2,3},{3,2},{4,5},{5,4},{6,7},{7,6},{8,9},{9,8},{10,11... | collective-permute-start | bytes 6291464 | tf_op jit(solution)/shard_map/ppermute | solution.py:18
  94.2 0.8 multiply_convert_fusion.1
  95.5 1.0 collective-permute-done.2
  96.5 1.5 fusion.1
  98.5 1.4 copy-done.5
  102.1 1.2 copy.35
  103.3 2.1 %convolution_convert_fusion.1 = bf16[4096,256]{1,0:T(8,128)(2,1)} fusion(bf16[128,4096]{1,0:T(8,128)(2,1)S(1)} %get-tuple-element.23, bf16[128,4096]{1,0:T(8,128)(2,1)S(1)} %get-tuple-element.21, bf16[128,256]{1,0:T(8,128)(2,1)S(1)} %get-tuple-element.29, bf16[128,256]{1,0:T(8,128)(2,1)S(1)} %get-tuple-element.26), kind=kOutput, calls=%fused_computation.1 | convolution fusion | flops 542375936 | bytes 4325376 | tf_op jit(solution)/shard_map/dot_general | solution.py:123
  105.4 2.5 %reshape.98 = bf16[32,128,2,128]{3,2,1,0:T(2,128)(2,1)S(1)} reshape(bf16[4096,256]{1,0:T(8,128)(2,1)} %convolution_convert_fusion.1) | data formatting | bytes 4194304 | tf_op jit(solution)/shard_map/reshape | solution.py:76
  108.0 1.5 fusion.23
  109.6 1.2 copy.34
  110.8 2.1 %convolution_convert_fusion.2 = bf16[4096,256]{1,0:T(8,128)(2,1)} fusion(bf16[128,4096]{1,0:T(8,128)(2,1)S(1)} %copy-done.11, bf16[128,4096]{1,0:T(8,128)(2,1)S(1)} %get-tuple-element.21, bf16[128,256]{1,0:T(8,128)(2,1)S(1)} %get-tuple-element.28, bf16[128,256]{1,0:T(8,128)(2,1)S(1)} %get-tuple-element.25), kind=kOutput, calls=%fused_computation.2 | convolution fusion | flops 542375936 | bytes 4325376 | tf_op jit(solution)/shard_map/dot_general | solution.py:122
  112.9 2.5 %reshape.97 = bf16[32,128,2,128]{3,2,1,0:T(2,128)(2,1)S(1)} reshape(bf16[4096,256]{1,0:T(8,128)(2,1)} %convolution_convert_fusion.2) | data formatting | bytes 4194304 | tf_op jit(solution)/shard_map/reshape | solution.py:76
  115.5 22.9 %reduce-scatter.2.cloned.1.call-done = bf16[16,4096]{1,0:T(8,128)(2,1)} async-done(((bf16[128,4096]{1,0:T(8,128)(2,1)}), bf16[16,4096]{1,0:T(8,128)(2,1)}) %reduce-scatter.2.cloned.1.call-update) | async-done | bytes 131088 | tf_op jit(solution)/shard_map/reduce_scatter | solution.py:32
  138.3 1.6 all_to_all.14
  140.0 7.4 %all-to-all-start.1 = ((bf16[4,4,4096]{2,1,0:T(4,128)(2,1)}), bf16[4,4,4096]{2,1,0:T(4,128)(2,1)S(1)}, u32[]{:S(2)}, u32[]{:S(2)}) async-start(bf16[4,4,4096]{2,1,0:T(4,128)(2,1)} %all_to_all.14), calls=%async_computation.2 | async-start | bytes 262144 | tf_op jit(solution)/shard_map/all_to_all | solution.py:34
  147.4 1.5 fusion.20
  149.0 1.2 copy.33
  150.2 5.9 %all-to-all-done.1 = bf16[4,4,4096]{2,1,0:T(4,128)(2,1)S(1)} async-done(((bf16[4,4,4096]{2,1,0:T(4,128)(2,1)}), bf16[4,4,4096]{2,1,0:T(4,128)(2,1)S(1)}, u32[]{:S(2)}, u32[]{:S(2)}) %all-to-all-start.1) | async-done | bytes 131104 | tf_op jit(solution)/shard_map/all_to_all | solution.py:34
  (51 shorter events, 11.8 us)
Async XLA Ops:
  7.2 29.8 %copy-start.7 = (bf16[1,26,128,128]{3,2,1,0:T(8,128)(2,1)S(1)}, bf16[1,26,128,128]{3,2,1,0:T(8,128)(2,1)}, u32[]{:S(2)}) copy-start(bf16[1,26,128,128]{3,2,1,0:T(8,128)(2,1)} %param.10) | copy-start | bytes 2555908
  7.2 70.3 %all-gather.2.cloned.1.call-start = ((), (), s32[]{:S(2)}) async-start(), calls=%async_computation.3 | async-start | bytes 2359296 | tf_op jit(solution)/shard_map/all_gather | solution.py:25
  7.2 6.6 %collective-permute-start = (bf16[1,4,4096]{2,1,0:T(4,128)(2,1)}, bf16[1,4,4096]{2,1,0:T(4,128)(2,1)S(1)}, u32[]{:S(2)}, u32[]{:S(2)}) collective-permute-start(bf16[1,4,4096]{2,1,0:T(4,128)(2,1)} %param.7), channel_id=1, source_target_pairs={{64,0},{128,64},{192,128},{256,192},{320,256},{384,320},{448,384},... | collective-permute-start | bytes 98312 | tf_op jit(solution)/shard_map/ppermute | solution.py:13
  36.1 102.2 %reduce-scatter.2.cloned.1.call-start = ((), (), s32[]{:S(2)}) async-start(), calls=%async_computation.4 | async-start | bytes 1179648 | tf_op jit(solution)/shard_map/reduce_scatter | solution.py:32
  36.9 12.2 %copy-start.12 = (f32[26,2]{0,1:T(2,128)}, f32[26,2]{0,1:T(2,128)S(1)}, u32[]{:S(2)}) copy-start(f32[26,2]{0,1:T(2,128)S(1)} %compare_convert_fusion) | copy-start | bytes 628
  37.8 3.8 %copy-start.8 = (bf16[1,26,128,128]{3,2,1,0:T(8,128)(2,1)S(1)}, bf16[1,26,128,128]{3,2,1,0:T(8,128)(2,1)}, u32[]{:S(2)}) copy-start(bf16[1,26,128,128]{3,2,1,0:T(8,128)(2,1)} %param.9) | copy-start | bytes 2555908
  46.4 2.7 %copy-start.9 = (bf16[1,26,128,128]{3,2,1,0:T(8,128)(2,1)S(1)}, bf16[1,26,128,128]{3,2,1,0:T(8,128)(2,1)}, u32[]{:S(2)}) copy-start(bf16[1,26,128,128]{3,2,1,0:T(8,128)(2,1)} %param.11) | copy-start | bytes 2555908
  49.1 1.6 copy-start.6
  77.5 6.3 %collective-permute-start.1 = (bf16[128,8192]{1,0:T(8,128)(2,1)}, bf16[128,8192]{1,0:T(8,128)(2,1)S(1)}, u32[]{:S(2)}, u32[]{:S(2)}) collective-permute-start(bf16[128,8192]{1,0:T(8,128)(2,1)} %all-gather.2.cloned.1.call-done), channel_id=1, source_target_pairs={{0,1},{1,0},{2,3},{3,2},{4,5},{5,4},{6,7},{7,6},{8,9},{9,8},{10,11... | collective-permute-start | bytes 6291464 | tf_op jit(solution)/shard_map/ppermute | solution.py:18
  83.7 4.0 %copy-start.4 = (bf16[128,8192]{1,0:T(8,128)(2,1)}, bf16[128,8192]{1,0:T(8,128)(2,1)S(1)}, u32[]{:S(2)}) copy-start(bf16[128,8192]{1,0:T(8,128)(2,1)S(1)} %collective-permute-done.1) | copy-start | bytes 6291460
  86.9 1.6 copy-start
  89.8 2.7 %copy-start.1 = (bf16[256,4096]{1,0:T(8,128)(2,1)S(1)}, bf16[256,4096]{1,0:T(8,128)(2,1)}, u32[]{:S(2)}) copy-start(bf16[256,4096]{1,0:T(8,128)(2,1)} %get-tuple-element.9) | copy-start | bytes 6291460
  89.8 2.7 %copy-start.2 = (bf16[128,8192]{1,0:T(8,128)(2,1)S(1)}, bf16[128,8192]{1,0:T(8,128)(2,1)}, u32[]{:S(2)}) copy-start(bf16[128,8192]{1,0:T(8,128)(2,1)} %all-gather.2.cloned.1.call-done) | copy-start | bytes 6291460
  90.3 6.2 %collective-permute-start.2 = (f32[128,4096]{1,0:T(8,128)S(1)}, f32[128,4096]{1,0:T(8,128)S(1)}, u32[]{:S(2)}, u32[]{:S(2)}) collective-permute-start(f32[128,4096]{1,0:T(8,128)S(1)} %convolution_add_fusion), channel_id=1, source_target_pairs={{0,1},{1,0},{2,3},{3,2},{4,5},{5,4},{6,7},{7,6},{8,9},{9,8},{10,11... | collective-permute-start | bytes 6291464 | tf_op jit(solution)/shard_map/ppermute | solution.py:18
  96.5 1.8 %copy-start.3 = (bf16[128,8192]{1,0:T(8,128)(2,1)S(1)}, bf16[128,8192]{1,0:T(8,128)(2,1)}, u32[]{:S(2)}) copy-start(bf16[128,8192]{1,0:T(8,128)(2,1)} %all-gather.2.cloned.1.call-done) | copy-start | bytes 6291460
  98.3 1.6 copy-start.5
  100.1 3.2 %copy-start.10 = (bf16[128,4096]{1,0:T(8,128)(2,1)}, bf16[128,4096]{1,0:T(8,128)(2,1)S(1)}, u32[]{:S(2)}) copy-start(bf16[128,4096]{1,0:T(8,128)(2,1)S(1)} %get-tuple-element.23) | copy-start | bytes 3145732
  100.9 0.7 copy-start.13
  108.0 2.8 %copy-start.11 = (bf16[128,4096]{1,0:T(8,128)(2,1)S(1)}, bf16[128,4096]{1,0:T(8,128)(2,1)}, u32[]{:S(2)}) copy-start(bf16[128,4096]{1,0:T(8,128)(2,1)} %copy-done.10) | copy-start | bytes 3145732
  140.0 16.2 %all-to-all-start.1 = ((bf16[4,4,4096]{2,1,0:T(4,128)(2,1)}), bf16[4,4,4096]{2,1,0:T(4,128)(2,1)S(1)}, u32[]{:S(2)}, u32[]{:S(2)}) async-start(bf16[4,4,4096]{2,1,0:T(4,128)(2,1)} %all_to_all.14), calls=%async_computation.2 | async-start | bytes 262144 | tf_op jit(solution)/shard_map/all_to_all | solution.py:34
Sparse Core Ops, SparseCore 0:
  36.3 41.1 all-gather.1
  98.2 40.0 reduce-scatter.1

commit v13 on v12

--- a/solution.py
+++ b/solution.py
@@ -28,15 +28,17 @@
 
 
 def scatter_rows(own, other):
-    block = (own + shifted(other, "core", 1)).astype(jnp.bfloat16)
-    block = lax.psum_scatter(block, "y", scatter_dimension=0, tiled=True)
-    n = lax.axis_size("zh")
-    got = lax.all_to_all(block, "zh", 0, 0, tiled=True).astype(jnp.float32)
-    own_rows = got.shape[0] // n
-    total = got[:own_rows]
-    for k in range(1, n):
-        total = total + got[k * own_rows:(k + 1) * own_rows]
-    return total
+    block = own + shifted(other, "core", 1)
+    n_y, n_zh = lax.axis_size("y"), lax.axis_size("zh")
+    by_zh = block.reshape(n_y, n_zh, -1, block.shape[1]).swapaxes(0, 1)
+    by_zh = by_zh.reshape(-1, block.shape[1]).astype(jnp.bfloat16)
+    got = lax.all_to_all(by_zh, "zh", 0, 0, tiled=True).astype(jnp.float32)
+    part = got.shape[0] // n_zh
+    total = got[:part]
+    for k in range(1, n_zh):
+        total = total + got[k * part:(k + 1) * part]
+    total = lax.psum_scatter(total.astype(jnp.bfloat16), "y", scatter_dimension=0, tiled=True)
+    return total.astype(jnp.float32)
 
 
 def per_device(saved_input, grad_sent, kept_blocks, gate_blocks, up_blocks, down_blocks):

time: 164 us -> 220 us (1.34)
  waiting for transfers between devices: 56.6 us -> 102 us
  local copies, waits for them, and re-layouts: 31.7 us -> 38.6 us
    unnamed x2 -> x3, waiting for transfers between devices: 0.03 us -> 64 us
    reduce_scatter x1 -> x0, waiting for transfers between devices: 22.9 us -> none  [scatter_rows(): block = lax.psum_scatter(block, 'y', scatter_dimension=0, tiled=True)]
    all_to_all x1, waiting for transfers between devices: 5.94 us -> 13 us  [scatter_rows(): got = lax.all_to_all(by_zh, 'zh', 0, 0, tiled=True).astype(jnp.float32)]
    slice x2, local copies, waits for them, and re-layouts: 0.36 us -> 3.23 us  [rows_part(): inputs, upstream = (both[:, :width], both[:, width:])]
    ppermute x2, waiting for transfers between devices: 5.16 us -> 2.36 us  [shifted(): return lax.ppermute(block, axis, [(i, (i + shift) % n) for i in range(n)])]
    unnamed x33 -> x34, local copies, waits for them, and re-layouts: 10.1 us -> 10.6 us
  transfers between devices with their start and end apart: 6 -> 6, of which waited for: 6 -> 5; matrix products, arithmetic and copies ran while one was open for 25% -> 22% of each run, Pallas kernels for 0% -> 0%
where the time goes in v13:
time: 220 us; the launch traced here: 219 us
  waiting for transfers between devices  102 us (46%)
  local copies, waits for them, and re-layouts  38.6 us (18%)
  matrix products  23.7 us (11%)
  blocking collectives  20.7 us (9%)
  starting transfers between devices  16.4 us (7%)
  between operations  15 us (7%)
  other arithmetic  2.56 us (1%)
    unnamed x3, waiting for transfers between devices  64 us
    all_gather x1, waiting for transfers between devices, gather_rows(): block = lax.all_gather(block, 'y', axis=0, tiled=True)  20.7 us
    all_to_all x1, blocking collectives, gather_rows(): block = lax.all_to_all(copies, 'zh', 0, 0, tiled=True)  20.7 us
    all_to_all x1, waiting for transfers between devices, scatter_rows(): got = lax.all_to_all(by_zh, 'zh', 0, 0, tiled=True).astype(jnp.float32)  13 us
    unnamed x34, local copies, waits for them, and re-layouts  10.6 us
    convert_element_type x2, local copies, waits for them, and re-layouts, dense_in(): return placed.astype(jnp.bfloat16).reshape(width, hidden_units)  7.63 us
    all_to_all x1, starting transfers between devices, scatter_rows(): got = lax.all_to_all(by_zh, 'zh', 0, 0, tiled=True).astype(jnp.float32)  7.39 us
    reshape x2, local copies, waits for them, and re-layouts, kept_in(): tiles = dense.astype(jnp.bfloat16).reshape(bands, block, columns, block)  6.51 us
  transfers between devices with their start and end apart: 6, of which 5 were waited for; matrix products, arithmetic and copies ran while one was open for 22% of the time, Pallas kernels for 0%

profile of v13, /device:TPU:6, one launch (start us, length us, event | category | flops | bytes accessed | tf_op | source)
XLA Modules:
  0.0 218.8 jit_solution(14563559896608807234)
XLA Ops:
  7.2 4.7 %collective-permute-start = (bf16[1,4,4096]{2,1,0:T(4,128)(2,1)}, bf16[1,4,4096]{2,1,0:T(4,128)(2,1)S(1)}, u32[]{:S(2)}, u32[]{:S(2)}) collective-permute-start(bf16[1,4,4096]{2,1,0:T(4,128)(2,1)} %param.7), channel_id=1, source_target_pairs={{64,0},{128,64},{192,128},{256,192},{320,256},{384,320},{448,384},... | collective-permute-start | bytes 98312 | tf_op jit(solution)/shard_map/ppermute | solution.py:13
  11.9 1.9 collective-permute-done
  14.7 20.7 %all_to_all.15 = bf16[4,4,8192]{2,1,0:T(4,128)(2,1)S(1)} all-to-all(bf16[4,4,8192]{2,1,0:T(4,128)(2,1)S(1)} %tile.2), channel_id=1, replica_groups=mesh['section'=8,'y'=8,'zh'=4,'core'=2] {'zh'}, dimensions={0} | all-to-all | bytes 524288 | tf_op jit(solution)/shard_map/all_to_all | solution.py:24
  37.8 3.8 %copy.43 = bf16[32,128,2,128]{1,0,3,2:T(8,128)(2,1)} copy(bf16[32,128,2,128]{3,0,1,2:T(8,128)(2,1)S(1)} %convert_bitcast_fusion) | data formatting | bytes 4194304 | tf_op jit(solution)/shard_map/convert_element_type | solution.py:68
  42.5 3.8 %copy.40 = bf16[32,128,2,128]{1,0,3,2:T(8,128)(2,1)} copy(bf16[32,128,2,128]{3,0,1,2:T(8,128)(2,1)S(1)} %convert_bitcast_fusion.1) | data formatting | bytes 4194304 | tf_op jit(solution)/shard_map/convert_element_type | solution.py:68
  46.4 2.7 %copy.96 = bf16[32,8,32,128]{3,1,2,0:T(8,128)(2,1)S(1)} copy(bf16[32,8,32,128]{3,2,1,0:T(8,128)(2,1)} %bitcast.132) | data formatting | bytes 4194304
  50.6 6.1 %copy_bitcast_fusion = (bf16[256,4096]{1,0:T(8,128)(2,1)}, bf16[4096,256]{0,1:T(8,128)(2,1)}) fusion(bf16[32,8,32,128]{3,2,1,0:T(8,128)(2,1)S(1)} %bitcast.134, bf16[32,8,32,128]{3,2,1,0:T(8,128)(2,1)S(1)} %bitcast.133), kind=kLoop, calls=%fused_computation.9 | loop fusion | bytes 8388608 | tf_op jit(solution)/shard_map/reshape | solution.py:75
  56.7 20.7 %all-gather.2.cloned.1.call-done = bf16[128,8192]{1,0:T(8,128)(2,1)} async-done(((bf16[16,8192]{1,0:T(8,128)(2,1)}), bf16[128,8192]{1,0:T(8,128)(2,1)}) %all-gather.2.cloned.1.call-update) | async-done | bytes 2097168 | tf_op jit(solution)/shard_map/all_gather | solution.py:25
  77.5 2.1 collective-permute-start.1
  79.6 1.3 dynamic-slice
  81.5 2.4 %collective-permute-done.1 = bf16[128,8192]{1,0:T(8,128)(2,1)} collective-permute-done((bf16[128,8192]{1,0:T(8,128)(2,1)}, bf16[128,8192]{1,0:T(8,128)(2,1)}, u32[]{:S(2)}, u32[]{:S(2)}) %collective-permute-start.1) | collective-permute-done | bytes 2097184 | tf_op jit(solution)/shard_map/ppermute | solution.py:18
  83.9 2.8 %fusion.68 = f32[128,256]{1,0:T(8,128)S(1)} fusion(bf16[256,4096]{1,0:T(8,128)(2,1)} %get-tuple-element.9, bf16[128,8192]{1,0:T(8,128)(2,1)} %collective-permute-done.1), kind=kOutput, calls=%fused_computation.92 | convolution fusion | flops 268435456 | bytes 3276800 | tf_op jit(solution)/shard_map/dot_general | solution.py:111
  86.6 2.2 %fusion.72 = f32[128,256]{1,0:T(8,128)S(1)} fusion(bf16[4096,256]{0,1:T(8,128)(2,1)S(1)} %bitcast.127, bf16[128,8192]{1,0:T(8,128)(2,1)} %collective-permute-done.1), kind=kOutput, calls=%fused_computation.96 | convolution fusion | flops 268435456 | bytes 3276800 | tf_op jit(solution)/shard_map/dot_general | solution.py:106
  88.9 2.1 multiply_convert_fusion
  91.9 2.2 collective-permute-start.2
  97.1 1.5 fusion.80
  100.2 1.1 convert_element_type.89
  101.3 7.4 %all-to-all-start.1 = ((bf16[4,32,4096]{2,1,0:T(8,128)(2,1)}), bf16[4,32,4096]{2,1,0:T(8,128)(2,1)S(1)}, u32[]{:S(2)}, u32[]{:S(2)}) async-start(bf16[4,32,4096]{2,1,0:T(8,128)(2,1)} %convert_element_type.89), calls=%async_computation.1 | async-start | bytes 2097152 | tf_op jit(solution)/shard_map/all_to_all | solution.py:35
  108.7 1.8 fusion.81
  112.5 2.1 convolution_convert_fusion.1
  114.6 4.0 %reshape.102 = bf16[32,128,2,128]{3,2,1,0:T(2,128)(2,1)} reshape(bf16[4096,256]{1,0:T(8,128)(2,1)} %convolution_convert_fusion.1) | data formatting | bytes 4194304 | tf_op jit(solution)/shard_map/reshape | solution.py:78
  118.5 1.5 fusion.26
  120.3 1.6 fusion.23
  121.8 13.0 %all-to-all-done.1 = bf16[4,32,4096]{2,1,0:T(8,128)(2,1)S(1)} async-done(((bf16[4,32,4096]{2,1,0:T(8,128)(2,1)}), bf16[4,32,4096]{2,1,0:T(8,128)(2,1)S(1)}, u32[]{:S(2)}, u32[]{:S(2)}) %all-to-all-start.1) | async-done | bytes 1048608 | tf_op jit(solution)/shard_map/all_to_all | solution.py:35
  136.7 2.1 convolution_convert_fusion.2
  138.8 1.2 copy.52
  140.0 1.2 copy.51
  141.3 2.5 %reshape.101 = bf16[32,128,2,128]{3,2,1,0:T(2,128)(2,1)S(1)} reshape(bf16[4096,256]{1,0:T(8,128)(2,1)} %convolution_convert_fusion.2) | data formatting | bytes 4194304 | tf_op jit(solution)/shard_map/reshape | solution.py:78
  143.8 1.5 fusion.20
  145.4 1.2 copy.50
  146.6 63.9 %all-reduce.3.cloned.1.call-done = bf16[32,4096]{1,0:T(8,128)(2,1)} async-done(((bf16[32,4096]{1,0:T(8,128)(2,1)}), bf16[32,4096]{1,0:T(8,128)(2,1)}) %all-reduce.3.cloned.1.call-update) | async-done | bytes 262160
  210.5 1.5 dynamic-slice_bitcast_fusion
  (55 shorter events, 15.4 us)
Async XLA Ops:
  7.2 29.7 %copy-start.7 = (bf16[1,26,128,128]{3,2,1,0:T(8,128)(2,1)S(1)}, bf16[1,26,128,128]{3,2,1,0:T(8,128)(2,1)}, u32[]{:S(2)}) copy-start(bf16[1,26,128,128]{3,2,1,0:T(8,128)(2,1)} %param.10) | copy-start | bytes 2555908
  7.2 70.3 %all-gather.2.cloned.1.call-start = ((), (), s32[]{:S(2)}) async-start(), calls=%async_computation.2 | async-start | bytes 2359296 | tf_op jit(solution)/shard_map/all_gather | solution.py:25
  7.2 6.6 %collective-permute-start = (bf16[1,4,4096]{2,1,0:T(4,128)(2,1)}, bf16[1,4,4096]{2,1,0:T(4,128)(2,1)S(1)}, u32[]{:S(2)}, u32[]{:S(2)}) collective-permute-start(bf16[1,4,4096]{2,1,0:T(4,128)(2,1)} %param.7), channel_id=1, source_target_pairs={{64,0},{128,64},{192,128},{256,192},{320,256},{384,320},{448,384},... | collective-permute-start | bytes 98312 | tf_op jit(solution)/shard_map/ppermute | solution.py:13
  37.8 3.8 %copy-start.8 = (bf16[1,26,128,128]{3,2,1,0:T(8,128)(2,1)S(1)}, bf16[1,26,128,128]{3,2,1,0:T(8,128)(2,1)}, u32[]{:S(2)}) copy-start(bf16[1,26,128,128]{3,2,1,0:T(8,128)(2,1)} %param.9) | copy-start | bytes 2555908
  46.4 2.7 %copy-start.9 = (bf16[1,26,128,128]{3,2,1,0:T(8,128)(2,1)S(1)}, bf16[1,26,128,128]{3,2,1,0:T(8,128)(2,1)}, u32[]{:S(2)}) copy-start(bf16[1,26,128,128]{3,2,1,0:T(8,128)(2,1)} %param.11) | copy-start | bytes 2555908
  49.0 1.6 copy-start.4
  77.5 6.4 %collective-permute-start.1 = (bf16[128,8192]{1,0:T(8,128)(2,1)}, bf16[128,8192]{1,0:T(8,128)(2,1)}, u32[]{:S(2)}, u32[]{:S(2)}) collective-permute-start(bf16[128,8192]{1,0:T(8,128)(2,1)} %all-gather.2.cloned.1.call-done), channel_id=1, source_target_pairs={{0,1},{1,0},{2,3},{3,2},{4,5},{5,4},{6,7},{7,6},{8,9},{9,8},{10,11... | collective-permute-start | bytes 6291464 | tf_op jit(solution)/shard_map/ppermute | solution.py:18
  86.6 2.2 %copy-start = (bf16[4096,256]{0,1:T(8,128)(2,1)S(1)}, bf16[4096,256]{0,1:T(8,128)(2,1)}, u32[]{:S(2)}) copy-start(bf16[4096,256]{0,1:T(8,128)(2,1)} %get-tuple-element.10) | copy-start | bytes 6291460
  91.4 2.7 %copy-start.1 = (bf16[256,4096]{1,0:T(8,128)(2,1)S(1)}, bf16[256,4096]{1,0:T(8,128)(2,1)}, u32[]{:S(2)}) copy-start(bf16[256,4096]{1,0:T(8,128)(2,1)} %get-tuple-element.9) | copy-start | bytes 6291460
  91.4 2.7 %copy-start.2 = (bf16[128,8192]{1,0:T(8,128)(2,1)S(1)}, bf16[128,8192]{1,0:T(8,128)(2,1)}, u32[]{:S(2)}) copy-start(bf16[128,8192]{1,0:T(8,128)(2,1)} %all-gather.2.cloned.1.call-done) | copy-start | bytes 6291460
  91.9 6.7 %collective-permute-start.2 = (f32[128,4096]{1,0:T(8,128)S(1)}, f32[128,4096]{1,0:T(8,128)S(1)}, u32[]{:S(2)}, u32[]{:S(2)}) collective-permute-start(f32[128,4096]{1,0:T(8,128)S(1)} %convolution_add_fusion), channel_id=1, source_target_pairs={{0,1},{1,0},{2,3},{3,2},{4,5},{5,4},{6,7},{7,6},{8,9},{9,8},{10,11... | collective-permute-start | bytes 6291464 | tf_op jit(solution)/shard_map/ppermute | solution.py:18
  101.3 33.6 %all-to-all-start.1 = ((bf16[4,32,4096]{2,1,0:T(8,128)(2,1)}), bf16[4,32,4096]{2,1,0:T(8,128)(2,1)S(1)}, u32[]{:S(2)}, u32[]{:S(2)}) async-start(bf16[4,32,4096]{2,1,0:T(8,128)(2,1)} %convert_element_type.89), calls=%async_computation.1 | async-start | bytes 2097152 | tf_op jit(solution)/shard_map/all_to_all | solution.py:35
  108.7 1.9 copy-start.6
  108.7 101.9 %all-reduce.3.cloned.1.call-start = ((), (), s32[]{:S(2)}) async-start(), calls=%async_computation.3 | async-start | bytes 524288
  110.4 1.3 copy-start.12
  111.3 1.2 copy-start.10
  118.5 1.8 copy-start.3
  135.0 1.3 copy-start.11
  135.0 1.6 copy-start.13
  136.7 2.1 copy-start.5
Sparse Core Ops, SparseCore 0:
  36.3 41.1 all-gather.1
  136.0 74.4 all-reduce.2

commit v14 on v12

--- a/solution.py
+++ b/solution.py
@@ -19,12 +19,17 @@
 
 
 def gather_rows(block, weights):
+    block = jnp.concatenate([block, shifted(block, "core", 1)], axis=0)
     n = lax.axis_size("zh")
     copies = jnp.tile(block, (n, 1))
     block = lax.all_to_all(copies, "zh", 0, 0, tiled=True)
     block = lax.all_gather(block, "y", axis=0, tiled=True)
     block, weights = lax.optimization_barrier((block, weights))
-    return (block, shifted(block, "core", 1)), weights
+    pairs = block.reshape(-1, 2, block.shape[0] // (2 * lax.axis_size("y") * n), block.shape[1])
+    return (
+        pairs[:, 0].reshape(-1, block.shape[1]),
+        pairs[:, 1].reshape(-1, block.shape[1]),
+    ), weights
 
 
 def scatter_rows(own, other):

time: 164 us -> 207 us (1.26)
  local copies, waits for them, and re-layouts: 31.7 us -> 52.7 us
  waiting for transfers between devices: 56.6 us -> 65 us
  matrix products: 21.6 us -> 29 us
  blocking collectives: 20.7 us -> 26.9 us
    all_gather x1, waiting for transfers between devices: 20.7 us -> 32.8 us  [gather_rows(): block = lax.all_gather(block, 'y', axis=0, tiled=True)]
    another operation x0 -> x2, local copies, waits for them, and re-layouts: none -> 7.96 us  [the longest x1 3.98 us: gather_rows(): pairs[:, 0].reshape(-1, block.shape[1])]
    reshape x0 -> x1, local copies, waits for them, and re-layouts: none -> 7.24 us  [gather_rows(): block.reshape(-1, 2, block.shape[0] // (2 * lax.axis_size('y') * n), bloc...]
    all_to_all x1, blocking collectives: 20.7 us -> 26.9 us  [gather_rows(): block = lax.all_to_all(copies, 'zh', 0, 0, tiled=True)]
    slice x0 -> x1, local copies, waits for them, and re-layouts: none -> 5.38 us  [gather_rows(): pairs[:, 0].reshape(-1, block.shape[1])]
    ppermute x2, waiting for transfers between devices: 5.16 us -> 1.22 us  [shifted(): return lax.ppermute(block, axis, [(i, (i + shift) % n) for i in range(n)])]
    dot_general x2, matrix products: 2.04 us -> 5.2 us  [rows_part(): lax.dot_general(grad_up_act, w_up, hid_t, preferred_element_type=f32)]
    unnamed x33 -> x35, local copies, waits for them, and re-layouts: 10.1 us -> 9.91 us
  transfers between devices with their start and end apart: 6 -> 6, of which waited for: 6 -> 5; matrix products, arithmetic and copies ran while one was open for 25% -> 24% of each run, Pallas kernels for 0% -> 0%
where the time goes in v14:
time: 207 us; the launch traced here: 206 us
  waiting for transfers between devices  65 us (31%)
  local copies, waits for them, and re-layouts  52.7 us (25%)
  matrix products  29 us (14%)
  blocking collectives  26.9 us (13%)
  starting transfers between devices  16 us (8%)
  between operations  14.4 us (7%)
  other arithmetic  2.37 us (1%)
    all_gather x1, waiting for transfers between devices, gather_rows(): block = lax.all_gather(block, 'y', axis=0, tiled=True)  32.8 us
    all_to_all x1, blocking collectives, gather_rows(): block = lax.all_to_all(copies, 'zh', 0, 0, tiled=True)  26.9 us
    reduce_scatter x1, waiting for transfers between devices, scatter_rows(): block = lax.psum_scatter(block, 'y', scatter_dimension=0, tiled=True)  23.2 us
    unnamed x35, local copies, waits for them, and re-layouts  9.91 us
    convert_element_type x2, local copies, waits for them, and re-layouts, dense_in(): return placed.astype(jnp.bfloat16).reshape(width, hidden_units)  9.09 us
    all_to_all x1, starting transfers between devices, scatter_rows(): got = lax.all_to_all(block, 'zh', 0, 0, tiled=True).astype(jnp.float32)  7.37 us
    reshape x1, local copies, waits for them, and re-layouts, gather_rows(): block.reshape(-1, 2, block.shape[0] // (2 * lax.axis_size('y') * n), bloc...  7.24 us
    reshape x1, local copies, waits for them, and re-layouts, dense_down(): return placed.astype(jnp.bfloat16).reshape(hidden_units, width)  6.13 us
  transfers between devices with their start and end apart: 6, of which 5 were waited for; matrix products, arithmetic and copies ran while one was open for 24% of the time, Pallas kernels for 0%

profile of v14, /device:TPU:6, one launch (start us, length us, event | category | flops | bytes accessed | tf_op | source)
XLA Modules:
  0.0 206.3 jit_solution(15632315542623375887)
XLA Ops:
  7.2 4.7 %collective-permute-start = (bf16[1,4,4096]{2,1,0:T(4,128)(2,1)}, bf16[1,4,4096]{2,1,0:T(4,128)(2,1)S(1)}, u32[]{:S(2)}, u32[]{:S(2)}) collective-permute-start(bf16[1,4,4096]{2,1,0:T(4,128)(2,1)} %param.7), channel_id=1, source_target_pairs={{64,0},{128,64},{192,128},{256,192},{320,256},{384,320},{448,384},... | collective-permute-start | bytes 98312 | tf_op jit(solution)/shard_map/ppermute | solution.py:13
  11.9 1.9 collective-permute-done
  14.6 1.9 collective-permute-start.1
  18.6 26.9 %all_to_all.18 = bf16[4,8,8192]{2,1,0:T(8,128)(2,1)} all-to-all(bf16[4,8,8192]{2,1,0:T(8,128)(2,1)S(1)} %tile.2), channel_id=1, replica_groups=mesh['section'=8,'y'=8,'zh'=4,'core'=2] {'zh'}, dimensions={0} | all-to-all | bytes 1048576 | tf_op jit(solution)/shard_map/all_to_all | solution.py:25
  46.6 3.8 %copy.24 = bf16[32,128,2,128]{1,0,3,2:T(8,128)(2,1)} copy(bf16[32,128,2,128]{3,0,1,2:T(8,128)(2,1)S(1)} %convert_bitcast_fusion.1) | data formatting | bytes 4194304 | tf_op jit(solution)/shard_map/convert_element_type | solution.py:71
  50.4 2.7 %copy.79 = bf16[32,8,32,128]{3,1,2,0:T(8,128)(2,1)S(1)} copy(bf16[32,8,32,128]{3,2,1,0:T(8,128)(2,1)} %bitcast.126) | data formatting | bytes 4194304
  53.1 2.3 %convert_bitcast_fusion = bf16[32,128,2,128]{3,0,1,2:T(8,128)(2,1)} fusion(bf16[26,128,128]{2,1,0:T(8,128)(2,1)S(1)} %bitcast.132, f32[26,32]{1,0:T(8,128)S(1)} %fusion.63, f32[26,2]{0,1:T(2,128)S(1)} %compare_convert_fusion), kind=kOutput, calls=%fused_computation.23 | convolution fusion | flops 55576192 | bytes 2952656 | tf_op jit(solution)/shard_map/kr,kc,kbn->rbcn/dot_general | solution.py:67
  55.4 5.3 %copy.27 = bf16[32,128,2,128]{1,0,3,2:T(8,128)(2,1)} copy(bf16[32,128,2,128]{3,0,1,2:T(8,128)(2,1)} %convert_bitcast_fusion) | data formatting | bytes 4194304 | tf_op jit(solution)/shard_map/convert_element_type | solution.py:71
  62.2 6.1 %copy_bitcast_fusion = (bf16[256,4096]{1,0:T(8,128)(2,1)}, bf16[4096,256]{0,1:T(8,128)(2,1)}) fusion(bf16[32,8,32,128]{3,2,1,0:T(8,128)(2,1)S(1)} %bitcast.129, bf16[32,8,32,128]{3,2,1,0:T(8,128)(2,1)S(1)} %bitcast.128), kind=kLoop, calls=%fused_computation.9 | loop fusion | bytes 8388608 | tf_op jit(solution)/shard_map/reshape | solution.py:78
  68.4 32.8 %all-gather.2.cloned.1.call-done = bf16[256,8192]{1,0:T(8,128)(2,1)} async-done(((bf16[32,8192]{1,0:T(8,128)(2,1)}), bf16[256,8192]{1,0:T(8,128)(2,1)}) %all-gather.2.cloned.1.call-update) | async-done | bytes 4194320 | tf_op jit(solution)/shard_map/all_gather | solution.py:26
  101.1 7.2 %reshape.100 = bf16[32,2,4,8192]{3,2,1,0:T(4,128)(2,1)} reshape(bf16[256,8192]{1,0:T(8,128)(2,1)} %all-gather.2.cloned.1.call-done) | data formatting | bytes 8388608 | tf_op jit(solution)/shard_map/reshape | solution.py:28
  108.4 5.4 %fusion.79 = (bf16[32,1,4,8192]{3,2,1,0:T(4,128)(2,1)}, bf16[32,1,4,8192]{3,2,1,0:T(4,128)(2,1)}) fusion(bf16[32,2,4,8192]{3,2,1,0:T(4,128)(2,1)} %reshape.100), kind=kLoop, calls=%fused_computation.103 | loop fusion | bytes 8388608 | tf_op jit(solution)/shard_map/slice | solution.py:30
  113.8 4.0 %reshape_squeeze.7 = bf16[128,8192]{1,0:T(8,128)(2,1)} reshape(bf16[32,1,4,8192]{3,2,1,0:T(4,128)(2,1)} %get-tuple-element.21) | data formatting | bytes 4194304 | tf_op jit(solution)/shard_map/reshape;squeeze | solution.py:31
  117.7 2.9 %fusion.67 = f32[128,256]{1,0:T(8,128)S(1)} fusion(bf16[256,4096]{1,0:T(8,128)(2,1)} %get-tuple-element.9, bf16[128,8192]{1,0:T(8,128)(2,1)} %reshape_squeeze.7), kind=kOutput, calls=%fused_computation.91 | convolution fusion | flops 268435456 | bytes 3276800 | tf_op jit(solution)/shard_map/dot_general | solution.py:114
  123.5 1.9 convolution_add_fusion
  125.4 1.9 collective-permute-start.2
  127.3 4.0 %reshape_squeeze.6 = bf16[128,8192]{1,0:T(8,128)(2,1)} reshape(bf16[32,1,4,8192]{3,2,1,0:T(4,128)(2,1)} %get-tuple-element.20) | data formatting | bytes 4194304 | tf_op jit(solution)/shard_map/reshape;squeeze | solution.py:30
  131.3 2.2 %fusion.75 = f32[128,256]{1,0:T(8,128)S(1)} fusion(bf16[4096,256]{0,1:T(8,128)(2,1)S(1)} %bitcast.124, bf16[128,8192]{1,0:T(8,128)(2,1)} %reshape_squeeze.6), kind=kOutput, calls=%fused_computation.99 | convolution fusion | flops 268435456 | bytes 3276800 | tf_op jit(solution)/shard_map/dot_general | solution.py:109
  133.6 2.6 %fusion.69 = f32[128,256]{1,0:T(8,128)S(1)} fusion(bf16[256,4096]{1,0:T(8,128)(2,1)} %get-tuple-element.9, bf16[128,8192]{1,0:T(8,128)(2,1)S(1)} %copy-done.4), kind=kOutput, calls=%fused_computation.93 | convolution fusion | flops 268435456 | bytes 3276800 | tf_op jit(solution)/shard_map/dot_general | solution.py:114
  137.5 3.3 %fusion.1 = bf16[128,4096]{1,0:T(8,128)(2,1)} fusion(f32[128,4096]{1,0:T(8,128)} %collective-permute-done.2, f32[128,4096]{1,0:T(8,128)S(1)} %fusion.82, bf16[128,256]{1,0:T(8,128)(2,1)S(1)} %get-tuple-element.28, bf16[4096,256]{0,1:T(8,128)(2,1)S(1)} %copy-done.3), kind=kOutput, calls=%fused_computation.6 | convolution fusion | flops 270008320 | bytes 7405568 | tf_op jit(solution)/shard_map/dot_general | solution.py:118
  141.0 1.4 copy-done.1
  144.5 1.2 copy.35
  145.8 2.1 %convolution_convert_fusion.2 = bf16[4096,256]{1,0:T(8,128)(2,1)} fusion(bf16[128,4096]{1,0:T(8,128)(2,1)S(1)} %get-tuple-element.25, bf16[128,4096]{1,0:T(8,128)(2,1)S(1)} %get-tuple-element.23, bf16[128,256]{1,0:T(8,128)(2,1)S(1)} %get-tuple-element.30, bf16[128,256]{1,0:T(8,128)(2,1)S(1)} %get-tuple-element.27), kind=kOutput, calls=%fused_computation.2 | convolution fusion | flops 542375936 | bytes 4325376 | tf_op jit(solution)/shard_map/dot_general | solution.py:127
  147.9 2.5 %reshape.101 = bf16[32,128,2,128]{3,2,1,0:T(2,128)(2,1)S(1)} reshape(bf16[4096,256]{1,0:T(8,128)(2,1)} %convolution_convert_fusion.2) | data formatting | bytes 4194304 | tf_op jit(solution)/shard_map/reshape | solution.py:81
  150.5 1.5 fusion.20
  153.2 2.1 %convolution_convert_fusion.1 = bf16[4096,256]{1,0:T(8,128)(2,1)} fusion(bf16[128,4096]{1,0:T(8,128)(2,1)S(1)} %copy-done.11, bf16[128,4096]{1,0:T(8,128)(2,1)S(1)} %get-tuple-element.23, bf16[128,256]{1,0:T(8,128)(2,1)S(1)} %get-tuple-element.31, bf16[128,256]{1,0:T(8,128)(2,1)S(1)} %get-tuple-element.28), kind=kOutput, calls=%fused_computation.1 | convolution fusion | flops 542375936 | bytes 4325376 | tf_op jit(solution)/shard_map/dot_general | solution.py:128
  155.4 2.5 %reshape.102 = bf16[32,128,2,128]{3,2,1,0:T(2,128)(2,1)S(1)} reshape(bf16[4096,256]{1,0:T(8,128)(2,1)} %convolution_convert_fusion.1) | data formatting | bytes 4194304 | tf_op jit(solution)/shard_map/reshape | solution.py:81
  157.9 23.2 %reduce-scatter.2.cloned.1.call-done = bf16[16,4096]{1,0:T(8,128)(2,1)} async-done(((bf16[128,4096]{1,0:T(8,128)(2,1)}), bf16[16,4096]{1,0:T(8,128)(2,1)}) %reduce-scatter.2.cloned.1.call-update) | async-done | bytes 131088 | tf_op jit(solution)/shard_map/reduce_scatter | solution.py:37
  181.1 1.6 all_to_all.14
  182.7 7.4 %all-to-all-start.1 = ((bf16[4,4,4096]{2,1,0:T(4,128)(2,1)}), bf16[4,4,4096]{2,1,0:T(4,128)(2,1)S(1)}, u32[]{:S(2)}, u32[]{:S(2)}) async-start(bf16[4,4,4096]{2,1,0:T(4,128)(2,1)} %all_to_all.14), calls=%async_computation.2 | async-start | bytes 262144 | tf_op jit(solution)/shard_map/all_to_all | solution.py:39
  190.1 1.5 fusion.23
  192.9 5.9 %all-to-all-done.1 = bf16[4,4,4096]{2,1,0:T(4,128)(2,1)S(1)} async-done(((bf16[4,4,4096]{2,1,0:T(4,128)(2,1)}), bf16[4,4,4096]{2,1,0:T(4,128)(2,1)S(1)}, u32[]{:S(2)}, u32[]{:S(2)}) %all-to-all-start.1) | async-done | bytes 131104 | tf_op jit(solution)/shard_map/all_to_all | solution.py:39
  (57 shorter events, 15.1 us)
Async XLA Ops:
  7.2 38.4 %copy-start.14 = (s32[1,26]{1,0:T(1,128)S(1)}, s32[1,26]{1,0:T(1,128)}, u32[]{:S(2)}) copy-start(s32[1,26]{1,0:T(1,128)} %param.8) | copy-start | bytes 316
  7.2 38.5 %copy-start.7 = (bf16[1,26,128,128]{3,2,1,0:T(8,128)(2,1)S(1)}, bf16[1,26,128,128]{3,2,1,0:T(8,128)(2,1)}, u32[]{:S(2)}) copy-start(bf16[1,26,128,128]{3,2,1,0:T(8,128)(2,1)} %param.9) | copy-start | bytes 2555908
  7.2 94.0 %all-gather.2.cloned.1.call-start = ((), (), s32[]{:S(2)}) async-start(), calls=%async_computation.3 | async-start | bytes 4718592 | tf_op jit(solution)/shard_map/all_gather | solution.py:26
  7.2 6.6 %collective-permute-start = (bf16[1,4,4096]{2,1,0:T(4,128)(2,1)}, bf16[1,4,4096]{2,1,0:T(4,128)(2,1)S(1)}, u32[]{:S(2)}, u32[]{:S(2)}) collective-permute-start(bf16[1,4,4096]{2,1,0:T(4,128)(2,1)} %param.7), channel_id=1, source_target_pairs={{64,0},{128,64},{192,128},{256,192},{320,256},{384,320},{448,384},... | collective-permute-start | bytes 98312 | tf_op jit(solution)/shard_map/ppermute | solution.py:13
  14.6 3.1 %collective-permute-start.1 = (bf16[4,8192]{1,0:T(4,128)(2,1)S(1)}, bf16[4,8192]{1,0:T(4,128)(2,1)S(1)}, u32[]{:S(2)}, u32[]{:S(2)}) collective-permute-start(bf16[4,8192]{1,0:T(4,128)(2,1)S(1)} %pad_maximum_fusion.4), channel_id=1, source_target_pairs={{0,1},{1,0},{2,3},{3,2},{4,5},{5,4},{6,7},{7,6},{8,9},{9,8},{10,11... | collective-permute-start | bytes 196616 | tf_op jit(solution)/shard_map/ppermute | solution.py:18
  45.5 135.6 %reduce-scatter.2.cloned.1.call-start = ((), (), s32[]{:S(2)}) async-start(), calls=%async_computation.4 | async-start | bytes 1179648 | tf_op jit(solution)/shard_map/reduce_scatter | solution.py:37
  45.6 15.0 %copy-start.12 = (f32[26,2]{0,1:T(2,128)}, f32[26,2]{0,1:T(2,128)S(1)}, u32[]{:S(2)}) copy-start(f32[26,2]{0,1:T(2,128)S(1)} %compare_convert_fusion) | copy-start | bytes 628
  50.4 2.7 %copy-start.8 = (bf16[1,26,128,128]{3,2,1,0:T(8,128)(2,1)S(1)}, bf16[1,26,128,128]{3,2,1,0:T(8,128)(2,1)}, u32[]{:S(2)}) copy-start(bf16[1,26,128,128]{3,2,1,0:T(8,128)(2,1)} %param.10) | copy-start | bytes 2555908
  55.4 5.3 %copy-start.9 = (bf16[1,26,128,128]{3,2,1,0:T(8,128)(2,1)S(1)}, bf16[1,26,128,128]{3,2,1,0:T(8,128)(2,1)}, u32[]{:S(2)}) copy-start(bf16[1,26,128,128]{3,2,1,0:T(8,128)(2,1)} %param.11) | copy-start | bytes 2555908
  60.6 1.6 copy-start.6
  117.7 2.9 %copy-start = (bf16[128,8192]{1,0:T(8,128)(2,1)S(1)}, bf16[128,8192]{1,0:T(8,128)(2,1)}, u32[]{:S(2)}) copy-start(bf16[128,8192]{1,0:T(8,128)(2,1)} %reshape_squeeze.7) | copy-start | bytes 6291460
  120.6 1.6 copy-start.2
  125.4 12.0 %collective-permute-start.2 = (f32[128,4096]{1,0:T(8,128)}, f32[128,4096]{1,0:T(8,128)}, u32[]{:S(2)}, u32[]{:S(2)}) collective-permute-start(f32[128,4096]{1,0:T(8,128)} %convolution_add_fusion), channel_id=1, source_target_pairs={{0,1},{1,0},{2,3},{3,2},{4,5},{5,4},{6,7},{7,6},{8,9},{9,8},{10,11... | collective-permute-start | bytes 6291464 | tf_op jit(solution)/shard_map/ppermute | solution.py:18
  131.3 2.2 %copy-start.4 = (bf16[128,8192]{1,0:T(8,128)(2,1)S(1)}, bf16[128,8192]{1,0:T(8,128)(2,1)}, u32[]{:S(2)}) copy-start(bf16[128,8192]{1,0:T(8,128)(2,1)} %reshape_squeeze.6) | copy-start | bytes 6291460
  133.5 2.6 %copy-start.3 = (bf16[4096,256]{0,1:T(8,128)(2,1)S(1)}, bf16[4096,256]{0,1:T(8,128)(2,1)}, u32[]{:S(2)}) copy-start(bf16[4096,256]{0,1:T(8,128)(2,1)} %get-tuple-element.10) | copy-start | bytes 6291460
  137.5 3.4 %copy-start.5 = (bf16[128,8192]{1,0:T(8,128)(2,1)S(1)}, bf16[128,8192]{1,0:T(8,128)(2,1)}, u32[]{:S(2)}) copy-start(bf16[128,8192]{1,0:T(8,128)(2,1)} %reshape_squeeze.6) | copy-start | bytes 6291460
  140.8 1.6 copy-start.1
  142.5 3.2 %copy-start.10 = (bf16[128,4096]{1,0:T(8,128)(2,1)}, bf16[128,4096]{1,0:T(8,128)(2,1)S(1)}, u32[]{:S(2)}) copy-start(bf16[128,4096]{1,0:T(8,128)(2,1)S(1)} %get-tuple-element.25) | copy-start | bytes 3145732
  143.3 0.7 copy-start.13
  150.4 2.8 %copy-start.11 = (bf16[128,4096]{1,0:T(8,128)(2,1)S(1)}, bf16[128,4096]{1,0:T(8,128)(2,1)}, u32[]{:S(2)}) copy-start(bf16[128,4096]{1,0:T(8,128)(2,1)} %copy-done.10) | copy-start | bytes 3145732
  182.7 16.1 %all-to-all-start.1 = ((bf16[4,4,4096]{2,1,0:T(4,128)(2,1)}), bf16[4,4,4096]{2,1,0:T(4,128)(2,1)S(1)}, u32[]{:S(2)}, u32[]{:S(2)}) async-start(bf16[4,4,4096]{2,1,0:T(4,128)(2,1)} %all_to_all.14), calls=%async_computation.2 | async-start | bytes 262144 | tf_op jit(solution)/shard_map/all_to_all | solution.py:39
Sparse Core Ops, SparseCore 0:
  45.6 55.4 all-gather.1
  140.9 40.1 reduce-scatter.1

commit v15 on v12

--- a/solution.py
+++ b/solution.py
@@ -27,8 +27,8 @@
     return (block, shifted(block, "core", 1)), weights
 
 
-def scatter_rows(own, other):
-    block = (own + shifted(other, "core", 1)).astype(jnp.bfloat16)
+def scatter_rows(block):
+    block = block.astype(jnp.bfloat16)
     block = lax.psum_scatter(block, "y", scatter_dimension=0, tiled=True)
     n = lax.axis_size("zh")
     got = lax.all_to_all(block, "zh", 0, 0, tiled=True).astype(jnp.float32)
@@ -93,36 +93,42 @@
     w_down = dense_down(down_blocks[0])
 
     incoming = passed_along(grad_sent, "section", -1)
-    halves, (w_gate, w_up, w_down) = gather_rows(
+    w_gate = jnp.concatenate([w_gate, shifted(w_gate, "core", 1)], axis=1)
+    w_up = jnp.concatenate([w_up, shifted(w_up, "core", 1)], axis=1)
+    w_down = jnp.concatenate([w_down, shifted(w_down, "core", 1)], axis=0)
+    (both, other_rows), (w_gate, w_up, w_down) = gather_rows(
         jnp.concatenate([saved_input[0], incoming[0]], axis=1), (w_gate, w_up, w_down)
     )
     f32 = jnp.float32
     hid_t = (((1,), (1,)), ((), ()))
+    inputs, upstream = both[:, :width], both[:, width:]
+    gate = jnp.dot(inputs, w_gate, preferred_element_type=f32)
+    up = jnp.dot(inputs, w_up, preferred_element_type=f32)
+    sig = jax.nn.sigmoid(gate)
+    act = gate * sig
+    hidden = (act * up).astype(jnp.bfloat16)
+    dhid = lax.dot_general(upstream, w_down, hid_t, preferred_element_type=f32)
+    grad_up_act = (dhid * act).astype(jnp.bfloat16)
+    grad_gate_act = (dhid * up * sig * (1.0 + gate * (1.0 - sig))).astype(jnp.bfloat16)
+    whole_term = lax.dot_general(grad_gate_act, w_gate, hid_t, preferred_element_type=f32)
+    whole_term = whole_term + lax.dot_general(
+        grad_up_act, w_up, hid_t, preferred_element_type=f32
+    )
+    summed = scatter_rows(whole_term)
 
-    def rows_part(both):
-        inputs, upstream = both[:, :width], both[:, width:]
-        gate = jnp.dot(inputs, w_gate, preferred_element_type=f32)
-        up = jnp.dot(inputs, w_up, preferred_element_type=f32)
-        sig = jax.nn.sigmoid(gate)
-        act = gate * sig
-        hidden = (act * up).astype(jnp.bfloat16)
-        dhid = lax.dot_general(upstream, w_down, hid_t, preferred_element_type=f32)
-        grad_up_act = (dhid * act).astype(jnp.bfloat16)
-        grad_gate_act = (dhid * up * sig * (1.0 + gate * (1.0 - sig))).astype(jnp.bfloat16)
-        term = lax.dot_general(grad_gate_act, w_gate, hid_t, preferred_element_type=f32)
-        term = term + lax.dot_general(grad_up_act, w_up, hid_t, preferred_element_type=f32)
-        return term, (inputs, upstream, hidden, grad_gate_act, grad_up_act)
+    def own_and_partner(values):
+        sent = shifted(values[:, hidden_units:], "core", 1)
+        return jnp.concatenate([values[:, :hidden_units], sent], axis=0)
 
-    term_own, saved_own = rows_part(halves[0])
-    term_other, saved_other = rows_part(halves[1])
-    inputs, upstream, hidden, grad_gate_act, grad_up_act = (
-        jnp.concatenate(pair, axis=0) for pair in zip(saved_own, saved_other)
+    grad_gate_act, grad_up_act, hidden = (
+        own_and_partner(v) for v in (grad_gate_act, grad_up_act, hidden)
     )
+    inputs = jnp.concatenate([inputs, other_rows[:, :width]], axis=0)
+    upstream = jnp.concatenate([upstream, other_rows[:, width:]], axis=0)
     rows_t = (((0,), (0,)), ((), ()))
     tiles_gate = kept_in(lax.dot_general(inputs, grad_gate_act, rows_t, preferred_element_type=f32))
     tiles_up = kept_in(lax.dot_general(inputs, grad_up_act, rows_t, preferred_element_type=f32))
     tiles_down = kept_down(lax.dot_general(hidden, upstream, rows_t, preferred_element_type=f32))
-    summed = scatter_rows(term_own, term_other)
     grad_input = summed.astype(jnp.bfloat16)[None]
     return (grad_input, tiles_gate[None], tiles_up[None], tiles_down[None])
 

time: 164 us -> 165 us (level)
  starting transfers between devices: 16.5 us -> 37.2 us
  blocking collectives: 20.7 us -> 0 us
  waiting for transfers between devices: 56.6 us -> 40.8 us
  other arithmetic: 2.2 us -> 14.1 us
  matrix products: 21.6 us -> 28 us
  local copies, waits for them, and re-layouts: 31.7 us -> 30 us
    all_to_all x1 -> x0, blocking collectives: 20.7 us -> none  [gather_rows(): block = lax.all_to_all(copies, 'zh', 0, 0, tiled=True)]
    concatenate x0 -> x3, other arithmetic: none -> 11.9 us  [the longest x1 4.75 us: per_device(): w_down = jnp.concatenate([w_down, shifted(w_down, 'core', 1)], axis=0)]
    ppermute x2 -> x7, starting transfers between devices: 4.26 us -> 15.3 us  [shifted(): return lax.ppermute(block, axis, [(i, (i + shift) % n) for i in range(n)])]
    all_to_all x0 -> x1, starting transfers between devices: none -> 9.87 us  [gather_rows(): block = lax.all_to_all(copies, 'zh', 0, 0, tiled=True)]
    reduce_scatter x1, waiting for transfers between devices: 22.9 us -> 13.6 us  [scatter_rows(): block = lax.psum_scatter(block, 'y', scatter_dimension=0, tiled=True)]
    reshape x1 -> x0, local copies, waits for them, and re-layouts: 6.13 us -> none  [dense_down(): return placed.astype(jnp.bfloat16).reshape(hidden_units, width)]
    ppermute x2 -> x7, waiting for transfers between devices: 5.16 us -> 0.02 us  [shifted(): return lax.ppermute(block, axis, [(i, (i + shift) % n) for i in range(n)])]
    dot_general x2, matrix products: 1.82 us -> 5.64 us  [dense_in(): jnp.einsum('kr,kc,kbn->rbcn', band_onehot, col_onehot, blocks, preferred_...]
  transfers between devices with their start and end apart: 6 -> 12, of which waited for: 6 -> 4; matrix products, arithmetic and copies ran while one was open for 25% -> 41% of each run, Pallas kernels for 0% -> 0%
where the time goes in v15:
time: 165 us; the launch traced here: 164 us
  waiting for transfers between devices  40.8 us (25%)
  starting transfers between devices  37.2 us (23%)
  local copies, waits for them, and re-layouts  30 us (18%)
  matrix products  28 us (17%)
  between operations  14.4 us (9%)
  other arithmetic  14.1 us (9%)
    all_gather x1, waiting for transfers between devices, gather_rows(): block = lax.all_gather(block, 'y', axis=0, tiled=True)  20 us
    ppermute x7, starting transfers between devices, shifted(): return lax.ppermute(block, axis, [(i, (i + shift) % n) for i in range(n)])  15.3 us
    reduce_scatter x1, waiting for transfers between devices, scatter_rows(): block = lax.psum_scatter(block, 'y', scatter_dimension=0, tiled=True)  13.6 us
    unnamed x21, local copies, waits for them, and re-layouts  9.91 us
    all_to_all x1, starting transfers between devices, gather_rows(): block = lax.all_to_all(copies, 'zh', 0, 0, tiled=True)  9.87 us
    convert_element_type x2, local copies, waits for them, and re-layouts, dense_in(): return placed.astype(jnp.bfloat16).reshape(width, hidden_units)  8.52 us
    all_to_all x1, starting transfers between devices, scatter_rows(): got = lax.all_to_all(block, 'zh', 0, 0, tiled=True).astype(jnp.float32)  7.37 us
    reshape x2, local copies, waits for them, and re-layouts, kept_in(): tiles = dense.astype(jnp.bfloat16).reshape(bands, block, columns, block)  6.52 us
  transfers between devices with their start and end apart: 12, of which 4 were waited for; matrix products, arithmetic and copies ran while one was open for 41% of the time, Pallas kernels for 0%

profile of v15, /device:TPU:6, one launch (start us, length us, event | category | flops | bytes accessed | tf_op | source)
XLA Modules:
  0.0 164.5 jit_solution(16037326671122731765)
XLA Ops:
  7.2 4.5 %collective-permute-start = (bf16[1,4,4096]{2,1,0:T(4,128)(2,1)}, bf16[1,4,4096]{2,1,0:T(4,128)(2,1)S(1)}, u32[]{:S(2)}, u32[]{:S(2)}) collective-permute-start(bf16[1,4,4096]{2,1,0:T(4,128)(2,1)} %param.7), channel_id=1, source_target_pairs={{64,0},{128,64},{192,128},{256,192},{320,256},{384,320},{448,384},... | collective-permute-start | bytes 98312 | tf_op jit(solution)/shard_map/ppermute | solution.py:13
  15.2 9.9 %all-to-all-start = ((bf16[4,4,8192]{2,1,0:T(4,128)(2,1)}), bf16[4,4,8192]{2,1,0:T(4,128)(2,1)S(1)}, u32[]{:S(2)}, u32[]{:S(2)}) async-start(bf16[4,4,8192]{2,1,0:T(4,128)(2,1)} %tile.2), calls=%async_computation | async-start | bytes 524288 | tf_op jit(solution)/shard_map/all_to_all | solution.py:24
  25.1 3.4 %convert_bitcast_fusion = bf16[32,128,2,128]{3,0,1,2:T(8,128)(2,1)} fusion(bf16[26,128,128]{2,1,0:T(8,128)(2,1)} %bitcast.122, f32[26,32]{1,0:T(8,128)S(1)} %fusion.61, f32[26,2]{0,1:T(2,128)S(1)} %compare_convert_fusion), kind=kOutput, calls=%fused_computation.24 | convolution fusion | flops 55576192 | bytes 2952656 | tf_op jit(solution)/shard_map/kr,kc,kbn->rbcn/dot_general | solution.py:62
  28.4 4.3 %copy.27 = bf16[32,128,2,128]{1,0,3,2:T(8,128)(2,1)S(1)} copy(bf16[32,128,2,128]{3,0,1,2:T(8,128)(2,1)} %convert_bitcast_fusion) | data formatting | bytes 4194304 | tf_op jit(solution)/shard_map/convert_element_type | solution.py:66
  32.7 2.4 %copy.80 = bf16[32,8,32,128]{3,1,2,0:T(8,128)(2,1)} copy(bf16[32,8,32,128]{3,2,1,0:T(8,128)(2,1)S(1)} %bitcast.117) | data formatting | bytes 4194304
  35.1 1.9 %collective-permute-start.2 = (bf16[4096,256]{0,1:T(8,128)(2,1)}, bf16[4096,256]{0,1:T(8,128)(2,1)}, u32[]{:S(2)}, u32[]{:S(2)}) collective-permute-start(bf16[4096,256]{0,1:T(8,128)(2,1)} %bitcast.112), channel_id=1, source_target_pairs={{0,1},{1,0},{2,3},{3,2},{4,5},{5,4},{6,7},{7,6},{8,9},{9,8},{10,11... | collective-permute-start | bytes 6291464 | tf_op jit(solution)/shard_map/ppermute | solution.py:18
  38.8 2.4 %copy.79 = bf16[32,8,32,128]{3,1,2,0:T(8,128)(2,1)} copy(bf16[32,8,32,128]{3,2,1,0:T(8,128)(2,1)S(1)} %bitcast.119) | data formatting | bytes 4194304
  41.1 2.4 %collective-permute-start.3 = (bf16[256,4096]{1,0:T(8,128)(2,1)}, bf16[256,4096]{1,0:T(8,128)(2,1)}, u32[]{:S(2)}, u32[]{:S(2)}) collective-permute-start(bf16[256,4096]{1,0:T(8,128)(2,1)} %bitcast.111), channel_id=1, source_target_pairs={{0,1},{1,0},{2,3},{3,2},{4,5},{5,4},{6,7},{7,6},{8,9},{9,8},{10,11... | collective-permute-start | bytes 6291464 | tf_op jit(solution)/shard_map/ppermute | solution.py:18
  43.6 2.2 %convert_bitcast_fusion.1 = bf16[32,128,2,128]{3,0,1,2:T(8,128)(2,1)} fusion(bf16[26,128,128]{2,1,0:T(8,128)(2,1)S(1)} %bitcast.124, f32[26,32]{1,0:T(8,128)S(1)} %fusion.61, f32[26,2]{0,1:T(2,128)S(1)} %compare_convert_fusion), kind=kOutput, calls=%fused_computation.25 | convolution fusion | flops 55576192 | bytes 2952656 | tf_op jit(solution)/shard_map/kr,kc,kbn->rbcn/dot_general | solution.py:62
  45.8 4.3 %copy.24 = bf16[32,128,2,128]{1,0,3,2:T(8,128)(2,1)S(1)} copy(bf16[32,128,2,128]{3,0,1,2:T(8,128)(2,1)} %convert_bitcast_fusion.1) | data formatting | bytes 4194304 | tf_op jit(solution)/shard_map/convert_element_type | solution.py:66
  51.1 1.9 %collective-permute-start.1 = (bf16[4096,256]{0,1:T(8,128)(2,1)S(1)}, bf16[4096,256]{0,1:T(8,128)(2,1)S(1)}, u32[]{:S(2)}, u32[]{:S(2)}) collective-permute-start(bf16[4096,256]{0,1:T(8,128)(2,1)S(1)} %bitcast.120), channel_id=1, source_target_pairs={{0,1},{1,0},{2,3},{3,2},{4,5},{5,4},{6,7},{7,6},{8,9},{9,8},{10,11... | collective-permute-start | bytes 6291464 | tf_op jit(solution)/shard_map/ppermute | solution.py:18
  53.0 4.7 %pad_maximum_fusion.1 = bf16[4096,512]{0,1:T(8,128)(2,1)} fusion(bf16[4096,256]{0,1:T(8,128)(2,1)} %collective-permute-done.2, bf16[4096,256]{0,1:T(8,128)(2,1)} %bitcast.112), kind=kLoop, calls=%fused_computation.6 | loop fusion | flops 8388608 | bytes 8388608 | tf_op jit(solution)/shard_map/concatenate | solution.py:97
  57.7 4.7 %pad_maximum_fusion.2 = bf16[512,4096]{1,0:T(8,128)(2,1)} fusion(bf16[256,4096]{1,0:T(8,128)(2,1)} %collective-permute-done.3, bf16[256,4096]{1,0:T(8,128)(2,1)} %bitcast.111), kind=kLoop, calls=%fused_computation.7 | loop fusion | flops 8388608 | bytes 8388608 | tf_op jit(solution)/shard_map/concatenate | solution.py:98
  62.5 2.5 %pad_maximum_fusion = bf16[4096,512]{0,1:T(8,128)(2,1)} fusion(bf16[4096,256]{0,1:T(8,128)(2,1)S(1)} %collective-permute-done.1, bf16[4096,256]{0,1:T(8,128)(2,1)S(1)} %bitcast.121), kind=kLoop, calls=%fused_computation.5 | loop fusion | flops 8388608 | bytes 8388608 | tf_op jit(solution)/shard_map/concatenate | solution.py:96
  64.9 20.0 %all-gather.2.cloned.1.call-done = bf16[128,8192]{1,0:T(8,128)(2,1)} async-done(((bf16[16,8192]{1,0:T(8,128)(2,1)}), bf16[128,8192]{1,0:T(8,128)(2,1)}) %all-gather.2.cloned.1.call-update) | async-done | bytes 2097168 | tf_op jit(solution)/shard_map/all_gather | solution.py:25
  85.0 2.4 %collective-permute-start.4 = (bf16[128,8192]{1,0:T(8,128)(2,1)}, bf16[128,8192]{1,0:T(8,128)(2,1)}, u32[]{:S(2)}, u32[]{:S(2)}) collective-permute-start(bf16[128,8192]{1,0:T(8,128)(2,1)} %all-gather.2.cloned.1.call-done), channel_id=1, source_target_pairs={{0,1},{1,0},{2,3},{3,2},{4,5},{5,4},{6,7},{7,6},{8,9},{9,8},{10,11... | collective-permute-start | bytes 6291464 | tf_op jit(solution)/shard_map/ppermute | solution.py:18
  87.4 4.2 %fusion.65 = f32[128,512]{1,0:T(8,128)S(1)} fusion(bf16[512,4096]{1,0:T(8,128)(2,1)} %pad_maximum_fusion.2, bf16[128,8192]{1,0:T(8,128)(2,1)} %all-gather.2.cloned.1.call-done), kind=kOutput, calls=%fused_computation.86 | convolution fusion | flops 536870912 | bytes 5505024 | tf_op jit(solution)/shard_map/dot_general | solution.py:110
  91.6 2.9 %fusion.67 = f32[128,512]{1,0:T(8,128)S(1)} fusion(bf16[4096,512]{0,1:T(8,128)(2,1)S(1)} %copy-done, bf16[128,8192]{1,0:T(8,128)(2,1)} %all-gather.2.cloned.1.call-done), kind=kOutput, calls=%fused_computation.88 | convolution fusion | flops 536870912 | bytes 5505024 | tf_op jit(solution)/shard_map/dot_general | solution.py:105
  96.9 1.9 %fusion = bf16[128,4096]{1,0:T(8,128)(2,1)} fusion(f32[128,4096]{1,0:T(8,128)S(1)} %fusion.76, bf16[128,512]{1,0:T(8,128)(2,1)S(1)} %get-tuple-element.26, bf16[4096,512]{0,1:T(8,128)(2,1)S(1)} %copy-done.1), kind=kOutput, calls=%fused_computation.4 | convolution fusion | flops 537919488 | bytes 7471104 | tf_op jit(solution)/shard_map/dot_general | solution.py:114
  98.9 2.4 %collective-permute-start.7 = (bf16[128,256]{1,0:T(8,128)(2,1)S(1)}, bf16[128,256]{1,0:T(8,128)(2,1)S(1)}, u32[]{:S(2)}, u32[]{:S(2)}) collective-permute-start(bf16[128,256]{1,0:T(8,128)(2,1)S(1)} %get-tuple-element.28), channel_id=1, source_target_pairs={{0,1},{1,0},{2,3},{3,2},{4,5},{5,4},{6,7},{7,6},{8,9},{9,8},{10,11... | collective-permute-start | bytes 196616 | tf_op jit(solution)/shard_map/ppermute | solution.py:18
  101.4 1.9 %collective-permute-start.6 = (bf16[128,256]{1,0:T(8,128)(2,1)S(1)}, bf16[128,256]{1,0:T(8,128)(2,1)S(1)}, u32[]{:S(2)}, u32[]{:S(2)}) collective-permute-start(bf16[128,256]{1,0:T(8,128)(2,1)S(1)} %get-tuple-element.30), channel_id=1, source_target_pairs={{0,1},{1,0},{2,3},{3,2},{4,5},{5,4},{6,7},{7,6},{8,9},{9,8},{10,11... | collective-permute-start | bytes 196616 | tf_op jit(solution)/shard_map/ppermute | solution.py:18
  103.3 2.4 %collective-permute-start.5 = (bf16[128,256]{1,0:T(8,128)(2,1)S(1)}, bf16[128,256]{1,0:T(8,128)(2,1)S(1)}, u32[]{:S(2)}, u32[]{:S(2)}) collective-permute-start(bf16[128,256]{1,0:T(8,128)(2,1)S(1)} %get-tuple-element.32), channel_id=1, source_target_pairs={{0,1},{1,0},{2,3},{3,2},{4,5},{5,4},{6,7},{7,6},{8,9},{9,8},{10,11... | collective-permute-start | bytes 196616 | tf_op jit(solution)/shard_map/ppermute | solution.py:18
  105.7 1.7 %fusion.72 = (bf16[128,4096]{1,0:T(8,128)(2,1)S(1)}, bf16[128,4096]{1,0:T(8,128)(2,1)S(1)}) fusion(bf16[128,8192]{1,0:T(8,128)(2,1)} %collective-permute-done.4), kind=kLoop, calls=%fused_computation.93 | loop fusion | bytes 4194304 | tf_op jit(solution)/shard_map/slice | solution.py:127
  108.7 2.1 %convolution_convert_fusion.1 = bf16[4096,256]{1,0:T(8,128)(2,1)} fusion(bf16[128,4096]{1,0:T(8,128)(2,1)S(1)} %get-tuple-element.23, bf16[128,4096]{1,0:T(8,128)(2,1)S(1)} %get-tuple-element.21, bf16[128,256]{1,0:T(8,128)(2,1)S(1)} %collective-permute-done.6, bf16[128,256]{1,0:T(8,128)(2,1)S(1)} %get-tuple-element.29), kind=kOutput, calls=%fused_computation.1 | convolution fusion | flops 542375936 | bytes 4325376 | tf_op jit(solution)/shard_map/dot_general | solution.py:130
  110.8 4.0 %reshape.98 = bf16[32,128,2,128]{3,2,1,0:T(2,128)(2,1)} reshape(bf16[4096,256]{1,0:T(8,128)(2,1)} %convolution_convert_fusion.1) | data formatting | bytes 4194304 | tf_op jit(solution)/shard_map/reshape | solution.py:76
  114.8 3.1 %fusion.22 = bf16[1,26,128,128]{3,1,2,0:T(8,128)(2,1)S(1)} fusion(bf16[32,128,2,128]{3,2,1,0:T(2,128)(2,1)} %reshape.98, f32[26,32]{1,0:T(8,128)S(1)} %fusion.61, f32[26,2]{0,1:T(2,128)S(1)} %compare_convert_fusion), kind=kOutput, calls=%fused_computation.29 | convolution fusion | flops 54953600 | bytes 2952656 | tf_op jit(solution)/shard_map/kr,kc,rbcn->kbn/dot_general | solution.py:77
  120.9 2.1 %convolution_convert_fusion.2 = bf16[4096,256]{1,0:T(8,128)(2,1)} fusion(bf16[128,4096]{1,0:T(8,128)(2,1)S(1)} %copy-done.6, bf16[128,4096]{1,0:T(8,128)(2,1)S(1)} %get-tuple-element.21, bf16[128,256]{1,0:T(8,128)(2,1)S(1)} %collective-permute-done.5, bf16[128,256]{1,0:T(8,128)(2,1)S(1)} %get-tuple-element.31), kind=kOutput, calls=%fused_computation.2 | convolution fusion | flops 542375936 | bytes 4325376 | tf_op jit(solution)/shard_map/dot_general | solution.py:129
  123.0 2.6 %reshape.97 = bf16[32,128,2,128]{3,2,1,0:T(2,128)(2,1)S(1)} reshape(bf16[4096,256]{1,0:T(8,128)(2,1)} %convolution_convert_fusion.2) | data formatting | bytes 4194304 | tf_op jit(solution)/shard_map/reshape | solution.py:76
  125.6 13.6 %reduce-scatter.2.cloned.1.call-done = bf16[16,4096]{1,0:T(8,128)(2,1)} async-done(((bf16[128,4096]{1,0:T(8,128)(2,1)}), bf16[16,4096]{1,0:T(8,128)(2,1)}) %reduce-scatter.2.cloned.1.call-update) | async-done | bytes 131088 | tf_op jit(solution)/shard_map/reduce_scatter | solution.py:32
  139.3 1.6 all_to_all.14
  140.9 7.4 %all-to-all-start.1 = ((bf16[4,4,4096]{2,1,0:T(4,128)(2,1)}), bf16[4,4,4096]{2,1,0:T(4,128)(2,1)S(1)}, u32[]{:S(2)}, u32[]{:S(2)}) async-start(bf16[4,4,4096]{2,1,0:T(4,128)(2,1)} %all_to_all.14), calls=%async_computation.2 | async-start | bytes 262144 | tf_op jit(solution)/shard_map/all_to_all | solution.py:34
  151.0 5.9 %all-to-all-done.1 = bf16[4,4,4096]{2,1,0:T(4,128)(2,1)S(1)} async-done(((bf16[4,4,4096]{2,1,0:T(4,128)(2,1)}), bf16[4,4,4096]{2,1,0:T(4,128)(2,1)S(1)}, u32[]{:S(2)}, u32[]{:S(2)}) %all-to-all-start.1) | async-done | bytes 131104 | tf_op jit(solution)/shard_map/all_to_all | solution.py:34
  (50 shorter events, 16.4 us)
Async XLA Ops:
  7.2 6.4 %collective-permute-start = (bf16[1,4,4096]{2,1,0:T(4,128)(2,1)}, bf16[1,4,4096]{2,1,0:T(4,128)(2,1)S(1)}, u32[]{:S(2)}, u32[]{:S(2)}) collective-permute-start(bf16[1,4,4096]{2,1,0:T(4,128)(2,1)} %param.7), channel_id=1, source_target_pairs={{64,0},{128,64},{192,128},{256,192},{320,256},{384,320},{448,384},... | collective-permute-start | bytes 98312 | tf_op jit(solution)/shard_map/ppermute | solution.py:13
  15.2 21.8 %all-to-all-start = ((bf16[4,4,8192]{2,1,0:T(4,128)(2,1)}), bf16[4,4,8192]{2,1,0:T(4,128)(2,1)S(1)}, u32[]{:S(2)}, u32[]{:S(2)}) async-start(bf16[4,4,8192]{2,1,0:T(4,128)(2,1)} %tile.2), calls=%async_computation | async-start | bytes 524288 | tf_op jit(solution)/shard_map/all_to_all | solution.py:24
  25.0 59.9 %all-gather.2.cloned.1.call-start = ((), (), s32[]{:S(2)}) async-start(), calls=%async_computation.3 | async-start | bytes 2359296 | tf_op jit(solution)/shard_map/all_gather | solution.py:25
  32.7 5.1 %copy-start.3 = (bf16[1,26,128,128]{3,2,1,0:T(8,128)(2,1)S(1)}, bf16[1,26,128,128]{3,2,1,0:T(8,128)(2,1)}, u32[]{:S(2)}) copy-start(bf16[1,26,128,128]{3,2,1,0:T(8,128)(2,1)} %param.11) | copy-start | bytes 2555908
  35.1 17.9 %collective-permute-start.2 = (bf16[4096,256]{0,1:T(8,128)(2,1)}, bf16[4096,256]{0,1:T(8,128)(2,1)}, u32[]{:S(2)}, u32[]{:S(2)}) collective-permute-start(bf16[4096,256]{0,1:T(8,128)(2,1)} %bitcast.112), channel_id=1, source_target_pairs={{0,1},{1,0},{2,3},{3,2},{4,5},{5,4},{6,7},{7,6},{8,9},{9,8},{10,11... | collective-permute-start | bytes 6291464 | tf_op jit(solution)/shard_map/ppermute | solution.py:18
  37.8 101.4 %reduce-scatter.2.cloned.1.call-start = ((), (), s32[]{:S(2)}) async-start(), calls=%async_computation.4 | async-start | bytes 1179648 | tf_op jit(solution)/shard_map/reduce_scatter | solution.py:32
  38.8 4.8 %copy-start.4 = (bf16[1,26,128,128]{3,2,1,0:T(8,128)(2,1)S(1)}, bf16[1,26,128,128]{3,2,1,0:T(8,128)(2,1)}, u32[]{:S(2)}) copy-start(bf16[1,26,128,128]{3,2,1,0:T(8,128)(2,1)} %param.9) | copy-start | bytes 2555908
  41.1 16.6 %collective-permute-start.3 = (bf16[256,4096]{1,0:T(8,128)(2,1)}, bf16[256,4096]{1,0:T(8,128)(2,1)}, u32[]{:S(2)}, u32[]{:S(2)}) collective-permute-start(bf16[256,4096]{1,0:T(8,128)(2,1)} %bitcast.111), channel_id=1, source_target_pairs={{0,1},{1,0},{2,3},{3,2},{4,5},{5,4},{6,7},{7,6},{8,9},{9,8},{10,11... | collective-permute-start | bytes 6291464 | tf_op jit(solution)/shard_map/ppermute | solution.py:18
  51.1 11.4 %collective-permute-start.1 = (bf16[4096,256]{0,1:T(8,128)(2,1)S(1)}, bf16[4096,256]{0,1:T(8,128)(2,1)S(1)}, u32[]{:S(2)}, u32[]{:S(2)}) collective-permute-start(bf16[4096,256]{0,1:T(8,128)(2,1)S(1)} %bitcast.120), channel_id=1, source_target_pairs={{0,1},{1,0},{2,3},{3,2},{4,5},{5,4},{6,7},{7,6},{8,9},{9,8},{10,11... | collective-permute-start | bytes 6291464 | tf_op jit(solution)/shard_map/ppermute | solution.py:18
  85.0 6.6 %copy-start = (bf16[4096,512]{0,1:T(8,128)(2,1)S(1)}, bf16[4096,512]{0,1:T(8,128)(2,1)}, u32[]{:S(2)}) copy-start(bf16[4096,512]{0,1:T(8,128)(2,1)} %pad_maximum_fusion) | copy-start | bytes 12582916
  85.0 20.7 %collective-permute-start.4 = (bf16[128,8192]{1,0:T(8,128)(2,1)}, bf16[128,8192]{1,0:T(8,128)(2,1)}, u32[]{:S(2)}, u32[]{:S(2)}) collective-permute-start(bf16[128,8192]{1,0:T(8,128)(2,1)} %all-gather.2.cloned.1.call-done), channel_id=1, source_target_pairs={{0,1},{1,0},{2,3},{3,2},{4,5},{5,4},{6,7},{7,6},{8,9},{9,8},{10,11... | collective-permute-start | bytes 6291464 | tf_op jit(solution)/shard_map/ppermute | solution.py:18
  87.4 7.1 %copy-start.2 = (bf16[128,8192]{1,0:T(8,128)(2,1)S(1)}, bf16[128,8192]{1,0:T(8,128)(2,1)}, u32[]{:S(2)}) copy-start(bf16[128,8192]{1,0:T(8,128)(2,1)} %all-gather.2.cloned.1.call-done) | copy-start | bytes 6291460
  91.6 2.9 %copy-start.1 = (bf16[4096,512]{0,1:T(8,128)(2,1)S(1)}, bf16[4096,512]{0,1:T(8,128)(2,1)}, u32[]{:S(2)}) copy-start(bf16[4096,512]{0,1:T(8,128)(2,1)} %pad_maximum_fusion.1) | copy-start | bytes 12582916
  98.9 8.5 %collective-permute-start.7 = (bf16[128,256]{1,0:T(8,128)(2,1)S(1)}, bf16[128,256]{1,0:T(8,128)(2,1)S(1)}, u32[]{:S(2)}, u32[]{:S(2)}) collective-permute-start(bf16[128,256]{1,0:T(8,128)(2,1)S(1)} %get-tuple-element.28), channel_id=1, source_target_pairs={{0,1},{1,0},{2,3},{3,2},{4,5},{5,4},{6,7},{7,6},{8,9},{9,8},{10,11... | collective-permute-start | bytes 196616 | tf_op jit(solution)/shard_map/ppermute | solution.py:18
  101.4 7.3 %collective-permute-start.6 = (bf16[128,256]{1,0:T(8,128)(2,1)S(1)}, bf16[128,256]{1,0:T(8,128)(2,1)S(1)}, u32[]{:S(2)}, u32[]{:S(2)}) collective-permute-start(bf16[128,256]{1,0:T(8,128)(2,1)S(1)} %get-tuple-element.30), channel_id=1, source_target_pairs={{0,1},{1,0},{2,3},{3,2},{4,5},{5,4},{6,7},{7,6},{8,9},{9,8},{10,11... | collective-permute-start | bytes 196616 | tf_op jit(solution)/shard_map/ppermute | solution.py:18
  103.3 17.6 %collective-permute-start.5 = (bf16[128,256]{1,0:T(8,128)(2,1)S(1)}, bf16[128,256]{1,0:T(8,128)(2,1)S(1)}, u32[]{:S(2)}, u32[]{:S(2)}) collective-permute-start(bf16[128,256]{1,0:T(8,128)(2,1)S(1)} %get-tuple-element.32), channel_id=1, source_target_pairs={{0,1},{1,0},{2,3},{3,2},{4,5},{5,4},{6,7},{7,6},{8,9},{9,8},{10,11... | collective-permute-start | bytes 196616 | tf_op jit(solution)/shard_map/ppermute | solution.py:18
  107.4 1.3 copy-start.5
  118.5 2.5 %copy-start.6 = (bf16[128,4096]{1,0:T(8,128)(2,1)S(1)}, bf16[128,4096]{1,0:T(8,128)(2,1)}, u32[]{:S(2)}) copy-start(bf16[128,4096]{1,0:T(8,128)(2,1)} %copy-done.5) | copy-start | bytes 3145732
  140.9 16.1 %all-to-all-start.1 = ((bf16[4,4,4096]{2,1,0:T(4,128)(2,1)}), bf16[4,4,4096]{2,1,0:T(4,128)(2,1)S(1)}, u32[]{:S(2)}, u32[]{:S(2)}) async-start(bf16[4,4,4096]{2,1,0:T(4,128)(2,1)} %all_to_all.14), calls=%async_computation.2 | async-start | bytes 262144 | tf_op jit(solution)/shard_map/all_to_all | solution.py:34
Sparse Core Ops, SparseCore 0:
  37.9 47.0 all-gather.1
  98.9 40.3 reduce-scatter.1

commit v16 on v12

--- a/solution.py
+++ b/solution.py
@@ -27,8 +27,8 @@
     return (block, shifted(block, "core", 1)), weights
 
 
-def scatter_rows(own, other):
-    block = (own + shifted(other, "core", 1)).astype(jnp.bfloat16)
+def scatter_rows(block):
+    block = block.astype(jnp.bfloat16)
     block = lax.psum_scatter(block, "y", scatter_dimension=0, tiled=True)
     n = lax.axis_size("zh")
     got = lax.all_to_all(block, "zh", 0, 0, tiled=True).astype(jnp.float32)
@@ -93,36 +93,42 @@
     w_down = dense_down(down_blocks[0])
 
     incoming = passed_along(grad_sent, "section", -1)
-    halves, (w_gate, w_up, w_down) = gather_rows(
-        jnp.concatenate([saved_input[0], incoming[0]], axis=1), (w_gate, w_up, w_down)
+    weights = (w_gate, w_up, w_down)
+    partner_weights = tuple(shifted(w, "core", 1) for w in weights)
+    (both, other_rows), (weights, partner_weights) = gather_rows(
+        jnp.concatenate([saved_input[0], incoming[0]], axis=1), (weights, partner_weights)
     )
     f32 = jnp.float32
     hid_t = (((1,), (1,)), ((), ()))
+    inputs, upstream = both[:, :width], both[:, width:]
 
-    def rows_part(both):
-        inputs, upstream = both[:, :width], both[:, width:]
-        gate = jnp.dot(inputs, w_gate, preferred_element_type=f32)
-        up = jnp.dot(inputs, w_up, preferred_element_type=f32)
+    def units_part(wg, wu, wd):
+        gate = jnp.dot(inputs, wg, preferred_element_type=f32)
+        up = jnp.dot(inputs, wu, preferred_element_type=f32)
         sig = jax.nn.sigmoid(gate)
         act = gate * sig
         hidden = (act * up).astype(jnp.bfloat16)
-        dhid = lax.dot_general(upstream, w_down, hid_t, preferred_element_type=f32)
+        dhid = lax.dot_general(upstream, wd, hid_t, preferred_element_type=f32)
         grad_up_act = (dhid * act).astype(jnp.bfloat16)
         grad_gate_act = (dhid * up * sig * (1.0 + gate * (1.0 - sig))).astype(jnp.bfloat16)
-        term = lax.dot_general(grad_gate_act, w_gate, hid_t, preferred_element_type=f32)
-        term = term + lax.dot_general(grad_up_act, w_up, hid_t, preferred_element_type=f32)
-        return term, (inputs, upstream, hidden, grad_gate_act, grad_up_act)
+        term = lax.dot_general(grad_gate_act, wg, hid_t, preferred_element_type=f32)
+        term = term + lax.dot_general(grad_up_act, wu, hid_t, preferred_element_type=f32)
+        return term, (grad_gate_act, grad_up_act, hidden)
 
-    term_own, saved_own = rows_part(halves[0])
-    term_other, saved_other = rows_part(halves[1])
-    inputs, upstream, hidden, grad_gate_act, grad_up_act = (
-        jnp.concatenate(pair, axis=0) for pair in zip(saved_own, saved_other)
+    term_own, acts_own = units_part(*weights)
+    term_partner, acts_partner = units_part(*partner_weights)
+    summed = scatter_rows(term_own + term_partner)
+
+    grad_gate_act, grad_up_act, hidden = (
+        jnp.concatenate([mine, shifted(theirs, "core", 1)], axis=0)
+        for mine, theirs in zip(acts_own, acts_partner)
     )
+    inputs = jnp.concatenate([inputs, other_rows[:, :width]], axis=0)
+    upstream = jnp.concatenate([upstream, other_rows[:, width:]], axis=0)
     rows_t = (((0,), (0,)), ((), ()))
     tiles_gate = kept_in(lax.dot_general(inputs, grad_gate_act, rows_t, preferred_element_type=f32))
     tiles_up = kept_in(lax.dot_general(inputs, grad_up_act, rows_t, preferred_element_type=f32))
     tiles_down = kept_down(lax.dot_general(hidden, upstream, rows_t, preferred_element_type=f32))
-    summed = scatter_rows(term_own, term_other)
     grad_input = summed.astype(jnp.bfloat16)[None]
     return (grad_input, tiles_gate[None], tiles_up[None], tiles_down[None])
 

time: 164 us -> 181 us (1.10)
  matrix products: 21.6 us -> 35.7 us
  waiting for transfers between devices: 56.6 us -> 44.3 us
  starting transfers between devices: 16.5 us -> 27.2 us
  local copies, waits for them, and re-layouts: 31.7 us -> 35.4 us
    all_gather x1, waiting for transfers between devices: 20.7 us -> 7.91 us  [gather_rows(): block = lax.all_gather(block, 'y', axis=0, tiled=True)]
    ppermute x2 -> x7, starting transfers between devices: 4.26 us -> 15.1 us  [shifted(): return lax.ppermute(block, axis, [(i, (i + shift) % n) for i in range(n)])]
    dot_general x10, matrix products: 10.3 us -> 18.8 us  [the longest x2 5.46 us: units_part(): dhid = lax.dot_general(upstream, wd, hid_t, preferred_element_type=f32)]
    reduce_scatter x1, waiting for transfers between devices: 22.9 us -> 30.4 us  [scatter_rows(): block = lax.psum_scatter(block, 'y', scatter_dimension=0, tiled=True)]
    reshape x1 -> x0, local copies, waits for them, and re-layouts: 6.13 us -> none  [dense_down(): return placed.astype(jnp.bfloat16).reshape(hidden_units, width)]
    all_to_all x1, waiting for transfers between devices: 5.94 us -> 0.01 us  [scatter_rows(): got = lax.all_to_all(block, 'zh', 0, 0, tiled=True).astype(jnp.float32)]
    unnamed x33, local copies, waits for them, and re-layouts: 10.1 us -> 14.7 us
    slice x2, local copies, waits for them, and re-layouts: 0.36 us -> 2.82 us  [the longest x1 1.68 us: per_device(): upstream = jnp.concatenate([upstream, other_rows[:, width:]], axis=0)]
  transfers between devices with their start and end apart: 6 -> 11, of which waited for: 6 -> 4; matrix products, arithmetic and copies ran while one was open for 25% -> 27% of each run, Pallas kernels for 0% -> 0%
where the time goes in v16:
time: 181 us; the launch traced here: 180 us
  waiting for transfers between devices  44.3 us (24%)
  matrix products  35.7 us (20%)
  local copies, waits for them, and re-layouts  35.4 us (20%)
  starting transfers between devices  27.2 us (15%)
  blocking collectives  20.7 us (11%)
  between operations  14.4 us (8%)
  other arithmetic  2.2 us (1%)
    reduce_scatter x1, waiting for transfers between devices, scatter_rows(): block = lax.psum_scatter(block, 'y', scatter_dimension=0, tiled=True)  30.4 us
    all_to_all x1, blocking collectives, gather_rows(): block = lax.all_to_all(copies, 'zh', 0, 0, tiled=True)  20.7 us
    ppermute x7, starting transfers between devices, shifted(): return lax.ppermute(block, axis, [(i, (i + shift) % n) for i in range(n)])  15.1 us
    unnamed x33, local copies, waits for them, and re-layouts  14.7 us
    convert_element_type x2, local copies, waits for them, and re-layouts, dense_in(): return placed.astype(jnp.bfloat16).reshape(width, hidden_units)  8.98 us
    all_gather x1, waiting for transfers between devices, gather_rows(): block = lax.all_gather(block, 'y', axis=0, tiled=True)  7.91 us
    all_to_all x1, starting transfers between devices, scatter_rows(): got = lax.all_to_all(block, 'zh', 0, 0, tiled=True).astype(jnp.float32)  7.37 us
    reshape x2, local copies, waits for them, and re-layouts, kept_in(): tiles = dense.astype(jnp.bfloat16).reshape(bands, block, columns, block)  6.53 us
  transfers between devices with their start and end apart: 11, of which 4 were waited for; matrix products, arithmetic and copies ran while one was open for 27% of the time, Pallas kernels for 0%

profile of v16, /device:TPU:6, one launch (start us, length us, event | category | flops | bytes accessed | tf_op | source)
XLA Modules:
  0.0 179.9 jit_solution(4896209089340388971)
XLA Ops:
  7.2 4.7 %collective-permute-start = (bf16[1,4,4096]{2,1,0:T(4,128)(2,1)}, bf16[1,4,4096]{2,1,0:T(4,128)(2,1)S(1)}, u32[]{:S(2)}, u32[]{:S(2)}) collective-permute-start(bf16[1,4,4096]{2,1,0:T(4,128)(2,1)} %param.7), channel_id=1, source_target_pairs={{64,0},{128,64},{192,128},{256,192},{320,256},{384,320},{448,384},... | collective-permute-start | bytes 98312 | tf_op jit(solution)/shard_map/ppermute | solution.py:13
  11.9 1.9 %collective-permute-done = bf16[1,4,4096]{2,1,0:T(4,128)(2,1)S(1)} collective-permute-done((bf16[1,4,4096]{2,1,0:T(4,128)(2,1)}, bf16[1,4,4096]{2,1,0:T(4,128)(2,1)S(1)}, u32[]{:S(2)}, u32[]{:S(2)}) %collective-permute-start) | collective-permute-done | bytes 32800 | tf_op jit(solution)/shard_map/ppermute | solution.py:13
  14.7 20.7 %all_to_all.18 = bf16[4,4,8192]{2,1,0:T(4,128)(2,1)S(1)} all-to-all(bf16[4,4,8192]{2,1,0:T(4,128)(2,1)S(1)} %tile.2), channel_id=1, replica_groups=mesh['section'=8,'y'=8,'zh'=4,'core'=2] {'zh'}, dimensions={0} | all-to-all | bytes 524288 | tf_op jit(solution)/shard_map/all_to_all | solution.py:24
  37.9 2.4 %copy.79 = bf16[32,8,32,128]{3,1,2,0:T(8,128)(2,1)} copy(bf16[32,8,32,128]{3,2,1,0:T(8,128)(2,1)S(1)} %bitcast.132) | data formatting | bytes 4194304
  40.2 1.9 %collective-permute-start.3 = (bf16[256,4096]{1,0:T(8,128)(2,1)}, bf16[256,4096]{1,0:T(8,128)(2,1)}, u32[]{:S(2)}, u32[]{:S(2)}) collective-permute-start(bf16[256,4096]{1,0:T(8,128)(2,1)} %bitcast.118), channel_id=1, source_target_pairs={{0,1},{1,0},{2,3},{3,2},{4,5},{5,4},{6,7},{7,6},{8,9},{9,8},{10,11... | collective-permute-start | bytes 6291464 | tf_op jit(solution)/shard_map/ppermute | solution.py:18
  43.1 3.9 %copy.27 = bf16[32,128,2,128]{1,0,3,2:T(8,128)(2,1)} copy(bf16[32,128,2,128]{3,0,1,2:T(8,128)(2,1)S(1)} %convert_bitcast_fusion) | data formatting | bytes 4194304 | tf_op jit(solution)/shard_map/convert_element_type | solution.py:66
  46.9 2.7 %copy.80 = bf16[32,8,32,128]{3,1,2,0:T(8,128)(2,1)S(1)} copy(bf16[32,8,32,128]{3,2,1,0:T(8,128)(2,1)} %bitcast.130) | data formatting | bytes 4194304
  49.7 2.4 %collective-permute-start.2 = (bf16[4096,256]{0,1:T(8,128)(2,1)S(1)}, bf16[4096,256]{0,1:T(8,128)(2,1)}, u32[]{:S(2)}, u32[]{:S(2)}) collective-permute-start(bf16[4096,256]{0,1:T(8,128)(2,1)S(1)} %bitcast.126), channel_id=1, source_target_pairs={{0,1},{1,0},{2,3},{3,2},{4,5},{5,4},{6,7},{7,6},{8,9},{9,8},{10,11... | collective-permute-start | bytes 6291464 | tf_op jit(solution)/shard_map/ppermute | solution.py:18
  52.1 2.3 %convert_bitcast_fusion.1 = bf16[32,128,2,128]{3,0,1,2:T(8,128)(2,1)} fusion(bf16[26,128,128]{2,1,0:T(8,128)(2,1)S(1)} %bitcast.135, f32[26,32]{1,0:T(8,128)S(1)} %fusion.63, f32[26,2]{0,1:T(2,128)S(1)} %compare_convert_fusion), kind=kOutput, calls=%fused_computation.24 | convolution fusion | flops 55576192 | bytes 2952656 | tf_op jit(solution)/shard_map/kr,kc,kbn->rbcn/dot_general | solution.py:62
  54.4 5.1 %copy.24 = bf16[32,128,2,128]{1,0,3,2:T(8,128)(2,1)} copy(bf16[32,128,2,128]{3,0,1,2:T(8,128)(2,1)} %convert_bitcast_fusion.1) | data formatting | bytes 4194304 | tf_op jit(solution)/shard_map/convert_element_type | solution.py:66
  59.5 2.6 %copy.81 = bf16[32,8,32,128]{3,1,2,0:T(8,128)(2,1)S(1)} copy(bf16[32,8,32,128]{3,2,1,0:T(8,128)(2,1)} %bitcast.131) | data formatting | bytes 4194304
  63.4 2.1 %collective-permute-start.1 = (bf16[4096,256]{0,1:T(8,128)(2,1)S(1)}, bf16[4096,256]{0,1:T(8,128)(2,1)}, u32[]{:S(2)}, u32[]{:S(2)}) collective-permute-start(bf16[4096,256]{0,1:T(8,128)(2,1)S(1)} %bitcast.123), channel_id=1, source_target_pairs={{0,1},{1,0},{2,3},{3,2},{4,5},{5,4},{6,7},{7,6},{8,9},{9,8},{10,11... | collective-permute-start | bytes 6291464 | tf_op jit(solution)/shard_map/ppermute | solution.py:18
  65.5 4.0 %collective-permute-done.1 = bf16[4096,256]{0,1:T(8,128)(2,1)} collective-permute-done((bf16[4096,256]{0,1:T(8,128)(2,1)S(1)}, bf16[4096,256]{0,1:T(8,128)(2,1)}, u32[]{:S(2)}, u32[]{:S(2)}) %collective-permute-start.1) | collective-permute-done | bytes 2097184 | tf_op jit(solution)/shard_map/ppermute | solution.py:18
  69.6 7.9 %all-gather.2.cloned.1.call-done = bf16[128,8192]{1,0:T(8,128)(2,1)} async-done(((bf16[16,8192]{1,0:T(8,128)(2,1)}), bf16[128,8192]{1,0:T(8,128)(2,1)}) %all-gather.2.cloned.1.call-update) | async-done | bytes 2097168 | tf_op jit(solution)/shard_map/all_gather | solution.py:25
  77.5 2.9 %fusion.69 = f32[128,256]{1,0:T(8,128)S(1)} fusion(bf16[256,4096]{1,0:T(8,128)(2,1)} %bitcast.118, bf16[128,8192]{1,0:T(8,128)(2,1)} %all-gather.2.cloned.1.call-done), kind=kOutput, calls=%fused_computation.92 | convolution fusion | flops 268435456 | bytes 3276800 | tf_op jit(solution)/shard_map/dot_general | solution.py:111
  80.4 2.6 %fusion.67 = f32[128,256]{1,0:T(8,128)S(1)} fusion(bf16[256,4096]{1,0:T(8,128)(2,1)} %collective-permute-done.3, bf16[128,8192]{1,0:T(8,128)(2,1)S(1)} %copy-done), kind=kOutput, calls=%fused_computation.90 | convolution fusion | flops 268435456 | bytes 3276800 | tf_op jit(solution)/shard_map/dot_general | solution.py:111
  85.9 2.4 %fusion.71 = f32[128,256]{1,0:T(8,128)S(1)} fusion(bf16[4096,256]{0,1:T(8,128)(2,1)} %collective-permute-done.1, bf16[128,8192]{1,0:T(8,128)(2,1)S(1)} %copy-done), kind=kOutput, calls=%fused_computation.94 | convolution fusion | flops 268435456 | bytes 3276800 | tf_op jit(solution)/shard_map/dot_general | solution.py:106
  88.3 3.1 %multiply_convert_fusion = (bf16[128,256]{1,0:T(8,128)(2,1)}, bf16[128,256]{1,0:T(8,128)(2,1)}, bf16[128,256]{1,0:T(8,128)(2,1)S(1)}) fusion(f32[128,256]{1,0:T(8,128)S(1)} %fusion.71, f32[128,256]{1,0:T(8,128)S(1)} %fusion.67, bf16[4096,256]{0,1:T(8,128)(2,1)} %collective-permute-done.2, bf16[128,8192]{1,0:T(8,128)(2,1)S(1)} %copy-done), kind=kOutput, calls=%fused_computation.45 | convolution fusion | flops 268926976 | bytes 3604480 | tf_op jit(solution)/shard_map/dot_general | solution.py:107
  91.4 2.0 %fusion.82 = f32[128,4096]{1,0:T(8,128)S(1)} fusion(bf16[128,256]{1,0:T(8,128)(2,1)S(1)} %get-tuple-element.35, bf16[4096,256]{0,1:T(8,128)(2,1)} %collective-permute-done.2), kind=kOutput, calls=%fused_computation.105 | convolution fusion | flops 268435456 | bytes 4259840 | tf_op jit(solution)/shard_map/dot_general | solution.py:115
  93.4 2.1 %convolution_add_fusion = f32[128,4096]{1,0:T(8,128)S(1)} fusion(f32[128,4096]{1,0:T(8,128)S(1)} %fusion.82, bf16[128,256]{1,0:T(8,128)(2,1)} %get-tuple-element.34, bf16[4096,256]{0,1:T(8,128)(2,1)} %collective-permute-done.1), kind=kOutput, calls=%fused_computation.3 | convolution fusion | flops 268959744 | bytes 6356992 | tf_op jit(solution)/shard_map/dot_general | solution.py:114
  97.2 1.9 %collective-permute-start.4 = (bf16[128,8192]{1,0:T(8,128)(2,1)S(1)}, bf16[128,8192]{1,0:T(8,128)(2,1)}, u32[]{:S(2)}, u32[]{:S(2)}) collective-permute-start(bf16[128,8192]{1,0:T(8,128)(2,1)S(1)} %copy-done), channel_id=1, source_target_pairs={{0,1},{1,0},{2,3},{3,2},{4,5},{5,4},{6,7},{7,6},{8,9},{9,8},{10,11... | collective-permute-start | bytes 6291464 | tf_op jit(solution)/shard_map/ppermute | solution.py:18
  99.1 2.4 %collective-permute-start.5 = (bf16[128,256]{1,0:T(8,128)(2,1)}, bf16[128,256]{1,0:T(8,128)(2,1)}, u32[]{:S(2)}, u32[]{:S(2)}) collective-permute-start(bf16[128,256]{1,0:T(8,128)(2,1)} %get-tuple-element.34), channel_id=1, source_target_pairs={{0,1},{1,0},{2,3},{3,2},{4,5},{5,4},{6,7},{7,6},{8,9},{9,8},{10,11... | collective-permute-start | bytes 196616 | tf_op jit(solution)/shard_map/ppermute | solution.py:18
  101.5 1.9 %collective-permute-start.6 = (bf16[128,256]{1,0:T(8,128)(2,1)S(1)}, bf16[128,256]{1,0:T(8,128)(2,1)}, u32[]{:S(2)}, u32[]{:S(2)}) collective-permute-start(bf16[128,256]{1,0:T(8,128)(2,1)S(1)} %get-tuple-element.35), channel_id=1, source_target_pairs={{0,1},{1,0},{2,3},{3,2},{4,5},{5,4},{6,7},{7,6},{8,9},{9,8},{10,11... | collective-permute-start | bytes 196616 | tf_op jit(solution)/shard_map/ppermute | solution.py:18
  103.4 2.4 %collective-permute-start.7 = (bf16[128,256]{1,0:T(8,128)(2,1)}, bf16[128,256]{1,0:T(8,128)(2,1)}, u32[]{:S(2)}, u32[]{:S(2)}) collective-permute-start(bf16[128,256]{1,0:T(8,128)(2,1)} %get-tuple-element.33), channel_id=1, source_target_pairs={{0,1},{1,0},{2,3},{3,2},{4,5},{5,4},{6,7},{7,6},{8,9},{9,8},{10,11... | collective-permute-start | bytes 196616 | tf_op jit(solution)/shard_map/ppermute | solution.py:18
  107.0 30.4 %reduce-scatter.2.cloned.1.call-done = bf16[16,4096]{1,0:T(8,128)(2,1)} async-done(((bf16[128,4096]{1,0:T(8,128)(2,1)}), bf16[16,4096]{1,0:T(8,128)(2,1)}) %reduce-scatter.2.cloned.1.call-update) | async-done | bytes 131088 | tf_op jit(solution)/shard_map/reduce_scatter | solution.py:32
  139.0 7.4 %all-to-all-start.1 = ((bf16[4,4,4096]{2,1,0:T(4,128)(2,1)}), bf16[4,4,4096]{2,1,0:T(4,128)(2,1)S(1)}, u32[]{:S(2)}, u32[]{:S(2)}) async-start(bf16[4,4,4096]{2,1,0:T(4,128)(2,1)} %all_to_all.14), calls=%async_computation.2 | async-start | bytes 262144 | tf_op jit(solution)/shard_map/all_to_all | solution.py:34
  146.4 1.7 fusion.80
  151.0 3.0 %convolution_convert_fusion.2 = bf16[4096,256]{1,0:T(8,128)(2,1)} fusion(bf16[128,4096]{1,0:T(8,128)(2,1)S(1)} %get-tuple-element.29, bf16[128,4096]{1,0:T(8,128)(2,1)S(1)} %copy-done.8, bf16[128,256]{1,0:T(8,128)(2,1)} %collective-permute-done.5, bf16[128,256]{1,0:T(8,128)(2,1)S(1)} %get-tuple-element.31), kind=kOutput, calls=%fused_computation.2 | convolution fusion | flops 542375936 | bytes 4325376 | tf_op jit(solution)/shard_map/dot_general | solution.py:129
  154.0 4.0 %reshape.97 = bf16[32,128,2,128]{3,2,1,0:T(2,128)(2,1)} reshape(bf16[4096,256]{1,0:T(8,128)(2,1)} %convolution_convert_fusion.2) | data formatting | bytes 4194304 | tf_op jit(solution)/shard_map/reshape | solution.py:76
  158.0 3.1 %fusion.20 = bf16[1,26,128,128]{3,1,2,0:T(8,128)(2,1)S(1)} fusion(bf16[32,128,2,128]{3,2,1,0:T(2,128)(2,1)} %reshape.97, f32[26,32]{1,0:T(8,128)S(1)} %fusion.63, f32[26,2]{0,1:T(2,128)S(1)} %copy-done.12), kind=kOutput, calls=%fused_computation.27 | convolution fusion | flops 54953600 | bytes 2952656 | tf_op jit(solution)/shard_map/kr,kc,rbcn->kbn/dot_general | solution.py:77
  164.1 3.0 %convolution_convert_fusion.1 = bf16[4096,256]{1,0:T(8,128)(2,1)} fusion(bf16[128,4096]{1,0:T(8,128)(2,1)S(1)} %copy-done.10, bf16[128,4096]{1,0:T(8,128)(2,1)S(1)} %copy-done.8, bf16[128,256]{1,0:T(8,128)(2,1)} %collective-permute-done.6, bf16[128,256]{1,0:T(8,128)(2,1)S(1)} %get-tuple-element.32), kind=kOutput, calls=%fused_computation.1 | convolution fusion | flops 542375936 | bytes 4325376 | tf_op jit(solution)/shard_map/dot_general | solution.py:130
  167.1 2.5 %reshape.98 = bf16[32,128,2,128]{3,2,1,0:T(2,128)(2,1)S(1)} reshape(bf16[4096,256]{1,0:T(8,128)(2,1)} %convolution_convert_fusion.1) | data formatting | bytes 4194304 | tf_op jit(solution)/shard_map/reshape | solution.py:76
  (60 shorter events, 22.1 us)
Async XLA Ops:
  7.2 29.8 %copy-start.5 = (bf16[1,26,128,128]{3,2,1,0:T(8,128)(2,1)S(1)}, bf16[1,26,128,128]{3,2,1,0:T(8,128)(2,1)}, u32[]{:S(2)}) copy-start(bf16[1,26,128,128]{3,2,1,0:T(8,128)(2,1)} %param.11) | copy-start | bytes 2555908
  7.2 70.3 %all-gather.2.cloned.1.call-start = ((), (), s32[]{:S(2)}) async-start(), calls=%async_computation.3 | async-start | bytes 2359296 | tf_op jit(solution)/shard_map/all_gather | solution.py:25
  7.2 6.6 %collective-permute-start = (bf16[1,4,4096]{2,1,0:T(4,128)(2,1)}, bf16[1,4,4096]{2,1,0:T(4,128)(2,1)S(1)}, u32[]{:S(2)}, u32[]{:S(2)}) collective-permute-start(bf16[1,4,4096]{2,1,0:T(4,128)(2,1)} %param.7), channel_id=1, source_target_pairs={{64,0},{128,64},{192,128},{256,192},{320,256},{384,320},{448,384},... | collective-permute-start | bytes 98312 | tf_op jit(solution)/shard_map/ppermute | solution.py:13
  36.1 101.3 %reduce-scatter.2.cloned.1.call-start = ((), (), s32[]{:S(2)}) async-start(), calls=%async_computation.4 | async-start | bytes 1179648 | tf_op jit(solution)/shard_map/reduce_scatter | solution.py:32
  36.9 15.2 %copy-start.11 = (f32[26,2]{0,1:T(2,128)}, f32[26,2]{0,1:T(2,128)S(1)}, u32[]{:S(2)}) copy-start(f32[26,2]{0,1:T(2,128)S(1)} %compare_convert_fusion) | copy-start | bytes 628
  37.8 4.3 %copy-start.6 = (bf16[1,26,128,128]{3,2,1,0:T(8,128)(2,1)S(1)}, bf16[1,26,128,128]{3,2,1,0:T(8,128)(2,1)}, u32[]{:S(2)}) copy-start(bf16[1,26,128,128]{3,2,1,0:T(8,128)(2,1)} %param.10) | copy-start | bytes 2555908
  40.2 25.3 %collective-permute-start.3 = (bf16[256,4096]{1,0:T(8,128)(2,1)}, bf16[256,4096]{1,0:T(8,128)(2,1)}, u32[]{:S(2)}, u32[]{:S(2)}) collective-permute-start(bf16[256,4096]{1,0:T(8,128)(2,1)} %bitcast.118), channel_id=1, source_target_pairs={{0,1},{1,0},{2,3},{3,2},{4,5},{5,4},{6,7},{7,6},{8,9},{9,8},{10,11... | collective-permute-start | bytes 6291464 | tf_op jit(solution)/shard_map/ppermute | solution.py:18
  46.9 5.2 %copy-start.7 = (bf16[1,26,128,128]{3,2,1,0:T(8,128)(2,1)S(1)}, bf16[1,26,128,128]{3,2,1,0:T(8,128)(2,1)}, u32[]{:S(2)}) copy-start(bf16[1,26,128,128]{3,2,1,0:T(8,128)(2,1)} %param.9) | copy-start | bytes 2555908
  49.7 9.8 %copy-start.3 = (bf16[32,8,32,128]{3,1,2,0:T(8,128)(2,1)}, bf16[32,8,32,128]{3,1,2,0:T(8,128)(2,1)S(1)}, u32[]{:S(2)}) copy-start(bf16[32,8,32,128]{3,1,2,0:T(8,128)(2,1)S(1)} %copy.80) | copy-start | bytes 6291460
  49.7 15.8 %collective-permute-start.2 = (bf16[4096,256]{0,1:T(8,128)(2,1)S(1)}, bf16[4096,256]{0,1:T(8,128)(2,1)}, u32[]{:S(2)}, u32[]{:S(2)}) collective-permute-start(bf16[4096,256]{0,1:T(8,128)(2,1)S(1)} %bitcast.126), channel_id=1, source_target_pairs={{0,1},{1,0},{2,3},{3,2},{4,5},{5,4},{6,7},{7,6},{8,9},{9,8},{10,11... | collective-permute-start | bytes 6291464 | tf_op jit(solution)/shard_map/ppermute | solution.py:18
  62.1 1.3 copy-start.1
  63.4 6.2 %collective-permute-start.1 = (bf16[4096,256]{0,1:T(8,128)(2,1)S(1)}, bf16[4096,256]{0,1:T(8,128)(2,1)}, u32[]{:S(2)}, u32[]{:S(2)}) collective-permute-start(bf16[4096,256]{0,1:T(8,128)(2,1)S(1)} %bitcast.123), channel_id=1, source_target_pairs={{0,1},{1,0},{2,3},{3,2},{4,5},{5,4},{6,7},{7,6},{8,9},{9,8},{10,11... | collective-permute-start | bytes 6291464 | tf_op jit(solution)/shard_map/ppermute | solution.py:18
  77.5 2.9 %copy-start = (bf16[128,8192]{1,0:T(8,128)(2,1)S(1)}, bf16[128,8192]{1,0:T(8,128)(2,1)}, u32[]{:S(2)}) copy-start(bf16[128,8192]{1,0:T(8,128)(2,1)} %all-gather.2.cloned.1.call-done) | copy-start | bytes 6291460
  80.4 2.6 %copy-start.2 = (bf16[32,8,32,128]{3,1,2,0:T(8,128)(2,1)S(1)}, bf16[32,8,32,128]{3,1,2,0:T(8,128)(2,1)}, u32[]{:S(2)}) copy-start(bf16[32,8,32,128]{3,1,2,0:T(8,128)(2,1)} %copy-done.1) | copy-start | bytes 6291460
  83.0 1.6 copy-start.4
  97.2 49.3 %collective-permute-start.4 = (bf16[128,8192]{1,0:T(8,128)(2,1)S(1)}, bf16[128,8192]{1,0:T(8,128)(2,1)}, u32[]{:S(2)}, u32[]{:S(2)}) collective-permute-start(bf16[128,8192]{1,0:T(8,128)(2,1)S(1)} %copy-done), channel_id=1, source_target_pairs={{0,1},{1,0},{2,3},{3,2},{4,5},{5,4},{6,7},{7,6},{8,9},{9,8},{10,11... | collective-permute-start | bytes 6291464 | tf_op jit(solution)/shard_map/ppermute | solution.py:18
  99.1 51.2 %collective-permute-start.5 = (bf16[128,256]{1,0:T(8,128)(2,1)}, bf16[128,256]{1,0:T(8,128)(2,1)}, u32[]{:S(2)}, u32[]{:S(2)}) collective-permute-start(bf16[128,256]{1,0:T(8,128)(2,1)} %get-tuple-element.34), channel_id=1, source_target_pairs={{0,1},{1,0},{2,3},{3,2},{4,5},{5,4},{6,7},{7,6},{8,9},{9,8},{10,11... | collective-permute-start | bytes 196616 | tf_op jit(solution)/shard_map/ppermute | solution.py:18
  101.5 62.6 %collective-permute-start.6 = (bf16[128,256]{1,0:T(8,128)(2,1)S(1)}, bf16[128,256]{1,0:T(8,128)(2,1)}, u32[]{:S(2)}, u32[]{:S(2)}) collective-permute-start(bf16[128,256]{1,0:T(8,128)(2,1)S(1)} %get-tuple-element.35), channel_id=1, source_target_pairs={{0,1},{1,0},{2,3},{3,2},{4,5},{5,4},{6,7},{7,6},{8,9},{9,8},{10,11... | collective-permute-start | bytes 196616 | tf_op jit(solution)/shard_map/ppermute | solution.py:18
  103.4 44.7 %collective-permute-start.7 = (bf16[128,256]{1,0:T(8,128)(2,1)}, bf16[128,256]{1,0:T(8,128)(2,1)}, u32[]{:S(2)}, u32[]{:S(2)}) collective-permute-start(bf16[128,256]{1,0:T(8,128)(2,1)} %get-tuple-element.33), channel_id=1, source_target_pairs={{0,1},{1,0},{2,3},{3,2},{4,5},{5,4},{6,7},{7,6},{8,9},{9,8},{10,11... | collective-permute-start | bytes 196616 | tf_op jit(solution)/shard_map/ppermute | solution.py:18
  139.0 33.4 %all-to-all-start.1 = ((bf16[4,4,4096]{2,1,0:T(4,128)(2,1)}), bf16[4,4,4096]{2,1,0:T(4,128)(2,1)S(1)}, u32[]{:S(2)}, u32[]{:S(2)}) async-start(bf16[4,4,4096]{2,1,0:T(4,128)(2,1)} %all_to_all.14), calls=%async_computation.2 | async-start | bytes 262144 | tf_op jit(solution)/shard_map/all_to_all | solution.py:34
  148.1 2.2 %copy-start.9 = (bf16[128,4096]{1,0:T(8,128)(2,1)}, bf16[128,4096]{1,0:T(8,128)(2,1)S(1)}, u32[]{:S(2)}) copy-start(bf16[128,4096]{1,0:T(8,128)(2,1)S(1)} %get-tuple-element.29) | copy-start | bytes 3145732
  149.8 1.2 copy-start.8
  154.0 4.0 %copy-start.12 = (f32[26,2]{0,1:T(2,128)S(1)}, f32[26,2]{0,1:T(2,128)}, u32[]{:S(2)}) copy-start(f32[26,2]{0,1:T(2,128)} %copy-done.11) | copy-start | bytes 628
  161.7 2.5 %copy-start.10 = (bf16[128,4096]{1,0:T(8,128)(2,1)S(1)}, bf16[128,4096]{1,0:T(8,128)(2,1)}, u32[]{:S(2)}) copy-start(bf16[128,4096]{1,0:T(8,128)(2,1)} %copy-done.9) | copy-start | bytes 3145732
Sparse Core Ops, SparseCore 0:
  36.3 41.1 all-gather.1
  97.3 40.1 reduce-scatter.1

commit v17 on v12

--- a/solution.py
+++ b/solution.py
@@ -19,9 +19,7 @@
 
 
 def gather_rows(block, weights):
-    n = lax.axis_size("zh")
-    copies = jnp.tile(block, (n, 1))
-    block = lax.all_to_all(copies, "zh", 0, 0, tiled=True)
+    block = lax.all_gather(block, "zh", axis=0, tiled=True)
     block = lax.all_gather(block, "y", axis=0, tiled=True)
     block, weights = lax.optimization_barrier((block, weights))
     return (block, shifted(block, "core", 1)), weights

time: 164 us -> 166 us (1.012)
    all_to_all x1 -> x0, blocking collectives: 20.7 us -> none  [gather_rows(): block = lax.all_to_all(copies, 'zh', 0, 0, tiled=True)]
    all_gather x0 -> x1, blocking collectives: none -> 20 us  [gather_rows(): block = lax.all_gather(block, 'zh', axis=0, tiled=True)]
    unnamed x33 -> x32, local copies, waits for them, and re-layouts: 10.1 us -> 10.9 us
  transfers between devices with their start and end apart: 6 -> 6, of which waited for: 6 -> 6; matrix products, arithmetic and copies ran while one was open for 25% -> 26% of each run, Pallas kernels for 0% -> 0%
where the time goes in v17:
time: 166 us; the launch traced here: 165 us
  waiting for transfers between devices  58.1 us (35%)
  local copies, waits for them, and re-layouts  31.7 us (19%)
  matrix products  22.7 us (14%)
  blocking collectives  20 us (12%)
  starting transfers between devices  16.2 us (10%)
  between operations  14.3 us (9%)
  other arithmetic  2.2 us (1%)
    reduce_scatter x1, waiting for transfers between devices, scatter_rows(): block = lax.psum_scatter(block, 'y', scatter_dimension=0, tiled=True)  23 us
    all_gather x1, waiting for transfers between devices, gather_rows(): block = lax.all_gather(block, 'y', axis=0, tiled=True)  22.1 us
    all_gather x1, blocking collectives, gather_rows(): block = lax.all_gather(block, 'zh', axis=0, tiled=True)  20 us
    unnamed x32, local copies, waits for them, and re-layouts  10.9 us
    convert_element_type x2, local copies, waits for them, and re-layouts, dense_in(): return placed.astype(jnp.bfloat16).reshape(width, hidden_units)  7.64 us
    all_to_all x1, starting transfers between devices, scatter_rows(): got = lax.all_to_all(block, 'zh', 0, 0, tiled=True).astype(jnp.float32)  7.36 us
    reshape x1, local copies, waits for them, and re-layouts, dense_down(): return placed.astype(jnp.bfloat16).reshape(hidden_units, width)  6.17 us
    all_to_all x1, waiting for transfers between devices, scatter_rows(): got = lax.all_to_all(block, 'zh', 0, 0, tiled=True).astype(jnp.float32)  5.94 us
  transfers between devices with their start and end apart: 6, of which 6 were waited for; matrix products, arithmetic and copies ran while one was open for 26% of the time, Pallas kernels for 0%

profile of v17, /device:TPU:6, one launch (start us, length us, event | category | flops | bytes accessed | tf_op | source)
XLA Modules:
  0.0 165.4 jit_solution(2747356973654563038)
XLA Ops:
  7.2 4.5 %collective-permute-start = (bf16[1,4,4096]{2,1,0:T(4,128)(2,1)}, bf16[1,4,4096]{2,1,0:T(4,128)(2,1)S(1)}, u32[]{:S(2)}, u32[]{:S(2)}) collective-permute-start(bf16[1,4,4096]{2,1,0:T(4,128)(2,1)} %param.7), channel_id=1, source_target_pairs={{64,0},{128,64},{192,128},{256,192},{320,256},{384,320},{448,384},... | collective-permute-start | bytes 98312 | tf_op jit(solution)/shard_map/ppermute | solution.py:13
  11.8 1.9 %collective-permute-done = bf16[1,4,4096]{2,1,0:T(4,128)(2,1)S(1)} collective-permute-done((bf16[1,4,4096]{2,1,0:T(4,128)(2,1)}, bf16[1,4,4096]{2,1,0:T(4,128)(2,1)S(1)}, u32[]{:S(2)}, u32[]{:S(2)}) %collective-permute-start) | collective-permute-done | bytes 32800 | tf_op jit(solution)/shard_map/ppermute | solution.py:13
  14.4 20.0 %all-gather = bf16[4,4,8192]{2,1,0:T(4,128)(2,1)S(1)} all-gather(bf16[1,4,8192]{2,1,0:T(4,128)(2,1)S(1)} %maximum_bitcast_fusion), channel_id=1, replica_groups=mesh['section'=8,'y'=8,'zh'=4,'core'=2] {'zh'}, dimensions={0}, use_global_device_ids=true | all-gather | bytes 327680 | tf_op jit(solution)/shard_map/all_gather | solution.py:22
  36.1 2.1 %convert_bitcast_fusion = bf16[32,128,2,128]{3,0,1,2:T(8,128)(2,1)S(1)} fusion(bf16[26,128,128]{2,1,0:T(8,128)(2,1)} %bitcast.131, f32[26,32]{1,0:T(8,128)S(1)} %fusion.63, f32[26,2]{0,1:T(2,128)S(1)} %compare_convert_fusion), kind=kOutput, calls=%fused_computation.23 | convolution fusion | flops 55576192 | bytes 2952656 | tf_op jit(solution)/shard_map/kr,kc,kbn->rbcn/dot_general | solution.py:60
  38.2 3.8 %copy.41 = bf16[32,128,2,128]{1,0,3,2:T(8,128)(2,1)} copy(bf16[32,128,2,128]{3,0,1,2:T(8,128)(2,1)S(1)} %convert_bitcast_fusion) | data formatting | bytes 4194304 | tf_op jit(solution)/shard_map/convert_element_type | solution.py:64
  42.0 0.9 convert_bitcast_fusion.1
  42.9 3.8 %copy.38 = bf16[32,128,2,128]{1,0,3,2:T(8,128)(2,1)} copy(bf16[32,128,2,128]{3,0,1,2:T(8,128)(2,1)S(1)} %convert_bitcast_fusion.1) | data formatting | bytes 4194304 | tf_op jit(solution)/shard_map/convert_element_type | solution.py:64
  46.7 2.7 %copy.93 = bf16[32,8,32,128]{3,1,2,0:T(8,128)(2,1)S(1)} copy(bf16[32,8,32,128]{3,2,1,0:T(8,128)(2,1)} %bitcast.127) | data formatting | bytes 4194304
  49.4 0.9 convolution_convert_fusion.3
  51.0 6.2 %copy_bitcast_fusion = (bf16[256,4096]{1,0:T(8,128)(2,1)}, bf16[4096,256]{0,1:T(8,128)(2,1)}) fusion(bf16[32,8,32,128]{3,2,1,0:T(8,128)(2,1)S(1)} %bitcast.130, bf16[32,8,32,128]{3,2,1,0:T(8,128)(2,1)S(1)} %bitcast.129), kind=kLoop, calls=%fused_computation.9 | loop fusion | bytes 8388608 | tf_op jit(solution)/shard_map/reshape | solution.py:71
  57.2 22.1 %all-gather.3.cloned.1.call-done = bf16[128,8192]{1,0:T(8,128)(2,1)} async-done(((bf16[16,8192]{1,0:T(8,128)(2,1)}), bf16[128,8192]{1,0:T(8,128)(2,1)}) %all-gather.3.cloned.1.call-update) | async-done | bytes 2097168 | tf_op jit(solution)/shard_map/all_gather | solution.py:23
  79.2 2.1 %collective-permute-start.1 = (bf16[128,8192]{1,0:T(8,128)(2,1)}, bf16[128,8192]{1,0:T(8,128)(2,1)S(1)}, u32[]{:S(2)}, u32[]{:S(2)}) collective-permute-start(bf16[128,8192]{1,0:T(8,128)(2,1)} %all-gather.3.cloned.1.call-done), channel_id=1, source_target_pairs={{0,1},{1,0},{2,3},{3,2},{4,5},{5,4},{6,7},{7,6},{8,9},{9,8},{10,11... | collective-permute-start | bytes 6291464 | tf_op jit(solution)/shard_map/ppermute | solution.py:18
  81.3 4.2 %collective-permute-done.1 = bf16[128,8192]{1,0:T(8,128)(2,1)S(1)} collective-permute-done((bf16[128,8192]{1,0:T(8,128)(2,1)}, bf16[128,8192]{1,0:T(8,128)(2,1)S(1)}, u32[]{:S(2)}, u32[]{:S(2)}) %collective-permute-start.1) | collective-permute-done | bytes 2097184 | tf_op jit(solution)/shard_map/ppermute | solution.py:18
  85.5 3.2 %fusion.67 = f32[128,256]{1,0:T(8,128)S(1)} fusion(bf16[256,4096]{1,0:T(8,128)(2,1)} %get-tuple-element.9, bf16[128,8192]{1,0:T(8,128)(2,1)S(1)} %collective-permute-done.1), kind=kOutput, calls=%fused_computation.90 | convolution fusion | flops 268435456 | bytes 3276800 | tf_op jit(solution)/shard_map/dot_general | solution.py:107
  92.1 2.2 %collective-permute-start.2 = (f32[128,4096]{1,0:T(8,128)S(1)}, f32[128,4096]{1,0:T(8,128)S(1)}, u32[]{:S(2)}, u32[]{:S(2)}) collective-permute-start(f32[128,4096]{1,0:T(8,128)S(1)} %convolution_add_fusion), channel_id=1, source_target_pairs={{0,1},{1,0},{2,3},{3,2},{4,5},{5,4},{6,7},{7,6},{8,9},{9,8},{10,11... | collective-permute-start | bytes 6291464 | tf_op jit(solution)/shard_map/ppermute | solution.py:18
  96.0 0.8 multiply_convert_fusion.1
  97.3 1.0 collective-permute-done.2
  98.3 1.5 fusion.1
  100.2 1.4 copy-done.5
  103.9 1.2 copy.49
  105.1 2.1 %convolution_convert_fusion.1 = bf16[4096,256]{1,0:T(8,128)(2,1)} fusion(bf16[128,4096]{1,0:T(8,128)(2,1)S(1)} %get-tuple-element.27, bf16[128,4096]{1,0:T(8,128)(2,1)S(1)} %get-tuple-element.25, bf16[128,256]{1,0:T(8,128)(2,1)S(1)} %get-tuple-element.33, bf16[128,256]{1,0:T(8,128)(2,1)S(1)} %get-tuple-element.30), kind=kOutput, calls=%fused_computation.1 | convolution fusion | flops 542375936 | bytes 4325376 | tf_op jit(solution)/shard_map/dot_general | solution.py:121
  107.2 2.5 %reshape.91 = bf16[32,128,2,128]{3,2,1,0:T(2,128)(2,1)S(1)} reshape(bf16[4096,256]{1,0:T(8,128)(2,1)} %convolution_convert_fusion.1) | data formatting | bytes 4194304 | tf_op jit(solution)/shard_map/reshape | solution.py:74
  109.8 1.5 fusion.23
  111.3 1.2 copy.48
  112.5 2.1 %convolution_convert_fusion.2 = bf16[4096,256]{1,0:T(8,128)(2,1)} fusion(bf16[128,4096]{1,0:T(8,128)(2,1)S(1)} %copy-done.10, bf16[128,4096]{1,0:T(8,128)(2,1)S(1)} %get-tuple-element.25, bf16[128,256]{1,0:T(8,128)(2,1)S(1)} %get-tuple-element.32, bf16[128,256]{1,0:T(8,128)(2,1)S(1)} %get-tuple-element.29), kind=kOutput, calls=%fused_computation.2 | convolution fusion | flops 542375936 | bytes 4325376 | tf_op jit(solution)/shard_map/dot_general | solution.py:120
  114.6 2.5 %reshape.90 = bf16[32,128,2,128]{3,2,1,0:T(2,128)(2,1)S(1)} reshape(bf16[4096,256]{1,0:T(8,128)(2,1)} %convolution_convert_fusion.2) | data formatting | bytes 4194304 | tf_op jit(solution)/shard_map/reshape | solution.py:74
  117.2 23.0 %reduce-scatter.2.cloned.1.call-done = bf16[16,4096]{1,0:T(8,128)(2,1)} async-done(((bf16[128,4096]{1,0:T(8,128)(2,1)}), bf16[16,4096]{1,0:T(8,128)(2,1)}) %reduce-scatter.2.cloned.1.call-update) | async-done | bytes 131088 | tf_op jit(solution)/shard_map/reduce_scatter | solution.py:30
  140.2 1.6 all_to_all.6
  141.8 7.4 %all-to-all-start = ((bf16[4,4,4096]{2,1,0:T(4,128)(2,1)}), bf16[4,4,4096]{2,1,0:T(4,128)(2,1)S(1)}, u32[]{:S(2)}, u32[]{:S(2)}) async-start(bf16[4,4,4096]{2,1,0:T(4,128)(2,1)} %all_to_all.6), calls=%async_computation.1 | async-start | bytes 262144 | tf_op jit(solution)/shard_map/all_to_all | solution.py:32
  149.1 1.5 fusion.20
  150.7 1.2 copy.47
  151.9 5.9 %all-to-all-done = bf16[4,4,4096]{2,1,0:T(4,128)(2,1)S(1)} async-done(((bf16[4,4,4096]{2,1,0:T(4,128)(2,1)}), bf16[4,4,4096]{2,1,0:T(4,128)(2,1)S(1)}, u32[]{:S(2)}, u32[]{:S(2)}) %all-to-all-start) | async-done | bytes 131104 | tf_op jit(solution)/shard_map/all_to_all | solution.py:32
  (48 shorter events, 11.8 us)
Async XLA Ops:
  7.2 72.1 %all-gather.3.cloned.1.call-start = ((), (), s32[]{:S(2)}) async-start(), calls=%async_computation.2 | async-start | bytes 2359296 | tf_op jit(solution)/shard_map/all_gather | solution.py:23
  7.2 6.4 %collective-permute-start = (bf16[1,4,4096]{2,1,0:T(4,128)(2,1)}, bf16[1,4,4096]{2,1,0:T(4,128)(2,1)S(1)}, u32[]{:S(2)}, u32[]{:S(2)}) collective-permute-start(bf16[1,4,4096]{2,1,0:T(4,128)(2,1)} %param.7), channel_id=1, source_target_pairs={{64,0},{128,64},{192,128},{256,192},{320,256},{384,320},{448,384},... | collective-permute-start | bytes 98312 | tf_op jit(solution)/shard_map/ppermute | solution.py:13
  35.3 104.9 %reduce-scatter.2.cloned.1.call-start = ((), (), s32[]{:S(2)}) async-start(), calls=%async_computation.3 | async-start | bytes 1179648 | tf_op jit(solution)/shard_map/reduce_scatter | solution.py:30
  36.0 13.4 %copy-start.11 = (f32[26,2]{0,1:T(2,128)}, f32[26,2]{0,1:T(2,128)S(1)}, u32[]{:S(2)}) copy-start(f32[26,2]{0,1:T(2,128)S(1)} %compare_convert_fusion) | copy-start | bytes 628
  38.2 3.8 %copy-start.7 = (bf16[1,26,128,128]{3,2,1,0:T(8,128)(2,1)S(1)}, bf16[1,26,128,128]{3,2,1,0:T(8,128)(2,1)}, u32[]{:S(2)}) copy-start(bf16[1,26,128,128]{3,2,1,0:T(8,128)(2,1)} %param.9) | copy-start | bytes 2555908
  46.7 2.7 %copy-start.8 = (bf16[1,26,128,128]{3,2,1,0:T(8,128)(2,1)S(1)}, bf16[1,26,128,128]{3,2,1,0:T(8,128)(2,1)}, u32[]{:S(2)}) copy-start(bf16[1,26,128,128]{3,2,1,0:T(8,128)(2,1)} %param.11) | copy-start | bytes 2555908
  49.4 1.6 copy-start.6
  79.2 6.3 %collective-permute-start.1 = (bf16[128,8192]{1,0:T(8,128)(2,1)}, bf16[128,8192]{1,0:T(8,128)(2,1)S(1)}, u32[]{:S(2)}, u32[]{:S(2)}) collective-permute-start(bf16[128,8192]{1,0:T(8,128)(2,1)} %all-gather.3.cloned.1.call-done), channel_id=1, source_target_pairs={{0,1},{1,0},{2,3},{3,2},{4,5},{5,4},{6,7},{7,6},{8,9},{9,8},{10,11... | collective-permute-start | bytes 6291464 | tf_op jit(solution)/shard_map/ppermute | solution.py:18
  85.5 4.0 %copy-start.4 = (bf16[128,8192]{1,0:T(8,128)(2,1)}, bf16[128,8192]{1,0:T(8,128)(2,1)S(1)}, u32[]{:S(2)}) copy-start(bf16[128,8192]{1,0:T(8,128)(2,1)S(1)} %collective-permute-done.1) | copy-start | bytes 6291460
  88.7 1.6 copy-start
  91.6 2.7 %copy-start.1 = (bf16[256,4096]{1,0:T(8,128)(2,1)S(1)}, bf16[256,4096]{1,0:T(8,128)(2,1)}, u32[]{:S(2)}) copy-start(bf16[256,4096]{1,0:T(8,128)(2,1)} %get-tuple-element.9) | copy-start | bytes 6291460
  91.6 2.7 %copy-start.2 = (bf16[128,8192]{1,0:T(8,128)(2,1)S(1)}, bf16[128,8192]{1,0:T(8,128)(2,1)}, u32[]{:S(2)}) copy-start(bf16[128,8192]{1,0:T(8,128)(2,1)} %all-gather.3.cloned.1.call-done) | copy-start | bytes 6291460
  92.1 6.2 %collective-permute-start.2 = (f32[128,4096]{1,0:T(8,128)S(1)}, f32[128,4096]{1,0:T(8,128)S(1)}, u32[]{:S(2)}, u32[]{:S(2)}) collective-permute-start(f32[128,4096]{1,0:T(8,128)S(1)} %convolution_add_fusion), channel_id=1, source_target_pairs={{0,1},{1,0},{2,3},{3,2},{4,5},{5,4},{6,7},{7,6},{8,9},{9,8},{10,11... | collective-permute-start | bytes 6291464 | tf_op jit(solution)/shard_map/ppermute | solution.py:18
  98.3 1.8 %copy-start.3 = (bf16[128,8192]{1,0:T(8,128)(2,1)S(1)}, bf16[128,8192]{1,0:T(8,128)(2,1)}, u32[]{:S(2)}) copy-start(bf16[128,8192]{1,0:T(8,128)(2,1)} %all-gather.3.cloned.1.call-done) | copy-start | bytes 6291460
  100.1 1.6 copy-start.5
  101.9 3.2 %copy-start.9 = (bf16[128,4096]{1,0:T(8,128)(2,1)}, bf16[128,4096]{1,0:T(8,128)(2,1)S(1)}, u32[]{:S(2)}) copy-start(bf16[128,4096]{1,0:T(8,128)(2,1)S(1)} %get-tuple-element.27) | copy-start | bytes 3145732
  102.6 0.7 copy-start.12
  109.7 2.8 %copy-start.10 = (bf16[128,4096]{1,0:T(8,128)(2,1)S(1)}, bf16[128,4096]{1,0:T(8,128)(2,1)}, u32[]{:S(2)}) copy-start(bf16[128,4096]{1,0:T(8,128)(2,1)} %copy-done.9) | copy-start | bytes 3145732
  141.8 16.1 %all-to-all-start = ((bf16[4,4,4096]{2,1,0:T(4,128)(2,1)}), bf16[4,4,4096]{2,1,0:T(4,128)(2,1)S(1)}, u32[]{:S(2)}, u32[]{:S(2)}) async-start(bf16[4,4,4096]{2,1,0:T(4,128)(2,1)} %all_to_all.6), calls=%async_computation.1 | async-start | bytes 262144 | tf_op jit(solution)/shard_map/all_to_all | solution.py:32
Sparse Core Ops, SparseCore 0:
  35.4 43.7 all-gather.2
  100.0 40.1 reduce-scatter.1

commit v18 on v12

--- a/solution.py
+++ b/solution.py
@@ -28,7 +28,8 @@
 
 
 def scatter_rows(own, other):
-    block = (own + shifted(other, "core", 1)).astype(jnp.bfloat16)
+    sent = shifted(other.astype(jnp.bfloat16), "core", 1)
+    block = (own + sent.astype(jnp.float32)).astype(jnp.bfloat16)
     block = lax.psum_scatter(block, "y", scatter_dimension=0, tiled=True)
     n = lax.axis_size("zh")
     got = lax.all_to_all(block, "zh", 0, 0, tiled=True).astype(jnp.float32)

time: 164 us -> 164 us (level)
  transfers between devices with their start and end apart: 6 -> 6, of which waited for: 6 -> 5; matrix products, arithmetic and copies ran while one was open for 25% -> 25% of each run, Pallas kernels for 0% -> 0%
where the time goes in v18:
time: 164 us; the launch traced here: 163 us
  waiting for transfers between devices  55.9 us (34%)
  local copies, waits for them, and re-layouts  31.5 us (19%)
  matrix products  21.7 us (13%)
  blocking collectives  20.7 us (13%)
  starting transfers between devices  16.4 us (10%)
  between operations  14.4 us (9%)
  other arithmetic  2.2 us (1%)
    reduce_scatter x1, waiting for transfers between devices, scatter_rows(): block = lax.psum_scatter(block, 'y', scatter_dimension=0, tiled=True)  23.2 us
    all_gather x1, waiting for transfers between devices, gather_rows(): block = lax.all_gather(block, 'y', axis=0, tiled=True)  20.7 us
    all_to_all x1, blocking collectives, gather_rows(): block = lax.all_to_all(copies, 'zh', 0, 0, tiled=True)  20.7 us
    unnamed x33, local copies, waits for them, and re-layouts  9.85 us
    convert_element_type x2, local copies, waits for them, and re-layouts, dense_in(): return placed.astype(jnp.bfloat16).reshape(width, hidden_units)  7.63 us
    all_to_all x1, starting transfers between devices, scatter_rows(): got = lax.all_to_all(block, 'zh', 0, 0, tiled=True).astype(jnp.float32)  7.34 us
    reshape x1, local copies, waits for them, and re-layouts, dense_down(): return placed.astype(jnp.bfloat16).reshape(hidden_units, width)  6.13 us
    all_to_all x1, waiting for transfers between devices, scatter_rows(): got = lax.all_to_all(block, 'zh', 0, 0, tiled=True).astype(jnp.float32)  5.94 us
  transfers between devices with their start and end apart: 6, of which 5 were waited for; matrix products, arithmetic and copies ran while one was open for 25% of the time, Pallas kernels for 0%

profile of v18, /device:TPU:6, one launch (start us, length us, event | category | flops | bytes accessed | tf_op | source)
XLA Modules:
  0.0 162.7 jit_solution(7650188837550491801)
XLA Ops:
  7.2 4.7 %collective-permute-start = (bf16[1,4,4096]{2,1,0:T(4,128)(2,1)}, bf16[1,4,4096]{2,1,0:T(4,128)(2,1)S(1)}, u32[]{:S(2)}, u32[]{:S(2)}) collective-permute-start(bf16[1,4,4096]{2,1,0:T(4,128)(2,1)} %param.7), channel_id=1, source_target_pairs={{64,0},{128,64},{192,128},{256,192},{320,256},{384,320},{448,384},... | collective-permute-start | bytes 98312 | tf_op jit(solution)/shard_map/ppermute | solution.py:13
  11.9 1.9 %collective-permute-done = bf16[1,4,4096]{2,1,0:T(4,128)(2,1)S(1)} collective-permute-done((bf16[1,4,4096]{2,1,0:T(4,128)(2,1)}, bf16[1,4,4096]{2,1,0:T(4,128)(2,1)S(1)}, u32[]{:S(2)}, u32[]{:S(2)}) %collective-permute-start) | collective-permute-done | bytes 32800 | tf_op jit(solution)/shard_map/ppermute | solution.py:13
  14.7 20.7 %all_to_all.18 = bf16[4,4,8192]{2,1,0:T(4,128)(2,1)S(1)} all-to-all(bf16[4,4,8192]{2,1,0:T(4,128)(2,1)S(1)} %tile.2), channel_id=1, replica_groups=mesh['section'=8,'y'=8,'zh'=4,'core'=2] {'zh'}, dimensions={0} | all-to-all | bytes 524288 | tf_op jit(solution)/shard_map/all_to_all | solution.py:24
  36.9 0.9 convert_bitcast_fusion
  37.9 3.8 %copy.27 = bf16[32,128,2,128]{1,0,3,2:T(8,128)(2,1)} copy(bf16[32,128,2,128]{3,0,1,2:T(8,128)(2,1)S(1)} %convert_bitcast_fusion) | data formatting | bytes 4194304 | tf_op jit(solution)/shard_map/convert_element_type | solution.py:67
  41.7 0.9 convert_bitcast_fusion.1
  42.6 3.8 %copy.24 = bf16[32,128,2,128]{1,0,3,2:T(8,128)(2,1)} copy(bf16[32,128,2,128]{3,0,1,2:T(8,128)(2,1)S(1)} %convert_bitcast_fusion.1) | data formatting | bytes 4194304 | tf_op jit(solution)/shard_map/convert_element_type | solution.py:67
  46.4 2.7 %copy.79 = bf16[32,8,32,128]{3,1,2,0:T(8,128)(2,1)S(1)} copy(bf16[32,8,32,128]{3,2,1,0:T(8,128)(2,1)} %bitcast.125) | data formatting | bytes 4194304
  49.1 0.9 convolution_convert_fusion.3
  50.7 6.1 %copy_bitcast_fusion = (bf16[256,4096]{1,0:T(8,128)(2,1)}, bf16[4096,256]{0,1:T(8,128)(2,1)}) fusion(bf16[32,8,32,128]{3,2,1,0:T(8,128)(2,1)S(1)} %bitcast.128, bf16[32,8,32,128]{3,2,1,0:T(8,128)(2,1)S(1)} %bitcast.127), kind=kLoop, calls=%fused_computation.8 | loop fusion | bytes 8388608 | tf_op jit(solution)/shard_map/reshape | solution.py:74
  56.8 20.7 %all-gather.2.cloned.1.call-done = bf16[128,8192]{1,0:T(8,128)(2,1)} async-done(((bf16[16,8192]{1,0:T(8,128)(2,1)}), bf16[128,8192]{1,0:T(8,128)(2,1)}) %all-gather.2.cloned.1.call-update) | async-done | bytes 2097168 | tf_op jit(solution)/shard_map/all_gather | solution.py:25
  77.5 2.1 %collective-permute-start.1 = (bf16[128,8192]{1,0:T(8,128)(2,1)}, bf16[128,8192]{1,0:T(8,128)(2,1)S(1)}, u32[]{:S(2)}, u32[]{:S(2)}) collective-permute-start(bf16[128,8192]{1,0:T(8,128)(2,1)} %all-gather.2.cloned.1.call-done), channel_id=1, source_target_pairs={{0,1},{1,0},{2,3},{3,2},{4,5},{5,4},{6,7},{7,6},{8,9},{9,8},{10,11... | collective-permute-start | bytes 6291464 | tf_op jit(solution)/shard_map/ppermute | solution.py:18
  79.6 4.2 %collective-permute-done.1 = bf16[128,8192]{1,0:T(8,128)(2,1)S(1)} collective-permute-done((bf16[128,8192]{1,0:T(8,128)(2,1)}, bf16[128,8192]{1,0:T(8,128)(2,1)S(1)}, u32[]{:S(2)}, u32[]{:S(2)}) %collective-permute-start.1) | collective-permute-done | bytes 2097184 | tf_op jit(solution)/shard_map/ppermute | solution.py:18
  83.7 3.2 %fusion.66 = f32[128,256]{1,0:T(8,128)S(1)} fusion(bf16[256,4096]{1,0:T(8,128)(2,1)} %get-tuple-element.9, bf16[128,8192]{1,0:T(8,128)(2,1)S(1)} %collective-permute-done.1), kind=kOutput, calls=%fused_computation.90 | convolution fusion | flops 268435456 | bytes 3276800 | tf_op jit(solution)/shard_map/dot_general | solution.py:110
  88.5 0.8 multiply_convert_fusion
  90.3 2.2 %collective-permute-start.2 = (bf16[128,4096]{1,0:T(8,128)(2,1)S(1)}, bf16[128,4096]{1,0:T(8,128)(2,1)S(1)}, u32[]{:S(2)}, u32[]{:S(2)}) collective-permute-start(bf16[128,4096]{1,0:T(8,128)(2,1)S(1)} %fusion), channel_id=1, source_target_pairs={{0,1},{1,0},{2,3},{3,2},{4,5},{5,4},{6,7},{7,6},{8,9},{9,8},{10,11... | collective-permute-start | bytes 3145736 | tf_op jit(solution)/shard_map/ppermute | solution.py:18
  94.2 0.8 multiply_convert_fusion.1
  95.5 1.6 %add_convert_fusion = bf16[128,4096]{1,0:T(8,128)(2,1)} fusion(bf16[128,4096]{1,0:T(8,128)(2,1)S(1)} %collective-permute-done.2, f32[128,4096]{1,0:T(8,128)S(1)} %fusion.80, bf16[128,256]{1,0:T(8,128)(2,1)S(1)} %get-tuple-element.26, bf16[4096,256]{0,1:T(8,128)(2,1)S(1)} %copy-done), kind=kOutput, calls=%fused_computation.22 | convolution fusion | flops 270532608 | bytes 6356992 | tf_op jit(solution)/shard_map/dot_general | solution.py:114
  97.4 1.4 copy-done.5
  101.0 1.2 copy.35
  102.2 2.1 %convolution_convert_fusion.1 = bf16[4096,256]{1,0:T(8,128)(2,1)} fusion(bf16[128,4096]{1,0:T(8,128)(2,1)S(1)} %get-tuple-element.23, bf16[128,4096]{1,0:T(8,128)(2,1)S(1)} %get-tuple-element.21, bf16[128,256]{1,0:T(8,128)(2,1)S(1)} %get-tuple-element.29, bf16[128,256]{1,0:T(8,128)(2,1)S(1)} %get-tuple-element.26), kind=kOutput, calls=%fused_computation.1 | convolution fusion | flops 542375936 | bytes 4325376 | tf_op jit(solution)/shard_map/dot_general | solution.py:124
  104.3 2.5 %reshape.98 = bf16[32,128,2,128]{3,2,1,0:T(2,128)(2,1)S(1)} reshape(bf16[4096,256]{1,0:T(8,128)(2,1)} %convolution_convert_fusion.1) | data formatting | bytes 4194304 | tf_op jit(solution)/shard_map/reshape | solution.py:77
  106.9 1.5 fusion.22
  108.5 1.2 copy.34
  109.7 2.1 %convolution_convert_fusion.2 = bf16[4096,256]{1,0:T(8,128)(2,1)} fusion(bf16[128,4096]{1,0:T(8,128)(2,1)S(1)} %copy-done.11, bf16[128,4096]{1,0:T(8,128)(2,1)S(1)} %get-tuple-element.21, bf16[128,256]{1,0:T(8,128)(2,1)S(1)} %get-tuple-element.28, bf16[128,256]{1,0:T(8,128)(2,1)S(1)} %get-tuple-element.25), kind=kOutput, calls=%fused_computation.2 | convolution fusion | flops 542375936 | bytes 4325376 | tf_op jit(solution)/shard_map/dot_general | solution.py:123
  111.8 2.5 %reshape.97 = bf16[32,128,2,128]{3,2,1,0:T(2,128)(2,1)S(1)} reshape(bf16[4096,256]{1,0:T(8,128)(2,1)} %convolution_convert_fusion.2) | data formatting | bytes 4194304 | tf_op jit(solution)/shard_map/reshape | solution.py:77
  114.4 23.2 %reduce-scatter.2.cloned.1.call-done = bf16[16,4096]{1,0:T(8,128)(2,1)} async-done(((bf16[128,4096]{1,0:T(8,128)(2,1)}), bf16[16,4096]{1,0:T(8,128)(2,1)}) %reduce-scatter.2.cloned.1.call-update) | async-done | bytes 131088 | tf_op jit(solution)/shard_map/reduce_scatter | solution.py:33
  137.5 1.6 all_to_all.14
  139.1 7.3 %all-to-all-start.1 = ((bf16[4,4,4096]{2,1,0:T(4,128)(2,1)}), bf16[4,4,4096]{2,1,0:T(4,128)(2,1)S(1)}, u32[]{:S(2)}, u32[]{:S(2)}) async-start(bf16[4,4,4096]{2,1,0:T(4,128)(2,1)} %all_to_all.14), calls=%async_computation.2 | async-start | bytes 262144 | tf_op jit(solution)/shard_map/all_to_all | solution.py:35
  146.5 1.5 fusion.19
  148.0 1.2 copy.33
  149.3 5.9 %all-to-all-done.1 = bf16[4,4,4096]{2,1,0:T(4,128)(2,1)S(1)} async-done(((bf16[4,4,4096]{2,1,0:T(4,128)(2,1)}), bf16[4,4,4096]{2,1,0:T(4,128)(2,1)S(1)}, u32[]{:S(2)}, u32[]{:S(2)}) %all-to-all-start.1) | async-done | bytes 131104 | tf_op jit(solution)/shard_map/all_to_all | solution.py:35
  (51 shorter events, 10.7 us)
Async XLA Ops:
  7.2 29.8 %copy-start.7 = (bf16[1,26,128,128]{3,2,1,0:T(8,128)(2,1)S(1)}, bf16[1,26,128,128]{3,2,1,0:T(8,128)(2,1)}, u32[]{:S(2)}) copy-start(bf16[1,26,128,128]{3,2,1,0:T(8,128)(2,1)} %param.10) | copy-start | bytes 2555908
  7.2 70.3 %all-gather.2.cloned.1.call-start = ((), (), s32[]{:S(2)}) async-start(), calls=%async_computation.3 | async-start | bytes 2359296 | tf_op jit(solution)/shard_map/all_gather | solution.py:25
  7.2 6.6 %collective-permute-start = (bf16[1,4,4096]{2,1,0:T(4,128)(2,1)}, bf16[1,4,4096]{2,1,0:T(4,128)(2,1)S(1)}, u32[]{:S(2)}, u32[]{:S(2)}) collective-permute-start(bf16[1,4,4096]{2,1,0:T(4,128)(2,1)} %param.7), channel_id=1, source_target_pairs={{64,0},{128,64},{192,128},{256,192},{320,256},{384,320},{448,384},... | collective-permute-start | bytes 98312 | tf_op jit(solution)/shard_map/ppermute | solution.py:13
  36.1 101.4 %reduce-scatter.2.cloned.1.call-start = ((), (), s32[]{:S(2)}) async-start(), calls=%async_computation.4 | async-start | bytes 1179648 | tf_op jit(solution)/shard_map/reduce_scatter | solution.py:33
  36.9 12.2 %copy-start.12 = (f32[26,2]{0,1:T(2,128)}, f32[26,2]{0,1:T(2,128)S(1)}, u32[]{:S(2)}) copy-start(f32[26,2]{0,1:T(2,128)S(1)} %compare_convert_fusion) | copy-start | bytes 628
  37.8 3.8 %copy-start.8 = (bf16[1,26,128,128]{3,2,1,0:T(8,128)(2,1)S(1)}, bf16[1,26,128,128]{3,2,1,0:T(8,128)(2,1)}, u32[]{:S(2)}) copy-start(bf16[1,26,128,128]{3,2,1,0:T(8,128)(2,1)} %param.9) | copy-start | bytes 2555908
  46.4 2.7 %copy-start.9 = (bf16[1,26,128,128]{3,2,1,0:T(8,128)(2,1)S(1)}, bf16[1,26,128,128]{3,2,1,0:T(8,128)(2,1)}, u32[]{:S(2)}) copy-start(bf16[1,26,128,128]{3,2,1,0:T(8,128)(2,1)} %param.11) | copy-start | bytes 2555908
  49.1 1.6 copy-start.6
  77.5 6.3 %collective-permute-start.1 = (bf16[128,8192]{1,0:T(8,128)(2,1)}, bf16[128,8192]{1,0:T(8,128)(2,1)S(1)}, u32[]{:S(2)}, u32[]{:S(2)}) collective-permute-start(bf16[128,8192]{1,0:T(8,128)(2,1)} %all-gather.2.cloned.1.call-done), channel_id=1, source_target_pairs={{0,1},{1,0},{2,3},{3,2},{4,5},{5,4},{6,7},{7,6},{8,9},{9,8},{10,11... | collective-permute-start | bytes 6291464 | tf_op jit(solution)/shard_map/ppermute | solution.py:18
  83.7 4.0 %copy-start.4 = (bf16[128,8192]{1,0:T(8,128)(2,1)}, bf16[128,8192]{1,0:T(8,128)(2,1)S(1)}, u32[]{:S(2)}) copy-start(bf16[128,8192]{1,0:T(8,128)(2,1)S(1)} %collective-permute-done.1) | copy-start | bytes 6291460
  86.9 1.6 copy-start
  89.8 2.7 %copy-start.1 = (bf16[256,4096]{1,0:T(8,128)(2,1)S(1)}, bf16[256,4096]{1,0:T(8,128)(2,1)}, u32[]{:S(2)}) copy-start(bf16[256,4096]{1,0:T(8,128)(2,1)} %get-tuple-element.9) | copy-start | bytes 6291460
  89.8 2.7 %copy-start.2 = (bf16[128,8192]{1,0:T(8,128)(2,1)S(1)}, bf16[128,8192]{1,0:T(8,128)(2,1)}, u32[]{:S(2)}) copy-start(bf16[128,8192]{1,0:T(8,128)(2,1)} %all-gather.2.cloned.1.call-done) | copy-start | bytes 6291460
  90.3 5.2 %collective-permute-start.2 = (bf16[128,4096]{1,0:T(8,128)(2,1)S(1)}, bf16[128,4096]{1,0:T(8,128)(2,1)S(1)}, u32[]{:S(2)}, u32[]{:S(2)}) collective-permute-start(bf16[128,4096]{1,0:T(8,128)(2,1)S(1)} %fusion), channel_id=1, source_target_pairs={{0,1},{1,0},{2,3},{3,2},{4,5},{5,4},{6,7},{7,6},{8,9},{9,8},{10,11... | collective-permute-start | bytes 3145736 | tf_op jit(solution)/shard_map/ppermute | solution.py:18
  95.5 1.7 %copy-start.3 = (bf16[128,8192]{1,0:T(8,128)(2,1)S(1)}, bf16[128,8192]{1,0:T(8,128)(2,1)}, u32[]{:S(2)}) copy-start(bf16[128,8192]{1,0:T(8,128)(2,1)} %all-gather.2.cloned.1.call-done) | copy-start | bytes 6291460
  97.2 1.6 copy-start.5
  99.0 3.2 %copy-start.10 = (bf16[128,4096]{1,0:T(8,128)(2,1)}, bf16[128,4096]{1,0:T(8,128)(2,1)S(1)}, u32[]{:S(2)}) copy-start(bf16[128,4096]{1,0:T(8,128)(2,1)S(1)} %get-tuple-element.23) | copy-start | bytes 3145732
  99.7 0.7 copy-start.13
  106.9 2.8 %copy-start.11 = (bf16[128,4096]{1,0:T(8,128)(2,1)S(1)}, bf16[128,4096]{1,0:T(8,128)(2,1)}, u32[]{:S(2)}) copy-start(bf16[128,4096]{1,0:T(8,128)(2,1)} %copy-done.10) | copy-start | bytes 3145732
  139.1 16.1 %all-to-all-start.1 = ((bf16[4,4,4096]{2,1,0:T(4,128)(2,1)}), bf16[4,4,4096]{2,1,0:T(4,128)(2,1)S(1)}, u32[]{:S(2)}, u32[]{:S(2)}) async-start(bf16[4,4,4096]{2,1,0:T(4,128)(2,1)} %all_to_all.14), calls=%async_computation.2 | async-start | bytes 262144 | tf_op jit(solution)/shard_map/all_to_all | solution.py:35
Sparse Core Ops, SparseCore 0:
  36.3 41.1 all-gather.1
  97.3 40.1 reduce-scatter.1
